TPU v7x, 32 devices: a whole 2x2x4 slice. The times are simulated.
32 devices in a mesh: beam: 2 (over y), band: 16 (over z, x, core).
Axes of the slice: x: 2, y: 2, z: 4, core: 2. Of those that a mesh axis runs over, the one named last changes fastest.
Arguments:
- filterbank: float32 [1024, 6144], P(('beam', 'band')), parts along dimension 0, may hold values from -40 to 40
- offsets: int32 [9, 512], P(None, 'band'), may hold values from 0 to 255, as said below
- widths: int32 [8], replicated, may hold values from 1 to 128, as said below
Outputs:
- detection: float32 [1024, 2048], P(('beam', 'band')), parts along dimension 0
- peak_series: float32 [4096], P('beam'), parts along dimension 0
There are 2 independent parts, one for each index of `beam`. A program takes and returns all parts, laid end to end along the dimension named above; an argument that names none is the same for every part. Nothing has to cross between parts.
Inputs may be any that keep to these rules, and one draw needn't show every extreme that they name: `offsets`: in every section some offset equals 255. Among the 8 widths are 1 and 128.
All inputs are finite; a program needn't handle non-finite values.
Results may differ from a plain program's by a relative error of at most 0.0002.
Values sent between devices are 32-bit elements; how exact they have to be, the bound alone decides.
No kernel may reach another device: no remote copies, remote signals or barrier semaphores. Data moves between devices by JAX's collectives and lax.ppermute only.
A program may use at most 64 MiB of HBM per device.

v0:
```python
import math

import jax
import jax.numpy as jnp
from jax import lax
from jax.sharding import PartitionSpec as P

TS = 2048
TIN = 6144
SHIFT = 256
TAPS = 128
TEMPLATES = 8


def from_partner(value, axis, distance):
    mask = 2**distance
    pairs = [(source, source ^ mask) for source in range(lax.axis_size(axis))]
    return lax.ppermute(value, axis, pairs)


def shift_rows(trial_rows, amounts, length):
    current = jnp.pad(trial_rows, ((0, 0), (0, 2 * SHIFT)))
    top_bit = (SHIFT - 1).bit_length()
    for bit_index in reversed(range(top_bit)):
        span = 2**bit_index
        keep_len = length + span - 1
        chosen = (amounts >> bit_index & 1)[:, None] == 1
        current = jnp.where(chosen, current[:, span : span + keep_len], current[:, :keep_len])
    return current


def merge_section(current, offsets_now, section_index, new_length):
    group_trials = 2**section_index
    total_rows = current.shape[0]
    groups = total_rows // (2 * group_trials)
    blocks = current.reshape(groups, 2, group_trials, current.shape[1])
    lower_part = blocks[:, 0, :, :new_length]
    upper_flat = blocks[:, 1].reshape(groups * group_trials, current.shape[1])
    amounts = offsets_now.reshape(groups, 2, group_trials)
    first_half = lower_part + shift_rows(upper_flat, amounts[:, 0].reshape(-1), new_length).reshape(
        groups, group_trials, new_length
    )
    second_half = lower_part + shift_rows(
        upper_flat, amounts[:, 1].reshape(-1), new_length
    ).reshape(groups, group_trials, new_length)
    return jnp.stack([first_half, second_half], axis=1).reshape(total_rows, new_length)


def template_tables(widths):
    source = lax.broadcasted_iota(jnp.int32, (2 * TAPS, TAPS), 0)
    target = lax.broadcasted_iota(jnp.int32, (2 * TAPS, TAPS), 1)
    tap_offset = source - target
    inside = (tap_offset[None] >= 0) & (tap_offset[None] < widths[:, None, None])
    tap_scale = 1.0 / jnp.sqrt(widths.astype(jnp.float32))
    return jnp.where(inside, tap_scale[:, None, None], jnp.zeros((), jnp.float32))


def boxcar_max(dedispersed, widths):
    total_rows = dedispersed.shape[0]
    blocks_time = TS // TAPS
    window = dedispersed.reshape(total_rows, blocks_time + 1, TAPS)
    paired = jnp.concatenate([window[:, :-1], window[:, 1:]], axis=2).reshape(
        total_rows * blocks_time, 2 * TAPS
    )
    tables = template_tables(widths)
    best_value = None
    for template_index in range(TEMPLATES):
        result = jnp.dot(
            paired,
            tables[template_index],
            precision=lax.Precision.HIGHEST,
            preferred_element_type=jnp.float32,
        )
        if template_index == 0:
            best_value = result
        else:
            best_value = jnp.maximum(best_value, result)
    return best_value.reshape(total_rows, TS)


def per_device(filterbank, offsets, widths):
    levels = offsets.shape[0]
    local_count = filterbank.shape[0].bit_length() - 1
    band_count = lax.axis_size("band")
    channels_all = filterbank.shape[0] * band_count

    def length_after(sections_done):
        needed = TS + TAPS + (levels - sections_done) * (SHIFT - 1)
        needed = -(-needed // 128) * 128
        return min(TIN, needed)

    partial_value = jnp.sum(filterbank, axis=0)
    channel_mean = lax.psum(partial_value, "band") / channels_all
    current = filterbank - channel_mean[None, :]
    for local_section_index in range(local_count):
        current = merge_section(
            current,
            offsets[local_section_index],
            local_section_index,
            length_after(local_section_index + 1),
        )
    band_index = lax.axis_index("band")
    for bit_index in range(band_count.bit_length() - 1):
        section_index = local_count + bit_index
        new_length = length_after(section_index + 1)
        partner = from_partner(current, "band", bit_index)
        upper_half = band_index // 2**bit_index % 2 == 1
        lower_part = jnp.where(upper_half, partner, current)
        upper_part = jnp.where(upper_half, current, partner)
        current = lower_part[:, :new_length] + shift_rows(
            upper_part, offsets[section_index], new_length
        )
    dedispersed = current * (1.0 / math.sqrt(channels_all))
    detection = boxcar_max(dedispersed, widths)
    peak_series = lax.pmax(jnp.max(detection, axis=0), "band")
    return (detection, peak_series)


def solution(mesh):
    placed = (P(("beam", "band"), None), P(None, "band"), P())
    return jax.shard_map(
        per_device,
        mesh=mesh,
        in_specs=placed,
        out_specs=(P(("beam", "band"), None), P("beam")),
        check_vma=False,
    )
```

profile of v0, /device:TPU:0, one launch (start us, length us, event | category | flops | bytes accessed | tf_op | source)
XLA Modules:
  0.0 164.7 jit_solution(757025383159185364)
XLA Ops:
  0.6 1.3 reduce_sum.9
  1.9 62.9 %psum.7 = f32[6144]{0:T(1024)S(1)} all-reduce(f32[6144]{0:T(1024)S(1)} %reduce_sum.9), channel_id=1, replica_groups=mesh['beam'=2,'band'=16] {'band'}, use_global_device_ids=true, to_apply=%region_1.0 | all-reduce | flops 6144 | bytes 49152 | tf_op jit(solution)/shard_map/psum | solution.py:93
  64.9 0.5 reshape.1647
  65.6 0.4 slice.1058
  66.0 0.3 copy-done.2
  69.7 0.4 fusion.24
  70.1 0.2 compare_reduce_fusion.15
  73.5 0.2 slice_select_fusion.36
  73.7 0.2 fusion.5
  74.3 0.3 slice.1092
  77.4 0.6 copy_add_fusion.1
  77.9 0.5 pad_maximum_fusion.1
  78.5 0.3 reshape_reshape.10
  78.8 0.3 slice.1126
  81.4 0.6 copy_add_fusion.3
  81.9 0.4 pad_maximum_fusion.2
  83.6 0.3 slice_select_fusion.89
  86.8 1.7 %collective-permute-done = f32[32,3200]{1,0:T(8,128)S(1)} collective-permute-done((f32[32,3200]{1,0:T(8,128)S(1)}, f32[32,3200]{1,0:T(8,128)S(1)}, u32[]{:S(2)}, u32[]{:S(2)}) %collective-permute-start) | collective-permute-done | bytes 409632 | tf_op jit(solution)/shard_map/ppermute | solution.py:18
  90.0 10.8 %collective-permute-done.1 = f32[32,2944]{1,0:T(8,128)S(1)} collective-permute-done((f32[32,2944]{1,0:T(8,128)S(1)}, f32[32,2944]{1,0:T(8,128)S(1)}, u32[]{:S(2)}, u32[]{:S(2)}) %collective-permute-start.1) | collective-permute-done | bytes 376864 | tf_op jit(solution)/shard_map/ppermute | solution.py:18
  102.2 0.6 copy-done.3
  102.9 8.5 %collective-permute-done.2 = f32[32,2688]{1,0:T(8,128)S(1)} collective-permute-done((f32[32,2688]{1,0:T(8,128)S(1)}, f32[32,2688]{1,0:T(8,128)S(1)}, u32[]{:S(2)}, u32[]{:S(2)}) %collective-permute-start.2) | collective-permute-done | bytes 344096 | tf_op jit(solution)/shard_map/ppermute | solution.py:18
  112.8 0.2 and_select_fusion
  113.0 14.9 %collective-permute-done.3 = f32[32,2432]{1,0:T(8,128)S(1)} collective-permute-done((f32[32,2432]{1,0:T(8,128)S(1)}, f32[32,2432]{1,0:T(8,128)S(1)}, u32[]{:S(2)}, u32[]{:S(2)}) %collective-permute-start.3) | collective-permute-done | bytes 311328 | tf_op jit(solution)/shard_map/ppermute | solution.py:18
  129.3 0.6 fusion.15
  129.9 0.6 convolution_maximum_fusion.6
  130.5 0.6 convolution_maximum_fusion.5
  131.0 0.6 convolution_maximum_fusion.4
  131.6 0.6 convolution_maximum_fusion.3
  132.2 0.6 convolution_maximum_fusion.2
  132.8 0.6 convolution_maximum_fusion.1
  133.4 0.6 convolution_maximum_fusion
  134.1 30.6 %pmax.7 = f32[2048]{0:T(1024)} all-reduce(f32[2048]{0:T(1024)S(1)} %reduce_max.9), channel_id=1, replica_groups=mesh['beam'=2,'band'=16] {'band'}, use_global_device_ids=true, to_apply=%region_3.4 | all-reduce | flops 2048 | bytes 16384 | tf_op jit(solution)/shard_map/pmax | solution.py:115
  (204 shorter events, 21.2 us)
Async XLA Ops:
  0.6 64.2 %copy-start = (f32[32,6144]{1,0:T(8,128)S(1)}, f32[32,6144]{1,0:T(8,128)}, u32[]{:S(2)}) copy-start(f32[32,6144]{1,0:T(8,128)} %param.3) | copy-start | bytes 2359300
  65.6 0.7 copy-start.2
  86.7 1.8 %collective-permute-start = (f32[32,3200]{1,0:T(8,128)S(1)}, f32[32,3200]{1,0:T(8,128)S(1)}, u32[]{:S(2)}, u32[]{:S(2)}) collective-permute-start(f32[32,3200]{1,0:T(8,128)S(1)} %bitcast.180), channel_id=1, source_target_pairs={{0,1},{1,0},{2,3},{3,2},{4,5},{5,4},{6,7},{7,6},{8,9},{9,8},{10,11... | collective-permute-start | bytes 1228808 | tf_op jit(solution)/shard_map/ppermute | solution.py:18
  89.9 10.9 %collective-permute-start.1 = (f32[32,2944]{1,0:T(8,128)S(1)}, f32[32,2944]{1,0:T(8,128)S(1)}, u32[]{:S(2)}, u32[]{:S(2)}) collective-permute-start(f32[32,2944]{1,0:T(8,128)S(1)} %fusion), channel_id=1, source_target_pairs={{0,2},{1,3},{2,0},{3,1},{4,6},{5,7},{6,4},{7,5},{8,10},{9,11},{10,... | collective-permute-start | bytes 1130504 | tf_op jit(solution)/shard_map/ppermute | solution.py:18
  102.1 9.3 %collective-permute-start.2 = (f32[32,2688]{1,0:T(8,128)S(1)}, f32[32,2688]{1,0:T(8,128)S(1)}, u32[]{:S(2)}, u32[]{:S(2)}) collective-permute-start(f32[32,2688]{1,0:T(8,128)S(1)} %fusion.1), channel_id=1, source_target_pairs={{0,4},{1,5},{2,6},{3,7},{4,0},{5,1},{6,2},{7,3},{8,12},{9,13},{10,... | collective-permute-start | bytes 1032200 | tf_op jit(solution)/shard_map/ppermute | solution.py:18
  102.2 0.7 copy-start.3
  112.7 15.3 %collective-permute-start.3 = (f32[32,2432]{1,0:T(8,128)S(1)}, f32[32,2432]{1,0:T(8,128)S(1)}, u32[]{:S(2)}, u32[]{:S(2)}) collective-permute-start(f32[32,2432]{1,0:T(8,128)S(1)} %fusion.2), channel_id=1, source_target_pairs={{0,8},{1,9},{2,10},{3,11},{4,12},{5,13},{6,14},{7,15},{8,0},{9,1},... | collective-permute-start | bytes 933896 | tf_op jit(solution)/shard_map/ppermute | solution.py:18
  134.0 30.6 %copy-start.1 = (f32[32,2048]{1,0:T(8,128)}, f32[32,2048]{1,0:T(8,128)S(1)}, u32[]{:S(2)}) copy-start(f32[32,2048]{1,0:T(8,128)S(1)} %reshape.1657) | copy-start | bytes 786436
where the time goes:
time: 165 us
  blocking collectives  93.5 us (57%)
  waiting for transfers between devices  35.9 us (22%)
  other arithmetic  19.1 us (12%)
  local copies, waits for them, and re-layouts  9.32 us (6%)
  matrix products  4.65 us (3%)
  between operations  1.91 us (1%)
    psum x1, blocking collectives, per_device(): channel_mean = lax.psum(partial_value, 'band') / channels_all  62.9 us
    ppermute x4, waiting for transfers between devices, from_partner(): return lax.ppermute(value, axis, pairs)  35.9 us
    pmax x1, blocking collectives, per_device(): peak_series = lax.pmax(jnp.max(detection, axis=0), 'band')  30.6 us
    select_n x96, other arithmetic, shift_rows(): jnp.where(chosen, current[:, span:span + keep_len], current[:, :keep_len])  13 us
    dot_general x8, matrix products, boxcar_max(): jnp.dot(paired, tables[template_index], precision=lax.Precision.HIGHEST,...  4.65 us
    eq x48, local copies, waits for them, and re-layouts, shift_rows(): chosen = (amounts >> bit_index & 1)[:, None] == 1  4.15 us
  transfers between devices with their start and end apart: 4, of which 4 were waited for; matrix products, arithmetic and copies ran while one was open for 0% of the time, Pallas kernels for 0%

commit v1 on v0

--- a/solution.py
+++ b/solution.py
@@ -16,6 +16,12 @@
     mask = 2**distance
     pairs = [(source, source ^ mask) for source in range(lax.axis_size(axis))]
     return lax.ppermute(value, axis, pairs)
+
+
+def butterfly(value, axis, combine):
+    for bit_index in range(lax.axis_size(axis).bit_length() - 1):
+        value = combine(value, from_partner(value, axis, bit_index))
+    return value
 
 
 def shift_rows(trial_rows, amounts, length):
@@ -90,7 +96,7 @@
         return min(TIN, needed)
 
     partial_value = jnp.sum(filterbank, axis=0)
-    channel_mean = lax.psum(partial_value, "band") / channels_all
+    channel_mean = butterfly(partial_value, "band", jnp.add) / channels_all
     current = filterbank - channel_mean[None, :]
     for local_section_index in range(local_count):
         current = merge_section(
@@ -112,7 +118,7 @@
         )
     dedispersed = current * (1.0 / math.sqrt(channels_all))
     detection = boxcar_max(dedispersed, widths)
-    peak_series = lax.pmax(jnp.max(detection, axis=0), "band")
+    peak_series = butterfly(jnp.max(detection, axis=0), "band", jnp.maximum)
     return (detection, peak_series)
 
 

time: 165 us -> 96.5 us (0.58)
  blocking collectives: 93.5 us -> 0 us
  starting transfers between devices: 0.28 us -> 13.8 us
  waiting for transfers between devices: 35.9 us -> 47.3 us
    psum x1 -> x0, blocking collectives: 62.9 us -> none  [per_device(): channel_mean = lax.psum(partial_value, 'band') / channels_all]
    pmax x1 -> x0, blocking collectives: 30.6 us -> none  [per_device(): peak_series = lax.pmax(jnp.max(detection, axis=0), 'band')]
    ppermute x4 -> x12, starting transfers between devices: 0.28 us -> 13.8 us  [from_partner(): return lax.ppermute(value, axis, pairs)]
    ppermute x4 -> x12, waiting for transfers between devices: 35.9 us -> 47.3 us  [from_partner(): return lax.ppermute(value, axis, pairs)]
  transfers between devices with their start and end apart: 4 -> 12, of which waited for: 4 -> 11; matrix products, arithmetic and copies ran while one was open for 0% -> 6% of each run, Pallas kernels for 0% -> 0%
where the time goes in v1:
time: 96.5 us; the launch traced here: 96.3 us
  waiting for transfers between devices  47.3 us (49%)
  other arithmetic  19.7 us (20%)
  starting transfers between devices  13.8 us (14%)
  local copies, waits for them, and re-layouts  9.07 us (9%)
  matrix products  4.65 us (5%)
  between operations  1.82 us (2%)
    ppermute x12, waiting for transfers between devices, from_partner(): return lax.ppermute(value, axis, pairs)  47.3 us
    ppermute x12, starting transfers between devices, from_partner(): return lax.ppermute(value, axis, pairs)  13.8 us
    select_n x96, other arithmetic, shift_rows(): jnp.where(chosen, current[:, span:span + keep_len], current[:, :keep_len])  13 us
    dot_general x8, matrix products, boxcar_max(): jnp.dot(paired, tables[template_index], precision=lax.Precision.HIGHEST,...  4.65 us
    eq x48, local copies, waits for them, and re-layouts, shift_rows(): chosen = (amounts >> bit_index & 1)[:, None] == 1  4.17 us
  transfers between devices with their start and end apart: 12, of which 11 were waited for; matrix products, arithmetic and copies ran while one was open for 6% of the time, Pallas kernels for 0%

profile of v1, /device:TPU:0, one launch (start us, length us, event | category | flops | bytes accessed | tf_op | source)
XLA Modules:
  0.0 96.3 jit_solution(6958161207607936702)
XLA Ops:
  0.6 1.3 %reduce_sum.9 = f32[6144]{0:T(1024)S(1)} reduce(f32[32,6144]{1,0:T(8,128)} %param.3, f32[]{:T(128)} %constant.95.clone.1), dimensions={0}, to_apply=%region_0.0 | reduce | flops 190464 | bytes 811012 | tf_op jit(solution)/shard_map/reduce_sum | solution.py:98
  1.9 0.5 collective-permute-start
  3.3 2.8 %collective-permute-start.1 = (f32[6144]{0:T(1024)S(1)}, f32[6144]{0:T(1024)S(1)}, u32[]{:S(2)}, u32[]{:S(2)}) collective-permute-start(f32[6144]{0:T(1024)S(1)} %add.85), channel_id=1, source_target_pairs={{0,2},{1,3},{2,0},{3,1},{4,6},{5,7},{6,4},{7,5},{8,10},{9,11},{10,... | collective-permute-start | bytes 73736 | tf_op jit(solution)/shard_map/ppermute | solution.py:18
  6.3 1.6 %collective-permute-done.1 = f32[6144]{0:T(1024)S(1)} collective-permute-done((f32[6144]{0:T(1024)S(1)}, f32[6144]{0:T(1024)S(1)}, u32[]{:S(2)}, u32[]{:S(2)}) %collective-permute-start.1) | collective-permute-done | bytes 24608 | tf_op jit(solution)/shard_map/ppermute | solution.py:18
  7.9 2.1 %collective-permute-start.2 = (f32[6144]{0:T(1024)S(1)}, f32[6144]{0:T(1024)S(1)}, u32[]{:S(2)}, u32[]{:S(2)}) collective-permute-start(f32[6144]{0:T(1024)S(1)} %add.86), channel_id=1, source_target_pairs={{0,4},{1,5},{2,6},{3,7},{4,0},{5,1},{6,2},{7,3},{8,12},{9,13},{10,... | collective-permute-start | bytes 73736 | tf_op jit(solution)/shard_map/ppermute | solution.py:18
  10.5 1.3 %collective-permute-done.2 = f32[6144]{0:T(1024)S(1)} collective-permute-done((f32[6144]{0:T(1024)S(1)}, f32[6144]{0:T(1024)S(1)}, u32[]{:S(2)}, u32[]{:S(2)}) %collective-permute-start.2) | collective-permute-done | bytes 24608 | tf_op jit(solution)/shard_map/ppermute | solution.py:18
  11.9 3.0 %collective-permute-start.3 = (f32[6144]{0:T(1024)S(1)}, f32[6144]{0:T(1024)S(1)}, u32[]{:S(2)}, u32[]{:S(2)}) collective-permute-start(f32[6144]{0:T(1024)S(1)} %add.87), channel_id=1, source_target_pairs={{0,8},{1,9},{2,10},{3,11},{4,12},{5,13},{6,14},{7,15},{8,0},{9,1},... | collective-permute-start | bytes 73736 | tf_op jit(solution)/shard_map/ppermute | solution.py:18
  19.3 0.5 reshape.1647
  25.9 0.6 copy_add_fusion.1
  29.9 0.6 copy_add_fusion.3
  35.4 1.7 %collective-permute-done.4 = f32[32,3200]{1,0:T(8,128)S(1)} collective-permute-done((f32[32,3200]{1,0:T(8,128)S(1)}, f32[32,3200]{1,0:T(8,128)S(1)}, u32[]{:S(2)}, u32[]{:S(2)}) %collective-permute-start.4) | collective-permute-done | bytes 409632 | tf_op jit(solution)/shard_map/ppermute | solution.py:18
  38.4 1.6 %collective-permute-start.5 = (f32[32,2944]{1,0:T(8,128)S(1)}, f32[32,2944]{1,0:T(8,128)S(1)}, u32[]{:S(2)}, u32[]{:S(2)}) collective-permute-start(f32[32,2944]{1,0:T(8,128)S(1)} %fusion), channel_id=1, source_target_pairs={{0,2},{1,3},{2,0},{3,1},{4,6},{5,7},{6,4},{7,5},{8,10},{9,11},{10,... | collective-permute-start | bytes 1130504 | tf_op jit(solution)/shard_map/ppermute | solution.py:18
  40.0 9.3 %collective-permute-done.5 = f32[32,2944]{1,0:T(8,128)S(1)} collective-permute-done((f32[32,2944]{1,0:T(8,128)S(1)}, f32[32,2944]{1,0:T(8,128)S(1)}, u32[]{:S(2)}, u32[]{:S(2)}) %collective-permute-start.5) | collective-permute-done | bytes 376864 | tf_op jit(solution)/shard_map/ppermute | solution.py:18
  50.6 1.6 %collective-permute-start.6 = (f32[32,2688]{1,0:T(8,128)S(1)}, f32[32,2688]{1,0:T(8,128)S(1)}, u32[]{:S(2)}, u32[]{:S(2)}) collective-permute-start(f32[32,2688]{1,0:T(8,128)S(1)} %fusion.1), channel_id=1, source_target_pairs={{0,4},{1,5},{2,6},{3,7},{4,0},{5,1},{6,2},{7,3},{8,12},{9,13},{10,... | collective-permute-start | bytes 1032200 | tf_op jit(solution)/shard_map/ppermute | solution.py:18
  52.3 0.6 copy-done.3
  52.9 7.0 %collective-permute-done.6 = f32[32,2688]{1,0:T(8,128)S(1)} collective-permute-done((f32[32,2688]{1,0:T(8,128)S(1)}, f32[32,2688]{1,0:T(8,128)S(1)}, u32[]{:S(2)}, u32[]{:S(2)}) %collective-permute-start.6) | collective-permute-done | bytes 344096 | tf_op jit(solution)/shard_map/ppermute | solution.py:18
  61.2 0.5 collective-permute-start.7
  62.0 14.5 %collective-permute-done.7 = f32[32,2432]{1,0:T(8,128)S(1)} collective-permute-done((f32[32,2432]{1,0:T(8,128)S(1)}, f32[32,2432]{1,0:T(8,128)S(1)}, u32[]{:S(2)}, u32[]{:S(2)}) %collective-permute-start.7) | collective-permute-done | bytes 311328 | tf_op jit(solution)/shard_map/ppermute | solution.py:18
  77.8 0.6 fusion.15
  78.4 0.6 convolution_maximum_fusion.6
  79.0 0.6 convolution_maximum_fusion.5
  79.6 0.6 convolution_maximum_fusion.4
  80.2 0.6 convolution_maximum_fusion.3
  80.8 0.6 convolution_maximum_fusion.2
  81.4 0.6 convolution_maximum_fusion.1
  81.9 0.6 convolution_maximum_fusion
  82.7 1.2 %collective-permute-done.8 = f32[2048]{0:T(1024)S(1)} collective-permute-done((f32[2048]{0:T(1024)S(1)}, f32[2048]{0:T(1024)S(1)}, u32[]{:S(2)}, u32[]{:S(2)}) %collective-permute-start.8) | collective-permute-done | bytes 8224 | tf_op jit(solution)/shard_map/ppermute | solution.py:18
  83.9 1.5 %collective-permute-start.9 = (f32[2048]{0:T(1024)S(1)}, f32[2048]{0:T(1024)S(1)}, u32[]{:S(2)}, u32[]{:S(2)}) collective-permute-start(f32[2048]{0:T(1024)S(1)} %max.40), channel_id=1, source_target_pairs={{0,2},{1,3},{2,0},{3,1},{4,6},{5,7},{6,4},{7,5},{8,10},{9,11},{10,... | collective-permute-start | bytes 24584 | tf_op jit(solution)/shard_map/ppermute | solution.py:18
  85.4 2.1 %collective-permute-done.9 = f32[2048]{0:T(1024)S(1)} collective-permute-done((f32[2048]{0:T(1024)S(1)}, f32[2048]{0:T(1024)S(1)}, u32[]{:S(2)}, u32[]{:S(2)}) %collective-permute-start.9) | collective-permute-done | bytes 8224 | tf_op jit(solution)/shard_map/ppermute | solution.py:18
  87.5 3.6 %collective-permute-done.10 = f32[2048]{0:T(1024)S(1)} collective-permute-done((f32[2048]{0:T(1024)S(1)}, f32[2048]{0:T(1024)S(1)}, u32[]{:S(2)}, u32[]{:S(2)}) %collective-permute-start.10) | collective-permute-done | bytes 8224 | tf_op jit(solution)/shard_map/ppermute | solution.py:18
  91.2 4.5 %collective-permute-done.11 = f32[2048]{0:T(1024)S(1)} collective-permute-done((f32[2048]{0:T(1024)S(1)}, f32[2048]{0:T(1024)S(1)}, u32[]{:S(2)}, u32[]{:S(2)}) %collective-permute-start.11) | collective-permute-done | bytes 8224 | tf_op jit(solution)/shard_map/ppermute | solution.py:18
  95.7 0.6 max.43
  (225 shorter events, 25.1 us)
Async XLA Ops:
  0.6 18.6 %copy-start = (f32[32,6144]{1,0:T(8,128)S(1)}, f32[32,6144]{1,0:T(8,128)}, u32[]{:S(2)}) copy-start(f32[32,6144]{1,0:T(8,128)} %param.3) | copy-start | bytes 2359300
  0.6 1.8 %copy-start.2 = (s32[9,32]{1,0:T(8,128)S(1)}, s32[9,32]{1,0:T(8,128)}, u32[]{:S(2)}) copy-start(s32[9,32]{1,0:T(8,128)} %param.4) | copy-start | bytes 3460
  1.9 1.4 %collective-permute-start = (f32[6144]{0:T(1024)S(1)}, f32[6144]{0:T(1024)S(1)}, u32[]{:S(2)}, u32[]{:S(2)}) collective-permute-start(f32[6144]{0:T(1024)S(1)} %reduce_sum.9), channel_id=1, source_target_pairs={{0,1},{1,0},{2,3},{3,2},{4,5},{5,4},{6,7},{7,6},{8,9},{9,8},{10,11... | collective-permute-start | bytes 73736 | tf_op jit(solution)/shard_map/ppermute | solution.py:18
  3.3 4.6 %collective-permute-start.1 = (f32[6144]{0:T(1024)S(1)}, f32[6144]{0:T(1024)S(1)}, u32[]{:S(2)}, u32[]{:S(2)}) collective-permute-start(f32[6144]{0:T(1024)S(1)} %add.85), channel_id=1, source_target_pairs={{0,2},{1,3},{2,0},{3,1},{4,6},{5,7},{6,4},{7,5},{8,10},{9,11},{10,... | collective-permute-start | bytes 73736 | tf_op jit(solution)/shard_map/ppermute | solution.py:18
  7.9 3.9 %collective-permute-start.2 = (f32[6144]{0:T(1024)S(1)}, f32[6144]{0:T(1024)S(1)}, u32[]{:S(2)}, u32[]{:S(2)}) collective-permute-start(f32[6144]{0:T(1024)S(1)} %add.86), channel_id=1, source_target_pairs={{0,4},{1,5},{2,6},{3,7},{4,0},{5,1},{6,2},{7,3},{8,12},{9,13},{10,... | collective-permute-start | bytes 73736 | tf_op jit(solution)/shard_map/ppermute | solution.py:18
  11.9 7.3 %collective-permute-start.3 = (f32[6144]{0:T(1024)S(1)}, f32[6144]{0:T(1024)S(1)}, u32[]{:S(2)}, u32[]{:S(2)}) collective-permute-start(f32[6144]{0:T(1024)S(1)} %add.87), channel_id=1, source_target_pairs={{0,8},{1,9},{2,10},{3,11},{4,12},{5,13},{6,14},{7,15},{8,0},{9,1},... | collective-permute-start | bytes 73736 | tf_op jit(solution)/shard_map/ppermute | solution.py:18
  35.2 1.8 %collective-permute-start.4 = (f32[32,3200]{1,0:T(8,128)S(1)}, f32[32,3200]{1,0:T(8,128)S(1)}, u32[]{:S(2)}, u32[]{:S(2)}) collective-permute-start(f32[32,3200]{1,0:T(8,128)S(1)} %bitcast.180), channel_id=1, source_target_pairs={{0,1},{1,0},{2,3},{3,2},{4,5},{5,4},{6,7},{7,6},{8,9},{9,8},{10,11... | collective-permute-start | bytes 1228808 | tf_op jit(solution)/shard_map/ppermute | solution.py:18
  38.4 10.9 %collective-permute-start.5 = (f32[32,2944]{1,0:T(8,128)S(1)}, f32[32,2944]{1,0:T(8,128)S(1)}, u32[]{:S(2)}, u32[]{:S(2)}) collective-permute-start(f32[32,2944]{1,0:T(8,128)S(1)} %fusion), channel_id=1, source_target_pairs={{0,2},{1,3},{2,0},{3,1},{4,6},{5,7},{6,4},{7,5},{8,10},{9,11},{10,... | collective-permute-start | bytes 1130504 | tf_op jit(solution)/shard_map/ppermute | solution.py:18
  50.6 9.3 %collective-permute-start.6 = (f32[32,2688]{1,0:T(8,128)S(1)}, f32[32,2688]{1,0:T(8,128)S(1)}, u32[]{:S(2)}, u32[]{:S(2)}) collective-permute-start(f32[32,2688]{1,0:T(8,128)S(1)} %fusion.1), channel_id=1, source_target_pairs={{0,4},{1,5},{2,6},{3,7},{4,0},{5,1},{6,2},{7,3},{8,12},{9,13},{10,... | collective-permute-start | bytes 1032200 | tf_op jit(solution)/shard_map/ppermute | solution.py:18
  52.3 0.7 copy-start.3
  61.2 15.3 %collective-permute-start.7 = (f32[32,2432]{1,0:T(8,128)S(1)}, f32[32,2432]{1,0:T(8,128)S(1)}, u32[]{:S(2)}, u32[]{:S(2)}) collective-permute-start(f32[32,2432]{1,0:T(8,128)S(1)} %fusion.2), channel_id=1, source_target_pairs={{0,8},{1,9},{2,10},{3,11},{4,12},{5,13},{6,14},{7,15},{8,0},{9,1},... | collective-permute-start | bytes 933896 | tf_op jit(solution)/shard_map/ppermute | solution.py:18
  82.6 13.8 %copy-start.1 = (f32[32,2048]{1,0:T(8,128)}, f32[32,2048]{1,0:T(8,128)S(1)}, u32[]{:S(2)}) copy-start(f32[32,2048]{1,0:T(8,128)S(1)} %reshape.1657) | copy-start | bytes 786436
  82.6 1.2 %collective-permute-start.8 = (f32[2048]{0:T(1024)S(1)}, f32[2048]{0:T(1024)S(1)}, u32[]{:S(2)}, u32[]{:S(2)}) collective-permute-start(f32[2048]{0:T(1024)S(1)} %reduce_max.9), channel_id=1, source_target_pairs={{0,1},{1,0},{2,3},{3,2},{4,5},{5,4},{6,7},{7,6},{8,9},{9,8},{10,11... | collective-permute-start | bytes 24584 | tf_op jit(solution)/shard_map/ppermute | solution.py:18
  83.9 3.7 %collective-permute-start.9 = (f32[2048]{0:T(1024)S(1)}, f32[2048]{0:T(1024)S(1)}, u32[]{:S(2)}, u32[]{:S(2)}) collective-permute-start(f32[2048]{0:T(1024)S(1)} %max.40), channel_id=1, source_target_pairs={{0,2},{1,3},{2,0},{3,1},{4,6},{5,7},{6,4},{7,5},{8,10},{9,11},{10,... | collective-permute-start | bytes 24584 | tf_op jit(solution)/shard_map/ppermute | solution.py:18
  87.5 3.7 %collective-permute-start.10 = (f32[2048]{0:T(1024)S(1)}, f32[2048]{0:T(1024)S(1)}, u32[]{:S(2)}, u32[]{:S(2)}) collective-permute-start(f32[2048]{0:T(1024)S(1)} %max.41), channel_id=1, source_target_pairs={{0,4},{1,5},{2,6},{3,7},{4,0},{5,1},{6,2},{7,3},{8,12},{9,13},{10,... | collective-permute-start | bytes 24584 | tf_op jit(solution)/shard_map/ppermute | solution.py:18
  91.2 4.5 %collective-permute-start.11 = (f32[2048]{0:T(1024)S(1)}, f32[2048]{0:T(1024)S(1)}, u32[]{:S(2)}, u32[]{:S(2)}) collective-permute-start(f32[2048]{0:T(1024)S(1)} %max.42), channel_id=1, source_target_pairs={{0,8},{1,9},{2,10},{3,11},{4,12},{5,13},{6,14},{7,15},{8,0},{9,1},... | collective-permute-start | bytes 24584 | tf_op jit(solution)/shard_map/ppermute | solution.py:18

commit v2 on v1

--- a/solution.py
+++ b/solution.py
@@ -18,9 +18,30 @@
     return lax.ppermute(value, axis, pairs)
 
 
+def from_xor(value, axis, mask):
+    pairs = [(source, source ^ mask) for source in range(lax.axis_size(axis))]
+    return lax.ppermute(value, axis, pairs)
+
+
 def butterfly(value, axis, combine):
-    for bit_index in range(lax.axis_size(axis).bit_length() - 1):
-        value = combine(value, from_partner(value, axis, bit_index))
+    bit_count = lax.axis_size(axis).bit_length() - 1
+    position = lax.axis_index(axis)
+    low_bit = 0
+    while low_bit < bit_count:
+        width = min(2, bit_count - low_bit)
+        group = 2**width
+        received = [value] + [from_xor(value, axis, k << low_bit) for k in range(1, group)]
+        mine = position >> low_bit & (group - 1)
+        ordered = []
+        for slot in range(group):
+            chosen = received[0]
+            for k in range(1, group):
+                chosen = jnp.where((mine ^ slot) == k, received[k], chosen)
+            ordered.append(chosen)
+        while len(ordered) > 1:
+            ordered = [combine(ordered[i], ordered[i + 1]) for i in range(0, len(ordered), 2)]
+        value = ordered[0]
+        low_bit += width
     return value
 
 

time: 96.5 us -> 95 us (0.984)
  waiting for transfers between devices: 47.3 us -> 43 us
  starting transfers between devices: 13.8 us -> 16.4 us
    ppermute x0 -> x12, starting transfers between devices: none -> 14 us  [from_xor(): return lax.ppermute(value, axis, pairs)]
    ppermute x12 -> x4, waiting for transfers between devices: 47.3 us -> 33.8 us  [from_partner(): return lax.ppermute(value, axis, pairs)]
    ppermute x12 -> x4, starting transfers between devices: 13.8 us -> 2.45 us  [from_partner(): return lax.ppermute(value, axis, pairs)]
    ppermute x0 -> x12, waiting for transfers between devices: none -> 9.23 us  [from_xor(): return lax.ppermute(value, axis, pairs)]
  transfers between devices with their start and end apart: 12 -> 16, of which waited for: 11 -> 11; matrix products, arithmetic and copies ran while one was open for 6% -> 6% of each run, Pallas kernels for 0% -> 0%
where the time goes in v2:
time: 95 us; the launch traced here: 94.9 us
  waiting for transfers between devices  43 us (45%)
  other arithmetic  19.6 us (21%)
  starting transfers between devices  16.4 us (17%)
  local copies, waits for them, and re-layouts  9.24 us (10%)
  matrix products  4.65 us (5%)
  between operations  1.98 us (2%)
    ppermute x4, waiting for transfers between devices, from_partner(): return lax.ppermute(value, axis, pairs)  33.8 us
    ppermute x12, starting transfers between devices, from_xor(): return lax.ppermute(value, axis, pairs)  14 us
    select_n x96, other arithmetic, shift_rows(): jnp.where(chosen, current[:, span:span + keep_len], current[:, :keep_len])  12.8 us
    ppermute x12, waiting for transfers between devices, from_xor(): return lax.ppermute(value, axis, pairs)  9.23 us
    dot_general x8, matrix products, boxcar_max(): jnp.dot(paired, tables[template_index], precision=lax.Precision.HIGHEST,...  4.65 us
    eq x48, local copies, waits for them, and re-layouts, shift_rows(): chosen = (amounts >> bit_index & 1)[:, None] == 1  4.17 us
    ppermute x4, starting transfers between devices, from_partner(): return lax.ppermute(value, axis, pairs)  2.45 us
  transfers between devices with their start and end apart: 16, of which 11 were waited for; matrix products, arithmetic and copies ran while one was open for 6% of the time, Pallas kernels for 0%

profile of v2, /device:TPU:0, one launch (start us, length us, event | category | flops | bytes accessed | tf_op | source)
XLA Modules:
  0.0 94.9 jit_solution(9358104008584583399)
XLA Ops:
  0.6 1.3 %reduce_sum.9 = f32[6144]{0:T(1024)S(1)} reduce(f32[32,6144]{1,0:T(8,128)} %param.3, f32[]{:T(128)} %constant.96.clone.1), dimensions={0}, to_apply=%region_0.0 | reduce | flops 190464 | bytes 811012 | tf_op jit(solution)/shard_map/reduce_sum | solution.py:119
  1.9 0.5 collective-permute-start.2
  2.5 2.6 %collective-permute-start.1 = (f32[6144]{0:T(1024)S(1)}, f32[6144]{0:T(1024)S(1)}, u32[]{:S(2)}, u32[]{:S(2)}) collective-permute-start(f32[6144]{0:T(1024)S(1)} %reduce_sum.9), channel_id=1, source_target_pairs={{0,2},{1,3},{2,0},{3,1},{4,6},{5,7},{6,4},{7,5},{8,10},{9,11},{10,... | collective-permute-start | bytes 73736 | tf_op jit(solution)/shard_map/ppermute | solution.py:23
  6.8 1.4 %collective-permute-done = f32[6144]{0:T(1024)S(1)} collective-permute-done((f32[6144]{0:T(1024)S(1)}, f32[6144]{0:T(1024)S(1)}, u32[]{:S(2)}, u32[]{:S(2)}) %collective-permute-start) | collective-permute-done | bytes 24608 | tf_op jit(solution)/shard_map/ppermute | solution.py:23
  8.3 1.6 %collective-permute-start.5 = (f32[6144]{0:T(1024)S(1)}, f32[6144]{0:T(1024)S(1)}, u32[]{:S(2)}, u32[]{:S(2)}) collective-permute-start(f32[6144]{0:T(1024)S(1)} %add_add_fusion), channel_id=1, source_target_pairs={{0,4},{1,5},{2,6},{3,7},{4,0},{5,1},{6,2},{7,3},{8,12},{9,13},{10,... | collective-permute-start | bytes 73736 | tf_op jit(solution)/shard_map/ppermute | solution.py:23
  9.9 2.6 %collective-permute-start.4 = (f32[6144]{0:T(1024)S(1)}, f32[6144]{0:T(1024)S(1)}, u32[]{:S(2)}, u32[]{:S(2)}) collective-permute-start(f32[6144]{0:T(1024)S(1)} %add_add_fusion), channel_id=1, source_target_pairs={{0,8},{1,9},{2,10},{3,11},{4,12},{5,13},{6,14},{7,15},{8,0},{9,1},... | collective-permute-start | bytes 73736 | tf_op jit(solution)/shard_map/ppermute | solution.py:23
  17.1 1.1 %collective-permute-done.3 = f32[6144]{0:T(1024)S(1)} collective-permute-done((f32[6144]{0:T(1024)S(1)}, f32[6144]{0:T(1024)S(1)}, u32[]{:S(2)}, u32[]{:S(2)}) %collective-permute-start.3) | collective-permute-done | bytes 24608 | tf_op jit(solution)/shard_map/ppermute | solution.py:23
  18.3 0.5 reshape.1647
  24.9 0.6 copy_add_fusion.1
  28.9 0.6 copy_add_fusion.3
  34.3 1.7 %collective-permute-done.6 = f32[32,3200]{1,0:T(8,128)S(1)} collective-permute-done((f32[32,3200]{1,0:T(8,128)S(1)}, f32[32,3200]{1,0:T(8,128)S(1)}, u32[]{:S(2)}, u32[]{:S(2)}) %collective-permute-start.6) | collective-permute-done | bytes 409632 | tf_op jit(solution)/shard_map/ppermute | solution.py:18
  37.4 0.9 collective-permute-start.7
  38.3 10.0 %collective-permute-done.7 = f32[32,2944]{1,0:T(8,128)S(1)} collective-permute-done((f32[32,2944]{1,0:T(8,128)S(1)}, f32[32,2944]{1,0:T(8,128)S(1)}, u32[]{:S(2)}, u32[]{:S(2)}) %collective-permute-start.7) | collective-permute-done | bytes 376864 | tf_op jit(solution)/shard_map/ppermute | solution.py:18
  49.8 0.6 copy-done.3
  50.4 8.5 %collective-permute-done.8 = f32[32,2688]{1,0:T(8,128)S(1)} collective-permute-done((f32[32,2688]{1,0:T(8,128)S(1)}, f32[32,2688]{1,0:T(8,128)S(1)}, u32[]{:S(2)}, u32[]{:S(2)}) %collective-permute-start.8) | collective-permute-done | bytes 344096 | tf_op jit(solution)/shard_map/ppermute | solution.py:18
  60.2 1.4 %collective-permute-start.9 = (f32[32,2432]{1,0:T(8,128)S(1)}, f32[32,2432]{1,0:T(8,128)S(1)}, u32[]{:S(2)}, u32[]{:S(2)}) collective-permute-start(f32[32,2432]{1,0:T(8,128)S(1)} %fusion.2), channel_id=1, source_target_pairs={{0,8},{1,9},{2,10},{3,11},{4,12},{5,13},{6,14},{7,15},{8,0},{9,1},... | collective-permute-start | bytes 933896 | tf_op jit(solution)/shard_map/ppermute | solution.py:18
  61.9 13.6 %collective-permute-done.9 = f32[32,2432]{1,0:T(8,128)S(1)} collective-permute-done((f32[32,2432]{1,0:T(8,128)S(1)}, f32[32,2432]{1,0:T(8,128)S(1)}, u32[]{:S(2)}, u32[]{:S(2)}) %collective-permute-start.9) | collective-permute-done | bytes 311328 | tf_op jit(solution)/shard_map/ppermute | solution.py:18
  76.8 0.6 fusion.15
  77.4 0.6 convolution_maximum_fusion.6
  78.0 0.6 convolution_maximum_fusion.5
  78.6 0.6 convolution_maximum_fusion.4
  79.2 0.6 convolution_maximum_fusion.3
  79.8 0.6 convolution_maximum_fusion.2
  80.3 0.6 convolution_maximum_fusion.1
  80.9 0.6 convolution_maximum_fusion
  81.7 0.9 collective-permute-start.11
  82.6 1.0 %collective-permute-start.10 = (f32[2048]{0:T(1024)S(1)}, f32[2048]{0:T(1024)S(1)}, u32[]{:S(2)}, u32[]{:S(2)}) collective-permute-start(f32[2048]{0:T(1024)S(1)} %reduce_max.9), channel_id=1, source_target_pairs={{0,3},{1,2},{2,1},{3,0},{4,7},{5,6},{6,5},{7,4},{8,11},{9,10},{10,... | collective-permute-start | bytes 24584 | tf_op jit(solution)/shard_map/ppermute | solution.py:23
  83.6 1.9 %collective-permute-done.11 = f32[2048]{0:T(1024)S(1)} collective-permute-done((f32[2048]{0:T(1024)S(1)}, f32[2048]{0:T(1024)S(1)}, u32[]{:S(2)}, u32[]{:S(2)}) %collective-permute-start.11) | collective-permute-done | bytes 8224 | tf_op jit(solution)/shard_map/ppermute | solution.py:23
  85.7 3.1 %collective-permute-start.14 = (f32[2048]{0:T(1024)S(1)}, f32[2048]{0:T(1024)S(1)}, u32[]{:S(2)}, u32[]{:S(2)}) collective-permute-start(f32[2048]{0:T(1024)S(1)} %maximum_maximum_fusion.1), channel_id=1, source_target_pairs={{0,8},{1,9},{2,10},{3,11},{4,12},{5,13},{6,14},{7,15},{8,0},{9,1},... | collective-permute-start | bytes 24584 | tf_op jit(solution)/shard_map/ppermute | solution.py:23
  88.8 1.3 %collective-permute-start.13 = (f32[2048]{0:T(1024)S(1)}, f32[2048]{0:T(1024)S(1)}, u32[]{:S(2)}, u32[]{:S(2)}) collective-permute-start(f32[2048]{0:T(1024)S(1)} %maximum_maximum_fusion.1), channel_id=1, source_target_pairs={{0,12},{1,13},{2,14},{3,15},{4,8},{5,9},{6,10},{7,11},{8,4},{9,5},... | collective-permute-start | bytes 24584 | tf_op jit(solution)/shard_map/ppermute | solution.py:23
  90.5 3.8 %collective-permute-done.13 = f32[2048]{0:T(1024)S(1)} collective-permute-done((f32[2048]{0:T(1024)S(1)}, f32[2048]{0:T(1024)S(1)}, u32[]{:S(2)}, u32[]{:S(2)}) %collective-permute-start.13) | collective-permute-done | bytes 8224 | tf_op jit(solution)/shard_map/ppermute | solution.py:23
  94.3 0.6 maximum_maximum_fusion
  (229 shorter events, 26.3 us)
Async XLA Ops:
  0.6 17.5 %copy-start = (f32[32,6144]{1,0:T(8,128)S(1)}, f32[32,6144]{1,0:T(8,128)}, u32[]{:S(2)}) copy-start(f32[32,6144]{1,0:T(8,128)} %param.3) | copy-start | bytes 2359300
  0.6 4.5 %copy-start.2 = (s32[9,32]{1,0:T(8,128)S(1)}, s32[9,32]{1,0:T(8,128)}, u32[]{:S(2)}) copy-start(s32[9,32]{1,0:T(8,128)} %param.4) | copy-start | bytes 3460
  1.9 4.4 %collective-permute-start.2 = (f32[6144]{0:T(1024)S(1)}, f32[6144]{0:T(1024)S(1)}, u32[]{:S(2)}, u32[]{:S(2)}) collective-permute-start(f32[6144]{0:T(1024)S(1)} %reduce_sum.9), channel_id=1, source_target_pairs={{0,1},{1,0},{2,3},{3,2},{4,5},{5,4},{6,7},{7,6},{8,9},{9,8},{10,11... | collective-permute-start | bytes 73736 | tf_op jit(solution)/shard_map/ppermute | solution.py:23
  2.5 4.4 %collective-permute-start.1 = (f32[6144]{0:T(1024)S(1)}, f32[6144]{0:T(1024)S(1)}, u32[]{:S(2)}, u32[]{:S(2)}) collective-permute-start(f32[6144]{0:T(1024)S(1)} %reduce_sum.9), channel_id=1, source_target_pairs={{0,2},{1,3},{2,0},{3,1},{4,6},{5,7},{6,4},{7,5},{8,10},{9,11},{10,... | collective-permute-start | bytes 73736 | tf_op jit(solution)/shard_map/ppermute | solution.py:23
  5.0 3.3 %collective-permute-start = (f32[6144]{0:T(1024)S(1)}, f32[6144]{0:T(1024)S(1)}, u32[]{:S(2)}, u32[]{:S(2)}) collective-permute-start(f32[6144]{0:T(1024)S(1)} %reduce_sum.9), channel_id=1, source_target_pairs={{0,3},{1,2},{2,1},{3,0},{4,7},{5,6},{6,5},{7,4},{8,11},{9,10},{10,... | collective-permute-start | bytes 73736 | tf_op jit(solution)/shard_map/ppermute | solution.py:23
  8.3 8.8 %collective-permute-start.5 = (f32[6144]{0:T(1024)S(1)}, f32[6144]{0:T(1024)S(1)}, u32[]{:S(2)}, u32[]{:S(2)}) collective-permute-start(f32[6144]{0:T(1024)S(1)} %add_add_fusion), channel_id=1, source_target_pairs={{0,4},{1,5},{2,6},{3,7},{4,0},{5,1},{6,2},{7,3},{8,12},{9,13},{10,... | collective-permute-start | bytes 73736 | tf_op jit(solution)/shard_map/ppermute | solution.py:23
  9.9 7.1 %collective-permute-start.4 = (f32[6144]{0:T(1024)S(1)}, f32[6144]{0:T(1024)S(1)}, u32[]{:S(2)}, u32[]{:S(2)}) collective-permute-start(f32[6144]{0:T(1024)S(1)} %add_add_fusion), channel_id=1, source_target_pairs={{0,8},{1,9},{2,10},{3,11},{4,12},{5,13},{6,14},{7,15},{8,0},{9,1},... | collective-permute-start | bytes 73736 | tf_op jit(solution)/shard_map/ppermute | solution.py:23
  12.5 5.6 %collective-permute-start.3 = (f32[6144]{0:T(1024)S(1)}, f32[6144]{0:T(1024)S(1)}, u32[]{:S(2)}, u32[]{:S(2)}) collective-permute-start(f32[6144]{0:T(1024)S(1)} %add_add_fusion), channel_id=1, source_target_pairs={{0,12},{1,13},{2,14},{3,15},{4,8},{5,9},{6,10},{7,11},{8,4},{9,5},... | collective-permute-start | bytes 73736 | tf_op jit(solution)/shard_map/ppermute | solution.py:23
  34.2 1.8 %collective-permute-start.6 = (f32[32,3200]{1,0:T(8,128)S(1)}, f32[32,3200]{1,0:T(8,128)S(1)}, u32[]{:S(2)}, u32[]{:S(2)}) collective-permute-start(f32[32,3200]{1,0:T(8,128)S(1)} %bitcast.180), channel_id=1, source_target_pairs={{0,1},{1,0},{2,3},{3,2},{4,5},{5,4},{6,7},{7,6},{8,9},{9,8},{10,11... | collective-permute-start | bytes 1228808 | tf_op jit(solution)/shard_map/ppermute | solution.py:18
  37.4 10.9 %collective-permute-start.7 = (f32[32,2944]{1,0:T(8,128)S(1)}, f32[32,2944]{1,0:T(8,128)S(1)}, u32[]{:S(2)}, u32[]{:S(2)}) collective-permute-start(f32[32,2944]{1,0:T(8,128)S(1)} %fusion), channel_id=1, source_target_pairs={{0,2},{1,3},{2,0},{3,1},{4,6},{5,7},{6,4},{7,5},{8,10},{9,11},{10,... | collective-permute-start | bytes 1130504 | tf_op jit(solution)/shard_map/ppermute | solution.py:18
  49.6 9.3 %collective-permute-start.8 = (f32[32,2688]{1,0:T(8,128)S(1)}, f32[32,2688]{1,0:T(8,128)S(1)}, u32[]{:S(2)}, u32[]{:S(2)}) collective-permute-start(f32[32,2688]{1,0:T(8,128)S(1)} %fusion.1), channel_id=1, source_target_pairs={{0,4},{1,5},{2,6},{3,7},{4,0},{5,1},{6,2},{7,3},{8,12},{9,13},{10,... | collective-permute-start | bytes 1032200 | tf_op jit(solution)/shard_map/ppermute | solution.py:18
  49.7 0.7 copy-start.3
  60.2 15.3 %collective-permute-start.9 = (f32[32,2432]{1,0:T(8,128)S(1)}, f32[32,2432]{1,0:T(8,128)S(1)}, u32[]{:S(2)}, u32[]{:S(2)}) collective-permute-start(f32[32,2432]{1,0:T(8,128)S(1)} %fusion.2), channel_id=1, source_target_pairs={{0,8},{1,9},{2,10},{3,11},{4,12},{5,13},{6,14},{7,15},{8,0},{9,1},... | collective-permute-start | bytes 933896 | tf_op jit(solution)/shard_map/ppermute | solution.py:18
  81.6 13.3 %copy-start.1 = (f32[32,2048]{1,0:T(8,128)}, f32[32,2048]{1,0:T(8,128)S(1)}, u32[]{:S(2)}) copy-start(f32[32,2048]{1,0:T(8,128)S(1)} %reshape.1657) | copy-start | bytes 786436
  81.6 1.9 %collective-permute-start.12 = (f32[2048]{0:T(1024)S(1)}, f32[2048]{0:T(1024)S(1)}, u32[]{:S(2)}, u32[]{:S(2)}) collective-permute-start(f32[2048]{0:T(1024)S(1)} %reduce_max.9), channel_id=1, source_target_pairs={{0,1},{1,0},{2,3},{3,2},{4,5},{5,4},{6,7},{7,6},{8,9},{9,8},{10,11... | collective-permute-start | bytes 24584 | tf_op jit(solution)/shard_map/ppermute | solution.py:23
  81.7 3.7 %collective-permute-start.11 = (f32[2048]{0:T(1024)S(1)}, f32[2048]{0:T(1024)S(1)}, u32[]{:S(2)}, u32[]{:S(2)}) collective-permute-start(f32[2048]{0:T(1024)S(1)} %reduce_max.9), channel_id=1, source_target_pairs={{0,2},{1,3},{2,0},{3,1},{4,6},{5,7},{6,4},{7,5},{8,10},{9,11},{10,... | collective-permute-start | bytes 24584 | tf_op jit(solution)/shard_map/ppermute | solution.py:23
  82.6 3.1 %collective-permute-start.10 = (f32[2048]{0:T(1024)S(1)}, f32[2048]{0:T(1024)S(1)}, u32[]{:S(2)}, u32[]{:S(2)}) collective-permute-start(f32[2048]{0:T(1024)S(1)} %reduce_max.9), channel_id=1, source_target_pairs={{0,3},{1,2},{2,1},{3,0},{4,7},{5,6},{6,5},{7,4},{8,11},{9,10},{10,... | collective-permute-start | bytes 24584 | tf_op jit(solution)/shard_map/ppermute | solution.py:23
  85.6 4.5 %collective-permute-start.15 = (f32[2048]{0:T(1024)S(1)}, f32[2048]{0:T(1024)S(1)}, u32[]{:S(2)}, u32[]{:S(2)}) collective-permute-start(f32[2048]{0:T(1024)S(1)} %maximum_maximum_fusion.1), channel_id=1, source_target_pairs={{0,4},{1,5},{2,6},{3,7},{4,0},{5,1},{6,2},{7,3},{8,12},{9,13},{10,... | collective-permute-start | bytes 24584 | tf_op jit(solution)/shard_map/ppermute | solution.py:23
  85.7 4.7 %collective-permute-start.14 = (f32[2048]{0:T(1024)S(1)}, f32[2048]{0:T(1024)S(1)}, u32[]{:S(2)}, u32[]{:S(2)}) collective-permute-start(f32[2048]{0:T(1024)S(1)} %maximum_maximum_fusion.1), channel_id=1, source_target_pairs={{0,8},{1,9},{2,10},{3,11},{4,12},{5,13},{6,14},{7,15},{8,0},{9,1},... | collective-permute-start | bytes 24584 | tf_op jit(solution)/shard_map/ppermute | solution.py:23
  88.8 5.4 %collective-permute-start.13 = (f32[2048]{0:T(1024)S(1)}, f32[2048]{0:T(1024)S(1)}, u32[]{:S(2)}, u32[]{:S(2)}) collective-permute-start(f32[2048]{0:T(1024)S(1)} %maximum_maximum_fusion.1), channel_id=1, source_target_pairs={{0,12},{1,13},{2,14},{3,15},{4,8},{5,9},{6,10},{7,11},{8,4},{9,5},... | collective-permute-start | bytes 24584 | tf_op jit(solution)/shard_map/ppermute | solution.py:23

commit v3 on v2

--- a/solution.py
+++ b/solution.py
@@ -90,18 +90,14 @@
         total_rows * blocks_time, 2 * TAPS
     )
     tables = template_tables(widths)
-    best_value = None
-    for template_index in range(TEMPLATES):
-        result = jnp.dot(
-            paired,
-            tables[template_index],
-            precision=lax.Precision.HIGHEST,
-            preferred_element_type=jnp.float32,
-        )
-        if template_index == 0:
-            best_value = result
-        else:
-            best_value = jnp.maximum(best_value, result)
+    joined = jnp.transpose(tables, (1, 0, 2)).reshape(2 * TAPS, TEMPLATES * TAPS)
+    result = jnp.dot(
+        paired,
+        joined,
+        precision=lax.Precision.HIGHEST,
+        preferred_element_type=jnp.float32,
+    )
+    best_value = jnp.max(result.reshape(total_rows * blocks_time, TEMPLATES, TAPS), axis=1)
     return best_value.reshape(total_rows, TS)
 
 

time: 95 us -> 92.4 us (0.973)
  matrix products: 4.65 us -> 1.87 us
  waiting for transfers between devices: 43 us -> 41.8 us
  local copies, waits for them, and re-layouts: 9.24 us -> 10.4 us
    dot_general x8 -> x1, matrix products: 4.65 us -> 1.87 us  [boxcar_max(): jnp.dot(paired, joined, precision=lax.Precision.HIGHEST, preferred_elemen...]
  transfers between devices with their start and end apart: 16 -> 16, of which waited for: 11 -> 10; matrix products, arithmetic and copies ran while one was open for 6% -> 7% of each run, Pallas kernels for 0% -> 0%
where the time goes in v3:
time: 92.4 us; the launch traced here: 92.1 us
  waiting for transfers between devices  41.8 us (45%)
  other arithmetic  19.7 us (21%)
  starting transfers between devices  16.4 us (18%)
  local copies, waits for them, and re-layouts  10.4 us (11%)
  between operations  1.88 us (2%)
  matrix products  1.87 us (2%)
    ppermute x4, waiting for transfers between devices, from_partner(): return lax.ppermute(value, axis, pairs)  33.5 us
    ppermute x12, starting transfers between devices, from_xor(): return lax.ppermute(value, axis, pairs)  14 us
    select_n x96, other arithmetic, shift_rows(): jnp.where(chosen, current[:, span:span + keep_len], current[:, :keep_len])  12.8 us
    ppermute x12, waiting for transfers between devices, from_xor(): return lax.ppermute(value, axis, pairs)  8.37 us
    eq x48, local copies, waits for them, and re-layouts, shift_rows(): chosen = (amounts >> bit_index & 1)[:, None] == 1  4.17 us
    ppermute x4, starting transfers between devices, from_partner(): return lax.ppermute(value, axis, pairs)  2.45 us
    dot_general x1, matrix products, boxcar_max(): jnp.dot(paired, joined, precision=lax.Precision.HIGHEST, preferred_elemen...  1.87 us
  transfers between devices with their start and end apart: 16, of which 10 were waited for; matrix products, arithmetic and copies ran while one was open for 7% of the time, Pallas kernels for 0%

profile of v3, /device:TPU:0, one launch (start us, length us, event | category | flops | bytes accessed | tf_op | source)
XLA Modules:
  0.0 92.1 jit_solution(377848207954869973)
XLA Ops:
  0.6 1.3 %reduce_sum.9 = f32[6144]{0:T(1024)S(1)} reduce(f32[32,6144]{1,0:T(8,128)} %param.3, f32[]{:T(128)} %constant.96.clone.1), dimensions={0}, to_apply=%region_0.0 | reduce | flops 190464 | bytes 811012 | tf_op jit(solution)/shard_map/reduce_sum | solution.py:115
  1.9 0.5 collective-permute-start.2
  2.4 2.6 %collective-permute-start.1 = (f32[6144]{0:T(1024)S(1)}, f32[6144]{0:T(1024)S(1)}, u32[]{:S(2)}, u32[]{:S(2)}) collective-permute-start(f32[6144]{0:T(1024)S(1)} %reduce_sum.9), channel_id=1, source_target_pairs={{0,2},{1,3},{2,0},{3,1},{4,6},{5,7},{6,4},{7,5},{8,10},{9,11},{10,... | collective-permute-start | bytes 73736 | tf_op jit(solution)/shard_map/ppermute | solution.py:23
  5.1 0.9 slice_reduce_fusion
  6.7 0.4 fusion.25
  7.2 1.0 %collective-permute-done = f32[6144]{0:T(1024)S(1)} collective-permute-done((f32[6144]{0:T(1024)S(1)}, f32[6144]{0:T(1024)S(1)}, u32[]{:S(2)}, u32[]{:S(2)}) %collective-permute-start) | collective-permute-done | bytes 24608 | tf_op jit(solution)/shard_map/ppermute | solution.py:23
  8.3 1.6 %collective-permute-start.5 = (f32[6144]{0:T(1024)S(1)}, f32[6144]{0:T(1024)S(1)}, u32[]{:S(2)}, u32[]{:S(2)}) collective-permute-start(f32[6144]{0:T(1024)S(1)} %add_add_fusion), channel_id=1, source_target_pairs={{0,4},{1,5},{2,6},{3,7},{4,0},{5,1},{6,2},{7,3},{8,12},{9,13},{10,... | collective-permute-start | bytes 73736 | tf_op jit(solution)/shard_map/ppermute | solution.py:23
  9.9 2.6 %collective-permute-start.4 = (f32[6144]{0:T(1024)S(1)}, f32[6144]{0:T(1024)S(1)}, u32[]{:S(2)}, u32[]{:S(2)}) collective-permute-start(f32[6144]{0:T(1024)S(1)} %add_add_fusion), channel_id=1, source_target_pairs={{0,8},{1,9},{2,10},{3,11},{4,12},{5,13},{6,14},{7,15},{8,0},{9,1},... | collective-permute-start | bytes 73736 | tf_op jit(solution)/shard_map/ppermute | solution.py:23
  17.1 1.1 %collective-permute-done.3 = f32[6144]{0:T(1024)S(1)} collective-permute-done((f32[6144]{0:T(1024)S(1)}, f32[6144]{0:T(1024)S(1)}, u32[]{:S(2)}, u32[]{:S(2)}) %collective-permute-start.3) | collective-permute-done | bytes 24608 | tf_op jit(solution)/shard_map/ppermute | solution.py:23
  18.2 0.5 reshape.1654
  18.9 0.4 slice.1026
  24.9 0.6 copy_add_fusion.1
  25.5 0.5 pad_maximum_fusion.1
  28.9 0.6 copy_add_fusion.3
  29.4 0.4 pad_maximum_fusion.2
  34.3 0.4 copy-done.2
  34.7 1.3 %collective-permute-done.6 = f32[32,3200]{1,0:T(8,128)S(1)} collective-permute-done((f32[32,3200]{1,0:T(8,128)S(1)}, f32[32,3200]{1,0:T(8,128)S(1)}, u32[]{:S(2)}, u32[]{:S(2)}) %collective-permute-start.6) | collective-permute-done | bytes 409632 | tf_op jit(solution)/shard_map/ppermute | solution.py:18
  37.4 0.9 collective-permute-start.7
  38.3 10.0 %collective-permute-done.7 = f32[32,2944]{1,0:T(8,128)S(1)} collective-permute-done((f32[32,2944]{1,0:T(8,128)S(1)}, f32[32,2944]{1,0:T(8,128)S(1)}, u32[]{:S(2)}, u32[]{:S(2)}) %collective-permute-start.7) | collective-permute-done | bytes 376864 | tf_op jit(solution)/shard_map/ppermute | solution.py:18
  49.7 0.4 copy-done.3
  50.2 8.8 %collective-permute-done.8 = f32[32,2688]{1,0:T(8,128)S(1)} collective-permute-done((f32[32,2688]{1,0:T(8,128)S(1)}, f32[32,2688]{1,0:T(8,128)S(1)}, u32[]{:S(2)}, u32[]{:S(2)}) %collective-permute-start.8) | collective-permute-done | bytes 344096 | tf_op jit(solution)/shard_map/ppermute | solution.py:18
  60.2 1.4 %collective-permute-start.9 = (f32[32,2432]{1,0:T(8,128)S(1)}, f32[32,2432]{1,0:T(8,128)S(1)}, u32[]{:S(2)}, u32[]{:S(2)}) collective-permute-start(f32[32,2432]{1,0:T(8,128)S(1)} %fusion.4), channel_id=1, source_target_pairs={{0,8},{1,9},{2,10},{3,11},{4,12},{5,13},{6,14},{7,15},{8,0},{9,1},... | collective-permute-start | bytes 933896 | tf_op jit(solution)/shard_map/ppermute | solution.py:18
  62.1 13.4 %collective-permute-done.9 = f32[32,2432]{1,0:T(8,128)S(1)} collective-permute-done((f32[32,2432]{1,0:T(8,128)S(1)}, f32[32,2432]{1,0:T(8,128)S(1)}, u32[]{:S(2)}, u32[]{:S(2)}) %collective-permute-start.9) | collective-permute-done | bytes 311328 | tf_op jit(solution)/shard_map/ppermute | solution.py:18
  76.8 1.9 %convolution_reduce_fusion = f32[512,128]{1,0:T(8,128)S(1)} fusion(f32[512,256,1]{1,0,2:T(8,128)S(1)} %bitcast.163, f32[8,128,256]{2,1,0:T(8,128)S(1)} %bitcast.159), kind=kOutput, calls=%fused_computation | convolution fusion | flops 1611071488 | bytes 1835008 | tf_op jit(solution)/shard_map/dot_general | solution.py:94
  78.9 0.9 collective-permute-start.11
  79.7 1.0 %collective-permute-start.10 = (f32[2048]{0:T(1024)S(1)}, f32[2048]{0:T(1024)S(1)}, u32[]{:S(2)}, u32[]{:S(2)}) collective-permute-start(f32[2048]{0:T(1024)S(1)} %reduce_max.19), channel_id=1, source_target_pairs={{0,3},{1,2},{2,1},{3,0},{4,7},{5,6},{6,5},{7,4},{8,11},{9,10},{10,... | collective-permute-start | bytes 24584 | tf_op jit(solution)/shard_map/ppermute | solution.py:23
  80.7 1.9 %collective-permute-done.11 = f32[2048]{0:T(1024)S(1)} collective-permute-done((f32[2048]{0:T(1024)S(1)}, f32[2048]{0:T(1024)S(1)}, u32[]{:S(2)}, u32[]{:S(2)}) %collective-permute-start.11) | collective-permute-done | bytes 8224 | tf_op jit(solution)/shard_map/ppermute | solution.py:23
  82.9 3.1 %collective-permute-start.14 = (f32[2048]{0:T(1024)S(1)}, f32[2048]{0:T(1024)S(1)}, u32[]{:S(2)}, u32[]{:S(2)}) collective-permute-start(f32[2048]{0:T(1024)S(1)} %maximum_maximum_fusion.1), channel_id=1, source_target_pairs={{0,8},{1,9},{2,10},{3,11},{4,12},{5,13},{6,14},{7,15},{8,0},{9,1},... | collective-permute-start | bytes 24584 | tf_op jit(solution)/shard_map/ppermute | solution.py:23
  86.0 1.3 %collective-permute-start.13 = (f32[2048]{0:T(1024)S(1)}, f32[2048]{0:T(1024)S(1)}, u32[]{:S(2)}, u32[]{:S(2)}) collective-permute-start(f32[2048]{0:T(1024)S(1)} %maximum_maximum_fusion.1), channel_id=1, source_target_pairs={{0,12},{1,13},{2,14},{3,15},{4,8},{5,9},{6,10},{7,11},{8,4},{9,5},... | collective-permute-start | bytes 24584 | tf_op jit(solution)/shard_map/ppermute | solution.py:23
  87.3 0.4 collective-permute-done.14
  87.7 3.8 %collective-permute-done.13 = f32[2048]{0:T(1024)S(1)} collective-permute-done((f32[2048]{0:T(1024)S(1)}, f32[2048]{0:T(1024)S(1)}, u32[]{:S(2)}, u32[]{:S(2)}) %collective-permute-start.13) | collective-permute-done | bytes 8224 | tf_op jit(solution)/shard_map/ppermute | solution.py:23
  91.5 0.6 maximum_maximum_fusion
  (224 shorter events, 24.0 us)
Async XLA Ops:
  0.6 17.5 %copy-start = (f32[32,6144]{1,0:T(8,128)S(1)}, f32[32,6144]{1,0:T(8,128)}, u32[]{:S(2)}) copy-start(f32[32,6144]{1,0:T(8,128)} %param.3) | copy-start | bytes 2359300
  1.9 5.3 %collective-permute-start.2 = (f32[6144]{0:T(1024)S(1)}, f32[6144]{0:T(1024)S(1)}, u32[]{:S(2)}, u32[]{:S(2)}) collective-permute-start(f32[6144]{0:T(1024)S(1)} %reduce_sum.9), channel_id=1, source_target_pairs={{0,1},{1,0},{2,3},{3,2},{4,5},{5,4},{6,7},{7,6},{8,9},{9,8},{10,11... | collective-permute-start | bytes 73736 | tf_op jit(solution)/shard_map/ppermute | solution.py:23
  2.4 4.8 %collective-permute-start.1 = (f32[6144]{0:T(1024)S(1)}, f32[6144]{0:T(1024)S(1)}, u32[]{:S(2)}, u32[]{:S(2)}) collective-permute-start(f32[6144]{0:T(1024)S(1)} %reduce_sum.9), channel_id=1, source_target_pairs={{0,2},{1,3},{2,0},{3,1},{4,6},{5,7},{6,4},{7,5},{8,10},{9,11},{10,... | collective-permute-start | bytes 73736 | tf_op jit(solution)/shard_map/ppermute | solution.py:23
  5.0 3.3 %collective-permute-start = (f32[6144]{0:T(1024)S(1)}, f32[6144]{0:T(1024)S(1)}, u32[]{:S(2)}, u32[]{:S(2)}) collective-permute-start(f32[6144]{0:T(1024)S(1)} %reduce_sum.9), channel_id=1, source_target_pairs={{0,3},{1,2},{2,1},{3,0},{4,7},{5,6},{6,5},{7,4},{8,11},{9,10},{10,... | collective-permute-start | bytes 73736 | tf_op jit(solution)/shard_map/ppermute | solution.py:23
  8.3 8.8 %collective-permute-start.5 = (f32[6144]{0:T(1024)S(1)}, f32[6144]{0:T(1024)S(1)}, u32[]{:S(2)}, u32[]{:S(2)}) collective-permute-start(f32[6144]{0:T(1024)S(1)} %add_add_fusion), channel_id=1, source_target_pairs={{0,4},{1,5},{2,6},{3,7},{4,0},{5,1},{6,2},{7,3},{8,12},{9,13},{10,... | collective-permute-start | bytes 73736 | tf_op jit(solution)/shard_map/ppermute | solution.py:23
  9.9 7.1 %collective-permute-start.4 = (f32[6144]{0:T(1024)S(1)}, f32[6144]{0:T(1024)S(1)}, u32[]{:S(2)}, u32[]{:S(2)}) collective-permute-start(f32[6144]{0:T(1024)S(1)} %add_add_fusion), channel_id=1, source_target_pairs={{0,8},{1,9},{2,10},{3,11},{4,12},{5,13},{6,14},{7,15},{8,0},{9,1},... | collective-permute-start | bytes 73736 | tf_op jit(solution)/shard_map/ppermute | solution.py:23
  12.5 5.6 %collective-permute-start.3 = (f32[6144]{0:T(1024)S(1)}, f32[6144]{0:T(1024)S(1)}, u32[]{:S(2)}, u32[]{:S(2)}) collective-permute-start(f32[6144]{0:T(1024)S(1)} %add_add_fusion), channel_id=1, source_target_pairs={{0,12},{1,13},{2,14},{3,15},{4,8},{5,9},{6,10},{7,11},{8,4},{9,5},... | collective-permute-start | bytes 73736 | tf_op jit(solution)/shard_map/ppermute | solution.py:23
  34.0 0.7 copy-start.2
  34.2 1.8 %collective-permute-start.6 = (f32[32,3200]{1,0:T(8,128)S(1)}, f32[32,3200]{1,0:T(8,128)S(1)}, u32[]{:S(2)}, u32[]{:S(2)}) collective-permute-start(f32[32,3200]{1,0:T(8,128)S(1)} %bitcast.160), channel_id=1, source_target_pairs={{0,1},{1,0},{2,3},{3,2},{4,5},{5,4},{6,7},{7,6},{8,9},{9,8},{10,11... | collective-permute-start | bytes 1228808 | tf_op jit(solution)/shard_map/ppermute | solution.py:18
  37.4 10.9 %collective-permute-start.7 = (f32[32,2944]{1,0:T(8,128)S(1)}, f32[32,2944]{1,0:T(8,128)S(1)}, u32[]{:S(2)}, u32[]{:S(2)}) collective-permute-start(f32[32,2944]{1,0:T(8,128)S(1)} %fusion.2), channel_id=1, source_target_pairs={{0,2},{1,3},{2,0},{3,1},{4,6},{5,7},{6,4},{7,5},{8,10},{9,11},{10,... | collective-permute-start | bytes 1130504 | tf_op jit(solution)/shard_map/ppermute | solution.py:18
  49.4 0.7 copy-start.3
  49.6 9.3 %collective-permute-start.8 = (f32[32,2688]{1,0:T(8,128)S(1)}, f32[32,2688]{1,0:T(8,128)S(1)}, u32[]{:S(2)}, u32[]{:S(2)}) collective-permute-start(f32[32,2688]{1,0:T(8,128)S(1)} %fusion.3), channel_id=1, source_target_pairs={{0,4},{1,5},{2,6},{3,7},{4,0},{5,1},{6,2},{7,3},{8,12},{9,13},{10,... | collective-permute-start | bytes 1032200 | tf_op jit(solution)/shard_map/ppermute | solution.py:18
  60.2 15.3 %collective-permute-start.9 = (f32[32,2432]{1,0:T(8,128)S(1)}, f32[32,2432]{1,0:T(8,128)S(1)}, u32[]{:S(2)}, u32[]{:S(2)}) collective-permute-start(f32[32,2432]{1,0:T(8,128)S(1)} %fusion.4), channel_id=1, source_target_pairs={{0,8},{1,9},{2,10},{3,11},{4,12},{5,13},{6,14},{7,15},{8,0},{9,1},... | collective-permute-start | bytes 933896 | tf_op jit(solution)/shard_map/ppermute | solution.py:18
  78.8 13.3 %copy-start.1 = (f32[32,2048]{1,0:T(8,128)}, f32[32,2048]{1,0:T(8,128)S(1)}, u32[]{:S(2)}) copy-start(f32[32,2048]{1,0:T(8,128)S(1)} %reshape.1664) | copy-start | bytes 786436
  78.8 1.9 %collective-permute-start.12 = (f32[2048]{0:T(1024)S(1)}, f32[2048]{0:T(1024)S(1)}, u32[]{:S(2)}, u32[]{:S(2)}) collective-permute-start(f32[2048]{0:T(1024)S(1)} %reduce_max.19), channel_id=1, source_target_pairs={{0,1},{1,0},{2,3},{3,2},{4,5},{5,4},{6,7},{7,6},{8,9},{9,8},{10,11... | collective-permute-start | bytes 24584 | tf_op jit(solution)/shard_map/ppermute | solution.py:23
  78.9 3.7 %collective-permute-start.11 = (f32[2048]{0:T(1024)S(1)}, f32[2048]{0:T(1024)S(1)}, u32[]{:S(2)}, u32[]{:S(2)}) collective-permute-start(f32[2048]{0:T(1024)S(1)} %reduce_max.19), channel_id=1, source_target_pairs={{0,2},{1,3},{2,0},{3,1},{4,6},{5,7},{6,4},{7,5},{8,10},{9,11},{10,... | collective-permute-start | bytes 24584 | tf_op jit(solution)/shard_map/ppermute | solution.py:23
  79.7 3.1 %collective-permute-start.10 = (f32[2048]{0:T(1024)S(1)}, f32[2048]{0:T(1024)S(1)}, u32[]{:S(2)}, u32[]{:S(2)}) collective-permute-start(f32[2048]{0:T(1024)S(1)} %reduce_max.19), channel_id=1, source_target_pairs={{0,3},{1,2},{2,1},{3,0},{4,7},{5,6},{6,5},{7,4},{8,11},{9,10},{10,... | collective-permute-start | bytes 24584 | tf_op jit(solution)/shard_map/ppermute | solution.py:23
  82.8 4.5 %collective-permute-start.15 = (f32[2048]{0:T(1024)S(1)}, f32[2048]{0:T(1024)S(1)}, u32[]{:S(2)}, u32[]{:S(2)}) collective-permute-start(f32[2048]{0:T(1024)S(1)} %maximum_maximum_fusion.1), channel_id=1, source_target_pairs={{0,4},{1,5},{2,6},{3,7},{4,0},{5,1},{6,2},{7,3},{8,12},{9,13},{10,... | collective-permute-start | bytes 24584 | tf_op jit(solution)/shard_map/ppermute | solution.py:23
  82.9 4.7 %collective-permute-start.14 = (f32[2048]{0:T(1024)S(1)}, f32[2048]{0:T(1024)S(1)}, u32[]{:S(2)}, u32[]{:S(2)}) collective-permute-start(f32[2048]{0:T(1024)S(1)} %maximum_maximum_fusion.1), channel_id=1, source_target_pairs={{0,8},{1,9},{2,10},{3,11},{4,12},{5,13},{6,14},{7,15},{8,0},{9,1},... | collective-permute-start | bytes 24584 | tf_op jit(solution)/shard_map/ppermute | solution.py:23
  86.0 5.4 %collective-permute-start.13 = (f32[2048]{0:T(1024)S(1)}, f32[2048]{0:T(1024)S(1)}, u32[]{:S(2)}, u32[]{:S(2)}) collective-permute-start(f32[2048]{0:T(1024)S(1)} %maximum_maximum_fusion.1), channel_id=1, source_target_pairs={{0,12},{1,13},{2,14},{3,15},{4,8},{5,9},{6,10},{7,11},{8,4},{9,5},... | collective-permute-start | bytes 24584 | tf_op jit(solution)/shard_map/ppermute | solution.py:23

commit v4 on v3

--- a/solution.py
+++ b/solution.py
@@ -1,8 +1,11 @@
+import functools
 import math
 
 import jax
 import jax.numpy as jnp
 from jax import lax
+from jax.experimental import pallas as pl
+from jax.experimental.pallas import tpu as pltpu
 from jax.sharding import PartitionSpec as P
 
 TS = 2048
@@ -54,6 +57,46 @@
         chosen = (amounts >> bit_index & 1)[:, None] == 1
         current = jnp.where(chosen, current[:, span : span + keep_len], current[:, :keep_len])
     return current
+
+
+def local_tree_kernel(widths_seq, x_ref, mean_ref, amount_ref, out_ref):
+    rows = x_ref.shape[0]
+    cur = x_ref[:, : widths_seq[0]] - mean_ref[:, : widths_seq[0]]
+    row_id = lax.broadcasted_iota(jnp.int32, (rows, 1), 0)
+    for section_index in range(len(widths_seq) - 1):
+        mask = 2**section_index
+        width = widths_seq[section_index]
+        new_width = widths_seq[section_index + 1]
+        is_upper = (row_id & mask) != 0
+        from_below = pltpu.roll(cur, rows - mask, axis=0)
+        from_above = pltpu.roll(cur, mask, axis=0)
+        partner = jnp.where(is_upper, from_above, from_below)
+        lower = jnp.where(is_upper, partner, cur)
+        shifted = jnp.where(is_upper, cur, partner)
+        amount = amount_ref[section_index][:, 0:1]
+        for bit_index in range((SHIFT - 1).bit_length()):
+            span = 2**bit_index
+            chosen = (amount >> bit_index & 1) == 1
+            shifted = jnp.where(chosen, pltpu.roll(shifted, width - span, axis=1), shifted)
+        cur = lower[:, :new_width] + shifted[:, :new_width]
+    out_ref[...] = cur
+
+
+def local_tree(filterbank, channel_mean, amounts, widths_seq):
+    rows = filterbank.shape[0]
+    vmem = pl.BlockSpec(memory_space=pltpu.VMEM)
+    lane_amounts = jnp.broadcast_to(amounts[:, :, None], amounts.shape + (128,))
+    levels = len(widths_seq) - 1
+    work = rows * sum(widths_seq[:-1])
+    return pl.pallas_call(
+        functools.partial(local_tree_kernel, tuple(widths_seq)),
+        out_shape=jax.ShapeDtypeStruct((rows, widths_seq[-1]), jnp.float32),
+        in_specs=[vmem, vmem, vmem],
+        out_specs=vmem,
+        cost_estimate=pl.CostEstimate(
+            flops=40 * work, transcendentals=0, bytes_accessed=4 * (rows * widths_seq[0] + rows * widths_seq[-1])
+        ),
+    )(filterbank, channel_mean[None, :], lane_amounts[:levels])
 
 
 def merge_section(current, offsets_now, section_index, new_length):
@@ -114,14 +157,8 @@
 
     partial_value = jnp.sum(filterbank, axis=0)
     channel_mean = butterfly(partial_value, "band", jnp.add) / channels_all
-    current = filterbank - channel_mean[None, :]
-    for local_section_index in range(local_count):
-        current = merge_section(
-            current,
-            offsets[local_section_index],
-            local_section_index,
-            length_after(local_section_index + 1),
-        )
+    widths_seq = [length_after(section) for section in range(local_count + 1)]
+    current = local_tree(filterbank, channel_mean, offsets[:local_count], widths_seq)
     band_index = lax.axis_index("band")
     for bit_index in range(band_count.bit_length() - 1):
         section_index = local_count + bit_index

time: 92.4 us -> 87.6 us (0.948)
  other arithmetic: 19.7 us -> 7.93 us
  Pallas kernels: 0 us -> 9.1 us
  waiting for transfers between devices: 41.8 us -> 50.4 us
  local copies, waits for them, and re-layouts: 10.4 us -> 2.06 us
  starting transfers between devices: 16.4 us -> 15 us
    pallas_call x0 -> x1, Pallas kernels: none -> 9.1 us  [local_tree(): pl.pallas_call(functools.partial(local_tree_kernel, tuple(widths_seq)), o...]
    select_n x96 -> x28, other arithmetic: 12.8 us -> 4.16 us  [shift_rows(): jnp.where(chosen, current[:, span:span + keep_len], current[:, :keep_len])]
    ppermute x4, waiting for transfers between devices: 33.5 us -> 37.8 us  [from_partner(): return lax.ppermute(value, axis, pairs)]
    ppermute x12, waiting for transfers between devices: 8.37 us -> 12.6 us  [from_xor(): return lax.ppermute(value, axis, pairs)]
    eq x48 -> x0, local copies, waits for them, and re-layouts: 4.17 us -> none  [shift_rows(): chosen = (amounts >> bit_index & 1)[:, None] == 1]
    slice x7 -> x2, local copies, waits for them, and re-layouts: 2.24 us -> 0.01 us  [per_device(): offsets[:local_count]]
    another operation x16 -> x0, local copies, waits for them, and re-layouts: 1.88 us -> none  [the longest x2 0.64 us: merge_section(): blocks = current.reshape(groups, 2, group_trials, current.shape[1])]
    add x4 -> x0, other arithmetic: 1.54 us -> none  [the longest x3 1.33 us: merge_section(): lower_part + shift_rows(upper_flat, amounts[:, 0].reshape(-1), new_length...]
  transfers between devices with their start and end apart: 16 -> 16, of which waited for: 10 -> 12; matrix products, arithmetic and copies ran while one was open for 7% -> 1% of each run, Pallas kernels for 0% -> 0%
where the time goes in v4:
time: 87.6 us; the launch traced here: 87.4 us
  waiting for transfers between devices  50.4 us (58%)
  starting transfers between devices  15 us (17%)
  Pallas kernels  9.1 us (10%)
  other arithmetic  7.93 us (9%)
  local copies, waits for them, and re-layouts  2.06 us (2%)
  matrix products  1.87 us (2%)
  between operations  0.99 us (1%)
    ppermute x4, waiting for transfers between devices, from_partner(): return lax.ppermute(value, axis, pairs)  37.8 us
    ppermute x12, starting transfers between devices, from_xor(): return lax.ppermute(value, axis, pairs)  14 us
    ppermute x12, waiting for transfers between devices, from_xor(): return lax.ppermute(value, axis, pairs)  12.6 us
    pallas_call x1, Pallas kernels, local_tree(): pl.pallas_call(functools.partial(local_tree_kernel, tuple(widths_seq)), o...  9.1 us
    select_n x28, other arithmetic, shift_rows(): jnp.where(chosen, current[:, span:span + keep_len], current[:, :keep_len])  4.16 us
    dot_general x1, matrix products, boxcar_max(): jnp.dot(paired, joined, precision=lax.Precision.HIGHEST, preferred_elemen...  1.87 us
  transfers between devices with their start and end apart: 16, of which 12 were waited for; matrix products, arithmetic and copies ran while one was open for 1% of the time, Pallas kernels for 0%

profile of v4, /device:TPU:0, one launch (start us, length us, event | category | flops | bytes accessed | tf_op | source)
XLA Modules:
  0.0 87.4 jit_solution(1860610663577267169)
XLA Ops:
  0.6 1.2 %reduce_sum.9 = f32[6144]{0:T(1024)S(1)} reduce(f32[32,6144]{1,0:T(8,128)} %x_ref.1, f32[]{:T(128)} %constant.87.clone.1), dimensions={0}, to_apply=%region_0.0 | reduce | flops 190464 | bytes 811012 | tf_op jit(solution)/shard_map/reduce_sum | solution.py:158
  1.9 0.5 collective-permute-start.2
  2.4 2.6 %collective-permute-start.1 = (f32[6144]{0:T(1024)S(1)}, f32[6144]{0:T(1024)S(1)}, u32[]{:S(2)}, u32[]{:S(2)}) collective-permute-start(f32[6144]{0:T(1024)S(1)} %reduce_sum.9), channel_id=1, source_target_pairs={{0,2},{1,3},{2,0},{3,1},{4,6},{5,7},{6,4},{7,5},{8,10},{9,11},{10,... | collective-permute-start | bytes 73736 | tf_op jit(solution)/shard_map/ppermute | solution.py:26
  5.0 1.7 %collective-permute-done.1 = f32[6144]{0:T(1024)S(1)} collective-permute-done((f32[6144]{0:T(1024)S(1)}, f32[6144]{0:T(1024)S(1)}, u32[]{:S(2)}, u32[]{:S(2)}) %collective-permute-start.1) | collective-permute-done | bytes 24608 | tf_op jit(solution)/shard_map/ppermute | solution.py:26
  6.8 1.4 %collective-permute-done = f32[6144]{0:T(1024)S(1)} collective-permute-done((f32[6144]{0:T(1024)S(1)}, f32[6144]{0:T(1024)S(1)}, u32[]{:S(2)}, u32[]{:S(2)}) %collective-permute-start) | collective-permute-done | bytes 24608 | tf_op jit(solution)/shard_map/ppermute | solution.py:26
  8.2 1.6 %collective-permute-start.5 = (f32[6144]{0:T(1024)S(1)}, f32[6144]{0:T(1024)S(1)}, u32[]{:S(2)}, u32[]{:S(2)}) collective-permute-start(f32[6144]{0:T(1024)S(1)} %add_add_fusion), channel_id=1, source_target_pairs={{0,4},{1,5},{2,6},{3,7},{4,0},{5,1},{6,2},{7,3},{8,12},{9,13},{10,... | collective-permute-start | bytes 73736 | tf_op jit(solution)/shard_map/ppermute | solution.py:26
  9.9 2.6 %collective-permute-start.4 = (f32[6144]{0:T(1024)S(1)}, f32[6144]{0:T(1024)S(1)}, u32[]{:S(2)}, u32[]{:S(2)}) collective-permute-start(f32[6144]{0:T(1024)S(1)} %add_add_fusion), channel_id=1, source_target_pairs={{0,8},{1,9},{2,10},{3,11},{4,12},{5,13},{6,14},{7,15},{8,0},{9,1},... | collective-permute-start | bytes 73736 | tf_op jit(solution)/shard_map/ppermute | solution.py:26
  12.5 0.2 collective-permute-start.3
  12.7 2.3 %collective-permute-done.4 = f32[6144]{0:T(1024)S(1)} collective-permute-done((f32[6144]{0:T(1024)S(1)}, f32[6144]{0:T(1024)S(1)}, u32[]{:S(2)}, u32[]{:S(2)}) %collective-permute-start.4) | collective-permute-done | bytes 24608 | tf_op jit(solution)/shard_map/ppermute | solution.py:26
  14.9 3.1 %collective-permute-done.3 = f32[6144]{0:T(1024)S(1)} collective-permute-done((f32[6144]{0:T(1024)S(1)}, f32[6144]{0:T(1024)S(1)}, u32[]{:S(2)}, u32[]{:S(2)}) %collective-permute-start.3) | collective-permute-done | bytes 24608 | tf_op jit(solution)/shard_map/ppermute | solution.py:26
  18.1 0.6 add_multiply_fusion
  18.7 0.7 broadcast_in_dim.318.amount_ref
  19.4 9.1 %shard_map.50 = f32[32,3200]{1,0:T(8,128)} custom-call(f32[32,6144]{1,0:T(8,128)} %x_ref.1, f32[1,6144]{1,0:T(1,128)} %bitcast.87, s32[5,32,128]{2,1,0:T(8,128)} %broadcast_in_dim.318.amount_ref), custom_call_target="tpu_custom_call" | custom-call | flops 25395200 | bytes 983040 | tf_op jit(solution)/shard_map/pallas_call | solution.py:91
  28.6 1.9 %collective-permute-done.6 = f32[32,3200]{1,0:T(8,128)S(1)} collective-permute-done((f32[32,3200]{1,0:T(8,128)}, f32[32,3200]{1,0:T(8,128)S(1)}, u32[]{:S(2)}, u32[]{:S(2)}) %collective-permute-start.6) | collective-permute-done | bytes 409632 | tf_op jit(solution)/shard_map/ppermute | solution.py:21
  31.7 0.6 copy-done
  32.4 0.2 fusion.2
  32.5 0.9 collective-permute-start.7
  33.4 10.7 %collective-permute-done.7 = f32[32,2944]{1,0:T(8,128)S(1)} collective-permute-done((f32[32,2944]{1,0:T(8,128)S(1)}, f32[32,2944]{1,0:T(8,128)S(1)}, u32[]{:S(2)}, u32[]{:S(2)}) %collective-permute-start.7) | collective-permute-done | bytes 376864 | tf_op jit(solution)/shard_map/ppermute | solution.py:21
  45.5 0.4 copy-done.3
  46.0 9.6 %collective-permute-done.8 = f32[32,2688]{1,0:T(8,128)S(1)} collective-permute-done((f32[32,2688]{1,0:T(8,128)S(1)}, f32[32,2688]{1,0:T(8,128)S(1)}, u32[]{:S(2)}, u32[]{:S(2)}) %collective-permute-start.8) | collective-permute-done | bytes 344096 | tf_op jit(solution)/shard_map/ppermute | solution.py:21
  57.0 0.3 fusion.1
  57.3 15.7 %collective-permute-done.9 = f32[32,2432]{1,0:T(8,128)S(1)} collective-permute-done((f32[32,2432]{1,0:T(8,128)S(1)}, f32[32,2432]{1,0:T(8,128)S(1)}, u32[]{:S(2)}, u32[]{:S(2)}) %collective-permute-start.9) | collective-permute-done | bytes 311328 | tf_op jit(solution)/shard_map/ppermute | solution.py:21
  74.3 1.9 %convolution_reduce_fusion = f32[512,128]{1,0:T(8,128)S(1)} fusion(f32[512,256,1]{1,0,2:T(8,128)S(1)} %bitcast.86, f32[8,128,256]{2,1,0:T(8,128)S(1)} %bitcast.85), kind=kOutput, calls=%fused_computation | convolution fusion | flops 1611071488 | bytes 1835008 | tf_op jit(solution)/shard_map/dot_general | solution.py:137
  76.4 0.9 collective-permute-start.11
  77.2 1.0 %collective-permute-start.10 = (f32[2048]{0:T(1024)S(1)}, f32[2048]{0:T(1024)S(1)}, u32[]{:S(2)}, u32[]{:S(2)}) collective-permute-start(f32[2048]{0:T(1024)S(1)} %reduce_max.19), channel_id=1, source_target_pairs={{0,3},{1,2},{2,1},{3,0},{4,7},{5,6},{6,5},{7,4},{8,11},{9,10},{10,... | collective-permute-start | bytes 24584 | tf_op jit(solution)/shard_map/ppermute | solution.py:26
  78.2 1.9 %collective-permute-done.11 = f32[2048]{0:T(1024)S(1)} collective-permute-done((f32[2048]{0:T(1024)S(1)}, f32[2048]{0:T(1024)S(1)}, u32[]{:S(2)}, u32[]{:S(2)}) %collective-permute-start.11) | collective-permute-done | bytes 8224 | tf_op jit(solution)/shard_map/ppermute | solution.py:26
  80.1 0.2 collective-permute-done.10
  80.4 0.9 %collective-permute-start.14 = (f32[2048]{0:T(1024)S(1)}, f32[2048]{0:T(1024)S(1)}, u32[]{:S(2)}, u32[]{:S(2)}) collective-permute-start(f32[2048]{0:T(1024)S(1)} %maximum_maximum_fusion.1), channel_id=1, source_target_pairs={{0,8},{1,9},{2,10},{3,11},{4,12},{5,13},{6,14},{7,15},{8,0},{9,1},... | collective-permute-start | bytes 24584 | tf_op jit(solution)/shard_map/ppermute | solution.py:26
  81.3 3.5 %collective-permute-start.13 = (f32[2048]{0:T(1024)S(1)}, f32[2048]{0:T(1024)S(1)}, u32[]{:S(2)}, u32[]{:S(2)}) collective-permute-start(f32[2048]{0:T(1024)S(1)} %maximum_maximum_fusion.1), channel_id=1, source_target_pairs={{0,12},{1,13},{2,14},{3,15},{4,8},{5,9},{6,10},{7,11},{8,4},{9,5},... | collective-permute-start | bytes 24584 | tf_op jit(solution)/shard_map/ppermute | solution.py:26
  84.8 0.2 collective-permute-done.14
  85.0 1.7 %collective-permute-done.13 = f32[2048]{0:T(1024)S(1)} collective-permute-done((f32[2048]{0:T(1024)S(1)}, f32[2048]{0:T(1024)S(1)}, u32[]{:S(2)}, u32[]{:S(2)}) %collective-permute-start.13) | collective-permute-done | bytes 8224 | tf_op jit(solution)/shard_map/ppermute | solution.py:26
  86.7 0.6 maximum_maximum_fusion
  (67 shorter events, 5.6 us)
Async XLA Ops:
  0.6 18.1 %slice-start = ((s32[9,32]{1,0:T(8,128)}), s32[5,32]{1,0:T(8,128)S(1)}, s32[]{:S(2)}) async-start(s32[9,32]{1,0:T(8,128)} %param.4), calls=%async_computation | async-start | bytes 8192 | tf_op jit(solution)/shard_map/slice | solution.py:161
  1.9 26.7 %copy-start.2 = (s32[9,32]{1,0:T(8,128)S(1)}, s32[9,32]{1,0:T(8,128)}, u32[]{:S(2)}) copy-start(s32[9,32]{1,0:T(8,128)} %param.4) | copy-start | bytes 3460
  1.9 3.2 %collective-permute-start.2 = (f32[6144]{0:T(1024)S(1)}, f32[6144]{0:T(1024)S(1)}, u32[]{:S(2)}, u32[]{:S(2)}) collective-permute-start(f32[6144]{0:T(1024)S(1)} %reduce_sum.9), channel_id=1, source_target_pairs={{0,1},{1,0},{2,3},{3,2},{4,5},{5,4},{6,7},{7,6},{8,9},{9,8},{10,11... | collective-permute-start | bytes 73736 | tf_op jit(solution)/shard_map/ppermute | solution.py:26
  2.4 4.4 %collective-permute-start.1 = (f32[6144]{0:T(1024)S(1)}, f32[6144]{0:T(1024)S(1)}, u32[]{:S(2)}, u32[]{:S(2)}) collective-permute-start(f32[6144]{0:T(1024)S(1)} %reduce_sum.9), channel_id=1, source_target_pairs={{0,2},{1,3},{2,0},{3,1},{4,6},{5,7},{6,4},{7,5},{8,10},{9,11},{10,... | collective-permute-start | bytes 73736 | tf_op jit(solution)/shard_map/ppermute | solution.py:26
  4.9 3.3 %collective-permute-start = (f32[6144]{0:T(1024)S(1)}, f32[6144]{0:T(1024)S(1)}, u32[]{:S(2)}, u32[]{:S(2)}) collective-permute-start(f32[6144]{0:T(1024)S(1)} %reduce_sum.9), channel_id=1, source_target_pairs={{0,3},{1,2},{2,1},{3,0},{4,7},{5,6},{6,5},{7,4},{8,11},{9,10},{10,... | collective-permute-start | bytes 73736 | tf_op jit(solution)/shard_map/ppermute | solution.py:26
  8.2 4.5 %collective-permute-start.5 = (f32[6144]{0:T(1024)S(1)}, f32[6144]{0:T(1024)S(1)}, u32[]{:S(2)}, u32[]{:S(2)}) collective-permute-start(f32[6144]{0:T(1024)S(1)} %add_add_fusion), channel_id=1, source_target_pairs={{0,4},{1,5},{2,6},{3,7},{4,0},{5,1},{6,2},{7,3},{8,12},{9,13},{10,... | collective-permute-start | bytes 73736 | tf_op jit(solution)/shard_map/ppermute | solution.py:26
  9.9 5.1 %collective-permute-start.4 = (f32[6144]{0:T(1024)S(1)}, f32[6144]{0:T(1024)S(1)}, u32[]{:S(2)}, u32[]{:S(2)}) collective-permute-start(f32[6144]{0:T(1024)S(1)} %add_add_fusion), channel_id=1, source_target_pairs={{0,8},{1,9},{2,10},{3,11},{4,12},{5,13},{6,14},{7,15},{8,0},{9,1},... | collective-permute-start | bytes 73736 | tf_op jit(solution)/shard_map/ppermute | solution.py:26
  12.5 5.6 %collective-permute-start.3 = (f32[6144]{0:T(1024)S(1)}, f32[6144]{0:T(1024)S(1)}, u32[]{:S(2)}, u32[]{:S(2)}) collective-permute-start(f32[6144]{0:T(1024)S(1)} %add_add_fusion), channel_id=1, source_target_pairs={{0,12},{1,13},{2,14},{3,15},{4,8},{5,9},{6,10},{7,11},{8,4},{9,5},... | collective-permute-start | bytes 73736 | tf_op jit(solution)/shard_map/ppermute | solution.py:26
  28.5 2.0 %collective-permute-start.6 = (f32[32,3200]{1,0:T(8,128)}, f32[32,3200]{1,0:T(8,128)S(1)}, u32[]{:S(2)}, u32[]{:S(2)}) collective-permute-start(f32[32,3200]{1,0:T(8,128)} %shard_map.50), channel_id=1, source_target_pairs={{0,1},{1,0},{2,3},{3,2},{4,5},{5,4},{6,7},{7,6},{8,9},{9,8},{10,11... | collective-permute-start | bytes 1228808 | tf_op jit(solution)/shard_map/ppermute | solution.py:21
  31.4 1.0 %copy-start = (f32[32,3200]{1,0:T(8,128)S(1)}, f32[32,3200]{1,0:T(8,128)}, u32[]{:S(2)}) copy-start(f32[32,3200]{1,0:T(8,128)} %shard_map.50) | copy-start | bytes 1228804
  32.5 11.5 %collective-permute-start.7 = (f32[32,2944]{1,0:T(8,128)S(1)}, f32[32,2944]{1,0:T(8,128)S(1)}, u32[]{:S(2)}, u32[]{:S(2)}) collective-permute-start(f32[32,2944]{1,0:T(8,128)S(1)} %fusion.2), channel_id=1, source_target_pairs={{0,2},{1,3},{2,0},{3,1},{4,6},{5,7},{6,4},{7,5},{8,10},{9,11},{10,... | collective-permute-start | bytes 1130504 | tf_op jit(solution)/shard_map/ppermute | solution.py:21
  45.2 0.7 copy-start.3
  45.4 10.1 %collective-permute-start.8 = (f32[32,2688]{1,0:T(8,128)S(1)}, f32[32,2688]{1,0:T(8,128)S(1)}, u32[]{:S(2)}, u32[]{:S(2)}) collective-permute-start(f32[32,2688]{1,0:T(8,128)S(1)} %fusion.3), channel_id=1, source_target_pairs={{0,4},{1,5},{2,6},{3,7},{4,0},{5,1},{6,2},{7,3},{8,12},{9,13},{10,... | collective-permute-start | bytes 1032200 | tf_op jit(solution)/shard_map/ppermute | solution.py:21
  56.8 16.2 %collective-permute-start.9 = (f32[32,2432]{1,0:T(8,128)S(1)}, f32[32,2432]{1,0:T(8,128)S(1)}, u32[]{:S(2)}, u32[]{:S(2)}) collective-permute-start(f32[32,2432]{1,0:T(8,128)S(1)} %fusion.4), channel_id=1, source_target_pairs={{0,8},{1,9},{2,10},{3,11},{4,12},{5,13},{6,14},{7,15},{8,0},{9,1},... | collective-permute-start | bytes 933896 | tf_op jit(solution)/shard_map/ppermute | solution.py:21
  76.2 11.1 %copy-start.1 = (f32[32,2048]{1,0:T(8,128)}, f32[32,2048]{1,0:T(8,128)S(1)}, u32[]{:S(2)}) copy-start(f32[32,2048]{1,0:T(8,128)S(1)} %reshape.486) | copy-start | bytes 786436
  76.3 1.9 %collective-permute-start.12 = (f32[2048]{0:T(1024)S(1)}, f32[2048]{0:T(1024)S(1)}, u32[]{:S(2)}, u32[]{:S(2)}) collective-permute-start(f32[2048]{0:T(1024)S(1)} %reduce_max.19), channel_id=1, source_target_pairs={{0,1},{1,0},{2,3},{3,2},{4,5},{5,4},{6,7},{7,6},{8,9},{9,8},{10,11... | collective-permute-start | bytes 24584 | tf_op jit(solution)/shard_map/ppermute | solution.py:26
  76.4 3.7 %collective-permute-start.11 = (f32[2048]{0:T(1024)S(1)}, f32[2048]{0:T(1024)S(1)}, u32[]{:S(2)}, u32[]{:S(2)}) collective-permute-start(f32[2048]{0:T(1024)S(1)} %reduce_max.19), channel_id=1, source_target_pairs={{0,2},{1,3},{2,0},{3,1},{4,6},{5,7},{6,4},{7,5},{8,10},{9,11},{10,... | collective-permute-start | bytes 24584 | tf_op jit(solution)/shard_map/ppermute | solution.py:26
  77.2 3.1 %collective-permute-start.10 = (f32[2048]{0:T(1024)S(1)}, f32[2048]{0:T(1024)S(1)}, u32[]{:S(2)}, u32[]{:S(2)}) collective-permute-start(f32[2048]{0:T(1024)S(1)} %reduce_max.19), channel_id=1, source_target_pairs={{0,3},{1,2},{2,1},{3,0},{4,7},{5,6},{6,5},{7,4},{8,11},{9,10},{10,... | collective-permute-start | bytes 24584 | tf_op jit(solution)/shard_map/ppermute | solution.py:26
  80.3 4.5 %collective-permute-start.15 = (f32[2048]{0:T(1024)S(1)}, f32[2048]{0:T(1024)S(1)}, u32[]{:S(2)}, u32[]{:S(2)}) collective-permute-start(f32[2048]{0:T(1024)S(1)} %maximum_maximum_fusion.1), channel_id=1, source_target_pairs={{0,4},{1,5},{2,6},{3,7},{4,0},{5,1},{6,2},{7,3},{8,12},{9,13},{10,... | collective-permute-start | bytes 24584 | tf_op jit(solution)/shard_map/ppermute | solution.py:26
  80.4 4.6 %collective-permute-start.14 = (f32[2048]{0:T(1024)S(1)}, f32[2048]{0:T(1024)S(1)}, u32[]{:S(2)}, u32[]{:S(2)}) collective-permute-start(f32[2048]{0:T(1024)S(1)} %maximum_maximum_fusion.1), channel_id=1, source_target_pairs={{0,8},{1,9},{2,10},{3,11},{4,12},{5,13},{6,14},{7,15},{8,0},{9,1},... | collective-permute-start | bytes 24584 | tf_op jit(solution)/shard_map/ppermute | solution.py:26
  81.3 5.4 %collective-permute-start.13 = (f32[2048]{0:T(1024)S(1)}, f32[2048]{0:T(1024)S(1)}, u32[]{:S(2)}, u32[]{:S(2)}) collective-permute-start(f32[2048]{0:T(1024)S(1)} %maximum_maximum_fusion.1), channel_id=1, source_target_pairs={{0,12},{1,13},{2,14},{3,15},{4,8},{5,9},{6,10},{7,11},{8,4},{9,5},... | collective-permute-start | bytes 24584 | tf_op jit(solution)/shard_map/ppermute | solution.py:26

commit v5 on v4

--- a/solution.py
+++ b/solution.py
@@ -13,6 +13,7 @@
 SHIFT = 256
 TAPS = 128
 TEMPLATES = 8
+TAIL_WIDTH = 1152
 
 
 def from_partner(value, axis, distance):
@@ -160,16 +161,33 @@
     widths_seq = [length_after(section) for section in range(local_count + 1)]
     current = local_tree(filterbank, channel_mean, offsets[:local_count], widths_seq)
     band_index = lax.axis_index("band")
-    for bit_index in range(band_count.bit_length() - 1):
-        section_index = local_count + bit_index
-        new_length = length_after(section_index + 1)
-        partner = from_partner(current, "band", bit_index)
+    bit_count = band_count.bit_length() - 1
+    tail_width = TAIL_WIDTH
+
+    def halves(own, partner, bit_index):
         upper_half = band_index // 2**bit_index % 2 == 1
-        lower_part = jnp.where(upper_half, partner, current)
-        upper_part = jnp.where(upper_half, current, partner)
-        current = lower_part[:, :new_length] + shift_rows(
-            upper_part, offsets[section_index], new_length
-        )
+        return jnp.where(upper_half, partner, own), jnp.where(upper_half, own, partner)
+
+    head = current[:, : current.shape[1] - tail_width]
+    tail = current[:, current.shape[1] - tail_width :]
+    partner_head = from_partner(head, "band", 0)
+    for bit_index in range(bit_count):
+        amounts = offsets[local_count + bit_index]
+        tail, partner_head = lax.optimization_barrier((tail, partner_head))
+        lower_head, upper_head = halves(head, partner_head, bit_index)
+        head_width = head.shape[1] - SHIFT
+        new_head = lower_head[:, :head_width] + shift_rows(upper_head, amounts, head_width)
+        partner_tail = from_partner(tail, "band", bit_index)
+        if bit_index + 1 < bit_count:
+            next_partner_head = from_partner(new_head, "band", bit_index + 1)
+            partner_tail, next_partner_head = lax.optimization_barrier((partner_tail, next_partner_head))
+            partner_head = next_partner_head
+        lower_tail, upper_tail = halves(tail, partner_tail, bit_index)
+        lower_window = jnp.concatenate([lower_head[:, head_width:], lower_tail], axis=1)
+        upper_window = jnp.concatenate([upper_head[:, head_width:], upper_tail], axis=1)
+        tail = lower_window[:, :tail_width] + shift_rows(upper_window, amounts, tail_width)
+        head = new_head
+    current = jnp.concatenate([head, tail], axis=1)
     dedispersed = current * (1.0 / math.sqrt(channels_all))
     detection = boxcar_max(dedispersed, widths)
     peak_series = butterfly(jnp.max(detection, axis=0), "band", jnp.maximum)

time: 87.6 us -> 84.9 us (0.969)
  waiting for transfers between devices: 50.4 us -> 41.1 us
  other arithmetic: 7.93 us -> 11.4 us
  starting transfers between devices: 15 us -> 16.9 us
  local copies, waits for them, and re-layouts: 2.06 us -> 2.94 us
    ppermute x4 -> x8, waiting for transfers between devices: 37.8 us -> 26.3 us  [from_partner(): return lax.ppermute(value, axis, pairs)]
    select_n x28 -> x56, other arithmetic: 4.16 us -> 6.37 us  [shift_rows(): jnp.where(chosen, current[:, span:span + keep_len], current[:, :keep_len])]
    ppermute x12, waiting for transfers between devices: 12.6 us -> 14.7 us  [from_xor(): return lax.ppermute(value, axis, pairs)]
    slice x0 -> x10, local copies, waits for them, and re-layouts: none -> 1.92 us  [the longest x1 0.97 us: per_device(): head = current[:, :current.shape[1] - tail_width]]
    ppermute x4 -> x8, starting transfers between devices: 1.01 us -> 2.91 us  [from_partner(): return lax.ppermute(value, axis, pairs)]
    unnamed x8 -> x6, local copies, waits for them, and re-layouts: 1.06 us -> 0.02 us
    select_n x4 -> x8, other arithmetic: 0.15 us -> 1.17 us  [halves(): jnp.where(upper_half, partner, own)]
  transfers between devices with their start and end apart: 16 -> 20, of which waited for: 12 -> 16; matrix products, arithmetic and copies ran while one was open for 1% -> 5% of each run, Pallas kernels for 0% -> 0%
where the time goes in v5:
time: 84.9 us; the launch traced here: 84.6 us
  waiting for transfers between devices  41.1 us (48%)
  starting transfers between devices  16.9 us (20%)
  other arithmetic  11.4 us (13%)
  Pallas kernels  9.1 us (11%)
  local copies, waits for them, and re-layouts  2.94 us (3%)
  matrix products  1.87 us (2%)
  between operations  1.34 us (2%)
    ppermute x8, waiting for transfers between devices, from_partner(): return lax.ppermute(value, axis, pairs)  26.3 us
    ppermute x12, waiting for transfers between devices, from_xor(): return lax.ppermute(value, axis, pairs)  14.7 us
    ppermute x12, starting transfers between devices, from_xor(): return lax.ppermute(value, axis, pairs)  14 us
    pallas_call x1, Pallas kernels, local_tree(): pl.pallas_call(functools.partial(local_tree_kernel, tuple(widths_seq)), o...  9.1 us
    select_n x56, other arithmetic, shift_rows(): jnp.where(chosen, current[:, span:span + keep_len], current[:, :keep_len])  6.37 us
    ppermute x8, starting transfers between devices, from_partner(): return lax.ppermute(value, axis, pairs)  2.91 us
    dot_general x1, matrix products, boxcar_max(): jnp.dot(paired, joined, precision=lax.Precision.HIGHEST, preferred_elemen...  1.87 us
  transfers between devices with their start and end apart: 20, of which 16 were waited for; matrix products, arithmetic and copies ran while one was open for 5% of the time, Pallas kernels for 0%

profile of v5, /device:TPU:0, one launch (start us, length us, event | category | flops | bytes accessed | tf_op | source)
XLA Modules:
  0.0 84.6 jit_solution(17285037654111719046)
XLA Ops:
  0.6 1.2 %reduce_sum.9 = f32[6144]{0:T(1024)S(1)} reduce(f32[32,6144]{1,0:T(8,128)} %x_ref.1, f32[]{:T(128)} %constant.103.clone.1), dimensions={0}, to_apply=%region_0.0 | reduce | flops 190464 | bytes 811012 | tf_op jit(solution)/shard_map/reduce_sum | solution.py:159
  2.4 2.6 %collective-permute-start.1 = (f32[6144]{0:T(1024)S(1)}, f32[6144]{0:T(1024)S(1)}, u32[]{:S(2)}, u32[]{:S(2)}) collective-permute-start(f32[6144]{0:T(1024)S(1)} %reduce_sum.9), channel_id=1, source_target_pairs={{0,2},{1,3},{2,0},{3,1},{4,6},{5,7},{6,4},{7,5},{8,10},{9,11},{10,... | collective-permute-start | bytes 73736 | tf_op jit(solution)/shard_map/ppermute | solution.py:27
  5.0 1.7 %collective-permute-done.1 = f32[6144]{0:T(1024)S(1)} collective-permute-done((f32[6144]{0:T(1024)S(1)}, f32[6144]{0:T(1024)S(1)}, u32[]{:S(2)}, u32[]{:S(2)}) %collective-permute-start.1) | collective-permute-done | bytes 24608 | tf_op jit(solution)/shard_map/ppermute | solution.py:27
  6.7 1.4 %collective-permute-done = f32[6144]{0:T(1024)S(1)} collective-permute-done((f32[6144]{0:T(1024)S(1)}, f32[6144]{0:T(1024)S(1)}, u32[]{:S(2)}, u32[]{:S(2)}) %collective-permute-start) | collective-permute-done | bytes 24608 | tf_op jit(solution)/shard_map/ppermute | solution.py:27
  8.2 1.6 %collective-permute-start.5 = (f32[6144]{0:T(1024)S(1)}, f32[6144]{0:T(1024)S(1)}, u32[]{:S(2)}, u32[]{:S(2)}) collective-permute-start(f32[6144]{0:T(1024)S(1)} %add_add_fusion), channel_id=1, source_target_pairs={{0,4},{1,5},{2,6},{3,7},{4,0},{5,1},{6,2},{7,3},{8,12},{9,13},{10,... | collective-permute-start | bytes 73736 | tf_op jit(solution)/shard_map/ppermute | solution.py:27
  9.9 2.6 %collective-permute-start.4 = (f32[6144]{0:T(1024)S(1)}, f32[6144]{0:T(1024)S(1)}, u32[]{:S(2)}, u32[]{:S(2)}) collective-permute-start(f32[6144]{0:T(1024)S(1)} %add_add_fusion), channel_id=1, source_target_pairs={{0,8},{1,9},{2,10},{3,11},{4,12},{5,13},{6,14},{7,15},{8,0},{9,1},... | collective-permute-start | bytes 73736 | tf_op jit(solution)/shard_map/ppermute | solution.py:27
  12.7 2.3 %collective-permute-done.4 = f32[6144]{0:T(1024)S(1)} collective-permute-done((f32[6144]{0:T(1024)S(1)}, f32[6144]{0:T(1024)S(1)}, u32[]{:S(2)}, u32[]{:S(2)}) %collective-permute-start.4) | collective-permute-done | bytes 24608 | tf_op jit(solution)/shard_map/ppermute | solution.py:27
  14.9 3.1 %collective-permute-done.3 = f32[6144]{0:T(1024)S(1)} collective-permute-done((f32[6144]{0:T(1024)S(1)}, f32[6144]{0:T(1024)S(1)}, u32[]{:S(2)}, u32[]{:S(2)}) %collective-permute-start.3) | collective-permute-done | bytes 24608 | tf_op jit(solution)/shard_map/ppermute | solution.py:27
  18.1 0.6 add_multiply_fusion
  18.7 0.7 broadcast_in_dim.534.amount_ref
  19.4 9.1 %shard_map.50 = f32[32,3200]{1,0:T(8,128)} custom-call(f32[32,6144]{1,0:T(8,128)} %x_ref.1, f32[1,6144]{1,0:T(1,128)} %bitcast.87, s32[5,32,128]{2,1,0:T(8,128)} %broadcast_in_dim.534.amount_ref), custom_call_target="tpu_custom_call" | custom-call | flops 25395200 | bytes 983040 | tf_op jit(solution)/shard_map/pallas_call | solution.py:92
  28.5 1.0 %slice.629 = f32[32,2048]{1,0:T(8,128)S(1)} slice(f32[32,3200]{1,0:T(8,128)} %shard_map.50), slice={[0:32], [0:2048]} | slice | bytes 524288 | tf_op jit(solution)/shard_map/slice | solution.py:171
  29.7 0.9 %slice.628 = f32[32,1152]{1,0:T(8,128)S(1)} slice(f32[32,3200]{1,0:T(8,128)} %shard_map.50), slice={[0:32], [2048:3200]} | slice | bytes 294912 | tf_op jit(solution)/shard_map/slice | solution.py:172
  31.1 1.0 %broadcast_select_fusion.1 = (f32[32,2048]{1,0:T(8,128)S(1)}, f32[32,2048]{1,0:T(8,128)S(1)}) fusion(f32[32,2048]{1,0:T(8,128)S(1)} %collective-permute-done.6, pred[]{:T(512)S(6)} %eq.508, f32[32,3200]{1,0:T(8,128)} %shard_map.50), kind=kLoop, calls=%fused_computation.100 | loop fusion | flops 131072 | bytes 1048577 | tf_op jit(solution)/shard_map/jit(_where)/select_n | solution.py:169
  33.2 0.9 %collective-permute-start.8 = (f32[32,1792]{1,0:T(8,128)S(1)}, f32[32,1792]{1,0:T(8,128)S(1)}, u32[]{:S(2)}, u32[]{:S(2)}) collective-permute-start(f32[32,1792]{1,0:T(8,128)S(1)} %fusion.2), channel_id=1, source_target_pairs={{0,2},{1,3},{2,0},{3,1},{4,6},{5,7},{6,4},{7,5},{8,10},{9,11},{10,... | collective-permute-start | bytes 688136 | tf_op jit(solution)/shard_map/ppermute | solution.py:22
  34.1 1.3 %collective-permute-done.7 = f32[32,1152]{1,0:T(8,128)S(1)} collective-permute-done((f32[32,1152]{1,0:T(8,128)S(1)}, f32[32,1152]{1,0:T(8,128)S(1)}, u32[]{:S(2)}, u32[]{:S(2)}) %collective-permute-start.7) | collective-permute-done | bytes 147488 | tf_op jit(solution)/shard_map/ppermute | solution.py:22
  35.5 5.4 %collective-permute-done.8 = f32[32,1792]{1,0:T(8,128)S(1)} collective-permute-done((f32[32,1792]{1,0:T(8,128)S(1)}, f32[32,1792]{1,0:T(8,128)S(1)}, u32[]{:S(2)}, u32[]{:S(2)}) %collective-permute-start.8) | collective-permute-done | bytes 229408 | tf_op jit(solution)/shard_map/ppermute | solution.py:22
  41.8 0.9 %collective-permute-start.9 = (f32[32,1152]{1,0:T(8,128)S(1)}, f32[32,1152]{1,0:T(8,128)S(1)}, u32[]{:S(2)}, u32[]{:S(2)}) collective-permute-start(f32[32,1152]{1,0:T(8,128)S(1)} %fusion.16), channel_id=1, source_target_pairs={{0,2},{1,3},{2,0},{3,1},{4,6},{5,7},{6,4},{7,5},{8,10},{9,11},{10,... | collective-permute-start | bytes 442376 | tf_op jit(solution)/shard_map/ppermute | solution.py:22
  43.9 3.2 %collective-permute-done.9 = f32[32,1152]{1,0:T(8,128)S(1)} collective-permute-done((f32[32,1152]{1,0:T(8,128)S(1)}, f32[32,1152]{1,0:T(8,128)S(1)}, u32[]{:S(2)}, u32[]{:S(2)}) %collective-permute-start.9) | collective-permute-done | bytes 147488 | tf_op jit(solution)/shard_map/ppermute | solution.py:22
  47.0 2.6 %collective-permute-done.10 = f32[32,1536]{1,0:T(8,128)S(1)} collective-permute-done((f32[32,1536]{1,0:T(8,128)S(1)}, f32[32,1536]{1,0:T(8,128)S(1)}, u32[]{:S(2)}, u32[]{:S(2)}) %collective-permute-start.10) | collective-permute-done | bytes 196640 | tf_op jit(solution)/shard_map/ppermute | solution.py:22
  51.9 0.6 collective-permute-start.12
  52.9 3.2 %collective-permute-done.11 = f32[32,1152]{1,0:T(8,128)S(1)} collective-permute-done((f32[32,1152]{1,0:T(8,128)S(1)}, f32[32,1152]{1,0:T(8,128)S(1)}, u32[]{:S(2)}, u32[]{:S(2)}) %collective-permute-start.11) | collective-permute-done | bytes 147488 | tf_op jit(solution)/shard_map/ppermute | solution.py:22
  56.1 4.4 %collective-permute-done.12 = f32[32,1280]{1,0:T(8,128)S(1)} collective-permute-done((f32[32,1280]{1,0:T(8,128)S(1)}, f32[32,1280]{1,0:T(8,128)S(1)}, u32[]{:S(2)}, u32[]{:S(2)}) %collective-permute-start.12) | collective-permute-done | bytes 163872 | tf_op jit(solution)/shard_map/ppermute | solution.py:22
  62.5 5.7 %collective-permute-done.13 = f32[32,1152]{1,0:T(8,128)S(1)} collective-permute-done((f32[32,1152]{1,0:T(8,128)S(1)}, f32[32,1152]{1,0:T(8,128)S(1)}, u32[]{:S(2)}, u32[]{:S(2)}) %collective-permute-start.13) | collective-permute-done | bytes 147488 | tf_op jit(solution)/shard_map/ppermute | solution.py:22
  69.5 1.9 %convolution_reduce_fusion = f32[512,128]{1,0:T(8,128)S(1)} fusion(f32[512,256,1]{1,0,2:T(8,128)S(1)} %bitcast.86, f32[8,128,256]{2,1,0:T(8,128)S(1)} %bitcast.85), kind=kOutput, calls=%fused_computation | convolution fusion | flops 1611071488 | bytes 1835008 | tf_op jit(solution)/shard_map/dot_general | solution.py:138
  71.5 1.3 %collective-permute-start.15 = (f32[2048]{0:T(1024)S(1)}, f32[2048]{0:T(1024)S(1)}, u32[]{:S(2)}, u32[]{:S(2)}) collective-permute-start(f32[2048]{0:T(1024)S(1)} %reduce_max.19), channel_id=1, source_target_pairs={{0,2},{1,3},{2,0},{3,1},{4,6},{5,7},{6,4},{7,5},{8,10},{9,11},{10,... | collective-permute-start | bytes 24584 | tf_op jit(solution)/shard_map/ppermute | solution.py:27
  73.4 1.9 %collective-permute-done.15 = f32[2048]{0:T(1024)S(1)} collective-permute-done((f32[2048]{0:T(1024)S(1)}, f32[2048]{0:T(1024)S(1)}, u32[]{:S(2)}, u32[]{:S(2)}) %collective-permute-start.15) | collective-permute-done | bytes 8224 | tf_op jit(solution)/shard_map/ppermute | solution.py:27
  75.3 0.6 collective-permute-done.14
  76.0 2.6 %collective-permute-start.18 = (f32[2048]{0:T(1024)S(1)}, f32[2048]{0:T(1024)S(1)}, u32[]{:S(2)}, u32[]{:S(2)}) collective-permute-start(f32[2048]{0:T(1024)S(1)} %maximum_maximum_fusion.1), channel_id=1, source_target_pairs={{0,8},{1,9},{2,10},{3,11},{4,12},{5,13},{6,14},{7,15},{8,0},{9,1},... | collective-permute-start | bytes 24584 | tf_op jit(solution)/shard_map/ppermute | solution.py:27
  78.6 1.8 %collective-permute-start.17 = (f32[2048]{0:T(1024)S(1)}, f32[2048]{0:T(1024)S(1)}, u32[]{:S(2)}, u32[]{:S(2)}) collective-permute-start(f32[2048]{0:T(1024)S(1)} %maximum_maximum_fusion.1), channel_id=1, source_target_pairs={{0,12},{1,13},{2,14},{3,15},{4,8},{5,9},{6,10},{7,11},{8,4},{9,5},... | collective-permute-start | bytes 24584 | tf_op jit(solution)/shard_map/ppermute | solution.py:27
  80.7 3.4 %collective-permute-done.17 = f32[2048]{0:T(1024)S(1)} collective-permute-done((f32[2048]{0:T(1024)S(1)}, f32[2048]{0:T(1024)S(1)}, u32[]{:S(2)}, u32[]{:S(2)}) %collective-permute-start.17) | collective-permute-done | bytes 8224 | tf_op jit(solution)/shard_map/ppermute | solution.py:27
  84.0 0.6 maximum_maximum_fusion
  (120 shorter events, 11.2 us)
Async XLA Ops:
  0.6 18.1 %slice-start = ((s32[9,32]{1,0:T(8,128)}), s32[5,32]{1,0:T(8,128)S(1)}, s32[]{:S(2)}) async-start(s32[9,32]{1,0:T(8,128)} %param.4), calls=%async_computation | async-start | bytes 8192 | tf_op jit(solution)/shard_map/slice | solution.py:162
  1.9 3.2 %collective-permute-start.2 = (f32[6144]{0:T(1024)S(1)}, f32[6144]{0:T(1024)S(1)}, u32[]{:S(2)}, u32[]{:S(2)}) collective-permute-start(f32[6144]{0:T(1024)S(1)} %reduce_sum.9), channel_id=1, source_target_pairs={{0,1},{1,0},{2,3},{3,2},{4,5},{5,4},{6,7},{7,6},{8,9},{9,8},{10,11... | collective-permute-start | bytes 73736 | tf_op jit(solution)/shard_map/ppermute | solution.py:27
  2.4 4.4 %collective-permute-start.1 = (f32[6144]{0:T(1024)S(1)}, f32[6144]{0:T(1024)S(1)}, u32[]{:S(2)}, u32[]{:S(2)}) collective-permute-start(f32[6144]{0:T(1024)S(1)} %reduce_sum.9), channel_id=1, source_target_pairs={{0,2},{1,3},{2,0},{3,1},{4,6},{5,7},{6,4},{7,5},{8,10},{9,11},{10,... | collective-permute-start | bytes 73736 | tf_op jit(solution)/shard_map/ppermute | solution.py:27
  4.9 3.3 %collective-permute-start = (f32[6144]{0:T(1024)S(1)}, f32[6144]{0:T(1024)S(1)}, u32[]{:S(2)}, u32[]{:S(2)}) collective-permute-start(f32[6144]{0:T(1024)S(1)} %reduce_sum.9), channel_id=1, source_target_pairs={{0,3},{1,2},{2,1},{3,0},{4,7},{5,6},{6,5},{7,4},{8,11},{9,10},{10,... | collective-permute-start | bytes 73736 | tf_op jit(solution)/shard_map/ppermute | solution.py:27
  8.2 21.4 %copy-start.1 = (s32[9,32]{1,0:T(8,128)S(1)}, s32[9,32]{1,0:T(8,128)}, u32[]{:S(2)}) copy-start(s32[9,32]{1,0:T(8,128)} %param.4) | copy-start | bytes 3460
  8.2 4.5 %collective-permute-start.5 = (f32[6144]{0:T(1024)S(1)}, f32[6144]{0:T(1024)S(1)}, u32[]{:S(2)}, u32[]{:S(2)}) collective-permute-start(f32[6144]{0:T(1024)S(1)} %add_add_fusion), channel_id=1, source_target_pairs={{0,4},{1,5},{2,6},{3,7},{4,0},{5,1},{6,2},{7,3},{8,12},{9,13},{10,... | collective-permute-start | bytes 73736 | tf_op jit(solution)/shard_map/ppermute | solution.py:27
  9.9 5.1 %collective-permute-start.4 = (f32[6144]{0:T(1024)S(1)}, f32[6144]{0:T(1024)S(1)}, u32[]{:S(2)}, u32[]{:S(2)}) collective-permute-start(f32[6144]{0:T(1024)S(1)} %add_add_fusion), channel_id=1, source_target_pairs={{0,8},{1,9},{2,10},{3,11},{4,12},{5,13},{6,14},{7,15},{8,0},{9,1},... | collective-permute-start | bytes 73736 | tf_op jit(solution)/shard_map/ppermute | solution.py:27
  12.5 5.6 %collective-permute-start.3 = (f32[6144]{0:T(1024)S(1)}, f32[6144]{0:T(1024)S(1)}, u32[]{:S(2)}, u32[]{:S(2)}) collective-permute-start(f32[6144]{0:T(1024)S(1)} %add_add_fusion), channel_id=1, source_target_pairs={{0,12},{1,13},{2,14},{3,15},{4,8},{5,9},{6,10},{7,11},{8,4},{9,5},... | collective-permute-start | bytes 73736 | tf_op jit(solution)/shard_map/ppermute | solution.py:27
  29.5 1.6 %collective-permute-start.6 = (f32[32,2048]{1,0:T(8,128)S(1)}, f32[32,2048]{1,0:T(8,128)S(1)}, u32[]{:S(2)}, u32[]{:S(2)}) collective-permute-start(f32[32,2048]{1,0:T(8,128)S(1)} %slice.629), channel_id=1, source_target_pairs={{0,1},{1,0},{2,3},{3,2},{4,5},{5,4},{6,7},{7,6},{8,9},{9,8},{10,11... | collective-permute-start | bytes 786440 | tf_op jit(solution)/shard_map/ppermute | solution.py:22
  32.8 1.3 %copy-start.2 = (s32[8]{0:T(128)S(1)}, s32[8]{0:T(128)}, u32[]{:S(2)}) copy-start(s32[8]{0:T(128)} %param.5) | copy-start | bytes 100
  33.2 7.7 %collective-permute-start.8 = (f32[32,1792]{1,0:T(8,128)S(1)}, f32[32,1792]{1,0:T(8,128)S(1)}, u32[]{:S(2)}, u32[]{:S(2)}) collective-permute-start(f32[32,1792]{1,0:T(8,128)S(1)} %fusion.2), channel_id=1, source_target_pairs={{0,2},{1,3},{2,0},{3,1},{4,6},{5,7},{6,4},{7,5},{8,10},{9,11},{10,... | collective-permute-start | bytes 688136 | tf_op jit(solution)/shard_map/ppermute | solution.py:22
  34.1 1.4 %collective-permute-start.7 = (f32[32,1152]{1,0:T(8,128)S(1)}, f32[32,1152]{1,0:T(8,128)S(1)}, u32[]{:S(2)}, u32[]{:S(2)}) collective-permute-start(f32[32,1152]{1,0:T(8,128)S(1)} %slice.628), channel_id=1, source_target_pairs={{0,1},{1,0},{2,3},{3,2},{4,5},{5,4},{6,7},{7,6},{8,9},{9,8},{10,11... | collective-permute-start | bytes 442376 | tf_op jit(solution)/shard_map/ppermute | solution.py:22
  41.8 5.2 %collective-permute-start.9 = (f32[32,1152]{1,0:T(8,128)S(1)}, f32[32,1152]{1,0:T(8,128)S(1)}, u32[]{:S(2)}, u32[]{:S(2)}) collective-permute-start(f32[32,1152]{1,0:T(8,128)S(1)} %fusion.16), channel_id=1, source_target_pairs={{0,2},{1,3},{2,0},{3,1},{4,6},{5,7},{6,4},{7,5},{8,10},{9,11},{10,... | collective-permute-start | bytes 442376 | tf_op jit(solution)/shard_map/ppermute | solution.py:22
  43.7 5.9 %collective-permute-start.10 = (f32[32,1536]{1,0:T(8,128)S(1)}, f32[32,1536]{1,0:T(8,128)S(1)}, u32[]{:S(2)}, u32[]{:S(2)}) collective-permute-start(f32[32,1536]{1,0:T(8,128)S(1)} %fusion.3), channel_id=1, source_target_pairs={{0,4},{1,5},{2,6},{3,7},{4,0},{5,1},{6,2},{7,3},{8,12},{9,13},{10,... | collective-permute-start | bytes 589832 | tf_op jit(solution)/shard_map/ppermute | solution.py:22
  50.6 5.6 %collective-permute-start.11 = (f32[32,1152]{1,0:T(8,128)S(1)}, f32[32,1152]{1,0:T(8,128)S(1)}, u32[]{:S(2)}, u32[]{:S(2)}) collective-permute-start(f32[32,1152]{1,0:T(8,128)S(1)} %fusion.15), channel_id=1, source_target_pairs={{0,4},{1,5},{2,6},{3,7},{4,0},{5,1},{6,2},{7,3},{8,12},{9,13},{10,... | collective-permute-start | bytes 442376 | tf_op jit(solution)/shard_map/ppermute | solution.py:22
  51.9 8.7 %collective-permute-start.12 = (f32[32,1280]{1,0:T(8,128)S(1)}, f32[32,1280]{1,0:T(8,128)S(1)}, u32[]{:S(2)}, u32[]{:S(2)}) collective-permute-start(f32[32,1280]{1,0:T(8,128)S(1)} %fusion.12), channel_id=1, source_target_pairs={{0,8},{1,9},{2,10},{3,11},{4,12},{5,13},{6,14},{7,15},{8,0},{9,1},... | collective-permute-start | bytes 491528 | tf_op jit(solution)/shard_map/ppermute | solution.py:22
  61.6 6.6 %collective-permute-start.13 = (f32[32,1152]{1,0:T(8,128)S(1)}, f32[32,1152]{1,0:T(8,128)S(1)}, u32[]{:S(2)}, u32[]{:S(2)}) collective-permute-start(f32[32,1152]{1,0:T(8,128)S(1)} %fusion.14), channel_id=1, source_target_pairs={{0,8},{1,9},{2,10},{3,11},{4,12},{5,13},{6,14},{7,15},{8,0},{9,1},... | collective-permute-start | bytes 442376 | tf_op jit(solution)/shard_map/ppermute | solution.py:22
  71.4 13.2 %copy-start = (f32[32,2048]{1,0:T(8,128)}, f32[32,2048]{1,0:T(8,128)S(1)}, u32[]{:S(2)}) copy-start(f32[32,2048]{1,0:T(8,128)S(1)} %reshape.486) | copy-start | bytes 786436
  71.5 1.9 %collective-permute-start.16 = (f32[2048]{0:T(1024)S(1)}, f32[2048]{0:T(1024)S(1)}, u32[]{:S(2)}, u32[]{:S(2)}) collective-permute-start(f32[2048]{0:T(1024)S(1)} %reduce_max.19), channel_id=1, source_target_pairs={{0,1},{1,0},{2,3},{3,2},{4,5},{5,4},{6,7},{7,6},{8,9},{9,8},{10,11... | collective-permute-start | bytes 24584 | tf_op jit(solution)/shard_map/ppermute | solution.py:27
  71.5 3.7 %collective-permute-start.15 = (f32[2048]{0:T(1024)S(1)}, f32[2048]{0:T(1024)S(1)}, u32[]{:S(2)}, u32[]{:S(2)}) collective-permute-start(f32[2048]{0:T(1024)S(1)} %reduce_max.19), channel_id=1, source_target_pairs={{0,2},{1,3},{2,0},{3,1},{4,6},{5,7},{6,4},{7,5},{8,10},{9,11},{10,... | collective-permute-start | bytes 24584 | tf_op jit(solution)/shard_map/ppermute | solution.py:27
  72.8 3.1 %collective-permute-start.14 = (f32[2048]{0:T(1024)S(1)}, f32[2048]{0:T(1024)S(1)}, u32[]{:S(2)}, u32[]{:S(2)}) collective-permute-start(f32[2048]{0:T(1024)S(1)} %reduce_max.19), channel_id=1, source_target_pairs={{0,3},{1,2},{2,1},{3,0},{4,7},{5,6},{6,5},{7,4},{8,11},{9,10},{10,... | collective-permute-start | bytes 24584 | tf_op jit(solution)/shard_map/ppermute | solution.py:27
  75.9 4.5 %collective-permute-start.19 = (f32[2048]{0:T(1024)S(1)}, f32[2048]{0:T(1024)S(1)}, u32[]{:S(2)}, u32[]{:S(2)}) collective-permute-start(f32[2048]{0:T(1024)S(1)} %maximum_maximum_fusion.1), channel_id=1, source_target_pairs={{0,4},{1,5},{2,6},{3,7},{4,0},{5,1},{6,2},{7,3},{8,12},{9,13},{10,... | collective-permute-start | bytes 24584 | tf_op jit(solution)/shard_map/ppermute | solution.py:27
  76.0 4.7 %collective-permute-start.18 = (f32[2048]{0:T(1024)S(1)}, f32[2048]{0:T(1024)S(1)}, u32[]{:S(2)}, u32[]{:S(2)}) collective-permute-start(f32[2048]{0:T(1024)S(1)} %maximum_maximum_fusion.1), channel_id=1, source_target_pairs={{0,8},{1,9},{2,10},{3,11},{4,12},{5,13},{6,14},{7,15},{8,0},{9,1},... | collective-permute-start | bytes 24584 | tf_op jit(solution)/shard_map/ppermute | solution.py:27
  78.6 5.4 %collective-permute-start.17 = (f32[2048]{0:T(1024)S(1)}, f32[2048]{0:T(1024)S(1)}, u32[]{:S(2)}, u32[]{:S(2)}) collective-permute-start(f32[2048]{0:T(1024)S(1)} %maximum_maximum_fusion.1), channel_id=1, source_target_pairs={{0,12},{1,13},{2,14},{3,15},{4,8},{5,9},{6,10},{7,11},{8,4},{9,5},... | collective-permute-start | bytes 24584 | tf_op jit(solution)/shard_map/ppermute | solution.py:27

commit v6 on v5

--- a/solution.py
+++ b/solution.py
@@ -60,10 +60,13 @@
     return current
 
 
-def local_tree_kernel(widths_seq, x_ref, mean_ref, amount_ref, out_ref):
+def local_tree_kernel(widths_seq, channels_all, x_ref, total_ref, offsets_ref, head_ref, tail_ref):
     rows = x_ref.shape[0]
-    cur = x_ref[:, : widths_seq[0]] - mean_ref[:, : widths_seq[0]]
+    cur = x_ref[:, : widths_seq[0]] - total_ref[:, : widths_seq[0]] / channels_all
     row_id = lax.broadcasted_iota(jnp.int32, (rows, 1), 0)
+    diagonal = lax.broadcasted_iota(jnp.int32, (rows, rows), 0) == lax.broadcasted_iota(
+        jnp.int32, (rows, rows), 1
+    )
     for section_index in range(len(widths_seq) - 1):
         mask = 2**section_index
         width = widths_seq[section_index]
@@ -74,30 +77,35 @@
         partner = jnp.where(is_upper, from_above, from_below)
         lower = jnp.where(is_upper, partner, cur)
         shifted = jnp.where(is_upper, cur, partner)
-        amount = amount_ref[section_index][:, 0:1]
+        amount_row = jnp.broadcast_to(offsets_ref[section_index : section_index + 1, :], (rows, rows))
+        amount = jnp.sum(jnp.where(diagonal, amount_row, 0), axis=1, keepdims=True)
         for bit_index in range((SHIFT - 1).bit_length()):
             span = 2**bit_index
             chosen = (amount >> bit_index & 1) == 1
             shifted = jnp.where(chosen, pltpu.roll(shifted, width - span, axis=1), shifted)
         cur = lower[:, :new_width] + shifted[:, :new_width]
-    out_ref[...] = cur
-
-
-def local_tree(filterbank, channel_mean, amounts, widths_seq):
+    head_width = head_ref.shape[1]
+    head_ref[...] = cur[:, :head_width]
+    tail_ref[...] = cur[:, head_width:]
+
+
+def local_tree(filterbank, channel_total, offsets, widths_seq, channels_all, tail_width):
     rows = filterbank.shape[0]
     vmem = pl.BlockSpec(memory_space=pltpu.VMEM)
-    lane_amounts = jnp.broadcast_to(amounts[:, :, None], amounts.shape + (128,))
-    levels = len(widths_seq) - 1
     work = rows * sum(widths_seq[:-1])
+    head_width = widths_seq[-1] - tail_width
     return pl.pallas_call(
-        functools.partial(local_tree_kernel, tuple(widths_seq)),
-        out_shape=jax.ShapeDtypeStruct((rows, widths_seq[-1]), jnp.float32),
+        functools.partial(local_tree_kernel, tuple(widths_seq), float(channels_all)),
+        out_shape=(
+            jax.ShapeDtypeStruct((rows, head_width), jnp.float32),
+            jax.ShapeDtypeStruct((rows, tail_width), jnp.float32),
+        ),
         in_specs=[vmem, vmem, vmem],
-        out_specs=vmem,
+        out_specs=(vmem, vmem),
         cost_estimate=pl.CostEstimate(
             flops=40 * work, transcendentals=0, bytes_accessed=4 * (rows * widths_seq[0] + rows * widths_seq[-1])
         ),
-    )(filterbank, channel_mean[None, :], lane_amounts[:levels])
+    )(filterbank, channel_total[None, :], offsets)
 
 
 def merge_section(current, offsets_now, section_index, new_length):
@@ -157,9 +165,9 @@
         return min(TIN, needed)
 
     partial_value = jnp.sum(filterbank, axis=0)
-    channel_mean = butterfly(partial_value, "band", jnp.add) / channels_all
+    channel_total = butterfly(partial_value, "band", jnp.add)
     widths_seq = [length_after(section) for section in range(local_count + 1)]
-    current = local_tree(filterbank, channel_mean, offsets[:local_count], widths_seq)
+    head, tail = local_tree(filterbank, channel_total, offsets, widths_seq, channels_all, TAIL_WIDTH)
     band_index = lax.axis_index("band")
     bit_count = band_count.bit_length() - 1
     tail_width = TAIL_WIDTH
@@ -168,8 +176,6 @@
         upper_half = band_index // 2**bit_index % 2 == 1
         return jnp.where(upper_half, partner, own), jnp.where(upper_half, own, partner)
 
-    head = current[:, : current.shape[1] - tail_width]
-    tail = current[:, current.shape[1] - tail_width :]
     partner_head = from_partner(head, "band", 0)
     for bit_index in range(bit_count):
         amounts = offsets[local_count + bit_index]

time: 84.9 us -> 80.8 us (0.952)
  local copies, waits for them, and re-layouts: 2.94 us -> 0.32 us
  Pallas kernels: 9.1 us -> 6.8 us
  waiting for transfers between devices: 41.1 us -> 42.2 us
    pallas_call x1, Pallas kernels: 9.1 us -> 6.8 us  [local_tree(): pl.pallas_call(functools.partial(local_tree_kernel, tuple(widths_seq), fl...]
    slice x4 -> x0, local copies, waits for them, and re-layouts: 1.9 us -> none  [the longest x1 0.97 us: per_device(): head = current[:, :current.shape[1] - tail_width]]
    ppermute x8, waiting for transfers between devices: 26.3 us -> 27.5 us  [from_partner(): return lax.ppermute(value, axis, pairs)]
  transfers between devices with their start and end apart: 20 -> 20, of which waited for: 16 -> 16; matrix products, arithmetic and copies ran while one was open for 5% -> 4% of each run, Pallas kernels for 0% -> 0%
where the time goes in v6:
time: 80.8 us; the launch traced here: 80.6 us
  waiting for transfers between devices  42.2 us (52%)
  starting transfers between devices  16.8 us (21%)
  other arithmetic  11.2 us (14%)
  Pallas kernels  6.8 us (8%)
  matrix products  1.87 us (2%)
  between operations  1.33 us (2%)
    ppermute x8, waiting for transfers between devices, from_partner(): return lax.ppermute(value, axis, pairs)  27.5 us
    ppermute x12, waiting for transfers between devices, from_xor(): return lax.ppermute(value, axis, pairs)  14.7 us
    ppermute x12, starting transfers between devices, from_xor(): return lax.ppermute(value, axis, pairs)  14 us
    pallas_call x1, Pallas kernels, local_tree(): pl.pallas_call(functools.partial(local_tree_kernel, tuple(widths_seq), fl...  6.8 us
    select_n x56, other arithmetic, shift_rows(): jnp.where(chosen, current[:, span:span + keep_len], current[:, :keep_len])  6.19 us
    ppermute x8, starting transfers between devices, from_partner(): return lax.ppermute(value, axis, pairs)  2.84 us
    dot_general x1, matrix products, boxcar_max(): jnp.dot(paired, joined, precision=lax.Precision.HIGHEST, preferred_elemen...  1.87 us
  transfers between devices with their start and end apart: 20, of which 16 were waited for; matrix products, arithmetic and copies ran while one was open for 4% of the time, Pallas kernels for 0%

profile of v6, /device:TPU:0, one launch (start us, length us, event | category | flops | bytes accessed | tf_op | source)
XLA Modules:
  0.0 80.6 jit_solution(12078915036645991314)
XLA Ops:
  0.6 1.2 %reduce_sum.9 = f32[6144]{0:T(1024)S(1)} reduce(f32[32,6144]{1,0:T(8,128)} %x_ref.1, f32[]{:T(128)} %constant.101.clone.1), dimensions={0}, to_apply=%region_0.0 | reduce | flops 190464 | bytes 811012 | tf_op jit(solution)/shard_map/reduce_sum | solution.py:167
  1.9 0.5 collective-permute-start.2
  2.4 2.6 %collective-permute-start.1 = (f32[6144]{0:T(1024)S(1)}, f32[6144]{0:T(1024)S(1)}, u32[]{:S(2)}, u32[]{:S(2)}) collective-permute-start(f32[6144]{0:T(1024)S(1)} %reduce_sum.9), channel_id=1, source_target_pairs={{0,2},{1,3},{2,0},{3,1},{4,6},{5,7},{6,4},{7,5},{8,10},{9,11},{10,... | collective-permute-start | bytes 73736 | tf_op jit(solution)/shard_map/ppermute | solution.py:27
  5.0 1.7 %collective-permute-done.1 = f32[6144]{0:T(1024)S(1)} collective-permute-done((f32[6144]{0:T(1024)S(1)}, f32[6144]{0:T(1024)S(1)}, u32[]{:S(2)}, u32[]{:S(2)}) %collective-permute-start.1) | collective-permute-done | bytes 24608 | tf_op jit(solution)/shard_map/ppermute | solution.py:27
  6.7 1.4 %collective-permute-done = f32[6144]{0:T(1024)S(1)} collective-permute-done((f32[6144]{0:T(1024)S(1)}, f32[6144]{0:T(1024)S(1)}, u32[]{:S(2)}, u32[]{:S(2)}) %collective-permute-start) | collective-permute-done | bytes 24608 | tf_op jit(solution)/shard_map/ppermute | solution.py:27
  8.2 1.6 %collective-permute-start.5 = (f32[6144]{0:T(1024)S(1)}, f32[6144]{0:T(1024)S(1)}, u32[]{:S(2)}, u32[]{:S(2)}) collective-permute-start(f32[6144]{0:T(1024)S(1)} %add_add_fusion.1), channel_id=1, source_target_pairs={{0,4},{1,5},{2,6},{3,7},{4,0},{5,1},{6,2},{7,3},{8,12},{9,13},{10,... | collective-permute-start | bytes 73736 | tf_op jit(solution)/shard_map/ppermute | solution.py:27
  9.9 2.6 %collective-permute-start.4 = (f32[6144]{0:T(1024)S(1)}, f32[6144]{0:T(1024)S(1)}, u32[]{:S(2)}, u32[]{:S(2)}) collective-permute-start(f32[6144]{0:T(1024)S(1)} %add_add_fusion.1), channel_id=1, source_target_pairs={{0,8},{1,9},{2,10},{3,11},{4,12},{5,13},{6,14},{7,15},{8,0},{9,1},... | collective-permute-start | bytes 73736 | tf_op jit(solution)/shard_map/ppermute | solution.py:27
  12.7 2.3 %collective-permute-done.4 = f32[6144]{0:T(1024)S(1)} collective-permute-done((f32[6144]{0:T(1024)S(1)}, f32[6144]{0:T(1024)S(1)}, u32[]{:S(2)}, u32[]{:S(2)}) %collective-permute-start.4) | collective-permute-done | bytes 24608 | tf_op jit(solution)/shard_map/ppermute | solution.py:27
  14.9 3.1 %collective-permute-done.3 = f32[6144]{0:T(1024)S(1)} collective-permute-done((f32[6144]{0:T(1024)S(1)}, f32[6144]{0:T(1024)S(1)}, u32[]{:S(2)}, u32[]{:S(2)}) %collective-permute-start.3) | collective-permute-done | bytes 24608 | tf_op jit(solution)/shard_map/ppermute | solution.py:27
  18.1 0.6 add_add_fusion
  18.7 6.8 %shard_map.50 = (f32[32,2048]{1,0:T(8,128)}, f32[32,1152]{1,0:T(8,128)}) custom-call(f32[32,6144]{1,0:T(8,128)} %x_ref.1, f32[1,6144]{1,0:T(1,128)} %bitcast.87, s32[9,32]{1,0:T(8,128)} %offsets_ref.1), custom_call_target="tpu_custom_call" | custom-call | flops 25395200 | bytes 983040 | tf_op jit(solution)/shard_map/pallas_call | solution.py:97
  25.6 1.7 %collective-permute-done.6 = f32[32,2048]{1,0:T(8,128)S(1)} collective-permute-done((f32[32,2048]{1,0:T(8,128)}, f32[32,2048]{1,0:T(8,128)S(1)}, u32[]{:S(2)}, u32[]{:S(2)}) %collective-permute-start.6) | collective-permute-done | bytes 262176 | tf_op jit(solution)/shard_map/ppermute | solution.py:22
  27.2 1.0 %broadcast_select_fusion.1 = (f32[32,2048]{1,0:T(8,128)S(1)}, f32[32,2048]{1,0:T(8,128)S(1)}) fusion(f32[32,2048]{1,0:T(8,128)S(1)} %collective-permute-done.6, f32[32,2048]{1,0:T(8,128)} %get-tuple-element.19, pred[]{:T(512)S(6)} %eq.508), kind=kLoop, calls=%fused_computation.100 | loop fusion | flops 131072 | bytes 1048577 | tf_op jit(solution)/shard_map/jit(_where)/select_n | solution.py:177
  29.3 0.9 %collective-permute-start.8 = (f32[32,1792]{1,0:T(8,128)S(1)}, f32[32,1792]{1,0:T(8,128)S(1)}, u32[]{:S(2)}, u32[]{:S(2)}) collective-permute-start(f32[32,1792]{1,0:T(8,128)S(1)} %fusion.2), channel_id=1, source_target_pairs={{0,2},{1,3},{2,0},{3,1},{4,6},{5,7},{6,4},{7,5},{8,10},{9,11},{10,... | collective-permute-start | bytes 688136 | tf_op jit(solution)/shard_map/ppermute | solution.py:22
  30.3 1.3 %collective-permute-done.7 = f32[32,1152]{1,0:T(8,128)S(1)} collective-permute-done((f32[32,1152]{1,0:T(8,128)S(1)}, f32[32,1152]{1,0:T(8,128)S(1)}, u32[]{:S(2)}, u32[]{:S(2)}) %collective-permute-start.7) | collective-permute-done | bytes 147488 | tf_op jit(solution)/shard_map/ppermute | solution.py:22
  31.6 5.4 %collective-permute-done.8 = f32[32,1792]{1,0:T(8,128)S(1)} collective-permute-done((f32[32,1792]{1,0:T(8,128)S(1)}, f32[32,1792]{1,0:T(8,128)S(1)}, u32[]{:S(2)}, u32[]{:S(2)}) %collective-permute-start.8) | collective-permute-done | bytes 229408 | tf_op jit(solution)/shard_map/ppermute | solution.py:22
  38.0 0.9 %collective-permute-start.9 = (f32[32,1152]{1,0:T(8,128)S(1)}, f32[32,1152]{1,0:T(8,128)S(1)}, u32[]{:S(2)}, u32[]{:S(2)}) collective-permute-start(f32[32,1152]{1,0:T(8,128)S(1)} %fusion.16), channel_id=1, source_target_pairs={{0,2},{1,3},{2,0},{3,1},{4,6},{5,7},{6,4},{7,5},{8,10},{9,11},{10,... | collective-permute-start | bytes 442376 | tf_op jit(solution)/shard_map/ppermute | solution.py:22
  40.0 3.2 %collective-permute-done.9 = f32[32,1152]{1,0:T(8,128)S(1)} collective-permute-done((f32[32,1152]{1,0:T(8,128)S(1)}, f32[32,1152]{1,0:T(8,128)S(1)}, u32[]{:S(2)}, u32[]{:S(2)}) %collective-permute-start.9) | collective-permute-done | bytes 147488 | tf_op jit(solution)/shard_map/ppermute | solution.py:22
  43.2 2.6 %collective-permute-done.10 = f32[32,1536]{1,0:T(8,128)S(1)} collective-permute-done((f32[32,1536]{1,0:T(8,128)S(1)}, f32[32,1536]{1,0:T(8,128)S(1)}, u32[]{:S(2)}, u32[]{:S(2)}) %collective-permute-start.10) | collective-permute-done | bytes 196640 | tf_op jit(solution)/shard_map/ppermute | solution.py:22
  48.0 0.6 collective-permute-start.12
  49.0 3.2 %collective-permute-done.11 = f32[32,1152]{1,0:T(8,128)S(1)} collective-permute-done((f32[32,1152]{1,0:T(8,128)S(1)}, f32[32,1152]{1,0:T(8,128)S(1)}, u32[]{:S(2)}, u32[]{:S(2)}) %collective-permute-start.11) | collective-permute-done | bytes 147488 | tf_op jit(solution)/shard_map/ppermute | solution.py:22
  52.2 4.4 %collective-permute-done.12 = f32[32,1280]{1,0:T(8,128)S(1)} collective-permute-done((f32[32,1280]{1,0:T(8,128)S(1)}, f32[32,1280]{1,0:T(8,128)S(1)}, u32[]{:S(2)}, u32[]{:S(2)}) %collective-permute-start.12) | collective-permute-done | bytes 163872 | tf_op jit(solution)/shard_map/ppermute | solution.py:22
  58.6 5.7 %collective-permute-done.13 = f32[32,1152]{1,0:T(8,128)S(1)} collective-permute-done((f32[32,1152]{1,0:T(8,128)S(1)}, f32[32,1152]{1,0:T(8,128)S(1)}, u32[]{:S(2)}, u32[]{:S(2)}) %collective-permute-start.13) | collective-permute-done | bytes 147488 | tf_op jit(solution)/shard_map/ppermute | solution.py:22
  65.4 1.9 %convolution_reduce_fusion = f32[512,128]{1,0:T(8,128)S(1)} fusion(f32[512,256,1]{1,0,2:T(8,128)S(1)} %bitcast.86, f32[8,128,256]{2,1,0:T(8,128)S(1)} %bitcast.85), kind=kOutput, calls=%fused_computation | convolution fusion | flops 1611071488 | bytes 1835008 | tf_op jit(solution)/shard_map/dot_general | solution.py:146
  67.5 1.3 %collective-permute-start.15 = (f32[2048]{0:T(1024)S(1)}, f32[2048]{0:T(1024)S(1)}, u32[]{:S(2)}, u32[]{:S(2)}) collective-permute-start(f32[2048]{0:T(1024)S(1)} %reduce_max.19), channel_id=1, source_target_pairs={{0,2},{1,3},{2,0},{3,1},{4,6},{5,7},{6,4},{7,5},{8,10},{9,11},{10,... | collective-permute-start | bytes 24584 | tf_op jit(solution)/shard_map/ppermute | solution.py:27
  68.8 0.6 collective-permute-start.14
  69.3 1.9 %collective-permute-done.15 = f32[2048]{0:T(1024)S(1)} collective-permute-done((f32[2048]{0:T(1024)S(1)}, f32[2048]{0:T(1024)S(1)}, u32[]{:S(2)}, u32[]{:S(2)}) %collective-permute-start.15) | collective-permute-done | bytes 8224 | tf_op jit(solution)/shard_map/ppermute | solution.py:27
  71.2 0.6 collective-permute-done.14
  71.9 2.6 %collective-permute-start.18 = (f32[2048]{0:T(1024)S(1)}, f32[2048]{0:T(1024)S(1)}, u32[]{:S(2)}, u32[]{:S(2)}) collective-permute-start(f32[2048]{0:T(1024)S(1)} %maximum_maximum_fusion.1), channel_id=1, source_target_pairs={{0,8},{1,9},{2,10},{3,11},{4,12},{5,13},{6,14},{7,15},{8,0},{9,1},... | collective-permute-start | bytes 24584 | tf_op jit(solution)/shard_map/ppermute | solution.py:27
  74.5 1.8 %collective-permute-start.17 = (f32[2048]{0:T(1024)S(1)}, f32[2048]{0:T(1024)S(1)}, u32[]{:S(2)}, u32[]{:S(2)}) collective-permute-start(f32[2048]{0:T(1024)S(1)} %maximum_maximum_fusion.1), channel_id=1, source_target_pairs={{0,12},{1,13},{2,14},{3,15},{4,8},{5,9},{6,10},{7,11},{8,4},{9,5},... | collective-permute-start | bytes 24584 | tf_op jit(solution)/shard_map/ppermute | solution.py:27
  76.6 3.4 %collective-permute-done.17 = f32[2048]{0:T(1024)S(1)} collective-permute-done((f32[2048]{0:T(1024)S(1)}, f32[2048]{0:T(1024)S(1)}, u32[]{:S(2)}, u32[]{:S(2)}) %collective-permute-start.17) | collective-permute-done | bytes 8224 | tf_op jit(solution)/shard_map/ppermute | solution.py:27
  80.0 0.6 maximum_maximum_fusion
  (117 shorter events, 9.4 us)
Async XLA Ops:
  0.6 24.9 %copy-start.2 = (s32[9,32]{1,0:T(8,128)S(1)}, s32[9,32]{1,0:T(8,128)}, u32[]{:S(2)}) copy-start(s32[9,32]{1,0:T(8,128)} %offsets_ref.1) | copy-start | bytes 3460
  1.9 3.2 %collective-permute-start.2 = (f32[6144]{0:T(1024)S(1)}, f32[6144]{0:T(1024)S(1)}, u32[]{:S(2)}, u32[]{:S(2)}) collective-permute-start(f32[6144]{0:T(1024)S(1)} %reduce_sum.9), channel_id=1, source_target_pairs={{0,1},{1,0},{2,3},{3,2},{4,5},{5,4},{6,7},{7,6},{8,9},{9,8},{10,11... | collective-permute-start | bytes 73736 | tf_op jit(solution)/shard_map/ppermute | solution.py:27
  2.4 4.4 %collective-permute-start.1 = (f32[6144]{0:T(1024)S(1)}, f32[6144]{0:T(1024)S(1)}, u32[]{:S(2)}, u32[]{:S(2)}) collective-permute-start(f32[6144]{0:T(1024)S(1)} %reduce_sum.9), channel_id=1, source_target_pairs={{0,2},{1,3},{2,0},{3,1},{4,6},{5,7},{6,4},{7,5},{8,10},{9,11},{10,... | collective-permute-start | bytes 73736 | tf_op jit(solution)/shard_map/ppermute | solution.py:27
  4.9 3.3 %collective-permute-start = (f32[6144]{0:T(1024)S(1)}, f32[6144]{0:T(1024)S(1)}, u32[]{:S(2)}, u32[]{:S(2)}) collective-permute-start(f32[6144]{0:T(1024)S(1)} %reduce_sum.9), channel_id=1, source_target_pairs={{0,3},{1,2},{2,1},{3,0},{4,7},{5,6},{6,5},{7,4},{8,11},{9,10},{10,... | collective-permute-start | bytes 73736 | tf_op jit(solution)/shard_map/ppermute | solution.py:27
  8.2 4.5 %collective-permute-start.5 = (f32[6144]{0:T(1024)S(1)}, f32[6144]{0:T(1024)S(1)}, u32[]{:S(2)}, u32[]{:S(2)}) collective-permute-start(f32[6144]{0:T(1024)S(1)} %add_add_fusion.1), channel_id=1, source_target_pairs={{0,4},{1,5},{2,6},{3,7},{4,0},{5,1},{6,2},{7,3},{8,12},{9,13},{10,... | collective-permute-start | bytes 73736 | tf_op jit(solution)/shard_map/ppermute | solution.py:27
  9.9 5.1 %collective-permute-start.4 = (f32[6144]{0:T(1024)S(1)}, f32[6144]{0:T(1024)S(1)}, u32[]{:S(2)}, u32[]{:S(2)}) collective-permute-start(f32[6144]{0:T(1024)S(1)} %add_add_fusion.1), channel_id=1, source_target_pairs={{0,8},{1,9},{2,10},{3,11},{4,12},{5,13},{6,14},{7,15},{8,0},{9,1},... | collective-permute-start | bytes 73736 | tf_op jit(solution)/shard_map/ppermute | solution.py:27
  12.4 5.6 %collective-permute-start.3 = (f32[6144]{0:T(1024)S(1)}, f32[6144]{0:T(1024)S(1)}, u32[]{:S(2)}, u32[]{:S(2)}) collective-permute-start(f32[6144]{0:T(1024)S(1)} %add_add_fusion.1), channel_id=1, source_target_pairs={{0,12},{1,13},{2,14},{3,15},{4,8},{5,9},{6,10},{7,11},{8,4},{9,5},... | collective-permute-start | bytes 73736 | tf_op jit(solution)/shard_map/ppermute | solution.py:27
  25.5 1.7 %collective-permute-start.6 = (f32[32,2048]{1,0:T(8,128)}, f32[32,2048]{1,0:T(8,128)S(1)}, u32[]{:S(2)}, u32[]{:S(2)}) collective-permute-start(f32[32,2048]{1,0:T(8,128)} %get-tuple-element.19), channel_id=1, source_target_pairs={{0,1},{1,0},{2,3},{3,2},{4,5},{5,4},{6,7},{7,6},{8,9},{9,8},{10,11... | collective-permute-start | bytes 786440 | tf_op jit(solution)/shard_map/ppermute | solution.py:22
  28.9 1.3 %copy-start.3 = (s32[8]{0:T(128)S(1)}, s32[8]{0:T(128)}, u32[]{:S(2)}) copy-start(s32[8]{0:T(128)} %param.5) | copy-start | bytes 100
  29.0 1.2 %copy-start.1 = (f32[32,1152]{1,0:T(8,128)S(1)}, f32[32,1152]{1,0:T(8,128)}, u32[]{:S(2)}) copy-start(f32[32,1152]{1,0:T(8,128)} %get-tuple-element.21) | copy-start | bytes 442372
  29.3 7.7 %collective-permute-start.8 = (f32[32,1792]{1,0:T(8,128)S(1)}, f32[32,1792]{1,0:T(8,128)S(1)}, u32[]{:S(2)}, u32[]{:S(2)}) collective-permute-start(f32[32,1792]{1,0:T(8,128)S(1)} %fusion.2), channel_id=1, source_target_pairs={{0,2},{1,3},{2,0},{3,1},{4,6},{5,7},{6,4},{7,5},{8,10},{9,11},{10,... | collective-permute-start | bytes 688136 | tf_op jit(solution)/shard_map/ppermute | solution.py:22
  30.3 1.4 %collective-permute-start.7 = (f32[32,1152]{1,0:T(8,128)S(1)}, f32[32,1152]{1,0:T(8,128)S(1)}, u32[]{:S(2)}, u32[]{:S(2)}) collective-permute-start(f32[32,1152]{1,0:T(8,128)S(1)} %copy-done.1), channel_id=1, source_target_pairs={{0,1},{1,0},{2,3},{3,2},{4,5},{5,4},{6,7},{7,6},{8,9},{9,8},{10,11... | collective-permute-start | bytes 442376 | tf_op jit(solution)/shard_map/ppermute | solution.py:22
  38.0 5.2 %collective-permute-start.9 = (f32[32,1152]{1,0:T(8,128)S(1)}, f32[32,1152]{1,0:T(8,128)S(1)}, u32[]{:S(2)}, u32[]{:S(2)}) collective-permute-start(f32[32,1152]{1,0:T(8,128)S(1)} %fusion.16), channel_id=1, source_target_pairs={{0,2},{1,3},{2,0},{3,1},{4,6},{5,7},{6,4},{7,5},{8,10},{9,11},{10,... | collective-permute-start | bytes 442376 | tf_op jit(solution)/shard_map/ppermute | solution.py:22
  39.8 5.9 %collective-permute-start.10 = (f32[32,1536]{1,0:T(8,128)S(1)}, f32[32,1536]{1,0:T(8,128)S(1)}, u32[]{:S(2)}, u32[]{:S(2)}) collective-permute-start(f32[32,1536]{1,0:T(8,128)S(1)} %fusion.3), channel_id=1, source_target_pairs={{0,4},{1,5},{2,6},{3,7},{4,0},{5,1},{6,2},{7,3},{8,12},{9,13},{10,... | collective-permute-start | bytes 589832 | tf_op jit(solution)/shard_map/ppermute | solution.py:22
  46.7 5.6 %collective-permute-start.11 = (f32[32,1152]{1,0:T(8,128)S(1)}, f32[32,1152]{1,0:T(8,128)S(1)}, u32[]{:S(2)}, u32[]{:S(2)}) collective-permute-start(f32[32,1152]{1,0:T(8,128)S(1)} %fusion.15), channel_id=1, source_target_pairs={{0,4},{1,5},{2,6},{3,7},{4,0},{5,1},{6,2},{7,3},{8,12},{9,13},{10,... | collective-permute-start | bytes 442376 | tf_op jit(solution)/shard_map/ppermute | solution.py:22
  48.0 8.7 %collective-permute-start.12 = (f32[32,1280]{1,0:T(8,128)S(1)}, f32[32,1280]{1,0:T(8,128)S(1)}, u32[]{:S(2)}, u32[]{:S(2)}) collective-permute-start(f32[32,1280]{1,0:T(8,128)S(1)} %fusion.12), channel_id=1, source_target_pairs={{0,8},{1,9},{2,10},{3,11},{4,12},{5,13},{6,14},{7,15},{8,0},{9,1},... | collective-permute-start | bytes 491528 | tf_op jit(solution)/shard_map/ppermute | solution.py:22
  57.8 6.6 %collective-permute-start.13 = (f32[32,1152]{1,0:T(8,128)S(1)}, f32[32,1152]{1,0:T(8,128)S(1)}, u32[]{:S(2)}, u32[]{:S(2)}) collective-permute-start(f32[32,1152]{1,0:T(8,128)S(1)} %fusion.14), channel_id=1, source_target_pairs={{0,8},{1,9},{2,10},{3,11},{4,12},{5,13},{6,14},{7,15},{8,0},{9,1},... | collective-permute-start | bytes 442376 | tf_op jit(solution)/shard_map/ppermute | solution.py:22
  67.4 13.2 %copy-start = (f32[32,2048]{1,0:T(8,128)}, f32[32,2048]{1,0:T(8,128)S(1)}, u32[]{:S(2)}) copy-start(f32[32,2048]{1,0:T(8,128)S(1)} %reshape.485) | copy-start | bytes 786436
  67.4 1.9 %collective-permute-start.16 = (f32[2048]{0:T(1024)S(1)}, f32[2048]{0:T(1024)S(1)}, u32[]{:S(2)}, u32[]{:S(2)}) collective-permute-start(f32[2048]{0:T(1024)S(1)} %reduce_max.19), channel_id=1, source_target_pairs={{0,1},{1,0},{2,3},{3,2},{4,5},{5,4},{6,7},{7,6},{8,9},{9,8},{10,11... | collective-permute-start | bytes 24584 | tf_op jit(solution)/shard_map/ppermute | solution.py:27
  67.5 3.7 %collective-permute-start.15 = (f32[2048]{0:T(1024)S(1)}, f32[2048]{0:T(1024)S(1)}, u32[]{:S(2)}, u32[]{:S(2)}) collective-permute-start(f32[2048]{0:T(1024)S(1)} %reduce_max.19), channel_id=1, source_target_pairs={{0,2},{1,3},{2,0},{3,1},{4,6},{5,7},{6,4},{7,5},{8,10},{9,11},{10,... | collective-permute-start | bytes 24584 | tf_op jit(solution)/shard_map/ppermute | solution.py:27
  68.8 3.1 %collective-permute-start.14 = (f32[2048]{0:T(1024)S(1)}, f32[2048]{0:T(1024)S(1)}, u32[]{:S(2)}, u32[]{:S(2)}) collective-permute-start(f32[2048]{0:T(1024)S(1)} %reduce_max.19), channel_id=1, source_target_pairs={{0,3},{1,2},{2,1},{3,0},{4,7},{5,6},{6,5},{7,4},{8,11},{9,10},{10,... | collective-permute-start | bytes 24584 | tf_op jit(solution)/shard_map/ppermute | solution.py:27
  71.9 4.5 %collective-permute-start.19 = (f32[2048]{0:T(1024)S(1)}, f32[2048]{0:T(1024)S(1)}, u32[]{:S(2)}, u32[]{:S(2)}) collective-permute-start(f32[2048]{0:T(1024)S(1)} %maximum_maximum_fusion.1), channel_id=1, source_target_pairs={{0,4},{1,5},{2,6},{3,7},{4,0},{5,1},{6,2},{7,3},{8,12},{9,13},{10,... | collective-permute-start | bytes 24584 | tf_op jit(solution)/shard_map/ppermute | solution.py:27
  71.9 4.7 %collective-permute-start.18 = (f32[2048]{0:T(1024)S(1)}, f32[2048]{0:T(1024)S(1)}, u32[]{:S(2)}, u32[]{:S(2)}) collective-permute-start(f32[2048]{0:T(1024)S(1)} %maximum_maximum_fusion.1), channel_id=1, source_target_pairs={{0,8},{1,9},{2,10},{3,11},{4,12},{5,13},{6,14},{7,15},{8,0},{9,1},... | collective-permute-start | bytes 24584 | tf_op jit(solution)/shard_map/ppermute | solution.py:27
  74.5 5.4 %collective-permute-start.17 = (f32[2048]{0:T(1024)S(1)}, f32[2048]{0:T(1024)S(1)}, u32[]{:S(2)}, u32[]{:S(2)}) collective-permute-start(f32[2048]{0:T(1024)S(1)} %maximum_maximum_fusion.1), channel_id=1, source_target_pairs={{0,12},{1,13},{2,14},{3,15},{4,8},{5,9},{6,10},{7,11},{8,4},{9,5},... | collective-permute-start | bytes 24584 | tf_op jit(solution)/shard_map/ppermute | solution.py:27

commit v7 on v6

--- a/solution.py
+++ b/solution.py
@@ -14,6 +14,7 @@
 TAPS = 128
 TEMPLATES = 8
 TAIL_WIDTH = 1152
+RADIX_BITS = 4
 
 
 def from_partner(value, axis, distance):
@@ -32,7 +33,7 @@
     position = lax.axis_index(axis)
     low_bit = 0
     while low_bit < bit_count:
-        width = min(2, bit_count - low_bit)
+        width = min(RADIX_BITS, bit_count - low_bit)
         group = 2**width
         received = [value] + [from_xor(value, axis, k << low_bit) for k in range(1, group)]
         mine = position >> low_bit & (group - 1)

time: 80.8 us -> 106 us (1.31)
  starting transfers between devices: 16.8 us -> 46 us
  waiting for transfers between devices: 42.2 us -> 36.8 us
  other arithmetic: 11.2 us -> 12.9 us
    ppermute x12 -> x30, starting transfers between devices: 14 us -> 43.1 us  [from_xor(): return lax.ppermute(value, axis, pairs)]
    ppermute x12 -> x30, waiting for transfers between devices: 14.7 us -> 9.64 us  [from_xor(): return lax.ppermute(value, axis, pairs)]
  transfers between devices with their start and end apart: 20 -> 38, of which waited for: 16 -> 13; matrix products, arithmetic and copies ran while one was open for 4% -> 3% of each run, Pallas kernels for 0% -> 0%
where the time goes in v7:
time: 106 us
  starting transfers between devices  46 us (43%)
  waiting for transfers between devices  36.8 us (35%)
  other arithmetic  12.9 us (12%)
  Pallas kernels  6.79 us (6%)
  matrix products  1.87 us (2%)
  between operations  1.31 us (1%)
    ppermute x30, starting transfers between devices, from_xor(): return lax.ppermute(value, axis, pairs)  43.1 us
    ppermute x8, waiting for transfers between devices, from_partner(): return lax.ppermute(value, axis, pairs)  27.2 us
    ppermute x30, waiting for transfers between devices, from_xor(): return lax.ppermute(value, axis, pairs)  9.64 us
    pallas_call x1, Pallas kernels, local_tree(): pl.pallas_call(functools.partial(local_tree_kernel, tuple(widths_seq), fl...  6.79 us
    select_n x56, other arithmetic, shift_rows(): jnp.where(chosen, current[:, span:span + keep_len], current[:, :keep_len])  6.37 us
    ppermute x8, starting transfers between devices, from_partner(): return lax.ppermute(value, axis, pairs)  2.93 us
  transfers between devices with their start and end apart: 38, of which 13 were waited for; matrix products, arithmetic and copies ran while one was open for 3% of the time, Pallas kernels for 0%

profile of v7, /device:TPU:0, one launch (start us, length us, event | category | flops | bytes accessed | tf_op | source)
XLA Modules:
  0.0 106.0 jit_solution(13997463280140290033)
XLA Ops:
  2.4 2.6 %collective-permute-start.13 = (f32[6144]{0:T(1024)S(1)}, f32[6144]{0:T(1024)S(1)}, u32[]{:S(2)}, u32[]{:S(2)}) collective-permute-start(f32[6144]{0:T(1024)S(1)} %reduce_sum.9), channel_id=1, source_target_pairs={{0,2},{1,3},{2,0},{3,1},{4,6},{5,7},{6,4},{7,5},{8,10},{9,11},{10,... | collective-permute-start | bytes 73736 | tf_op jit(solution)/shard_map/ppermute | solution.py:28
  5.0 1.8 %collective-permute-start.11 = (f32[6144]{0:T(1024)S(1)}, f32[6144]{0:T(1024)S(1)}, u32[]{:S(2)}, u32[]{:S(2)}) collective-permute-start(f32[6144]{0:T(1024)S(1)} %reduce_sum.9), channel_id=1, source_target_pairs={{0,4},{1,5},{2,6},{3,7},{4,0},{5,1},{6,2},{7,3},{8,12},{9,13},{10,... | collective-permute-start | bytes 73736 | tf_op jit(solution)/shard_map/ppermute | solution.py:28
  6.8 2.6 %collective-permute-start.9 = (f32[6144]{0:T(1024)S(1)}, f32[6144]{0:T(1024)S(1)}, u32[]{:S(2)}, u32[]{:S(2)}) collective-permute-start(f32[6144]{0:T(1024)S(1)} %reduce_sum.9), channel_id=1, source_target_pairs={{0,6},{1,7},{2,4},{3,5},{4,2},{5,3},{6,0},{7,1},{8,14},{9,15},{10,... | collective-permute-start | bytes 73736 | tf_op jit(solution)/shard_map/ppermute | solution.py:28
  9.6 2.7 %collective-permute-start.7 = (f32[6144]{0:T(1024)S(1)}, f32[6144]{0:T(1024)S(1)}, u32[]{:S(2)}, u32[]{:S(2)}) collective-permute-start(f32[6144]{0:T(1024)S(1)} %reduce_sum.9), channel_id=1, source_target_pairs={{0,8},{1,9},{2,10},{3,11},{4,12},{5,13},{6,14},{7,15},{8,0},{9,1},... | collective-permute-start | bytes 73736 | tf_op jit(solution)/shard_map/ppermute | solution.py:28
  12.4 3.4 %collective-permute-start.5 = (f32[6144]{0:T(1024)S(1)}, f32[6144]{0:T(1024)S(1)}, u32[]{:S(2)}, u32[]{:S(2)}) collective-permute-start(f32[6144]{0:T(1024)S(1)} %reduce_sum.9), channel_id=1, source_target_pairs={{0,10},{1,11},{2,8},{3,9},{4,14},{5,15},{6,12},{7,13},{8,2},{9,3},... | collective-permute-start | bytes 73736 | tf_op jit(solution)/shard_map/ppermute | solution.py:28
  15.9 3.6 %collective-permute-start.3 = (f32[6144]{0:T(1024)S(1)}, f32[6144]{0:T(1024)S(1)}, u32[]{:S(2)}, u32[]{:S(2)}) collective-permute-start(f32[6144]{0:T(1024)S(1)} %reduce_sum.9), channel_id=1, source_target_pairs={{0,12},{1,13},{2,14},{3,15},{4,8},{5,9},{6,10},{7,11},{8,4},{9,5},... | collective-permute-start | bytes 73736 | tf_op jit(solution)/shard_map/ppermute | solution.py:28
  19.5 4.4 %collective-permute-start.1 = (f32[6144]{0:T(1024)S(1)}, f32[6144]{0:T(1024)S(1)}, u32[]{:S(2)}, u32[]{:S(2)}) collective-permute-start(f32[6144]{0:T(1024)S(1)} %reduce_sum.9), channel_id=1, source_target_pairs={{0,14},{1,15},{2,12},{3,13},{4,10},{5,11},{6,8},{7,9},{8,6},{9,7},... | collective-permute-start | bytes 73736 | tf_op jit(solution)/shard_map/ppermute | solution.py:28
  24.6 1.7 %collective-permute-done.1 = f32[6144]{0:T(1024)S(1)} collective-permute-done((f32[6144]{0:T(1024)S(1)}, f32[6144]{0:T(1024)S(1)}, u32[]{:S(2)}, u32[]{:S(2)}) %collective-permute-start.1) | collective-permute-done | bytes 24608 | tf_op jit(solution)/shard_map/ppermute | solution.py:28
  26.3 3.5 %collective-permute-done = f32[6144]{0:T(1024)S(1)} collective-permute-done((f32[6144]{0:T(1024)S(1)}, f32[6144]{0:T(1024)S(1)}, u32[]{:S(2)}, u32[]{:S(2)}) %collective-permute-start) | collective-permute-done | bytes 24608 | tf_op jit(solution)/shard_map/ppermute | solution.py:28
  29.8 1.6 %add_add_fusion = f32[6144]{0:T(1024)} fusion(f32[6144]{0:T(1024)S(1)} %collective-permute-done, f32[6144]{0:T(1024)S(1)} %collective-permute-done.1, f32[6144]{0:T(1024)S(1)} %collective-permute-done.2, f32[6144]{0:T(1024)S(1)} %collective-permute-done.3, f32[6144]{0:T(1024)S(1)} %collective-permute-done.4, f32[6144]{0:T(1024)S(1)} %collective-permute-done.5, ...), kind=kLoop, calls=%fused_computation.116 | loop fusion | flops 1566720 | bytes 418032 | tf_op jit(solution)/shard_map/add | solution.py:47
  31.4 6.8 %shard_map.50 = (f32[32,2048]{1,0:T(8,128)}, f32[32,1152]{1,0:T(8,128)}) custom-call(f32[32,6144]{1,0:T(8,128)} %x_ref.1, f32[1,6144]{1,0:T(1,128)} %bitcast.87, s32[9,32]{1,0:T(8,128)} %offsets_ref.1), custom_call_target="tpu_custom_call" | custom-call | flops 25395200 | bytes 983040 | tf_op jit(solution)/shard_map/pallas_call | solution.py:98
  38.5 1.5 %collective-permute-done.15 = f32[32,2048]{1,0:T(8,128)S(1)} collective-permute-done((f32[32,2048]{1,0:T(8,128)}, f32[32,2048]{1,0:T(8,128)S(1)}, u32[]{:S(2)}, u32[]{:S(2)}) %collective-permute-start.15) | collective-permute-done | bytes 262176 | tf_op jit(solution)/shard_map/ppermute | solution.py:23
  42.9 1.2 %collective-permute-done.16 = f32[32,1152]{1,0:T(8,128)S(1)} collective-permute-done((f32[32,1152]{1,0:T(8,128)S(1)}, f32[32,1152]{1,0:T(8,128)S(1)}, u32[]{:S(2)}, u32[]{:S(2)}) %collective-permute-start.16) | collective-permute-done | bytes 147488 | tf_op jit(solution)/shard_map/ppermute | solution.py:23
  44.1 5.7 %collective-permute-done.17 = f32[32,1792]{1,0:T(8,128)S(1)} collective-permute-done((f32[32,1792]{1,0:T(8,128)S(1)}, f32[32,1792]{1,0:T(8,128)S(1)}, u32[]{:S(2)}, u32[]{:S(2)}) %collective-permute-start.17) | collective-permute-done | bytes 229408 | tf_op jit(solution)/shard_map/ppermute | solution.py:23
  52.5 3.4 %collective-permute-done.18 = f32[32,1152]{1,0:T(8,128)S(1)} collective-permute-done((f32[32,1152]{1,0:T(8,128)S(1)}, f32[32,1152]{1,0:T(8,128)S(1)}, u32[]{:S(2)}, u32[]{:S(2)}) %collective-permute-start.18) | collective-permute-done | bytes 147488 | tf_op jit(solution)/shard_map/ppermute | solution.py:23
  55.9 2.4 %collective-permute-done.19 = f32[32,1536]{1,0:T(8,128)S(1)} collective-permute-done((f32[32,1536]{1,0:T(8,128)S(1)}, f32[32,1536]{1,0:T(8,128)S(1)}, u32[]{:S(2)}, u32[]{:S(2)}) %collective-permute-start.19) | collective-permute-done | bytes 196640 | tf_op jit(solution)/shard_map/ppermute | solution.py:23
  61.9 3.1 %collective-permute-done.20 = f32[32,1152]{1,0:T(8,128)S(1)} collective-permute-done((f32[32,1152]{1,0:T(8,128)S(1)}, f32[32,1152]{1,0:T(8,128)S(1)}, u32[]{:S(2)}, u32[]{:S(2)}) %collective-permute-start.20) | collective-permute-done | bytes 147488 | tf_op jit(solution)/shard_map/ppermute | solution.py:23
  65.0 4.3 %collective-permute-done.21 = f32[32,1280]{1,0:T(8,128)S(1)} collective-permute-done((f32[32,1280]{1,0:T(8,128)S(1)}, f32[32,1280]{1,0:T(8,128)S(1)}, u32[]{:S(2)}, u32[]{:S(2)}) %collective-permute-start.21) | collective-permute-done | bytes 163872 | tf_op jit(solution)/shard_map/ppermute | solution.py:23
  71.4 5.7 %collective-permute-done.22 = f32[32,1152]{1,0:T(8,128)S(1)} collective-permute-done((f32[32,1152]{1,0:T(8,128)S(1)}, f32[32,1152]{1,0:T(8,128)S(1)}, u32[]{:S(2)}, u32[]{:S(2)}) %collective-permute-start.22) | collective-permute-done | bytes 147488 | tf_op jit(solution)/shard_map/ppermute | solution.py:23
  78.1 1.9 %convolution_reduce_fusion = f32[512,128]{1,0:T(8,128)S(1)} fusion(f32[512,256,1]{1,0,2:T(8,128)S(1)} %bitcast.86, f32[8,128,256]{2,1,0:T(8,128)S(1)} %bitcast.85), kind=kOutput, calls=%fused_computation | convolution fusion | flops 1611071488 | bytes 1835008 | tf_op jit(solution)/shard_map/dot_general | solution.py:147
  80.2 2.3 %collective-permute-start.36 = (f32[2048]{0:T(1024)S(1)}, f32[2048]{0:T(1024)S(1)}, u32[]{:S(2)}, u32[]{:S(2)}) collective-permute-start(f32[2048]{0:T(1024)S(1)} %reduce_max.19), channel_id=1, source_target_pairs={{0,2},{1,3},{2,0},{3,1},{4,6},{5,7},{6,4},{7,5},{8,10},{9,11},{10,... | collective-permute-start | bytes 24584 | tf_op jit(solution)/shard_map/ppermute | solution.py:28
  82.6 1.5 %collective-permute-start.33 = (f32[2048]{0:T(1024)S(1)}, f32[2048]{0:T(1024)S(1)}, u32[]{:S(2)}, u32[]{:S(2)}) collective-permute-start(f32[2048]{0:T(1024)S(1)} %reduce_max.19), channel_id=1, source_target_pairs={{0,5},{1,4},{2,7},{3,6},{4,1},{5,0},{6,3},{7,2},{8,13},{9,12},{10,... | collective-permute-start | bytes 24584 | tf_op jit(solution)/shard_map/ppermute | solution.py:28
  84.0 1.7 %collective-permute-start.32 = (f32[2048]{0:T(1024)S(1)}, f32[2048]{0:T(1024)S(1)}, u32[]{:S(2)}, u32[]{:S(2)}) collective-permute-start(f32[2048]{0:T(1024)S(1)} %reduce_max.19), channel_id=1, source_target_pairs={{0,6},{1,7},{2,4},{3,5},{4,2},{5,3},{6,0},{7,1},{8,14},{9,15},{10,... | collective-permute-start | bytes 24584 | tf_op jit(solution)/shard_map/ppermute | solution.py:28
  87.4 1.9 %collective-permute-start.29 = (f32[2048]{0:T(1024)S(1)}, f32[2048]{0:T(1024)S(1)}, u32[]{:S(2)}, u32[]{:S(2)}) collective-permute-start(f32[2048]{0:T(1024)S(1)} %reduce_max.19), channel_id=1, source_target_pairs={{0,9},{1,8},{2,11},{3,10},{4,13},{5,12},{6,15},{7,14},{8,1},{9,0},... | collective-permute-start | bytes 24584 | tf_op jit(solution)/shard_map/ppermute | solution.py:28
  89.4 1.8 %collective-permute-start.28 = (f32[2048]{0:T(1024)S(1)}, f32[2048]{0:T(1024)S(1)}, u32[]{:S(2)}, u32[]{:S(2)}) collective-permute-start(f32[2048]{0:T(1024)S(1)} %reduce_max.19), channel_id=1, source_target_pairs={{0,10},{1,11},{2,8},{3,9},{4,14},{5,15},{6,12},{7,13},{8,2},{9,3},... | collective-permute-start | bytes 24584 | tf_op jit(solution)/shard_map/ppermute | solution.py:28
  91.1 2.0 %collective-permute-start.27 = (f32[2048]{0:T(1024)S(1)}, f32[2048]{0:T(1024)S(1)}, u32[]{:S(2)}, u32[]{:S(2)}) collective-permute-start(f32[2048]{0:T(1024)S(1)} %reduce_max.19), channel_id=1, source_target_pairs={{0,11},{1,10},{2,9},{3,8},{4,15},{5,14},{6,13},{7,12},{8,3},{9,2},... | collective-permute-start | bytes 24584 | tf_op jit(solution)/shard_map/ppermute | solution.py:28
  93.2 1.6 %collective-permute-start.26 = (f32[2048]{0:T(1024)S(1)}, f32[2048]{0:T(1024)S(1)}, u32[]{:S(2)}, u32[]{:S(2)}) collective-permute-start(f32[2048]{0:T(1024)S(1)} %reduce_max.19), channel_id=1, source_target_pairs={{0,12},{1,13},{2,14},{3,15},{4,8},{5,9},{6,10},{7,11},{8,4},{9,5},... | collective-permute-start | bytes 24584 | tf_op jit(solution)/shard_map/ppermute | solution.py:28
  94.7 1.7 %collective-permute-start.25 = (f32[2048]{0:T(1024)S(1)}, f32[2048]{0:T(1024)S(1)}, u32[]{:S(2)}, u32[]{:S(2)}) collective-permute-start(f32[2048]{0:T(1024)S(1)} %reduce_max.19), channel_id=1, source_target_pairs={{0,13},{1,12},{2,15},{3,14},{4,9},{5,8},{6,11},{7,10},{8,5},{9,4},... | collective-permute-start | bytes 24584 | tf_op jit(solution)/shard_map/ppermute | solution.py:28
  96.5 2.7 %collective-permute-start.24 = (f32[2048]{0:T(1024)S(1)}, f32[2048]{0:T(1024)S(1)}, u32[]{:S(2)}, u32[]{:S(2)}) collective-permute-start(f32[2048]{0:T(1024)S(1)} %reduce_max.19), channel_id=1, source_target_pairs={{0,14},{1,15},{2,12},{3,13},{4,10},{5,11},{6,8},{7,9},{8,6},{9,7},... | collective-permute-start | bytes 24584 | tf_op jit(solution)/shard_map/ppermute | solution.py:28
  99.2 2.0 %collective-permute-start.23 = (f32[2048]{0:T(1024)S(1)}, f32[2048]{0:T(1024)S(1)}, u32[]{:S(2)}, u32[]{:S(2)}) collective-permute-start(f32[2048]{0:T(1024)S(1)} %reduce_max.19), channel_id=1, source_target_pairs={{0,15},{1,14},{2,13},{3,12},{4,11},{5,10},{6,9},{7,8},{8,7},{9,6},... | collective-permute-start | bytes 24584 | tf_op jit(solution)/shard_map/ppermute | solution.py:28
  101.2 1.7 %collective-permute-done.24 = f32[2048]{0:T(1024)S(1)} collective-permute-done((f32[2048]{0:T(1024)S(1)}, f32[2048]{0:T(1024)S(1)}, u32[]{:S(2)}, u32[]{:S(2)}) %collective-permute-start.24) | collective-permute-done | bytes 8224 | tf_op jit(solution)/shard_map/ppermute | solution.py:28
  102.8 2.1 %collective-permute-done.23 = f32[2048]{0:T(1024)S(1)} collective-permute-done((f32[2048]{0:T(1024)S(1)}, f32[2048]{0:T(1024)S(1)}, u32[]{:S(2)}, u32[]{:S(2)}) %collective-permute-start.23) | collective-permute-done | bytes 8224 | tf_op jit(solution)/shard_map/ppermute | solution.py:28
  (151 shorter events, 18.2 us)
Async XLA Ops:
  1.9 5.0 %collective-permute-start.14 = (f32[6144]{0:T(1024)S(1)}, f32[6144]{0:T(1024)S(1)}, u32[]{:S(2)}, u32[]{:S(2)}) collective-permute-start(f32[6144]{0:T(1024)S(1)} %reduce_sum.9), channel_id=1, source_target_pairs={{0,1},{1,0},{2,3},{3,2},{4,5},{5,4},{6,7},{7,6},{8,9},{9,8},{10,11... | collective-permute-start | bytes 73736 | tf_op jit(solution)/shard_map/ppermute | solution.py:28
  2.4 7.1 %collective-permute-start.13 = (f32[6144]{0:T(1024)S(1)}, f32[6144]{0:T(1024)S(1)}, u32[]{:S(2)}, u32[]{:S(2)}) collective-permute-start(f32[6144]{0:T(1024)S(1)} %reduce_sum.9), channel_id=1, source_target_pairs={{0,2},{1,3},{2,0},{3,1},{4,6},{5,7},{6,4},{7,5},{8,10},{9,11},{10,... | collective-permute-start | bytes 73736 | tf_op jit(solution)/shard_map/ppermute | solution.py:28
  5.0 7.2 %collective-permute-start.11 = (f32[6144]{0:T(1024)S(1)}, f32[6144]{0:T(1024)S(1)}, u32[]{:S(2)}, u32[]{:S(2)}) collective-permute-start(f32[6144]{0:T(1024)S(1)} %reduce_sum.9), channel_id=1, source_target_pairs={{0,4},{1,5},{2,6},{3,7},{4,0},{5,1},{6,2},{7,3},{8,12},{9,13},{10,... | collective-permute-start | bytes 73736 | tf_op jit(solution)/shard_map/ppermute | solution.py:28
  6.8 5.6 %collective-permute-start.10 = (f32[6144]{0:T(1024)S(1)}, f32[6144]{0:T(1024)S(1)}, u32[]{:S(2)}, u32[]{:S(2)}) collective-permute-start(f32[6144]{0:T(1024)S(1)} %reduce_sum.9), channel_id=1, source_target_pairs={{0,5},{1,4},{2,7},{3,6},{4,1},{5,0},{6,3},{7,2},{8,13},{9,12},{10,... | collective-permute-start | bytes 73736 | tf_op jit(solution)/shard_map/ppermute | solution.py:28
  6.8 8.9 %collective-permute-start.9 = (f32[6144]{0:T(1024)S(1)}, f32[6144]{0:T(1024)S(1)}, u32[]{:S(2)}, u32[]{:S(2)}) collective-permute-start(f32[6144]{0:T(1024)S(1)} %reduce_sum.9), channel_id=1, source_target_pairs={{0,6},{1,7},{2,4},{3,5},{4,2},{5,3},{6,0},{7,1},{8,14},{9,15},{10,... | collective-permute-start | bytes 73736 | tf_op jit(solution)/shard_map/ppermute | solution.py:28
  9.4 6.4 %collective-permute-start.8 = (f32[6144]{0:T(1024)S(1)}, f32[6144]{0:T(1024)S(1)}, u32[]{:S(2)}, u32[]{:S(2)}) collective-permute-start(f32[6144]{0:T(1024)S(1)} %reduce_sum.9), channel_id=1, source_target_pairs={{0,7},{1,6},{2,5},{3,4},{4,3},{5,2},{6,1},{7,0},{8,15},{9,14},{10,... | collective-permute-start | bytes 73736 | tf_op jit(solution)/shard_map/ppermute | solution.py:28
  9.6 9.9 %collective-permute-start.7 = (f32[6144]{0:T(1024)S(1)}, f32[6144]{0:T(1024)S(1)}, u32[]{:S(2)}, u32[]{:S(2)}) collective-permute-start(f32[6144]{0:T(1024)S(1)} %reduce_sum.9), channel_id=1, source_target_pairs={{0,8},{1,9},{2,10},{3,11},{4,12},{5,13},{6,14},{7,15},{8,0},{9,1},... | collective-permute-start | bytes 73736 | tf_op jit(solution)/shard_map/ppermute | solution.py:28
  12.2 7.3 %collective-permute-start.6 = (f32[6144]{0:T(1024)S(1)}, f32[6144]{0:T(1024)S(1)}, u32[]{:S(2)}, u32[]{:S(2)}) collective-permute-start(f32[6144]{0:T(1024)S(1)} %reduce_sum.9), channel_id=1, source_target_pairs={{0,9},{1,8},{2,11},{3,10},{4,13},{5,12},{6,15},{7,14},{8,1},{9,0},... | collective-permute-start | bytes 73736 | tf_op jit(solution)/shard_map/ppermute | solution.py:28
  12.4 11.5 %collective-permute-start.5 = (f32[6144]{0:T(1024)S(1)}, f32[6144]{0:T(1024)S(1)}, u32[]{:S(2)}, u32[]{:S(2)}) collective-permute-start(f32[6144]{0:T(1024)S(1)} %reduce_sum.9), channel_id=1, source_target_pairs={{0,10},{1,11},{2,8},{3,9},{4,14},{5,15},{6,12},{7,13},{8,2},{9,3},... | collective-permute-start | bytes 73736 | tf_op jit(solution)/shard_map/ppermute | solution.py:28
  15.8 8.2 %collective-permute-start.4 = (f32[6144]{0:T(1024)S(1)}, f32[6144]{0:T(1024)S(1)}, u32[]{:S(2)}, u32[]{:S(2)}) collective-permute-start(f32[6144]{0:T(1024)S(1)} %reduce_sum.9), channel_id=1, source_target_pairs={{0,11},{1,10},{2,9},{3,8},{4,15},{5,14},{6,13},{7,12},{8,3},{9,2},... | collective-permute-start | bytes 73736 | tf_op jit(solution)/shard_map/ppermute | solution.py:28
  15.9 8.1 %collective-permute-start.3 = (f32[6144]{0:T(1024)S(1)}, f32[6144]{0:T(1024)S(1)}, u32[]{:S(2)}, u32[]{:S(2)}) collective-permute-start(f32[6144]{0:T(1024)S(1)} %reduce_sum.9), channel_id=1, source_target_pairs={{0,12},{1,13},{2,14},{3,15},{4,8},{5,9},{6,10},{7,11},{8,4},{9,5},... | collective-permute-start | bytes 73736 | tf_op jit(solution)/shard_map/ppermute | solution.py:28
  19.5 5.2 %collective-permute-start.2 = (f32[6144]{0:T(1024)S(1)}, f32[6144]{0:T(1024)S(1)}, u32[]{:S(2)}, u32[]{:S(2)}) collective-permute-start(f32[6144]{0:T(1024)S(1)} %reduce_sum.9), channel_id=1, source_target_pairs={{0,13},{1,12},{2,15},{3,14},{4,9},{5,8},{6,11},{7,10},{8,5},{9,4},... | collective-permute-start | bytes 73736 | tf_op jit(solution)/shard_map/ppermute | solution.py:28
  19.5 6.8 %collective-permute-start.1 = (f32[6144]{0:T(1024)S(1)}, f32[6144]{0:T(1024)S(1)}, u32[]{:S(2)}, u32[]{:S(2)}) collective-permute-start(f32[6144]{0:T(1024)S(1)} %reduce_sum.9), channel_id=1, source_target_pairs={{0,14},{1,15},{2,12},{3,13},{4,10},{5,11},{6,8},{7,9},{8,6},{9,7},... | collective-permute-start | bytes 73736 | tf_op jit(solution)/shard_map/ppermute | solution.py:28
  23.9 5.9 %collective-permute-start = (f32[6144]{0:T(1024)S(1)}, f32[6144]{0:T(1024)S(1)}, u32[]{:S(2)}, u32[]{:S(2)}) collective-permute-start(f32[6144]{0:T(1024)S(1)} %reduce_sum.9), channel_id=1, source_target_pairs={{0,15},{1,14},{2,13},{3,12},{4,11},{5,10},{6,9},{7,8},{8,7},{9,6},... | collective-permute-start | bytes 73736 | tf_op jit(solution)/shard_map/ppermute | solution.py:28
  42.0 7.7 %collective-permute-start.17 = (f32[32,1792]{1,0:T(8,128)S(1)}, f32[32,1792]{1,0:T(8,128)S(1)}, u32[]{:S(2)}, u32[]{:S(2)}) collective-permute-start(f32[32,1792]{1,0:T(8,128)S(1)} %fusion.2), channel_id=1, source_target_pairs={{0,2},{1,3},{2,0},{3,1},{4,6},{5,7},{6,4},{7,5},{8,10},{9,11},{10,... | collective-permute-start | bytes 688136 | tf_op jit(solution)/shard_map/ppermute | solution.py:23
  50.7 5.2 %collective-permute-start.18 = (f32[32,1152]{1,0:T(8,128)S(1)}, f32[32,1152]{1,0:T(8,128)S(1)}, u32[]{:S(2)}, u32[]{:S(2)}) collective-permute-start(f32[32,1152]{1,0:T(8,128)S(1)} %fusion.16), channel_id=1, source_target_pairs={{0,2},{1,3},{2,0},{3,1},{4,6},{5,7},{6,4},{7,5},{8,10},{9,11},{10,... | collective-permute-start | bytes 442376 | tf_op jit(solution)/shard_map/ppermute | solution.py:23
  52.4 5.9 %collective-permute-start.19 = (f32[32,1536]{1,0:T(8,128)S(1)}, f32[32,1536]{1,0:T(8,128)S(1)}, u32[]{:S(2)}, u32[]{:S(2)}) collective-permute-start(f32[32,1536]{1,0:T(8,128)S(1)} %fusion.3), channel_id=1, source_target_pairs={{0,4},{1,5},{2,6},{3,7},{4,0},{5,1},{6,2},{7,3},{8,12},{9,13},{10,... | collective-permute-start | bytes 589832 | tf_op jit(solution)/shard_map/ppermute | solution.py:23
  59.2 5.8 %collective-permute-start.20 = (f32[32,1152]{1,0:T(8,128)S(1)}, f32[32,1152]{1,0:T(8,128)S(1)}, u32[]{:S(2)}, u32[]{:S(2)}) collective-permute-start(f32[32,1152]{1,0:T(8,128)S(1)} %fusion.15), channel_id=1, source_target_pairs={{0,4},{1,5},{2,6},{3,7},{4,0},{5,1},{6,2},{7,3},{8,12},{9,13},{10,... | collective-permute-start | bytes 442376 | tf_op jit(solution)/shard_map/ppermute | solution.py:23
  60.5 8.7 %collective-permute-start.21 = (f32[32,1280]{1,0:T(8,128)S(1)}, f32[32,1280]{1,0:T(8,128)S(1)}, u32[]{:S(2)}, u32[]{:S(2)}) collective-permute-start(f32[32,1280]{1,0:T(8,128)S(1)} %fusion.12), channel_id=1, source_target_pairs={{0,8},{1,9},{2,10},{3,11},{4,12},{5,13},{6,14},{7,15},{8,0},{9,1},... | collective-permute-start | bytes 491528 | tf_op jit(solution)/shard_map/ppermute | solution.py:23
  70.5 6.5 %collective-permute-start.22 = (f32[32,1152]{1,0:T(8,128)S(1)}, f32[32,1152]{1,0:T(8,128)S(1)}, u32[]{:S(2)}, u32[]{:S(2)}) collective-permute-start(f32[32,1152]{1,0:T(8,128)S(1)} %fusion.14), channel_id=1, source_target_pairs={{0,8},{1,9},{2,10},{3,11},{4,12},{5,13},{6,14},{7,15},{8,0},{9,1},... | collective-permute-start | bytes 442376 | tf_op jit(solution)/shard_map/ppermute | solution.py:23
  80.2 5.6 %collective-permute-start.36 = (f32[2048]{0:T(1024)S(1)}, f32[2048]{0:T(1024)S(1)}, u32[]{:S(2)}, u32[]{:S(2)}) collective-permute-start(f32[2048]{0:T(1024)S(1)} %reduce_max.19), channel_id=1, source_target_pairs={{0,2},{1,3},{2,0},{3,1},{4,6},{5,7},{6,4},{7,5},{8,10},{9,11},{10,... | collective-permute-start | bytes 24584 | tf_op jit(solution)/shard_map/ppermute | solution.py:28
  82.6 6.8 %collective-permute-start.33 = (f32[2048]{0:T(1024)S(1)}, f32[2048]{0:T(1024)S(1)}, u32[]{:S(2)}, u32[]{:S(2)}) collective-permute-start(f32[2048]{0:T(1024)S(1)} %reduce_max.19), channel_id=1, source_target_pairs={{0,5},{1,4},{2,7},{3,6},{4,1},{5,0},{6,3},{7,2},{8,13},{9,12},{10,... | collective-permute-start | bytes 24584 | tf_op jit(solution)/shard_map/ppermute | solution.py:28
  84.0 7.1 %collective-permute-start.32 = (f32[2048]{0:T(1024)S(1)}, f32[2048]{0:T(1024)S(1)}, u32[]{:S(2)}, u32[]{:S(2)}) collective-permute-start(f32[2048]{0:T(1024)S(1)} %reduce_max.19), channel_id=1, source_target_pairs={{0,6},{1,7},{2,4},{3,5},{4,2},{5,3},{6,0},{7,1},{8,14},{9,15},{10,... | collective-permute-start | bytes 24584 | tf_op jit(solution)/shard_map/ppermute | solution.py:28
  85.8 7.4 %collective-permute-start.31 = (f32[2048]{0:T(1024)S(1)}, f32[2048]{0:T(1024)S(1)}, u32[]{:S(2)}, u32[]{:S(2)}) collective-permute-start(f32[2048]{0:T(1024)S(1)} %reduce_max.19), channel_id=1, source_target_pairs={{0,7},{1,6},{2,5},{3,4},{4,3},{5,2},{6,1},{7,0},{8,15},{9,14},{10,... | collective-permute-start | bytes 24584 | tf_op jit(solution)/shard_map/ppermute | solution.py:28
  87.0 7.8 %collective-permute-start.30 = (f32[2048]{0:T(1024)S(1)}, f32[2048]{0:T(1024)S(1)}, u32[]{:S(2)}, u32[]{:S(2)}) collective-permute-start(f32[2048]{0:T(1024)S(1)} %reduce_max.19), channel_id=1, source_target_pairs={{0,8},{1,9},{2,10},{3,11},{4,12},{5,13},{6,14},{7,15},{8,0},{9,1},... | collective-permute-start | bytes 24584 | tf_op jit(solution)/shard_map/ppermute | solution.py:28
  87.4 9.0 %collective-permute-start.29 = (f32[2048]{0:T(1024)S(1)}, f32[2048]{0:T(1024)S(1)}, u32[]{:S(2)}, u32[]{:S(2)}) collective-permute-start(f32[2048]{0:T(1024)S(1)} %reduce_max.19), channel_id=1, source_target_pairs={{0,9},{1,8},{2,11},{3,10},{4,13},{5,12},{6,15},{7,14},{8,1},{9,0},... | collective-permute-start | bytes 24584 | tf_op jit(solution)/shard_map/ppermute | solution.py:28
  89.4 9.8 %collective-permute-start.28 = (f32[2048]{0:T(1024)S(1)}, f32[2048]{0:T(1024)S(1)}, u32[]{:S(2)}, u32[]{:S(2)}) collective-permute-start(f32[2048]{0:T(1024)S(1)} %reduce_max.19), channel_id=1, source_target_pairs={{0,10},{1,11},{2,8},{3,9},{4,14},{5,15},{6,12},{7,13},{8,2},{9,3},... | collective-permute-start | bytes 24584 | tf_op jit(solution)/shard_map/ppermute | solution.py:28
  91.1 10.0 %collective-permute-start.27 = (f32[2048]{0:T(1024)S(1)}, f32[2048]{0:T(1024)S(1)}, u32[]{:S(2)}, u32[]{:S(2)}) collective-permute-start(f32[2048]{0:T(1024)S(1)} %reduce_max.19), channel_id=1, source_target_pairs={{0,11},{1,10},{2,9},{3,8},{4,15},{5,14},{6,13},{7,12},{8,3},{9,2},... | collective-permute-start | bytes 24584 | tf_op jit(solution)/shard_map/ppermute | solution.py:28
  93.2 8.0 %collective-permute-start.26 = (f32[2048]{0:T(1024)S(1)}, f32[2048]{0:T(1024)S(1)}, u32[]{:S(2)}, u32[]{:S(2)}) collective-permute-start(f32[2048]{0:T(1024)S(1)} %reduce_max.19), channel_id=1, source_target_pairs={{0,12},{1,13},{2,14},{3,15},{4,8},{5,9},{6,10},{7,11},{8,4},{9,5},... | collective-permute-start | bytes 24584 | tf_op jit(solution)/shard_map/ppermute | solution.py:28
  94.7 6.4 %collective-permute-start.25 = (f32[2048]{0:T(1024)S(1)}, f32[2048]{0:T(1024)S(1)}, u32[]{:S(2)}, u32[]{:S(2)}) collective-permute-start(f32[2048]{0:T(1024)S(1)} %reduce_max.19), channel_id=1, source_target_pairs={{0,13},{1,12},{2,15},{3,14},{4,9},{5,8},{6,11},{7,10},{8,5},{9,4},... | collective-permute-start | bytes 24584 | tf_op jit(solution)/shard_map/ppermute | solution.py:28
  96.5 6.3 %collective-permute-start.24 = (f32[2048]{0:T(1024)S(1)}, f32[2048]{0:T(1024)S(1)}, u32[]{:S(2)}, u32[]{:S(2)}) collective-permute-start(f32[2048]{0:T(1024)S(1)} %reduce_max.19), channel_id=1, source_target_pairs={{0,14},{1,15},{2,12},{3,13},{4,10},{5,11},{6,8},{7,9},{8,6},{9,7},... | collective-permute-start | bytes 24584 | tf_op jit(solution)/shard_map/ppermute | solution.py:28
  99.2 5.8 %collective-permute-start.23 = (f32[2048]{0:T(1024)S(1)}, f32[2048]{0:T(1024)S(1)}, u32[]{:S(2)}, u32[]{:S(2)}) collective-permute-start(f32[2048]{0:T(1024)S(1)} %reduce_max.19), channel_id=1, source_target_pairs={{0,15},{1,14},{2,13},{3,12},{4,11},{5,10},{6,9},{7,8},{8,7},{9,6},... | collective-permute-start | bytes 24584 | tf_op jit(solution)/shard_map/ppermute | solution.py:28
  (10 other events, 85.6 us)

commit v8 on v6

--- a/solution.py
+++ b/solution.py
@@ -27,14 +27,20 @@
     return lax.ppermute(value, axis, pairs)
 
 
-def butterfly(value, axis, combine):
+def butterfly(value, axis, combine, side=None):
     bit_count = lax.axis_size(axis).bit_length() - 1
     position = lax.axis_index(axis)
+    partners = {}
     low_bit = 0
     while low_bit < bit_count:
         width = min(2, bit_count - low_bit)
         group = 2**width
-        received = [value] + [from_xor(value, axis, k << low_bit) for k in range(1, group)]
+        payload = value if side is None else jnp.concatenate([value, side])
+        received = [payload] + [from_xor(payload, axis, k << low_bit) for k in range(1, group)]
+        if side is not None:
+            for k in range(1, group):
+                partners[k << low_bit] = received[k][value.shape[0] :]
+            received = [item[: value.shape[0]] for item in received]
         mine = position >> low_bit & (group - 1)
         ordered = []
         for slot in range(group):
@@ -46,7 +52,7 @@
             ordered = [combine(ordered[i], ordered[i + 1]) for i in range(0, len(ordered), 2)]
         value = ordered[0]
         low_bit += width
-    return value
+    return value, partners
 
 
 def shift_rows(trial_rows, amounts, length):
@@ -165,38 +171,47 @@
         return min(TIN, needed)
 
     partial_value = jnp.sum(filterbank, axis=0)
-    channel_total = butterfly(partial_value, "band", jnp.add)
+    own_side = offsets.astype(jnp.float32).reshape(-1)
+    channel_total, partner_sides = butterfly(partial_value, "band", jnp.add, own_side)
     widths_seq = [length_after(section) for section in range(local_count + 1)]
     head, tail = local_tree(filterbank, channel_total, offsets, widths_seq, channels_all, TAIL_WIDTH)
     band_index = lax.axis_index("band")
     bit_count = band_count.bit_length() - 1
     tail_width = TAIL_WIDTH
 
-    def halves(own, partner, bit_index):
+    def amounts_for(bit_index, own):
+        section_index = local_count + bit_index
+        if own:
+            values = offsets[section_index]
+        else:
+            side = partner_sides[2**bit_index].reshape(levels, -1)
+            values = side[section_index].astype(jnp.int32)
         upper_half = band_index // 2**bit_index % 2 == 1
-        return jnp.where(upper_half, partner, own), jnp.where(upper_half, own, partner)
-
-    partner_head = from_partner(head, "band", 0)
+        return jnp.where(upper_half, values, 0)
+
+    head_width = head.shape[1] - SHIFT
+    partner_head = from_partner(shift_rows(head, amounts_for(0, False), head_width), "band", 0)
     for bit_index in range(bit_count):
-        amounts = offsets[local_count + bit_index]
-        tail, partner_head = lax.optimization_barrier((tail, partner_head))
-        lower_head, upper_head = halves(head, partner_head, bit_index)
+        head, tail, partner_head = lax.optimization_barrier((head, tail, partner_head))
         head_width = head.shape[1] - SHIFT
-        new_head = lower_head[:, :head_width] + shift_rows(upper_head, amounts, head_width)
-        partner_tail = from_partner(tail, "band", bit_index)
+        new_head = shift_rows(head, amounts_for(bit_index, True), head_width) + partner_head
+        window = jnp.concatenate([head[:, head_width:], tail], axis=1)
+        partner_tail = from_partner(
+            shift_rows(window, amounts_for(bit_index, False), tail_width), "band", bit_index
+        )
         if bit_index + 1 < bit_count:
-            next_partner_head = from_partner(new_head, "band", bit_index + 1)
+            next_width = head_width - SHIFT
+            next_partner_head = from_partner(
+                shift_rows(new_head, amounts_for(bit_index + 1, False), next_width), "band", bit_index + 1
+            )
             partner_tail, next_partner_head = lax.optimization_barrier((partner_tail, next_partner_head))
             partner_head = next_partner_head
-        lower_tail, upper_tail = halves(tail, partner_tail, bit_index)
-        lower_window = jnp.concatenate([lower_head[:, head_width:], lower_tail], axis=1)
-        upper_window = jnp.concatenate([upper_head[:, head_width:], upper_tail], axis=1)
-        tail = lower_window[:, :tail_width] + shift_rows(upper_window, amounts, tail_width)
+        tail = shift_rows(window, amounts_for(bit_index, True), tail_width) + partner_tail
         head = new_head
     current = jnp.concatenate([head, tail], axis=1)
     dedispersed = current * (1.0 / math.sqrt(channels_all))
     detection = boxcar_max(dedispersed, widths)
-    peak_series = butterfly(jnp.max(detection, axis=0), "band", jnp.maximum)
+    peak_series, _ = butterfly(jnp.max(detection, axis=0), "band", jnp.maximum)
     return (detection, peak_series)
 
 

time: 80.8 us -> 87.6 us (1.084)
  other arithmetic: 11.2 us -> 20.5 us
  waiting for transfers between devices: 42.2 us -> 35.5 us
  starting transfers between devices: 16.8 us -> 19.7 us
    select_n x56 -> x116, other arithmetic: 6.19 us -> 14.2 us  [shift_rows(): jnp.where(chosen, current[:, span:span + keep_len], current[:, :keep_len])]
    ppermute x8, waiting for transfers between devices: 27.5 us -> 23.4 us  [from_partner(): return lax.ppermute(value, axis, pairs)]
    ppermute x8, starting transfers between devices: 2.84 us -> 5.73 us  [from_partner(): return lax.ppermute(value, axis, pairs)]
    ppermute x12, waiting for transfers between devices: 14.7 us -> 12.2 us  [from_xor(): return lax.ppermute(value, axis, pairs)]
    select_n x8 -> x0, other arithmetic: 1.16 us -> none  [halves(): jnp.where(upper_half, partner, own)]
    eq x2 -> x11, other arithmetic: 0.04 us -> 1.14 us  [shift_rows(): chosen = (amounts >> bit_index & 1)[:, None] == 1]
  transfers between devices with their start and end apart: 20 -> 20, of which waited for: 16 -> 14; matrix products, arithmetic and copies ran while one was open for 4% -> 7% of each run, Pallas kernels for 0% -> 0%
where the time goes in v8:
time: 87.6 us; the launch traced here: 87.3 us
  waiting for transfers between devices  35.5 us (41%)
  other arithmetic  20.5 us (23%)
  starting transfers between devices  19.7 us (22%)
  Pallas kernels  6.8 us (8%)
  matrix products  1.87 us (2%)
  between operations  1.78 us (2%)
  local copies, waits for them, and re-layouts  1.04 us (1%)
    ppermute x8, waiting for transfers between devices, from_partner(): return lax.ppermute(value, axis, pairs)  23.4 us
    select_n x116, other arithmetic, shift_rows(): jnp.where(chosen, current[:, span:span + keep_len], current[:, :keep_len])  14.2 us
    ppermute x12, starting transfers between devices, from_xor(): return lax.ppermute(value, axis, pairs)  14 us
    ppermute x12, waiting for transfers between devices, from_xor(): return lax.ppermute(value, axis, pairs)  12.2 us
    pallas_call x1, Pallas kernels, local_tree(): pl.pallas_call(functools.partial(local_tree_kernel, tuple(widths_seq), fl...  6.8 us
    ppermute x8, starting transfers between devices, from_partner(): return lax.ppermute(value, axis, pairs)  5.73 us
    dot_general x1, matrix products, boxcar_max(): jnp.dot(paired, joined, precision=lax.Precision.HIGHEST, preferred_elemen...  1.87 us
  transfers between devices with their start and end apart: 20, of which 14 were waited for; matrix products, arithmetic and copies ran while one was open for 7% of the time, Pallas kernels for 0%

profile of v8, /device:TPU:0, one launch (start us, length us, event | category | flops | bytes accessed | tf_op | source)
XLA Modules:
  0.0 87.3 jit_solution(13074299793784966306)
XLA Ops:
  0.6 0.7 convert_element_type.79
  1.4 1.2 %reduce_sum.9 = f32[6144]{0:T(1024)S(1)} reduce(f32[32,6144]{1,0:T(8,128)} %x_ref.1, f32[]{:T(128)} %constant.136.clone.1), dimensions={0}, to_apply=%region_0.0 | reduce | flops 190464 | bytes 811012 | tf_op jit(solution)/shard_map/reduce_sum | solution.py:173
  3.2 2.6 %collective-permute-start.1 = (f32[6432]{0:T(1024)S(1)}, f32[6432]{0:T(1024)S(1)}, u32[]{:S(2)}, u32[]{:S(2)}) collective-permute-start(f32[6432]{0:T(1024)S(1)} %pad_maximum_fusion.6), channel_id=1, source_target_pairs={{0,2},{1,3},{2,0},{3,1},{4,6},{5,7},{6,4},{7,5},{8,10},{9,11},{10,... | collective-permute-start | bytes 77192 | tf_op jit(solution)/shard_map/ppermute | solution.py:27
  5.8 0.7 convert_rsqrt_fusion
  6.4 0.7 broadcast_bitcast_fusion.1
  7.3 0.8 compare_bitcast_fusion.31
  9.0 1.6 %collective-permute-start.5 = (f32[6432]{0:T(1024)S(1)}, f32[6432]{0:T(1024)S(1)}, u32[]{:S(2)}, u32[]{:S(2)}) collective-permute-start(f32[6432]{0:T(1024)S(1)} %pad_maximum_fusion.5), channel_id=1, source_target_pairs={{0,4},{1,5},{2,6},{3,7},{4,0},{5,1},{6,2},{7,3},{8,12},{9,13},{10,... | collective-permute-start | bytes 77192 | tf_op jit(solution)/shard_map/ppermute | solution.py:27
  10.7 2.6 %collective-permute-start.4 = (f32[6432]{0:T(1024)S(1)}, f32[6432]{0:T(1024)S(1)}, u32[]{:S(2)}, u32[]{:S(2)}) collective-permute-start(f32[6432]{0:T(1024)S(1)} %pad_maximum_fusion.5), channel_id=1, source_target_pairs={{0,8},{1,9},{2,10},{3,11},{4,12},{5,13},{6,14},{7,15},{8,0},{9,1},... | collective-permute-start | bytes 77192 | tf_op jit(solution)/shard_map/ppermute | solution.py:27
  13.7 2.2 %collective-permute-done.4 = f32[6432]{0:T(1024)S(1)} collective-permute-done((f32[6432]{0:T(1024)S(1)}, f32[6432]{0:T(1024)S(1)}, u32[]{:S(2)}, u32[]{:S(2)}) %collective-permute-start.4) | collective-permute-done | bytes 25760 | tf_op jit(solution)/shard_map/ppermute | solution.py:27
  15.9 3.0 %collective-permute-done.3 = f32[6432]{0:T(1024)S(1)} collective-permute-done((f32[6432]{0:T(1024)S(1)}, f32[6432]{0:T(1024)S(1)}, u32[]{:S(2)}, u32[]{:S(2)}) %collective-permute-start.3) | collective-permute-done | bytes 25760 | tf_op jit(solution)/shard_map/ppermute | solution.py:27
  18.9 0.6 add_add_fusion
  19.6 6.8 %shard_map.50 = (f32[32,2048]{1,0:T(8,128)}, f32[32,1152]{1,0:T(8,128)}) custom-call(f32[32,6144]{1,0:T(8,128)} %x_ref.1, f32[1,6144]{1,0:T(1,128)} %bitcast.87, s32[9,32]{1,0:T(8,128)} %offsets_ref.1), custom_call_target="tpu_custom_call" | custom-call | flops 25395200 | bytes 983040 | tf_op jit(solution)/shard_map/pallas_call | solution.py:103
  26.4 1.2 %slice_select_fusion.13 = f32[32,1919]{1,0:T(8,128)S(1)} fusion(f32[32,2048]{1,0:T(8,128)} %get-tuple-element.24, pred[32]{0:T(512)(128)(4,1)S(1)} %get-tuple-element.129), kind=kLoop, calls=%fused_computation.19 | loop fusion | flops 61408 | bytes 736928 | tf_op jit(solution)/shard_map/jit(_where)/select_n | solution.py:65
  28.7 1.3 %collective-permute-done.6 = f32[32,1792]{1,0:T(8,128)S(1)} collective-permute-done((f32[32,1792]{1,0:T(8,128)S(1)}, f32[32,1792]{1,0:T(8,128)S(1)}, u32[]{:S(2)}, u32[]{:S(2)}) %collective-permute-start.6) | collective-permute-done | bytes 229408 | tf_op jit(solution)/shard_map/ppermute | solution.py:22
  33.8 1.4 %collective-permute-start.8 = (f32[32,1536]{1,0:T(8,128)S(1)}, f32[32,1536]{1,0:T(8,128)S(1)}, u32[]{:S(2)}, u32[]{:S(2)}) collective-permute-start(f32[32,1536]{1,0:T(8,128)S(1)} %slice_select_fusion.31), channel_id=1, source_target_pairs={{0,2},{1,3},{2,0},{3,1},{4,6},{5,7},{6,4},{7,5},{8,10},{9,11},{10,... | collective-permute-start | bytes 589832 | tf_op jit(solution)/shard_map/ppermute | solution.py:22
  35.4 5.7 %collective-permute-done.8 = f32[32,1536]{1,0:T(8,128)S(1)} collective-permute-done((f32[32,1536]{1,0:T(8,128)S(1)}, f32[32,1536]{1,0:T(8,128)S(1)}, u32[]{:S(2)}, u32[]{:S(2)}) %collective-permute-start.8) | collective-permute-done | bytes 196640 | tf_op jit(solution)/shard_map/ppermute | solution.py:22
  43.4 1.4 %collective-permute-start.9 = (f32[32,1152]{1,0:T(8,128)S(1)}, f32[32,1152]{1,0:T(8,128)S(1)}, u32[]{:S(2)}, u32[]{:S(2)}) collective-permute-start(f32[32,1152]{1,0:T(8,128)S(1)} %slice_select_fusion.113), channel_id=1, source_target_pairs={{0,2},{1,3},{2,0},{3,1},{4,6},{5,7},{6,4},{7,5},{8,10},{9,11},{10,... | collective-permute-start | bytes 442376 | tf_op jit(solution)/shard_map/ppermute | solution.py:22
  46.2 2.6 %collective-permute-done.9 = f32[32,1152]{1,0:T(8,128)S(1)} collective-permute-done((f32[32,1152]{1,0:T(8,128)S(1)}, f32[32,1152]{1,0:T(8,128)S(1)}, u32[]{:S(2)}, u32[]{:S(2)}) %collective-permute-start.9) | collective-permute-done | bytes 147488 | tf_op jit(solution)/shard_map/ppermute | solution.py:22
  48.8 2.7 %collective-permute-done.10 = f32[32,1280]{1,0:T(8,128)S(1)} collective-permute-done((f32[32,1280]{1,0:T(8,128)S(1)}, f32[32,1280]{1,0:T(8,128)S(1)}, u32[]{:S(2)}, u32[]{:S(2)}) %collective-permute-start.10) | collective-permute-done | bytes 163872 | tf_op jit(solution)/shard_map/ppermute | solution.py:22
  55.2 1.0 %collective-permute-start.11 = (f32[32,1152]{1,0:T(8,128)S(1)}, f32[32,1152]{1,0:T(8,128)S(1)}, u32[]{:S(2)}, u32[]{:S(2)}) collective-permute-start(f32[32,1152]{1,0:T(8,128)S(1)} %slice_select_fusion.111), channel_id=1, source_target_pairs={{0,4},{1,5},{2,6},{3,7},{4,0},{5,1},{6,2},{7,3},{8,12},{9,13},{10,... | collective-permute-start | bytes 442376 | tf_op jit(solution)/shard_map/ppermute | solution.py:22
  56.3 5.3 %collective-permute-done.12 = f32[32,1024]{1,0:T(8,128)S(1)} collective-permute-done((f32[32,1024]{1,0:T(8,128)S(1)}, f32[32,1024]{1,0:T(8,128)S(1)}, u32[]{:S(2)}, u32[]{:S(2)}) %collective-permute-start.12) | collective-permute-done | bytes 131104 | tf_op jit(solution)/shard_map/ppermute | solution.py:22
  64.4 1.5 %collective-permute-start.13 = (f32[32,1152]{1,0:T(8,128)S(1)}, f32[32,1152]{1,0:T(8,128)S(1)}, u32[]{:S(2)}, u32[]{:S(2)}) collective-permute-start(f32[32,1152]{1,0:T(8,128)S(1)} %slice_select_fusion.96), channel_id=1, source_target_pairs={{0,8},{1,9},{2,10},{3,11},{4,12},{5,13},{6,14},{7,15},{8,0},{9,1},... | collective-permute-start | bytes 442376 | tf_op jit(solution)/shard_map/ppermute | solution.py:22
  66.0 5.5 %collective-permute-done.13 = f32[32,1152]{1,0:T(8,128)S(1)} collective-permute-done((f32[32,1152]{1,0:T(8,128)S(1)}, f32[32,1152]{1,0:T(8,128)S(1)}, u32[]{:S(2)}, u32[]{:S(2)}) %collective-permute-start.13) | collective-permute-done | bytes 147488 | tf_op jit(solution)/shard_map/ppermute | solution.py:22
  71.8 1.9 %convolution_reduce_fusion = f32[512,128]{1,0:T(8,128)S(1)} fusion(f32[512,256,1]{1,0,2:T(8,128)S(1)} %bitcast.86, f32[8,128,256]{2,1,0:T(8,128)S(1)} %bitcast.85), kind=kOutput, calls=%fused_computation | convolution fusion | flops 1611071488 | bytes 1835008 | tf_op jit(solution)/shard_map/dot_general | solution.py:152
  73.8 1.0 %collective-permute-start.15 = (f32[2048]{0:T(1024)S(1)}, f32[2048]{0:T(1024)S(1)}, u32[]{:S(2)}, u32[]{:S(2)}) collective-permute-start(f32[2048]{0:T(1024)S(1)} %reduce_max.19), channel_id=1, source_target_pairs={{0,2},{1,3},{2,0},{3,1},{4,6},{5,7},{6,4},{7,5},{8,10},{9,11},{10,... | collective-permute-start | bytes 24584 | tf_op jit(solution)/shard_map/ppermute | solution.py:27
  74.8 0.9 %collective-permute-start.14 = (f32[2048]{0:T(1024)S(1)}, f32[2048]{0:T(1024)S(1)}, u32[]{:S(2)}, u32[]{:S(2)}) collective-permute-start(f32[2048]{0:T(1024)S(1)} %reduce_max.19), channel_id=1, source_target_pairs={{0,3},{1,2},{2,1},{3,0},{4,7},{5,6},{6,5},{7,4},{8,11},{9,10},{10,... | collective-permute-start | bytes 24584 | tf_op jit(solution)/shard_map/ppermute | solution.py:27
  75.7 1.9 %collective-permute-done.15 = f32[2048]{0:T(1024)S(1)} collective-permute-done((f32[2048]{0:T(1024)S(1)}, f32[2048]{0:T(1024)S(1)}, u32[]{:S(2)}, u32[]{:S(2)}) %collective-permute-start.15) | collective-permute-done | bytes 8224 | tf_op jit(solution)/shard_map/ppermute | solution.py:27
  77.9 3.3 %collective-permute-start.18 = (f32[2048]{0:T(1024)S(1)}, f32[2048]{0:T(1024)S(1)}, u32[]{:S(2)}, u32[]{:S(2)}) collective-permute-start(f32[2048]{0:T(1024)S(1)} %maximum_maximum_fusion.1), channel_id=1, source_target_pairs={{0,8},{1,9},{2,10},{3,11},{4,12},{5,13},{6,14},{7,15},{8,0},{9,1},... | collective-permute-start | bytes 24584 | tf_op jit(solution)/shard_map/ppermute | solution.py:27
  81.2 1.1 %collective-permute-start.17 = (f32[2048]{0:T(1024)S(1)}, f32[2048]{0:T(1024)S(1)}, u32[]{:S(2)}, u32[]{:S(2)}) collective-permute-start(f32[2048]{0:T(1024)S(1)} %maximum_maximum_fusion.1), channel_id=1, source_target_pairs={{0,12},{1,13},{2,14},{3,15},{4,8},{5,9},{6,10},{7,11},{8,4},{9,5},... | collective-permute-start | bytes 24584 | tf_op jit(solution)/shard_map/ppermute | solution.py:27
  82.3 0.5 collective-permute-done.18
  82.8 3.8 %collective-permute-done.17 = f32[2048]{0:T(1024)S(1)} collective-permute-done((f32[2048]{0:T(1024)S(1)}, f32[2048]{0:T(1024)S(1)}, u32[]{:S(2)}, u32[]{:S(2)}) %collective-permute-start.17) | collective-permute-done | bytes 8224 | tf_op jit(solution)/shard_map/ppermute | solution.py:27
  86.7 0.6 maximum_maximum_fusion
  (176 shorter events, 17.5 us)
Async XLA Ops:
  2.6 6.0 %collective-permute-start.2 = (f32[6432]{0:T(1024)S(1)}, f32[6432]{0:T(1024)S(1)}, u32[]{:S(2)}, u32[]{:S(2)}) collective-permute-start(f32[6432]{0:T(1024)S(1)} %pad_maximum_fusion.6), channel_id=1, source_target_pairs={{0,1},{1,0},{2,3},{3,2},{4,5},{5,4},{6,7},{7,6},{8,9},{9,8},{10,11... | collective-permute-start | bytes 77192 | tf_op jit(solution)/shard_map/ppermute | solution.py:27
  3.2 5.5 %collective-permute-start.1 = (f32[6432]{0:T(1024)S(1)}, f32[6432]{0:T(1024)S(1)}, u32[]{:S(2)}, u32[]{:S(2)}) collective-permute-start(f32[6432]{0:T(1024)S(1)} %pad_maximum_fusion.6), channel_id=1, source_target_pairs={{0,2},{1,3},{2,0},{3,1},{4,6},{5,7},{6,4},{7,5},{8,10},{9,11},{10,... | collective-permute-start | bytes 77192 | tf_op jit(solution)/shard_map/ppermute | solution.py:27
  5.7 3.3 %collective-permute-start = (f32[6432]{0:T(1024)S(1)}, f32[6432]{0:T(1024)S(1)}, u32[]{:S(2)}, u32[]{:S(2)}) collective-permute-start(f32[6432]{0:T(1024)S(1)} %pad_maximum_fusion.6), channel_id=1, source_target_pairs={{0,3},{1,2},{2,1},{3,0},{4,7},{5,6},{6,5},{7,4},{8,11},{9,10},{10,... | collective-permute-start | bytes 77192 | tf_op jit(solution)/shard_map/ppermute | solution.py:27
  9.0 4.6 %collective-permute-start.5 = (f32[6432]{0:T(1024)S(1)}, f32[6432]{0:T(1024)S(1)}, u32[]{:S(2)}, u32[]{:S(2)}) collective-permute-start(f32[6432]{0:T(1024)S(1)} %pad_maximum_fusion.5), channel_id=1, source_target_pairs={{0,4},{1,5},{2,6},{3,7},{4,0},{5,1},{6,2},{7,3},{8,12},{9,13},{10,... | collective-permute-start | bytes 77192 | tf_op jit(solution)/shard_map/ppermute | solution.py:27
  10.7 5.2 %collective-permute-start.4 = (f32[6432]{0:T(1024)S(1)}, f32[6432]{0:T(1024)S(1)}, u32[]{:S(2)}, u32[]{:S(2)}) collective-permute-start(f32[6432]{0:T(1024)S(1)} %pad_maximum_fusion.5), channel_id=1, source_target_pairs={{0,8},{1,9},{2,10},{3,11},{4,12},{5,13},{6,14},{7,15},{8,0},{9,1},... | collective-permute-start | bytes 77192 | tf_op jit(solution)/shard_map/ppermute | solution.py:27
  13.3 5.7 %collective-permute-start.3 = (f32[6432]{0:T(1024)S(1)}, f32[6432]{0:T(1024)S(1)}, u32[]{:S(2)}, u32[]{:S(2)}) collective-permute-start(f32[6432]{0:T(1024)S(1)} %pad_maximum_fusion.5), channel_id=1, source_target_pairs={{0,12},{1,13},{2,14},{3,15},{4,8},{5,9},{6,10},{7,11},{8,4},{9,5},... | collective-permute-start | bytes 77192 | tf_op jit(solution)/shard_map/ppermute | solution.py:27
  28.1 2.0 %copy-start = (f32[32,2048]{1,0:T(8,128)S(1)}, f32[32,2048]{1,0:T(8,128)}, u32[]{:S(2)}) copy-start(f32[32,2048]{1,0:T(8,128)} %get-tuple-element.24) | copy-start | bytes 786436
  28.4 1.9 %copy-start.2 = (f32[32,1152]{1,0:T(8,128)S(1)}, f32[32,1152]{1,0:T(8,128)}, u32[]{:S(2)}) copy-start(f32[32,1152]{1,0:T(8,128)} %get-tuple-element.26) | copy-start | bytes 442372
  28.5 1.6 %collective-permute-start.6 = (f32[32,1792]{1,0:T(8,128)S(1)}, f32[32,1792]{1,0:T(8,128)S(1)}, u32[]{:S(2)}, u32[]{:S(2)}) collective-permute-start(f32[32,1792]{1,0:T(8,128)S(1)} %slice_select_fusion.15), channel_id=1, source_target_pairs={{0,1},{1,0},{2,3},{3,2},{4,5},{5,4},{6,7},{7,6},{8,9},{9,8},{10,11... | collective-permute-start | bytes 688136 | tf_op jit(solution)/shard_map/ppermute | solution.py:22
  32.4 3.0 %collective-permute-start.7 = (f32[32,1152]{1,0:T(8,128)S(1)}, f32[32,1152]{1,0:T(8,128)S(1)}, u32[]{:S(2)}, u32[]{:S(2)}) collective-permute-start(f32[32,1152]{1,0:T(8,128)S(1)} %slice_select_fusion.115), channel_id=1, source_target_pairs={{0,1},{1,0},{2,3},{3,2},{4,5},{5,4},{6,7},{7,6},{8,9},{9,8},{10,11... | collective-permute-start | bytes 442376 | tf_op jit(solution)/shard_map/ppermute | solution.py:22
  33.8 7.2 %collective-permute-start.8 = (f32[32,1536]{1,0:T(8,128)S(1)}, f32[32,1536]{1,0:T(8,128)S(1)}, u32[]{:S(2)}, u32[]{:S(2)}) collective-permute-start(f32[32,1536]{1,0:T(8,128)S(1)} %slice_select_fusion.31), channel_id=1, source_target_pairs={{0,2},{1,3},{2,0},{3,1},{4,6},{5,7},{6,4},{7,5},{8,10},{9,11},{10,... | collective-permute-start | bytes 589832 | tf_op jit(solution)/shard_map/ppermute | solution.py:22
  43.4 5.4 %collective-permute-start.9 = (f32[32,1152]{1,0:T(8,128)S(1)}, f32[32,1152]{1,0:T(8,128)S(1)}, u32[]{:S(2)}, u32[]{:S(2)}) collective-permute-start(f32[32,1152]{1,0:T(8,128)S(1)} %slice_select_fusion.113), channel_id=1, source_target_pairs={{0,2},{1,3},{2,0},{3,1},{4,6},{5,7},{6,4},{7,5},{8,10},{9,11},{10,... | collective-permute-start | bytes 442376 | tf_op jit(solution)/shard_map/ppermute | solution.py:22
  46.0 5.4 %collective-permute-start.10 = (f32[32,1280]{1,0:T(8,128)S(1)}, f32[32,1280]{1,0:T(8,128)S(1)}, u32[]{:S(2)}, u32[]{:S(2)}) collective-permute-start(f32[32,1280]{1,0:T(8,128)S(1)} %slice_select_fusion.71), channel_id=1, source_target_pairs={{0,4},{1,5},{2,6},{3,7},{4,0},{5,1},{6,2},{7,3},{8,12},{9,13},{10,... | collective-permute-start | bytes 491528 | tf_op jit(solution)/shard_map/ppermute | solution.py:22
  54.3 7.3 %collective-permute-start.12 = (f32[32,1024]{1,0:T(8,128)S(1)}, f32[32,1024]{1,0:T(8,128)S(1)}, u32[]{:S(2)}, u32[]{:S(2)}) collective-permute-start(f32[32,1024]{1,0:T(8,128)S(1)} %slice_select_fusion.119), channel_id=1, source_target_pairs={{0,8},{1,9},{2,10},{3,11},{4,12},{5,13},{6,14},{7,15},{8,0},{9,1},... | collective-permute-start | bytes 393224 | tf_op jit(solution)/shard_map/ppermute | solution.py:22
  55.2 6.7 %collective-permute-start.11 = (f32[32,1152]{1,0:T(8,128)S(1)}, f32[32,1152]{1,0:T(8,128)S(1)}, u32[]{:S(2)}, u32[]{:S(2)}) collective-permute-start(f32[32,1152]{1,0:T(8,128)S(1)} %slice_select_fusion.111), channel_id=1, source_target_pairs={{0,4},{1,5},{2,6},{3,7},{4,0},{5,1},{6,2},{7,3},{8,12},{9,13},{10,... | collective-permute-start | bytes 442376 | tf_op jit(solution)/shard_map/ppermute | solution.py:22
  64.4 7.1 %collective-permute-start.13 = (f32[32,1152]{1,0:T(8,128)S(1)}, f32[32,1152]{1,0:T(8,128)S(1)}, u32[]{:S(2)}, u32[]{:S(2)}) collective-permute-start(f32[32,1152]{1,0:T(8,128)S(1)} %slice_select_fusion.96), channel_id=1, source_target_pairs={{0,8},{1,9},{2,10},{3,11},{4,12},{5,13},{6,14},{7,15},{8,0},{9,1},... | collective-permute-start | bytes 442376 | tf_op jit(solution)/shard_map/ppermute | solution.py:22
  73.7 13.6 %copy-start.1 = (f32[32,2048]{1,0:T(8,128)}, f32[32,2048]{1,0:T(8,128)S(1)}, u32[]{:S(2)}) copy-start(f32[32,2048]{1,0:T(8,128)S(1)} %reshape.693) | copy-start | bytes 786436
  73.7 1.9 %collective-permute-start.16 = (f32[2048]{0:T(1024)S(1)}, f32[2048]{0:T(1024)S(1)}, u32[]{:S(2)}, u32[]{:S(2)}) collective-permute-start(f32[2048]{0:T(1024)S(1)} %reduce_max.19), channel_id=1, source_target_pairs={{0,1},{1,0},{2,3},{3,2},{4,5},{5,4},{6,7},{7,6},{8,9},{9,8},{10,11... | collective-permute-start | bytes 24584 | tf_op jit(solution)/shard_map/ppermute | solution.py:27
  73.8 3.7 %collective-permute-start.15 = (f32[2048]{0:T(1024)S(1)}, f32[2048]{0:T(1024)S(1)}, u32[]{:S(2)}, u32[]{:S(2)}) collective-permute-start(f32[2048]{0:T(1024)S(1)} %reduce_max.19), channel_id=1, source_target_pairs={{0,2},{1,3},{2,0},{3,1},{4,6},{5,7},{6,4},{7,5},{8,10},{9,11},{10,... | collective-permute-start | bytes 24584 | tf_op jit(solution)/shard_map/ppermute | solution.py:27
  74.8 3.1 %collective-permute-start.14 = (f32[2048]{0:T(1024)S(1)}, f32[2048]{0:T(1024)S(1)}, u32[]{:S(2)}, u32[]{:S(2)}) collective-permute-start(f32[2048]{0:T(1024)S(1)} %reduce_max.19), channel_id=1, source_target_pairs={{0,3},{1,2},{2,1},{3,0},{4,7},{5,6},{6,5},{7,4},{8,11},{9,10},{10,... | collective-permute-start | bytes 24584 | tf_op jit(solution)/shard_map/ppermute | solution.py:27
  77.9 4.5 %collective-permute-start.19 = (f32[2048]{0:T(1024)S(1)}, f32[2048]{0:T(1024)S(1)}, u32[]{:S(2)}, u32[]{:S(2)}) collective-permute-start(f32[2048]{0:T(1024)S(1)} %maximum_maximum_fusion.1), channel_id=1, source_target_pairs={{0,4},{1,5},{2,6},{3,7},{4,0},{5,1},{6,2},{7,3},{8,12},{9,13},{10,... | collective-permute-start | bytes 24584 | tf_op jit(solution)/shard_map/ppermute | solution.py:27
  77.9 4.9 %collective-permute-start.18 = (f32[2048]{0:T(1024)S(1)}, f32[2048]{0:T(1024)S(1)}, u32[]{:S(2)}, u32[]{:S(2)}) collective-permute-start(f32[2048]{0:T(1024)S(1)} %maximum_maximum_fusion.1), channel_id=1, source_target_pairs={{0,8},{1,9},{2,10},{3,11},{4,12},{5,13},{6,14},{7,15},{8,0},{9,1},... | collective-permute-start | bytes 24584 | tf_op jit(solution)/shard_map/ppermute | solution.py:27
  81.2 5.4 %collective-permute-start.17 = (f32[2048]{0:T(1024)S(1)}, f32[2048]{0:T(1024)S(1)}, u32[]{:S(2)}, u32[]{:S(2)}) collective-permute-start(f32[2048]{0:T(1024)S(1)} %maximum_maximum_fusion.1), channel_id=1, source_target_pairs={{0,12},{1,13},{2,14},{3,15},{4,8},{5,9},{6,10},{7,11},{8,4},{9,5},... | collective-permute-start | bytes 24584 | tf_op jit(solution)/shard_map/ppermute | solution.py:27

commit v9 on v6

--- a/solution.py
+++ b/solution.py
@@ -146,7 +146,7 @@
     result = jnp.dot(
         paired,
         joined,
-        precision=lax.Precision.HIGHEST,
+        precision=lax.Precision.HIGH,
         preferred_element_type=jnp.float32,
     )
     best_value = jnp.max(result.reshape(total_rows * blocks_time, TEMPLATES, TAPS), axis=1)
@@ -164,7 +164,7 @@
         needed = -(-needed // 128) * 128
         return min(TIN, needed)
 
-    partial_value = jnp.sum(filterbank, axis=0)
+    partial_value = jnp.sum(filterbank[:, : length_after(0)], axis=0)
     channel_total = butterfly(partial_value, "band", jnp.add)
     widths_seq = [length_after(section) for section in range(local_count + 1)]
     head, tail = local_tree(filterbank, channel_total, offsets, widths_seq, channels_all, TAIL_WIDTH)

time: 80.8 us -> 79.8 us (0.988)
  matrix products: 1.87 us -> 1.03 us
    dot_general x1, matrix products: 1.87 us -> 1.03 us  [boxcar_max(): jnp.dot(paired, joined, precision=lax.Precision.HIGH, preferred_element_t...]
where the time goes in v9:
time: 79.8 us; the launch traced here: 79.6 us
  waiting for transfers between devices  42.3 us (53%)
  starting transfers between devices  16.7 us (21%)
  other arithmetic  10.5 us (13%)
  Pallas kernels  6.8 us (9%)
  between operations  1.33 us (2%)
  matrix products  1.03 us (1%)
  local copies, waits for them, and re-layouts  0.94 us (1%)
    ppermute x8, waiting for transfers between devices, from_partner(): return lax.ppermute(value, axis, pairs)  27.6 us
    ppermute x12, waiting for transfers between devices, from_xor(): return lax.ppermute(value, axis, pairs)  14.7 us
    ppermute x12, starting transfers between devices, from_xor(): return lax.ppermute(value, axis, pairs)  14 us
    pallas_call x1, Pallas kernels, local_tree(): pl.pallas_call(functools.partial(local_tree_kernel, tuple(widths_seq), fl...  6.8 us
    select_n x56, other arithmetic, shift_rows(): jnp.where(chosen, current[:, span:span + keep_len], current[:, :keep_len])  6.19 us
    ppermute x8, starting transfers between devices, from_partner(): return lax.ppermute(value, axis, pairs)  2.71 us
  transfers between devices with their start and end apart: 20, of which 16 were waited for; matrix products, arithmetic and copies ran while one was open for 4% of the time, Pallas kernels for 0%

profile of v9, /device:TPU:0, one launch (start us, length us, event | category | flops | bytes accessed | tf_op | source)
XLA Modules:
  0.0 79.6 jit_solution(12588560910887127720)
XLA Ops:
  0.6 1.1 %slice_reduce_fusion = f32[4480]{0:T(1024)S(1)} fusion(f32[32,6144]{1,0:T(8,128)} %x_ref.1), kind=kLoop, calls=%fused_computation.4 | loop fusion | flops 138880 | bytes 591360 | tf_op jit(solution)/shard_map/reduce_sum | solution.py:167
  1.8 0.5 collective-permute-start.2
  2.3 2.6 %collective-permute-start.1 = (f32[4480]{0:T(1024)S(1)}, f32[4480]{0:T(1024)S(1)}, u32[]{:S(2)}, u32[]{:S(2)}) collective-permute-start(f32[4480]{0:T(1024)S(1)} %slice_reduce_fusion), channel_id=1, source_target_pairs={{0,2},{1,3},{2,0},{3,1},{4,6},{5,7},{6,4},{7,5},{8,10},{9,11},{10,... | collective-permute-start | bytes 53768 | tf_op jit(solution)/shard_map/ppermute | solution.py:27
  4.9 1.7 %collective-permute-done.1 = f32[4480]{0:T(1024)S(1)} collective-permute-done((f32[4480]{0:T(1024)S(1)}, f32[4480]{0:T(1024)S(1)}, u32[]{:S(2)}, u32[]{:S(2)}) %collective-permute-start.1) | collective-permute-done | bytes 17952 | tf_op jit(solution)/shard_map/ppermute | solution.py:27
  6.6 1.4 %collective-permute-done = f32[4480]{0:T(1024)S(1)} collective-permute-done((f32[4480]{0:T(1024)S(1)}, f32[4480]{0:T(1024)S(1)}, u32[]{:S(2)}, u32[]{:S(2)}) %collective-permute-start) | collective-permute-done | bytes 17952 | tf_op jit(solution)/shard_map/ppermute | solution.py:27
  8.1 1.6 %collective-permute-start.5 = (f32[4480]{0:T(1024)S(1)}, f32[4480]{0:T(1024)S(1)}, u32[]{:S(2)}, u32[]{:S(2)}) collective-permute-start(f32[4480]{0:T(1024)S(1)} %add_add_fusion.1), channel_id=1, source_target_pairs={{0,4},{1,5},{2,6},{3,7},{4,0},{5,1},{6,2},{7,3},{8,12},{9,13},{10,... | collective-permute-start | bytes 53768 | tf_op jit(solution)/shard_map/ppermute | solution.py:27
  9.7 2.6 %collective-permute-start.4 = (f32[4480]{0:T(1024)S(1)}, f32[4480]{0:T(1024)S(1)}, u32[]{:S(2)}, u32[]{:S(2)}) collective-permute-start(f32[4480]{0:T(1024)S(1)} %add_add_fusion.1), channel_id=1, source_target_pairs={{0,8},{1,9},{2,10},{3,11},{4,12},{5,13},{6,14},{7,15},{8,0},{9,1},... | collective-permute-start | bytes 53768 | tf_op jit(solution)/shard_map/ppermute | solution.py:27
  12.5 2.1 %collective-permute-done.4 = f32[4480]{0:T(1024)S(1)} collective-permute-done((f32[4480]{0:T(1024)S(1)}, f32[4480]{0:T(1024)S(1)}, u32[]{:S(2)}, u32[]{:S(2)}) %collective-permute-start.4) | collective-permute-done | bytes 17952 | tf_op jit(solution)/shard_map/ppermute | solution.py:27
  14.6 3.3 %collective-permute-done.3 = f32[4480]{0:T(1024)S(1)} collective-permute-done((f32[4480]{0:T(1024)S(1)}, f32[4480]{0:T(1024)S(1)}, u32[]{:S(2)}, u32[]{:S(2)}) %collective-permute-start.3) | collective-permute-done | bytes 17952 | tf_op jit(solution)/shard_map/ppermute | solution.py:27
  17.9 0.6 broadcast_in_dim.527.total_ref
  18.5 6.8 %shard_map.50 = (f32[32,2048]{1,0:T(8,128)}, f32[32,1152]{1,0:T(8,128)}) custom-call(f32[32,6144]{1,0:T(8,128)} %x_ref.1, f32[1,4480]{1,0:T(1,128)} %broadcast_in_dim.527.total_ref, s32[9,32]{1,0:T(8,128)} %offsets_ref.1), custom_call_target="tpu_custom_call" | custom-call | flops 25395200 | bytes 983040 | tf_op jit(solution)/shard_map/pallas_call | solution.py:97
  25.4 1.7 %collective-permute-done.6 = f32[32,2048]{1,0:T(8,128)S(1)} collective-permute-done((f32[32,2048]{1,0:T(8,128)}, f32[32,2048]{1,0:T(8,128)S(1)}, u32[]{:S(2)}, u32[]{:S(2)}) %collective-permute-start.6) | collective-permute-done | bytes 262176 | tf_op jit(solution)/shard_map/ppermute | solution.py:22
  27.1 1.0 %broadcast_select_fusion.1 = (f32[32,2048]{1,0:T(8,128)S(1)}, f32[32,2048]{1,0:T(8,128)S(1)}) fusion(f32[32,2048]{1,0:T(8,128)S(1)} %collective-permute-done.6, f32[32,2048]{1,0:T(8,128)} %get-tuple-element.19, pred[]{:T(512)S(6)} %eq.508), kind=kLoop, calls=%fused_computation.101 | loop fusion | flops 131072 | bytes 1048577 | tf_op jit(solution)/shard_map/jit(_where)/select_n | solution.py:177
  29.1 0.8 %collective-permute-start.8 = (f32[32,1792]{1,0:T(8,128)S(1)}, f32[32,1792]{1,0:T(8,128)S(1)}, u32[]{:S(2)}, u32[]{:S(2)}) collective-permute-start(f32[32,1792]{1,0:T(8,128)S(1)} %fusion.2), channel_id=1, source_target_pairs={{0,2},{1,3},{2,0},{3,1},{4,6},{5,7},{6,4},{7,5},{8,10},{9,11},{10,... | collective-permute-start | bytes 688136 | tf_op jit(solution)/shard_map/ppermute | solution.py:22
  30.1 1.3 %collective-permute-done.7 = f32[32,1152]{1,0:T(8,128)S(1)} collective-permute-done((f32[32,1152]{1,0:T(8,128)S(1)}, f32[32,1152]{1,0:T(8,128)S(1)}, u32[]{:S(2)}, u32[]{:S(2)}) %collective-permute-start.7) | collective-permute-done | bytes 147488 | tf_op jit(solution)/shard_map/ppermute | solution.py:22
  31.4 5.4 %collective-permute-done.8 = f32[32,1792]{1,0:T(8,128)S(1)} collective-permute-done((f32[32,1792]{1,0:T(8,128)S(1)}, f32[32,1792]{1,0:T(8,128)S(1)}, u32[]{:S(2)}, u32[]{:S(2)}) %collective-permute-start.8) | collective-permute-done | bytes 229408 | tf_op jit(solution)/shard_map/ppermute | solution.py:22
  37.8 0.8 %collective-permute-start.9 = (f32[32,1152]{1,0:T(8,128)S(1)}, f32[32,1152]{1,0:T(8,128)S(1)}, u32[]{:S(2)}, u32[]{:S(2)}) collective-permute-start(f32[32,1152]{1,0:T(8,128)S(1)} %fusion.16), channel_id=1, source_target_pairs={{0,2},{1,3},{2,0},{3,1},{4,6},{5,7},{6,4},{7,5},{8,10},{9,11},{10,... | collective-permute-start | bytes 442376 | tf_op jit(solution)/shard_map/ppermute | solution.py:22
  39.8 3.2 %collective-permute-done.9 = f32[32,1152]{1,0:T(8,128)S(1)} collective-permute-done((f32[32,1152]{1,0:T(8,128)S(1)}, f32[32,1152]{1,0:T(8,128)S(1)}, u32[]{:S(2)}, u32[]{:S(2)}) %collective-permute-start.9) | collective-permute-done | bytes 147488 | tf_op jit(solution)/shard_map/ppermute | solution.py:22
  43.0 2.5 %collective-permute-done.10 = f32[32,1536]{1,0:T(8,128)S(1)} collective-permute-done((f32[32,1536]{1,0:T(8,128)S(1)}, f32[32,1536]{1,0:T(8,128)S(1)}, u32[]{:S(2)}, u32[]{:S(2)}) %collective-permute-start.10) | collective-permute-done | bytes 196640 | tf_op jit(solution)/shard_map/ppermute | solution.py:22
  47.8 0.6 collective-permute-start.12
  48.8 3.2 %collective-permute-done.11 = f32[32,1152]{1,0:T(8,128)S(1)} collective-permute-done((f32[32,1152]{1,0:T(8,128)S(1)}, f32[32,1152]{1,0:T(8,128)S(1)}, u32[]{:S(2)}, u32[]{:S(2)}) %collective-permute-start.11) | collective-permute-done | bytes 147488 | tf_op jit(solution)/shard_map/ppermute | solution.py:22
  52.0 4.4 %collective-permute-done.12 = f32[32,1280]{1,0:T(8,128)S(1)} collective-permute-done((f32[32,1280]{1,0:T(8,128)S(1)}, f32[32,1280]{1,0:T(8,128)S(1)}, u32[]{:S(2)}, u32[]{:S(2)}) %collective-permute-start.12) | collective-permute-done | bytes 163872 | tf_op jit(solution)/shard_map/ppermute | solution.py:22
  58.4 5.7 %collective-permute-done.13 = f32[32,1152]{1,0:T(8,128)S(1)} collective-permute-done((f32[32,1152]{1,0:T(8,128)S(1)}, f32[32,1152]{1,0:T(8,128)S(1)}, u32[]{:S(2)}, u32[]{:S(2)}) %collective-permute-start.13) | collective-permute-done | bytes 147488 | tf_op jit(solution)/shard_map/ppermute | solution.py:22
  65.2 1.0 %convolution_reduce_fusion = f32[512,128]{1,0:T(8,128)S(1)} fusion(f32[512,256,1]{1,0,2:T(8,128)S(1)} %bitcast.85, f32[8,128,256]{2,1,0:T(8,128)S(1)} %bitcast.84), kind=kOutput, calls=%fused_computation | convolution fusion | flops 805765120 | bytes 1835008 | tf_op jit(solution)/shard_map/dot_general | solution.py:146
  66.4 1.3 %collective-permute-start.15 = (f32[2048]{0:T(1024)S(1)}, f32[2048]{0:T(1024)S(1)}, u32[]{:S(2)}, u32[]{:S(2)}) collective-permute-start(f32[2048]{0:T(1024)S(1)} %reduce_max.19), channel_id=1, source_target_pairs={{0,2},{1,3},{2,0},{3,1},{4,6},{5,7},{6,4},{7,5},{8,10},{9,11},{10,... | collective-permute-start | bytes 24584 | tf_op jit(solution)/shard_map/ppermute | solution.py:27
  67.8 0.5 collective-permute-start.14
  68.3 1.9 %collective-permute-done.15 = f32[2048]{0:T(1024)S(1)} collective-permute-done((f32[2048]{0:T(1024)S(1)}, f32[2048]{0:T(1024)S(1)}, u32[]{:S(2)}, u32[]{:S(2)}) %collective-permute-start.15) | collective-permute-done | bytes 8224 | tf_op jit(solution)/shard_map/ppermute | solution.py:27
  70.1 0.7 collective-permute-done.14
  70.9 2.6 %collective-permute-start.18 = (f32[2048]{0:T(1024)S(1)}, f32[2048]{0:T(1024)S(1)}, u32[]{:S(2)}, u32[]{:S(2)}) collective-permute-start(f32[2048]{0:T(1024)S(1)} %maximum_maximum_fusion.1), channel_id=1, source_target_pairs={{0,8},{1,9},{2,10},{3,11},{4,12},{5,13},{6,14},{7,15},{8,0},{9,1},... | collective-permute-start | bytes 24584 | tf_op jit(solution)/shard_map/ppermute | solution.py:27
  73.5 1.8 %collective-permute-start.17 = (f32[2048]{0:T(1024)S(1)}, f32[2048]{0:T(1024)S(1)}, u32[]{:S(2)}, u32[]{:S(2)}) collective-permute-start(f32[2048]{0:T(1024)S(1)} %maximum_maximum_fusion.1), channel_id=1, source_target_pairs={{0,12},{1,13},{2,14},{3,15},{4,8},{5,9},{6,10},{7,11},{8,4},{9,5},... | collective-permute-start | bytes 24584 | tf_op jit(solution)/shard_map/ppermute | solution.py:27
  75.6 3.4 %collective-permute-done.17 = f32[2048]{0:T(1024)S(1)} collective-permute-done((f32[2048]{0:T(1024)S(1)}, f32[2048]{0:T(1024)S(1)}, u32[]{:S(2)}, u32[]{:S(2)}) %collective-permute-start.17) | collective-permute-done | bytes 8224 | tf_op jit(solution)/shard_map/ppermute | solution.py:27
  79.0 0.6 maximum_maximum_fusion
  (118 shorter events, 9.4 us)
Async XLA Ops:
  0.6 24.7 %copy-start.2 = (s32[9,32]{1,0:T(8,128)S(1)}, s32[9,32]{1,0:T(8,128)}, u32[]{:S(2)}) copy-start(s32[9,32]{1,0:T(8,128)} %offsets_ref.1) | copy-start | bytes 3460
  1.8 3.2 %collective-permute-start.2 = (f32[4480]{0:T(1024)S(1)}, f32[4480]{0:T(1024)S(1)}, u32[]{:S(2)}, u32[]{:S(2)}) collective-permute-start(f32[4480]{0:T(1024)S(1)} %slice_reduce_fusion), channel_id=1, source_target_pairs={{0,1},{1,0},{2,3},{3,2},{4,5},{5,4},{6,7},{7,6},{8,9},{9,8},{10,11... | collective-permute-start | bytes 53768 | tf_op jit(solution)/shard_map/ppermute | solution.py:27
  2.3 4.3 %collective-permute-start.1 = (f32[4480]{0:T(1024)S(1)}, f32[4480]{0:T(1024)S(1)}, u32[]{:S(2)}, u32[]{:S(2)}) collective-permute-start(f32[4480]{0:T(1024)S(1)} %slice_reduce_fusion), channel_id=1, source_target_pairs={{0,2},{1,3},{2,0},{3,1},{4,6},{5,7},{6,4},{7,5},{8,10},{9,11},{10,... | collective-permute-start | bytes 53768 | tf_op jit(solution)/shard_map/ppermute | solution.py:27
  4.8 3.2 %collective-permute-start = (f32[4480]{0:T(1024)S(1)}, f32[4480]{0:T(1024)S(1)}, u32[]{:S(2)}, u32[]{:S(2)}) collective-permute-start(f32[4480]{0:T(1024)S(1)} %slice_reduce_fusion), channel_id=1, source_target_pairs={{0,3},{1,2},{2,1},{3,0},{4,7},{5,6},{6,5},{7,4},{8,11},{9,10},{10,... | collective-permute-start | bytes 53768 | tf_op jit(solution)/shard_map/ppermute | solution.py:27
  8.1 4.5 %collective-permute-start.5 = (f32[4480]{0:T(1024)S(1)}, f32[4480]{0:T(1024)S(1)}, u32[]{:S(2)}, u32[]{:S(2)}) collective-permute-start(f32[4480]{0:T(1024)S(1)} %add_add_fusion.1), channel_id=1, source_target_pairs={{0,4},{1,5},{2,6},{3,7},{4,0},{5,1},{6,2},{7,3},{8,12},{9,13},{10,... | collective-permute-start | bytes 53768 | tf_op jit(solution)/shard_map/ppermute | solution.py:27
  9.7 4.9 %collective-permute-start.4 = (f32[4480]{0:T(1024)S(1)}, f32[4480]{0:T(1024)S(1)}, u32[]{:S(2)}, u32[]{:S(2)}) collective-permute-start(f32[4480]{0:T(1024)S(1)} %add_add_fusion.1), channel_id=1, source_target_pairs={{0,8},{1,9},{2,10},{3,11},{4,12},{5,13},{6,14},{7,15},{8,0},{9,1},... | collective-permute-start | bytes 53768 | tf_op jit(solution)/shard_map/ppermute | solution.py:27
  12.3 5.6 %collective-permute-start.3 = (f32[4480]{0:T(1024)S(1)}, f32[4480]{0:T(1024)S(1)}, u32[]{:S(2)}, u32[]{:S(2)}) collective-permute-start(f32[4480]{0:T(1024)S(1)} %add_add_fusion.1), channel_id=1, source_target_pairs={{0,12},{1,13},{2,14},{3,15},{4,8},{5,9},{6,10},{7,11},{8,4},{9,5},... | collective-permute-start | bytes 53768 | tf_op jit(solution)/shard_map/ppermute | solution.py:27
  25.3 1.7 %collective-permute-start.6 = (f32[32,2048]{1,0:T(8,128)}, f32[32,2048]{1,0:T(8,128)S(1)}, u32[]{:S(2)}, u32[]{:S(2)}) collective-permute-start(f32[32,2048]{1,0:T(8,128)} %get-tuple-element.19), channel_id=1, source_target_pairs={{0,1},{1,0},{2,3},{3,2},{4,5},{5,4},{6,7},{7,6},{8,9},{9,8},{10,11... | collective-permute-start | bytes 786440 | tf_op jit(solution)/shard_map/ppermute | solution.py:22
  28.7 1.3 %copy-start.3 = (s32[8]{0:T(128)S(1)}, s32[8]{0:T(128)}, u32[]{:S(2)}) copy-start(s32[8]{0:T(128)} %param.5) | copy-start | bytes 100
  28.9 1.2 %copy-start.1 = (f32[32,1152]{1,0:T(8,128)S(1)}, f32[32,1152]{1,0:T(8,128)}, u32[]{:S(2)}) copy-start(f32[32,1152]{1,0:T(8,128)} %get-tuple-element.21) | copy-start | bytes 442372
  29.1 7.7 %collective-permute-start.8 = (f32[32,1792]{1,0:T(8,128)S(1)}, f32[32,1792]{1,0:T(8,128)S(1)}, u32[]{:S(2)}, u32[]{:S(2)}) collective-permute-start(f32[32,1792]{1,0:T(8,128)S(1)} %fusion.2), channel_id=1, source_target_pairs={{0,2},{1,3},{2,0},{3,1},{4,6},{5,7},{6,4},{7,5},{8,10},{9,11},{10,... | collective-permute-start | bytes 688136 | tf_op jit(solution)/shard_map/ppermute | solution.py:22
  30.0 1.4 %collective-permute-start.7 = (f32[32,1152]{1,0:T(8,128)S(1)}, f32[32,1152]{1,0:T(8,128)S(1)}, u32[]{:S(2)}, u32[]{:S(2)}) collective-permute-start(f32[32,1152]{1,0:T(8,128)S(1)} %copy-done.1), channel_id=1, source_target_pairs={{0,1},{1,0},{2,3},{3,2},{4,5},{5,4},{6,7},{7,6},{8,9},{9,8},{10,11... | collective-permute-start | bytes 442376 | tf_op jit(solution)/shard_map/ppermute | solution.py:22
  37.8 5.2 %collective-permute-start.9 = (f32[32,1152]{1,0:T(8,128)S(1)}, f32[32,1152]{1,0:T(8,128)S(1)}, u32[]{:S(2)}, u32[]{:S(2)}) collective-permute-start(f32[32,1152]{1,0:T(8,128)S(1)} %fusion.16), channel_id=1, source_target_pairs={{0,2},{1,3},{2,0},{3,1},{4,6},{5,7},{6,4},{7,5},{8,10},{9,11},{10,... | collective-permute-start | bytes 442376 | tf_op jit(solution)/shard_map/ppermute | solution.py:22
  39.6 5.9 %collective-permute-start.10 = (f32[32,1536]{1,0:T(8,128)S(1)}, f32[32,1536]{1,0:T(8,128)S(1)}, u32[]{:S(2)}, u32[]{:S(2)}) collective-permute-start(f32[32,1536]{1,0:T(8,128)S(1)} %fusion.3), channel_id=1, source_target_pairs={{0,4},{1,5},{2,6},{3,7},{4,0},{5,1},{6,2},{7,3},{8,12},{9,13},{10,... | collective-permute-start | bytes 589832 | tf_op jit(solution)/shard_map/ppermute | solution.py:22
  46.5 5.6 %collective-permute-start.11 = (f32[32,1152]{1,0:T(8,128)S(1)}, f32[32,1152]{1,0:T(8,128)S(1)}, u32[]{:S(2)}, u32[]{:S(2)}) collective-permute-start(f32[32,1152]{1,0:T(8,128)S(1)} %fusion.15), channel_id=1, source_target_pairs={{0,4},{1,5},{2,6},{3,7},{4,0},{5,1},{6,2},{7,3},{8,12},{9,13},{10,... | collective-permute-start | bytes 442376 | tf_op jit(solution)/shard_map/ppermute | solution.py:22
  47.8 8.7 %collective-permute-start.12 = (f32[32,1280]{1,0:T(8,128)S(1)}, f32[32,1280]{1,0:T(8,128)S(1)}, u32[]{:S(2)}, u32[]{:S(2)}) collective-permute-start(f32[32,1280]{1,0:T(8,128)S(1)} %fusion.12), channel_id=1, source_target_pairs={{0,8},{1,9},{2,10},{3,11},{4,12},{5,13},{6,14},{7,15},{8,0},{9,1},... | collective-permute-start | bytes 491528 | tf_op jit(solution)/shard_map/ppermute | solution.py:22
  57.5 6.6 %collective-permute-start.13 = (f32[32,1152]{1,0:T(8,128)S(1)}, f32[32,1152]{1,0:T(8,128)S(1)}, u32[]{:S(2)}, u32[]{:S(2)}) collective-permute-start(f32[32,1152]{1,0:T(8,128)S(1)} %fusion.14), channel_id=1, source_target_pairs={{0,8},{1,9},{2,10},{3,11},{4,12},{5,13},{6,14},{7,15},{8,0},{9,1},... | collective-permute-start | bytes 442376 | tf_op jit(solution)/shard_map/ppermute | solution.py:22
  66.3 13.3 %copy-start = (f32[32,2048]{1,0:T(8,128)}, f32[32,2048]{1,0:T(8,128)S(1)}, u32[]{:S(2)}) copy-start(f32[32,2048]{1,0:T(8,128)S(1)} %reshape.485) | copy-start | bytes 786436
  66.4 1.9 %collective-permute-start.16 = (f32[2048]{0:T(1024)S(1)}, f32[2048]{0:T(1024)S(1)}, u32[]{:S(2)}, u32[]{:S(2)}) collective-permute-start(f32[2048]{0:T(1024)S(1)} %reduce_max.19), channel_id=1, source_target_pairs={{0,1},{1,0},{2,3},{3,2},{4,5},{5,4},{6,7},{7,6},{8,9},{9,8},{10,11... | collective-permute-start | bytes 24584 | tf_op jit(solution)/shard_map/ppermute | solution.py:27
  66.4 3.7 %collective-permute-start.15 = (f32[2048]{0:T(1024)S(1)}, f32[2048]{0:T(1024)S(1)}, u32[]{:S(2)}, u32[]{:S(2)}) collective-permute-start(f32[2048]{0:T(1024)S(1)} %reduce_max.19), channel_id=1, source_target_pairs={{0,2},{1,3},{2,0},{3,1},{4,6},{5,7},{6,4},{7,5},{8,10},{9,11},{10,... | collective-permute-start | bytes 24584 | tf_op jit(solution)/shard_map/ppermute | solution.py:27
  67.8 3.1 %collective-permute-start.14 = (f32[2048]{0:T(1024)S(1)}, f32[2048]{0:T(1024)S(1)}, u32[]{:S(2)}, u32[]{:S(2)}) collective-permute-start(f32[2048]{0:T(1024)S(1)} %reduce_max.19), channel_id=1, source_target_pairs={{0,3},{1,2},{2,1},{3,0},{4,7},{5,6},{6,5},{7,4},{8,11},{9,10},{10,... | collective-permute-start | bytes 24584 | tf_op jit(solution)/shard_map/ppermute | solution.py:27
  70.9 4.5 %collective-permute-start.19 = (f32[2048]{0:T(1024)S(1)}, f32[2048]{0:T(1024)S(1)}, u32[]{:S(2)}, u32[]{:S(2)}) collective-permute-start(f32[2048]{0:T(1024)S(1)} %maximum_maximum_fusion.1), channel_id=1, source_target_pairs={{0,4},{1,5},{2,6},{3,7},{4,0},{5,1},{6,2},{7,3},{8,12},{9,13},{10,... | collective-permute-start | bytes 24584 | tf_op jit(solution)/shard_map/ppermute | solution.py:27
  70.9 4.7 %collective-permute-start.18 = (f32[2048]{0:T(1024)S(1)}, f32[2048]{0:T(1024)S(1)}, u32[]{:S(2)}, u32[]{:S(2)}) collective-permute-start(f32[2048]{0:T(1024)S(1)} %maximum_maximum_fusion.1), channel_id=1, source_target_pairs={{0,8},{1,9},{2,10},{3,11},{4,12},{5,13},{6,14},{7,15},{8,0},{9,1},... | collective-permute-start | bytes 24584 | tf_op jit(solution)/shard_map/ppermute | solution.py:27
  73.5 5.4 %collective-permute-start.17 = (f32[2048]{0:T(1024)S(1)}, f32[2048]{0:T(1024)S(1)}, u32[]{:S(2)}, u32[]{:S(2)}) collective-permute-start(f32[2048]{0:T(1024)S(1)} %maximum_maximum_fusion.1), channel_id=1, source_target_pairs={{0,12},{1,13},{2,14},{3,15},{4,8},{5,9},{6,10},{7,11},{8,4},{9,5},... | collective-permute-start | bytes 24584 | tf_op jit(solution)/shard_map/ppermute | solution.py:27

commit v10 on v9

--- a/solution.py
+++ b/solution.py
@@ -13,7 +13,7 @@
 SHIFT = 256
 TAPS = 128
 TEMPLATES = 8
-TAIL_WIDTH = 1152
+TAIL_WIDTH = 1280
 
 
 def from_partner(value, axis, distance):

time: 79.8 us -> 80 us (level)
  waiting for transfers between devices: 42.3 us -> 40 us
  other arithmetic: 10.5 us -> 12.1 us
  starting transfers between devices: 16.7 us -> 17.6 us
    eq x2, other arithmetic: 0.04 us -> 1.64 us  [shift_rows(): chosen = (amounts >> bit_index & 1)[:, None] == 1]
    ppermute x12, waiting for transfers between devices: 14.7 us -> 13.5 us  [from_xor(): return lax.ppermute(value, axis, pairs)]
    ppermute x8, waiting for transfers between devices: 27.6 us -> 26.5 us  [from_partner(): return lax.ppermute(value, axis, pairs)]
    ppermute x8, starting transfers between devices: 2.71 us -> 3.58 us  [from_partner(): return lax.ppermute(value, axis, pairs)]
  transfers between devices with their start and end apart: 20 -> 20, of which waited for: 16 -> 15; matrix products, arithmetic and copies ran while one was open for 4% -> 7% of each run, Pallas kernels for 0% -> 0%
where the time goes in v10:
time: 80 us; the launch traced here: 79.7 us
  waiting for transfers between devices  40 us (50%)
  starting transfers between devices  17.6 us (22%)
  other arithmetic  12.1 us (15%)
  Pallas kernels  6.79 us (8%)
  between operations  1.34 us (2%)
  matrix products  1.03 us (1%)
  local copies, waits for them, and re-layouts  0.93 us (1%)
    ppermute x8, waiting for transfers between devices, from_partner(): return lax.ppermute(value, axis, pairs)  26.5 us
    ppermute x12, starting transfers between devices, from_xor(): return lax.ppermute(value, axis, pairs)  14 us
    ppermute x12, waiting for transfers between devices, from_xor(): return lax.ppermute(value, axis, pairs)  13.5 us
    pallas_call x1, Pallas kernels, local_tree(): pl.pallas_call(functools.partial(local_tree_kernel, tuple(widths_seq), fl...  6.79 us
    select_n x56, other arithmetic, shift_rows(): jnp.where(chosen, current[:, span:span + keep_len], current[:, :keep_len])  6.18 us
    ppermute x8, starting transfers between devices, from_partner(): return lax.ppermute(value, axis, pairs)  3.58 us
    eq x2, other arithmetic, shift_rows(): chosen = (amounts >> bit_index & 1)[:, None] == 1  1.64 us
  transfers between devices with their start and end apart: 20, of which 15 were waited for; matrix products, arithmetic and copies ran while one was open for 7% of the time, Pallas kernels for 0%

profile of v10, /device:TPU:0, one launch (start us, length us, event | category | flops | bytes accessed | tf_op | source)
XLA Modules:
  0.0 79.7 jit_solution(11379741276605728104)
XLA Ops:
  0.6 1.1 %slice_reduce_fusion = f32[4480]{0:T(1024)S(1)} fusion(f32[32,6144]{1,0:T(8,128)} %x_ref.1), kind=kLoop, calls=%fused_computation.4 | loop fusion | flops 138880 | bytes 591360 | tf_op jit(solution)/shard_map/reduce_sum | solution.py:167
  2.3 2.6 %collective-permute-start.1 = (f32[4480]{0:T(1024)S(1)}, f32[4480]{0:T(1024)S(1)}, u32[]{:S(2)}, u32[]{:S(2)}) collective-permute-start(f32[4480]{0:T(1024)S(1)} %slice_reduce_fusion), channel_id=1, source_target_pairs={{0,2},{1,3},{2,0},{3,1},{4,6},{5,7},{6,4},{7,5},{8,10},{9,11},{10,... | collective-permute-start | bytes 53768 | tf_op jit(solution)/shard_map/ppermute | solution.py:27
  4.9 1.7 %collective-permute-done.1 = f32[4480]{0:T(1024)S(1)} collective-permute-done((f32[4480]{0:T(1024)S(1)}, f32[4480]{0:T(1024)S(1)}, u32[]{:S(2)}, u32[]{:S(2)}) %collective-permute-start.1) | collective-permute-done | bytes 17952 | tf_op jit(solution)/shard_map/ppermute | solution.py:27
  6.6 1.4 %collective-permute-done = f32[4480]{0:T(1024)S(1)} collective-permute-done((f32[4480]{0:T(1024)S(1)}, f32[4480]{0:T(1024)S(1)}, u32[]{:S(2)}, u32[]{:S(2)}) %collective-permute-start) | collective-permute-done | bytes 17952 | tf_op jit(solution)/shard_map/ppermute | solution.py:27
  8.1 1.6 %collective-permute-start.5 = (f32[4480]{0:T(1024)S(1)}, f32[4480]{0:T(1024)S(1)}, u32[]{:S(2)}, u32[]{:S(2)}) collective-permute-start(f32[4480]{0:T(1024)S(1)} %add_add_fusion.1), channel_id=1, source_target_pairs={{0,4},{1,5},{2,6},{3,7},{4,0},{5,1},{6,2},{7,3},{8,12},{9,13},{10,... | collective-permute-start | bytes 53768 | tf_op jit(solution)/shard_map/ppermute | solution.py:27
  9.7 2.6 %collective-permute-start.4 = (f32[4480]{0:T(1024)S(1)}, f32[4480]{0:T(1024)S(1)}, u32[]{:S(2)}, u32[]{:S(2)}) collective-permute-start(f32[4480]{0:T(1024)S(1)} %add_add_fusion.1), channel_id=1, source_target_pairs={{0,8},{1,9},{2,10},{3,11},{4,12},{5,13},{6,14},{7,15},{8,0},{9,1},... | collective-permute-start | bytes 53768 | tf_op jit(solution)/shard_map/ppermute | solution.py:27
  12.5 0.8 %compare_bitcast_fusion.6 = (pred[32]{0:T(512)(128)(4,1)S(1)}, pred[32]{0:T(512)(128)(4,1)S(1)}, pred[32]{0:T(512)(128)(4,1)S(1)}, pred[32]{0:T(512)(128)(4,1)S(...) fusion(s32[9,32]{1,0:T(8,128)} %offsets_ref.1), kind=kLoop, calls=%fused_computation.129 | loop fusion | flops 1248 | bytes 928 | tf_op jit(solution)/shard_map/eq | solution.py:58
  13.4 1.2 %collective-permute-done.4 = f32[4480]{0:T(1024)S(1)} collective-permute-done((f32[4480]{0:T(1024)S(1)}, f32[4480]{0:T(1024)S(1)}, u32[]{:S(2)}, u32[]{:S(2)}) %collective-permute-start.4) | collective-permute-done | bytes 17952 | tf_op jit(solution)/shard_map/ppermute | solution.py:27
  14.6 3.3 %collective-permute-done.3 = f32[4480]{0:T(1024)S(1)} collective-permute-done((f32[4480]{0:T(1024)S(1)}, f32[4480]{0:T(1024)S(1)}, u32[]{:S(2)}, u32[]{:S(2)}) %collective-permute-start.3) | collective-permute-done | bytes 17952 | tf_op jit(solution)/shard_map/ppermute | solution.py:27
  17.9 0.6 broadcast_in_dim.527.total_ref
  18.5 6.8 %shard_map.50 = (f32[32,1920]{1,0:T(8,128)}, f32[32,1280]{1,0:T(8,128)}) custom-call(f32[32,6144]{1,0:T(8,128)} %x_ref.1, f32[1,4480]{1,0:T(1,128)} %broadcast_in_dim.527.total_ref, s32[9,32]{1,0:T(8,128)} %offsets_ref.1), custom_call_target="tpu_custom_call" | custom-call | flops 25395200 | bytes 983040 | tf_op jit(solution)/shard_map/pallas_call | solution.py:97
  25.4 0.8 %compare_bitcast_fusion.7 = (pred[32]{0:T(512)(128)(4,1)S(1)}, pred[32]{0:T(512)(128)(4,1)S(1)}, pred[32]{0:T(512)(128)(4,1)S(1)}, pred[32]{0:T(512)(128)(4,1)S(...) fusion(s32[9,32]{1,0:T(8,128)} %offsets_ref.1), kind=kLoop, calls=%fused_computation.130 | loop fusion | flops 1824 | bytes 1120 | tf_op jit(solution)/shard_map/eq | solution.py:58
  26.2 0.8 %collective-permute-done.6 = f32[32,1920]{1,0:T(8,128)S(1)} collective-permute-done((f32[32,1920]{1,0:T(8,128)}, f32[32,1920]{1,0:T(8,128)S(1)}, u32[]{:S(2)}, u32[]{:S(2)}) %collective-permute-start.6) | collective-permute-done | bytes 245792 | tf_op jit(solution)/shard_map/ppermute | solution.py:22
  27.2 1.0 %broadcast_select_fusion.1 = (f32[32,1920]{1,0:T(8,128)S(1)}, f32[32,1920]{1,0:T(8,128)S(1)}) fusion(f32[32,1920]{1,0:T(8,128)S(1)} %collective-permute-done.6, f32[32,1920]{1,0:T(8,128)} %get-tuple-element.19, pred[]{:T(512)S(6)} %eq.508), kind=kLoop, calls=%fused_computation.99 | loop fusion | flops 122880 | bytes 983041 | tf_op jit(solution)/shard_map/jit(_where)/select_n | solution.py:177
  29.2 0.8 %collective-permute-start.8 = (f32[32,1664]{1,0:T(8,128)S(1)}, f32[32,1664]{1,0:T(8,128)S(1)}, u32[]{:S(2)}, u32[]{:S(2)}) collective-permute-start(f32[32,1664]{1,0:T(8,128)S(1)} %fusion.2), channel_id=1, source_target_pairs={{0,2},{1,3},{2,0},{3,1},{4,6},{5,7},{6,4},{7,5},{8,10},{9,11},{10,... | collective-permute-start | bytes 638984 | tf_op jit(solution)/shard_map/ppermute | solution.py:22
  30.1 6.7 %collective-permute-done.8 = f32[32,1664]{1,0:T(8,128)S(1)} collective-permute-done((f32[32,1664]{1,0:T(8,128)S(1)}, f32[32,1664]{1,0:T(8,128)S(1)}, u32[]{:S(2)}, u32[]{:S(2)}) %collective-permute-start.8) | collective-permute-done | bytes 213024 | tf_op jit(solution)/shard_map/ppermute | solution.py:22
  37.8 0.8 %collective-permute-start.9 = (f32[32,1280]{1,0:T(8,128)S(1)}, f32[32,1280]{1,0:T(8,128)S(1)}, u32[]{:S(2)}, u32[]{:S(2)}) collective-permute-start(f32[32,1280]{1,0:T(8,128)S(1)} %fusion.15), channel_id=1, source_target_pairs={{0,2},{1,3},{2,0},{3,1},{4,6},{5,7},{6,4},{7,5},{8,10},{9,11},{10,... | collective-permute-start | bytes 491528 | tf_op jit(solution)/shard_map/ppermute | solution.py:22
  39.7 3.7 %collective-permute-done.9 = f32[32,1280]{1,0:T(8,128)S(1)} collective-permute-done((f32[32,1280]{1,0:T(8,128)S(1)}, f32[32,1280]{1,0:T(8,128)S(1)}, u32[]{:S(2)}, u32[]{:S(2)}) %collective-permute-start.9) | collective-permute-done | bytes 163872 | tf_op jit(solution)/shard_map/ppermute | solution.py:22
  43.5 1.9 %collective-permute-done.10 = f32[32,1408]{1,0:T(8,128)S(1)} collective-permute-done((f32[32,1408]{1,0:T(8,128)S(1)}, f32[32,1408]{1,0:T(8,128)S(1)}, u32[]{:S(2)}, u32[]{:S(2)}) %collective-permute-start.10) | collective-permute-done | bytes 180256 | tf_op jit(solution)/shard_map/ppermute | solution.py:22
  47.4 0.8 collective-permute-start.11
  48.6 7.0 %collective-permute-done.12 = f32[32,1152]{1,0:T(8,128)S(1)} collective-permute-done((f32[32,1152]{1,0:T(8,128)S(1)}, f32[32,1152]{1,0:T(8,128)S(1)}, u32[]{:S(2)}, u32[]{:S(2)}) %collective-permute-start.12) | collective-permute-done | bytes 147488 | tf_op jit(solution)/shard_map/ppermute | solution.py:22
  56.8 0.9 %collective-permute-start.13 = (f32[32,1280]{1,0:T(8,128)S(1)}, f32[32,1280]{1,0:T(8,128)S(1)}, u32[]{:S(2)}, u32[]{:S(2)}) collective-permute-start(f32[32,1280]{1,0:T(8,128)S(1)} %fusion.13), channel_id=1, source_target_pairs={{0,8},{1,9},{2,10},{3,11},{4,12},{5,13},{6,14},{7,15},{8,0},{9,1},... | collective-permute-start | bytes 491528 | tf_op jit(solution)/shard_map/ppermute | solution.py:22
  58.4 6.1 %collective-permute-done.13 = f32[32,1280]{1,0:T(8,128)S(1)} collective-permute-done((f32[32,1280]{1,0:T(8,128)S(1)}, f32[32,1280]{1,0:T(8,128)S(1)}, u32[]{:S(2)}, u32[]{:S(2)}) %collective-permute-start.13) | collective-permute-done | bytes 163872 | tf_op jit(solution)/shard_map/ppermute | solution.py:22
  65.7 1.0 %convolution_reduce_fusion = f32[512,128]{1,0:T(8,128)S(1)} fusion(f32[512,256,1]{1,0,2:T(8,128)S(1)} %bitcast.85, f32[8,128,256]{2,1,0:T(8,128)S(1)} %bitcast.84), kind=kOutput, calls=%fused_computation | convolution fusion | flops 805765120 | bytes 1835008 | tf_op jit(solution)/shard_map/dot_general | solution.py:146
  66.9 1.3 %collective-permute-start.15 = (f32[2048]{0:T(1024)S(1)}, f32[2048]{0:T(1024)S(1)}, u32[]{:S(2)}, u32[]{:S(2)}) collective-permute-start(f32[2048]{0:T(1024)S(1)} %reduce_max.19), channel_id=1, source_target_pairs={{0,2},{1,3},{2,0},{3,1},{4,6},{5,7},{6,4},{7,5},{8,10},{9,11},{10,... | collective-permute-start | bytes 24584 | tf_op jit(solution)/shard_map/ppermute | solution.py:27
  68.2 0.5 collective-permute-start.14
  68.8 1.9 %collective-permute-done.15 = f32[2048]{0:T(1024)S(1)} collective-permute-done((f32[2048]{0:T(1024)S(1)}, f32[2048]{0:T(1024)S(1)}, u32[]{:S(2)}, u32[]{:S(2)}) %collective-permute-start.15) | collective-permute-done | bytes 8224 | tf_op jit(solution)/shard_map/ppermute | solution.py:27
  70.6 0.7 collective-permute-done.14
  71.4 2.2 %collective-permute-start.18 = (f32[2048]{0:T(1024)S(1)}, f32[2048]{0:T(1024)S(1)}, u32[]{:S(2)}, u32[]{:S(2)}) collective-permute-start(f32[2048]{0:T(1024)S(1)} %maximum_maximum_fusion.1), channel_id=1, source_target_pairs={{0,8},{1,9},{2,10},{3,11},{4,12},{5,13},{6,14},{7,15},{8,0},{9,1},... | collective-permute-start | bytes 24584 | tf_op jit(solution)/shard_map/ppermute | solution.py:27
  73.7 2.1 %collective-permute-start.17 = (f32[2048]{0:T(1024)S(1)}, f32[2048]{0:T(1024)S(1)}, u32[]{:S(2)}, u32[]{:S(2)}) collective-permute-start(f32[2048]{0:T(1024)S(1)} %maximum_maximum_fusion.1), channel_id=1, source_target_pairs={{0,12},{1,13},{2,14},{3,15},{4,8},{5,9},{6,10},{7,11},{8,4},{9,5},... | collective-permute-start | bytes 24584 | tf_op jit(solution)/shard_map/ppermute | solution.py:27
  76.0 3.1 %collective-permute-done.17 = f32[2048]{0:T(1024)S(1)} collective-permute-done((f32[2048]{0:T(1024)S(1)}, f32[2048]{0:T(1024)S(1)}, u32[]{:S(2)}, u32[]{:S(2)}) %collective-permute-start.17) | collective-permute-done | bytes 8224 | tf_op jit(solution)/shard_map/ppermute | solution.py:27
  79.1 0.6 maximum_maximum_fusion
  (116 shorter events, 9.6 us)
Async XLA Ops:
  0.6 24.7 %copy-start.2 = (s32[8]{0:T(128)S(1)}, s32[8]{0:T(128)}, u32[]{:S(2)}) copy-start(s32[8]{0:T(128)} %param.5) | copy-start | bytes 100
  1.8 3.2 %collective-permute-start.2 = (f32[4480]{0:T(1024)S(1)}, f32[4480]{0:T(1024)S(1)}, u32[]{:S(2)}, u32[]{:S(2)}) collective-permute-start(f32[4480]{0:T(1024)S(1)} %slice_reduce_fusion), channel_id=1, source_target_pairs={{0,1},{1,0},{2,3},{3,2},{4,5},{5,4},{6,7},{7,6},{8,9},{9,8},{10,11... | collective-permute-start | bytes 53768 | tf_op jit(solution)/shard_map/ppermute | solution.py:27
  2.3 4.3 %collective-permute-start.1 = (f32[4480]{0:T(1024)S(1)}, f32[4480]{0:T(1024)S(1)}, u32[]{:S(2)}, u32[]{:S(2)}) collective-permute-start(f32[4480]{0:T(1024)S(1)} %slice_reduce_fusion), channel_id=1, source_target_pairs={{0,2},{1,3},{2,0},{3,1},{4,6},{5,7},{6,4},{7,5},{8,10},{9,11},{10,... | collective-permute-start | bytes 53768 | tf_op jit(solution)/shard_map/ppermute | solution.py:27
  4.8 3.2 %collective-permute-start = (f32[4480]{0:T(1024)S(1)}, f32[4480]{0:T(1024)S(1)}, u32[]{:S(2)}, u32[]{:S(2)}) collective-permute-start(f32[4480]{0:T(1024)S(1)} %slice_reduce_fusion), channel_id=1, source_target_pairs={{0,3},{1,2},{2,1},{3,0},{4,7},{5,6},{6,5},{7,4},{8,11},{9,10},{10,... | collective-permute-start | bytes 53768 | tf_op jit(solution)/shard_map/ppermute | solution.py:27
  8.1 5.3 %collective-permute-start.5 = (f32[4480]{0:T(1024)S(1)}, f32[4480]{0:T(1024)S(1)}, u32[]{:S(2)}, u32[]{:S(2)}) collective-permute-start(f32[4480]{0:T(1024)S(1)} %add_add_fusion.1), channel_id=1, source_target_pairs={{0,4},{1,5},{2,6},{3,7},{4,0},{5,1},{6,2},{7,3},{8,12},{9,13},{10,... | collective-permute-start | bytes 53768 | tf_op jit(solution)/shard_map/ppermute | solution.py:27
  9.7 4.9 %collective-permute-start.4 = (f32[4480]{0:T(1024)S(1)}, f32[4480]{0:T(1024)S(1)}, u32[]{:S(2)}, u32[]{:S(2)}) collective-permute-start(f32[4480]{0:T(1024)S(1)} %add_add_fusion.1), channel_id=1, source_target_pairs={{0,8},{1,9},{2,10},{3,11},{4,12},{5,13},{6,14},{7,15},{8,0},{9,1},... | collective-permute-start | bytes 53768 | tf_op jit(solution)/shard_map/ppermute | solution.py:27
  12.3 5.6 %collective-permute-start.3 = (f32[4480]{0:T(1024)S(1)}, f32[4480]{0:T(1024)S(1)}, u32[]{:S(2)}, u32[]{:S(2)}) collective-permute-start(f32[4480]{0:T(1024)S(1)} %add_add_fusion.1), channel_id=1, source_target_pairs={{0,12},{1,13},{2,14},{3,15},{4,8},{5,9},{6,10},{7,11},{8,4},{9,5},... | collective-permute-start | bytes 53768 | tf_op jit(solution)/shard_map/ppermute | solution.py:27
  25.3 1.7 %collective-permute-start.6 = (f32[32,1920]{1,0:T(8,128)}, f32[32,1920]{1,0:T(8,128)S(1)}, u32[]{:S(2)}, u32[]{:S(2)}) collective-permute-start(f32[32,1920]{1,0:T(8,128)} %get-tuple-element.19), channel_id=1, source_target_pairs={{0,1},{1,0},{2,3},{3,2},{4,5},{5,4},{6,7},{7,6},{8,9},{9,8},{10,11... | collective-permute-start | bytes 737288 | tf_op jit(solution)/shard_map/ppermute | solution.py:22
  27.0 3.0 %collective-permute-start.7 = (f32[32,1280]{1,0:T(8,128)}, f32[32,1280]{1,0:T(8,128)S(1)}, u32[]{:S(2)}, u32[]{:S(2)}) collective-permute-start(f32[32,1280]{1,0:T(8,128)} %get-tuple-element.21), channel_id=1, source_target_pairs={{0,1},{1,0},{2,3},{3,2},{4,5},{5,4},{6,7},{7,6},{8,9},{9,8},{10,11... | collective-permute-start | bytes 491528 | tf_op jit(solution)/shard_map/ppermute | solution.py:22
  28.8 8.0 %copy-start.1 = (f32[32,1280]{1,0:T(8,128)S(1)}, f32[32,1280]{1,0:T(8,128)}, u32[]{:S(2)}) copy-start(f32[32,1280]{1,0:T(8,128)} %get-tuple-element.21) | copy-start | bytes 491524
  29.2 7.6 %collective-permute-start.8 = (f32[32,1664]{1,0:T(8,128)S(1)}, f32[32,1664]{1,0:T(8,128)S(1)}, u32[]{:S(2)}, u32[]{:S(2)}) collective-permute-start(f32[32,1664]{1,0:T(8,128)S(1)} %fusion.2), channel_id=1, source_target_pairs={{0,2},{1,3},{2,0},{3,1},{4,6},{5,7},{6,4},{7,5},{8,10},{9,11},{10,... | collective-permute-start | bytes 638984 | tf_op jit(solution)/shard_map/ppermute | solution.py:22
  37.8 5.7 %collective-permute-start.9 = (f32[32,1280]{1,0:T(8,128)S(1)}, f32[32,1280]{1,0:T(8,128)S(1)}, u32[]{:S(2)}, u32[]{:S(2)}) collective-permute-start(f32[32,1280]{1,0:T(8,128)S(1)} %fusion.15), channel_id=1, source_target_pairs={{0,2},{1,3},{2,0},{3,1},{4,6},{5,7},{6,4},{7,5},{8,10},{9,11},{10,... | collective-permute-start | bytes 491528 | tf_op jit(solution)/shard_map/ppermute | solution.py:22
  39.6 5.8 %collective-permute-start.10 = (f32[32,1408]{1,0:T(8,128)S(1)}, f32[32,1408]{1,0:T(8,128)S(1)}, u32[]{:S(2)}, u32[]{:S(2)}) collective-permute-start(f32[32,1408]{1,0:T(8,128)S(1)} %fusion.11), channel_id=1, source_target_pairs={{0,4},{1,5},{2,6},{3,7},{4,0},{5,1},{6,2},{7,3},{8,12},{9,13},{10,... | collective-permute-start | bytes 540680 | tf_op jit(solution)/shard_map/ppermute | solution.py:22
  47.3 8.3 %collective-permute-start.12 = (f32[32,1152]{1,0:T(8,128)S(1)}, f32[32,1152]{1,0:T(8,128)S(1)}, u32[]{:S(2)}, u32[]{:S(2)}) collective-permute-start(f32[32,1152]{1,0:T(8,128)S(1)} %fusion.16), channel_id=1, source_target_pairs={{0,8},{1,9},{2,10},{3,11},{4,12},{5,13},{6,14},{7,15},{8,0},{9,1},... | collective-permute-start | bytes 442376 | tf_op jit(solution)/shard_map/ppermute | solution.py:22
  47.4 8.3 %collective-permute-start.11 = (f32[32,1280]{1,0:T(8,128)S(1)}, f32[32,1280]{1,0:T(8,128)S(1)}, u32[]{:S(2)}, u32[]{:S(2)}) collective-permute-start(f32[32,1280]{1,0:T(8,128)S(1)} %fusion.14), channel_id=1, source_target_pairs={{0,4},{1,5},{2,6},{3,7},{4,0},{5,1},{6,2},{7,3},{8,12},{9,13},{10,... | collective-permute-start | bytes 491528 | tf_op jit(solution)/shard_map/ppermute | solution.py:22
  56.8 7.8 %collective-permute-start.13 = (f32[32,1280]{1,0:T(8,128)S(1)}, f32[32,1280]{1,0:T(8,128)S(1)}, u32[]{:S(2)}, u32[]{:S(2)}) collective-permute-start(f32[32,1280]{1,0:T(8,128)S(1)} %fusion.13), channel_id=1, source_target_pairs={{0,8},{1,9},{2,10},{3,11},{4,12},{5,13},{6,14},{7,15},{8,0},{9,1},... | collective-permute-start | bytes 491528 | tf_op jit(solution)/shard_map/ppermute | solution.py:22
  66.8 12.9 %copy-start = (f32[32,2048]{1,0:T(8,128)}, f32[32,2048]{1,0:T(8,128)S(1)}, u32[]{:S(2)}) copy-start(f32[32,2048]{1,0:T(8,128)S(1)} %reshape.485) | copy-start | bytes 786436
  66.8 1.9 %collective-permute-start.16 = (f32[2048]{0:T(1024)S(1)}, f32[2048]{0:T(1024)S(1)}, u32[]{:S(2)}, u32[]{:S(2)}) collective-permute-start(f32[2048]{0:T(1024)S(1)} %reduce_max.19), channel_id=1, source_target_pairs={{0,1},{1,0},{2,3},{3,2},{4,5},{5,4},{6,7},{7,6},{8,9},{9,8},{10,11... | collective-permute-start | bytes 24584 | tf_op jit(solution)/shard_map/ppermute | solution.py:27
  66.9 3.7 %collective-permute-start.15 = (f32[2048]{0:T(1024)S(1)}, f32[2048]{0:T(1024)S(1)}, u32[]{:S(2)}, u32[]{:S(2)}) collective-permute-start(f32[2048]{0:T(1024)S(1)} %reduce_max.19), channel_id=1, source_target_pairs={{0,2},{1,3},{2,0},{3,1},{4,6},{5,7},{6,4},{7,5},{8,10},{9,11},{10,... | collective-permute-start | bytes 24584 | tf_op jit(solution)/shard_map/ppermute | solution.py:27
  68.2 3.1 %collective-permute-start.14 = (f32[2048]{0:T(1024)S(1)}, f32[2048]{0:T(1024)S(1)}, u32[]{:S(2)}, u32[]{:S(2)}) collective-permute-start(f32[2048]{0:T(1024)S(1)} %reduce_max.19), channel_id=1, source_target_pairs={{0,3},{1,2},{2,1},{3,0},{4,7},{5,6},{6,5},{7,4},{8,11},{9,10},{10,... | collective-permute-start | bytes 24584 | tf_op jit(solution)/shard_map/ppermute | solution.py:27
  71.3 4.5 %collective-permute-start.19 = (f32[2048]{0:T(1024)S(1)}, f32[2048]{0:T(1024)S(1)}, u32[]{:S(2)}, u32[]{:S(2)}) collective-permute-start(f32[2048]{0:T(1024)S(1)} %maximum_maximum_fusion.1), channel_id=1, source_target_pairs={{0,4},{1,5},{2,6},{3,7},{4,0},{5,1},{6,2},{7,3},{8,12},{9,13},{10,... | collective-permute-start | bytes 24584 | tf_op jit(solution)/shard_map/ppermute | solution.py:27
  71.4 4.6 %collective-permute-start.18 = (f32[2048]{0:T(1024)S(1)}, f32[2048]{0:T(1024)S(1)}, u32[]{:S(2)}, u32[]{:S(2)}) collective-permute-start(f32[2048]{0:T(1024)S(1)} %maximum_maximum_fusion.1), channel_id=1, source_target_pairs={{0,8},{1,9},{2,10},{3,11},{4,12},{5,13},{6,14},{7,15},{8,0},{9,1},... | collective-permute-start | bytes 24584 | tf_op jit(solution)/shard_map/ppermute | solution.py:27
  73.7 5.4 %collective-permute-start.17 = (f32[2048]{0:T(1024)S(1)}, f32[2048]{0:T(1024)S(1)}, u32[]{:S(2)}, u32[]{:S(2)}) collective-permute-start(f32[2048]{0:T(1024)S(1)} %maximum_maximum_fusion.1), channel_id=1, source_target_pairs={{0,12},{1,13},{2,14},{3,15},{4,8},{5,9},{6,10},{7,11},{8,4},{9,5},... | collective-permute-start | bytes 24584 | tf_op jit(solution)/shard_map/ppermute | solution.py:27

commit v11 on v10

--- a/solution.py
+++ b/solution.py
@@ -13,7 +13,7 @@
 SHIFT = 256
 TAPS = 128
 TEMPLATES = 8
-TAIL_WIDTH = 1280
+TAIL_WIDTH = 1024
 
 
 def from_partner(value, axis, distance):

time: 80 us -> 81.8 us (1.022)
  waiting for transfers between devices: 40 us -> 44.3 us
  other arithmetic: 12.1 us -> 10.6 us
  starting transfers between devices: 17.6 us -> 16.7 us
    ppermute x8, waiting for transfers between devices: 26.5 us -> 29.1 us  [from_partner(): return lax.ppermute(value, axis, pairs)]
    ppermute x12, waiting for transfers between devices: 13.5 us -> 15.2 us  [from_xor(): return lax.ppermute(value, axis, pairs)]
    eq x2, other arithmetic: 1.64 us -> 0.04 us  [shift_rows(): chosen = (amounts >> bit_index & 1)[:, None] == 1]
    ppermute x8, starting transfers between devices: 3.58 us -> 2.71 us  [from_partner(): return lax.ppermute(value, axis, pairs)]
  transfers between devices with their start and end apart: 20 -> 20, of which waited for: 15 -> 16; matrix products, arithmetic and copies ran while one was open for 7% -> 4% of each run, Pallas kernels for 0% -> 0%
where the time goes in v11:
time: 81.8 us; the launch traced here: 81.6 us
  waiting for transfers between devices  44.3 us (54%)
  starting transfers between devices  16.7 us (20%)
  other arithmetic  10.6 us (13%)
  Pallas kernels  6.8 us (8%)
  between operations  1.32 us (2%)
  matrix products  1.03 us (1%)
  local copies, waits for them, and re-layouts  0.94 us (1%)
    ppermute x8, waiting for transfers between devices, from_partner(): return lax.ppermute(value, axis, pairs)  29.1 us
    ppermute x12, waiting for transfers between devices, from_xor(): return lax.ppermute(value, axis, pairs)  15.2 us
    ppermute x12, starting transfers between devices, from_xor(): return lax.ppermute(value, axis, pairs)  14 us
    pallas_call x1, Pallas kernels, local_tree(): pl.pallas_call(functools.partial(local_tree_kernel, tuple(widths_seq), fl...  6.8 us
    select_n x56, other arithmetic, shift_rows(): jnp.where(chosen, current[:, span:span + keep_len], current[:, :keep_len])  6.19 us
    ppermute x8, starting transfers between devices, from_partner(): return lax.ppermute(value, axis, pairs)  2.71 us
  transfers between devices with their start and end apart: 20, of which 16 were waited for; matrix products, arithmetic and copies ran while one was open for 4% of the time, Pallas kernels for 0%

profile of v11, /device:TPU:0, one launch (start us, length us, event | category | flops | bytes accessed | tf_op | source)
XLA Modules:
  0.0 81.6 jit_solution(1154951071938209511)
XLA Ops:
  0.6 1.1 %slice_reduce_fusion = f32[4480]{0:T(1024)S(1)} fusion(f32[32,6144]{1,0:T(8,128)} %x_ref.1), kind=kLoop, calls=%fused_computation.4 | loop fusion | flops 138880 | bytes 591360 | tf_op jit(solution)/shard_map/reduce_sum | solution.py:167
  1.8 0.5 collective-permute-start.2
  2.3 2.6 %collective-permute-start.1 = (f32[4480]{0:T(1024)S(1)}, f32[4480]{0:T(1024)S(1)}, u32[]{:S(2)}, u32[]{:S(2)}) collective-permute-start(f32[4480]{0:T(1024)S(1)} %slice_reduce_fusion), channel_id=1, source_target_pairs={{0,2},{1,3},{2,0},{3,1},{4,6},{5,7},{6,4},{7,5},{8,10},{9,11},{10,... | collective-permute-start | bytes 53768 | tf_op jit(solution)/shard_map/ppermute | solution.py:27
  4.9 1.7 %collective-permute-done.1 = f32[4480]{0:T(1024)S(1)} collective-permute-done((f32[4480]{0:T(1024)S(1)}, f32[4480]{0:T(1024)S(1)}, u32[]{:S(2)}, u32[]{:S(2)}) %collective-permute-start.1) | collective-permute-done | bytes 17952 | tf_op jit(solution)/shard_map/ppermute | solution.py:27
  6.6 1.4 %collective-permute-done = f32[4480]{0:T(1024)S(1)} collective-permute-done((f32[4480]{0:T(1024)S(1)}, f32[4480]{0:T(1024)S(1)}, u32[]{:S(2)}, u32[]{:S(2)}) %collective-permute-start) | collective-permute-done | bytes 17952 | tf_op jit(solution)/shard_map/ppermute | solution.py:27
  8.1 1.6 %collective-permute-start.5 = (f32[4480]{0:T(1024)S(1)}, f32[4480]{0:T(1024)S(1)}, u32[]{:S(2)}, u32[]{:S(2)}) collective-permute-start(f32[4480]{0:T(1024)S(1)} %add_add_fusion.1), channel_id=1, source_target_pairs={{0,4},{1,5},{2,6},{3,7},{4,0},{5,1},{6,2},{7,3},{8,12},{9,13},{10,... | collective-permute-start | bytes 53768 | tf_op jit(solution)/shard_map/ppermute | solution.py:27
  9.7 2.6 %collective-permute-start.4 = (f32[4480]{0:T(1024)S(1)}, f32[4480]{0:T(1024)S(1)}, u32[]{:S(2)}, u32[]{:S(2)}) collective-permute-start(f32[4480]{0:T(1024)S(1)} %add_add_fusion.1), channel_id=1, source_target_pairs={{0,8},{1,9},{2,10},{3,11},{4,12},{5,13},{6,14},{7,15},{8,0},{9,1},... | collective-permute-start | bytes 53768 | tf_op jit(solution)/shard_map/ppermute | solution.py:27
  12.5 2.1 %collective-permute-done.4 = f32[4480]{0:T(1024)S(1)} collective-permute-done((f32[4480]{0:T(1024)S(1)}, f32[4480]{0:T(1024)S(1)}, u32[]{:S(2)}, u32[]{:S(2)}) %collective-permute-start.4) | collective-permute-done | bytes 17952 | tf_op jit(solution)/shard_map/ppermute | solution.py:27
  14.6 3.3 %collective-permute-done.3 = f32[4480]{0:T(1024)S(1)} collective-permute-done((f32[4480]{0:T(1024)S(1)}, f32[4480]{0:T(1024)S(1)}, u32[]{:S(2)}, u32[]{:S(2)}) %collective-permute-start.3) | collective-permute-done | bytes 17952 | tf_op jit(solution)/shard_map/ppermute | solution.py:27
  17.9 0.6 broadcast_in_dim.527.total_ref
  18.5 6.8 %shard_map.50 = (f32[32,2176]{1,0:T(8,128)}, f32[32,1024]{1,0:T(8,128)}) custom-call(f32[32,6144]{1,0:T(8,128)} %x_ref.1, f32[1,4480]{1,0:T(1,128)} %broadcast_in_dim.527.total_ref, s32[9,32]{1,0:T(8,128)} %offsets_ref.1), custom_call_target="tpu_custom_call" | custom-call | flops 25395200 | bytes 983040 | tf_op jit(solution)/shard_map/pallas_call | solution.py:97
  25.4 1.7 %collective-permute-done.6 = f32[32,2176]{1,0:T(8,128)S(1)} collective-permute-done((f32[32,2176]{1,0:T(8,128)}, f32[32,2176]{1,0:T(8,128)S(1)}, u32[]{:S(2)}, u32[]{:S(2)}) %collective-permute-start.6) | collective-permute-done | bytes 278560 | tf_op jit(solution)/shard_map/ppermute | solution.py:22
  27.1 1.0 %broadcast_select_fusion.1 = (f32[32,2176]{1,0:T(8,128)S(1)}, f32[32,2176]{1,0:T(8,128)S(1)}) fusion(f32[32,2176]{1,0:T(8,128)S(1)} %collective-permute-done.6, f32[32,2176]{1,0:T(8,128)} %get-tuple-element.19, pred[]{:T(512)S(6)} %eq.508), kind=kLoop, calls=%fused_computation.88 | loop fusion | flops 139264 | bytes 1114113 | tf_op jit(solution)/shard_map/jit(_where)/select_n | solution.py:177
  29.2 0.8 %collective-permute-start.8 = (f32[32,1920]{1,0:T(8,128)S(1)}, f32[32,1920]{1,0:T(8,128)S(1)}, u32[]{:S(2)}, u32[]{:S(2)}) collective-permute-start(f32[32,1920]{1,0:T(8,128)S(1)} %fusion.2), channel_id=1, source_target_pairs={{0,2},{1,3},{2,0},{3,1},{4,6},{5,7},{6,4},{7,5},{8,10},{9,11},{10,... | collective-permute-start | bytes 737288 | tf_op jit(solution)/shard_map/ppermute | solution.py:22
  30.1 1.3 %collective-permute-done.7 = f32[32,1024]{1,0:T(8,128)S(1)} collective-permute-done((f32[32,1024]{1,0:T(8,128)S(1)}, f32[32,1024]{1,0:T(8,128)S(1)}, u32[]{:S(2)}, u32[]{:S(2)}) %collective-permute-start.7) | collective-permute-done | bytes 131104 | tf_op jit(solution)/shard_map/ppermute | solution.py:22
  31.4 5.8 %collective-permute-done.8 = f32[32,1920]{1,0:T(8,128)S(1)} collective-permute-done((f32[32,1920]{1,0:T(8,128)S(1)}, f32[32,1920]{1,0:T(8,128)S(1)}, u32[]{:S(2)}, u32[]{:S(2)}) %collective-permute-start.8) | collective-permute-done | bytes 245792 | tf_op jit(solution)/shard_map/ppermute | solution.py:22
  38.2 0.8 %collective-permute-start.9 = (f32[32,1024]{1,0:T(8,128)S(1)}, f32[32,1024]{1,0:T(8,128)S(1)}, u32[]{:S(2)}, u32[]{:S(2)}) collective-permute-start(f32[32,1024]{1,0:T(8,128)S(1)} %fusion.17), channel_id=1, source_target_pairs={{0,2},{1,3},{2,0},{3,1},{4,6},{5,7},{6,4},{7,5},{8,10},{9,11},{10,... | collective-permute-start | bytes 393224 | tf_op jit(solution)/shard_map/ppermute | solution.py:22
  40.2 3.0 %collective-permute-done.9 = f32[32,1024]{1,0:T(8,128)S(1)} collective-permute-done((f32[32,1024]{1,0:T(8,128)S(1)}, f32[32,1024]{1,0:T(8,128)S(1)}, u32[]{:S(2)}, u32[]{:S(2)}) %collective-permute-start.9) | collective-permute-done | bytes 131104 | tf_op jit(solution)/shard_map/ppermute | solution.py:22
  43.2 3.1 %collective-permute-done.10 = f32[32,1664]{1,0:T(8,128)S(1)} collective-permute-done((f32[32,1664]{1,0:T(8,128)S(1)}, f32[32,1664]{1,0:T(8,128)S(1)}, u32[]{:S(2)}, u32[]{:S(2)}) %collective-permute-start.10) | collective-permute-done | bytes 213024 | tf_op jit(solution)/shard_map/ppermute | solution.py:22
  48.5 0.6 collective-permute-start.12
  49.5 3.1 %collective-permute-done.11 = f32[32,1024]{1,0:T(8,128)S(1)} collective-permute-done((f32[32,1024]{1,0:T(8,128)S(1)}, f32[32,1024]{1,0:T(8,128)S(1)}, u32[]{:S(2)}, u32[]{:S(2)}) %collective-permute-start.11) | collective-permute-done | bytes 131104 | tf_op jit(solution)/shard_map/ppermute | solution.py:22
  52.6 5.3 %collective-permute-done.12 = f32[32,1408]{1,0:T(8,128)S(1)} collective-permute-done((f32[32,1408]{1,0:T(8,128)S(1)}, f32[32,1408]{1,0:T(8,128)S(1)}, u32[]{:S(2)}, u32[]{:S(2)}) %collective-permute-start.12) | collective-permute-done | bytes 180256 | tf_op jit(solution)/shard_map/ppermute | solution.py:22
  59.9 5.8 %collective-permute-done.13 = f32[32,1024]{1,0:T(8,128)S(1)} collective-permute-done((f32[32,1024]{1,0:T(8,128)S(1)}, f32[32,1024]{1,0:T(8,128)S(1)}, u32[]{:S(2)}, u32[]{:S(2)}) %collective-permute-start.13) | collective-permute-done | bytes 131104 | tf_op jit(solution)/shard_map/ppermute | solution.py:22
  66.7 1.0 %convolution_reduce_fusion = f32[512,128]{1,0:T(8,128)S(1)} fusion(f32[512,256,1]{1,0,2:T(8,128)S(1)} %bitcast.85, f32[8,128,256]{2,1,0:T(8,128)S(1)} %bitcast.84), kind=kOutput, calls=%fused_computation | convolution fusion | flops 805765120 | bytes 1835008 | tf_op jit(solution)/shard_map/dot_general | solution.py:146
  67.9 1.3 %collective-permute-start.15 = (f32[2048]{0:T(1024)S(1)}, f32[2048]{0:T(1024)S(1)}, u32[]{:S(2)}, u32[]{:S(2)}) collective-permute-start(f32[2048]{0:T(1024)S(1)} %reduce_max.19), channel_id=1, source_target_pairs={{0,2},{1,3},{2,0},{3,1},{4,6},{5,7},{6,4},{7,5},{8,10},{9,11},{10,... | collective-permute-start | bytes 24584 | tf_op jit(solution)/shard_map/ppermute | solution.py:27
  69.3 0.5 collective-permute-start.14
  69.8 1.9 %collective-permute-done.15 = f32[2048]{0:T(1024)S(1)} collective-permute-done((f32[2048]{0:T(1024)S(1)}, f32[2048]{0:T(1024)S(1)}, u32[]{:S(2)}, u32[]{:S(2)}) %collective-permute-start.15) | collective-permute-done | bytes 8224 | tf_op jit(solution)/shard_map/ppermute | solution.py:27
  71.7 0.7 collective-permute-done.14
  72.5 3.1 %collective-permute-start.18 = (f32[2048]{0:T(1024)S(1)}, f32[2048]{0:T(1024)S(1)}, u32[]{:S(2)}, u32[]{:S(2)}) collective-permute-start(f32[2048]{0:T(1024)S(1)} %maximum_maximum_fusion.1), channel_id=1, source_target_pairs={{0,8},{1,9},{2,10},{3,11},{4,12},{5,13},{6,14},{7,15},{8,0},{9,1},... | collective-permute-start | bytes 24584 | tf_op jit(solution)/shard_map/ppermute | solution.py:27
  75.6 1.3 %collective-permute-start.17 = (f32[2048]{0:T(1024)S(1)}, f32[2048]{0:T(1024)S(1)}, u32[]{:S(2)}, u32[]{:S(2)}) collective-permute-start(f32[2048]{0:T(1024)S(1)} %maximum_maximum_fusion.1), channel_id=1, source_target_pairs={{0,12},{1,13},{2,14},{3,15},{4,8},{5,9},{6,10},{7,11},{8,4},{9,5},... | collective-permute-start | bytes 24584 | tf_op jit(solution)/shard_map/ppermute | solution.py:27
  77.2 3.8 %collective-permute-done.17 = f32[2048]{0:T(1024)S(1)} collective-permute-done((f32[2048]{0:T(1024)S(1)}, f32[2048]{0:T(1024)S(1)}, u32[]{:S(2)}, u32[]{:S(2)}) %collective-permute-start.17) | collective-permute-done | bytes 8224 | tf_op jit(solution)/shard_map/ppermute | solution.py:27
  81.0 0.6 maximum_maximum_fusion
  (118 shorter events, 9.5 us)
Async XLA Ops:
  0.6 24.7 %copy-start.2 = (s32[9,32]{1,0:T(8,128)S(1)}, s32[9,32]{1,0:T(8,128)}, u32[]{:S(2)}) copy-start(s32[9,32]{1,0:T(8,128)} %offsets_ref.1) | copy-start | bytes 3460
  1.8 3.2 %collective-permute-start.2 = (f32[4480]{0:T(1024)S(1)}, f32[4480]{0:T(1024)S(1)}, u32[]{:S(2)}, u32[]{:S(2)}) collective-permute-start(f32[4480]{0:T(1024)S(1)} %slice_reduce_fusion), channel_id=1, source_target_pairs={{0,1},{1,0},{2,3},{3,2},{4,5},{5,4},{6,7},{7,6},{8,9},{9,8},{10,11... | collective-permute-start | bytes 53768 | tf_op jit(solution)/shard_map/ppermute | solution.py:27
  2.3 4.3 %collective-permute-start.1 = (f32[4480]{0:T(1024)S(1)}, f32[4480]{0:T(1024)S(1)}, u32[]{:S(2)}, u32[]{:S(2)}) collective-permute-start(f32[4480]{0:T(1024)S(1)} %slice_reduce_fusion), channel_id=1, source_target_pairs={{0,2},{1,3},{2,0},{3,1},{4,6},{5,7},{6,4},{7,5},{8,10},{9,11},{10,... | collective-permute-start | bytes 53768 | tf_op jit(solution)/shard_map/ppermute | solution.py:27
  4.8 3.2 %collective-permute-start = (f32[4480]{0:T(1024)S(1)}, f32[4480]{0:T(1024)S(1)}, u32[]{:S(2)}, u32[]{:S(2)}) collective-permute-start(f32[4480]{0:T(1024)S(1)} %slice_reduce_fusion), channel_id=1, source_target_pairs={{0,3},{1,2},{2,1},{3,0},{4,7},{5,6},{6,5},{7,4},{8,11},{9,10},{10,... | collective-permute-start | bytes 53768 | tf_op jit(solution)/shard_map/ppermute | solution.py:27
  8.1 4.5 %collective-permute-start.5 = (f32[4480]{0:T(1024)S(1)}, f32[4480]{0:T(1024)S(1)}, u32[]{:S(2)}, u32[]{:S(2)}) collective-permute-start(f32[4480]{0:T(1024)S(1)} %add_add_fusion.1), channel_id=1, source_target_pairs={{0,4},{1,5},{2,6},{3,7},{4,0},{5,1},{6,2},{7,3},{8,12},{9,13},{10,... | collective-permute-start | bytes 53768 | tf_op jit(solution)/shard_map/ppermute | solution.py:27
  9.7 4.9 %collective-permute-start.4 = (f32[4480]{0:T(1024)S(1)}, f32[4480]{0:T(1024)S(1)}, u32[]{:S(2)}, u32[]{:S(2)}) collective-permute-start(f32[4480]{0:T(1024)S(1)} %add_add_fusion.1), channel_id=1, source_target_pairs={{0,8},{1,9},{2,10},{3,11},{4,12},{5,13},{6,14},{7,15},{8,0},{9,1},... | collective-permute-start | bytes 53768 | tf_op jit(solution)/shard_map/ppermute | solution.py:27
  12.3 5.6 %collective-permute-start.3 = (f32[4480]{0:T(1024)S(1)}, f32[4480]{0:T(1024)S(1)}, u32[]{:S(2)}, u32[]{:S(2)}) collective-permute-start(f32[4480]{0:T(1024)S(1)} %add_add_fusion.1), channel_id=1, source_target_pairs={{0,12},{1,13},{2,14},{3,15},{4,8},{5,9},{6,10},{7,11},{8,4},{9,5},... | collective-permute-start | bytes 53768 | tf_op jit(solution)/shard_map/ppermute | solution.py:27
  25.3 1.8 %collective-permute-start.6 = (f32[32,2176]{1,0:T(8,128)}, f32[32,2176]{1,0:T(8,128)S(1)}, u32[]{:S(2)}, u32[]{:S(2)}) collective-permute-start(f32[32,2176]{1,0:T(8,128)} %get-tuple-element.19), channel_id=1, source_target_pairs={{0,1},{1,0},{2,3},{3,2},{4,5},{5,4},{6,7},{7,6},{8,9},{9,8},{10,11... | collective-permute-start | bytes 835592 | tf_op jit(solution)/shard_map/ppermute | solution.py:22
  28.9 1.1 %copy-start.3 = (s32[8]{0:T(128)S(1)}, s32[8]{0:T(128)}, u32[]{:S(2)}) copy-start(s32[8]{0:T(128)} %param.5) | copy-start | bytes 100
  28.9 1.2 %copy-start.1 = (f32[32,1024]{1,0:T(8,128)S(1)}, f32[32,1024]{1,0:T(8,128)}, u32[]{:S(2)}) copy-start(f32[32,1024]{1,0:T(8,128)} %get-tuple-element.21) | copy-start | bytes 393220
  29.2 8.1 %collective-permute-start.8 = (f32[32,1920]{1,0:T(8,128)S(1)}, f32[32,1920]{1,0:T(8,128)S(1)}, u32[]{:S(2)}, u32[]{:S(2)}) collective-permute-start(f32[32,1920]{1,0:T(8,128)S(1)} %fusion.2), channel_id=1, source_target_pairs={{0,2},{1,3},{2,0},{3,1},{4,6},{5,7},{6,4},{7,5},{8,10},{9,11},{10,... | collective-permute-start | bytes 737288 | tf_op jit(solution)/shard_map/ppermute | solution.py:22
  30.1 1.4 %collective-permute-start.7 = (f32[32,1024]{1,0:T(8,128)S(1)}, f32[32,1024]{1,0:T(8,128)S(1)}, u32[]{:S(2)}, u32[]{:S(2)}) collective-permute-start(f32[32,1024]{1,0:T(8,128)S(1)} %copy-done.1), channel_id=1, source_target_pairs={{0,1},{1,0},{2,3},{3,2},{4,5},{5,4},{6,7},{7,6},{8,9},{9,8},{10,11... | collective-permute-start | bytes 393224 | tf_op jit(solution)/shard_map/ppermute | solution.py:22
  38.2 5.0 %collective-permute-start.9 = (f32[32,1024]{1,0:T(8,128)S(1)}, f32[32,1024]{1,0:T(8,128)S(1)}, u32[]{:S(2)}, u32[]{:S(2)}) collective-permute-start(f32[32,1024]{1,0:T(8,128)S(1)} %fusion.17), channel_id=1, source_target_pairs={{0,2},{1,3},{2,0},{3,1},{4,6},{5,7},{6,4},{7,5},{8,10},{9,11},{10,... | collective-permute-start | bytes 393224 | tf_op jit(solution)/shard_map/ppermute | solution.py:22
  40.0 6.3 %collective-permute-start.10 = (f32[32,1664]{1,0:T(8,128)S(1)}, f32[32,1664]{1,0:T(8,128)S(1)}, u32[]{:S(2)}, u32[]{:S(2)}) collective-permute-start(f32[32,1664]{1,0:T(8,128)S(1)} %fusion.3), channel_id=1, source_target_pairs={{0,4},{1,5},{2,6},{3,7},{4,0},{5,1},{6,2},{7,3},{8,12},{9,13},{10,... | collective-permute-start | bytes 638984 | tf_op jit(solution)/shard_map/ppermute | solution.py:22
  47.2 5.4 %collective-permute-start.11 = (f32[32,1024]{1,0:T(8,128)S(1)}, f32[32,1024]{1,0:T(8,128)S(1)}, u32[]{:S(2)}, u32[]{:S(2)}) collective-permute-start(f32[32,1024]{1,0:T(8,128)S(1)} %fusion.16), channel_id=1, source_target_pairs={{0,4},{1,5},{2,6},{3,7},{4,0},{5,1},{6,2},{7,3},{8,12},{9,13},{10,... | collective-permute-start | bytes 393224 | tf_op jit(solution)/shard_map/ppermute | solution.py:22
  48.5 9.4 %collective-permute-start.12 = (f32[32,1408]{1,0:T(8,128)S(1)}, f32[32,1408]{1,0:T(8,128)S(1)}, u32[]{:S(2)}, u32[]{:S(2)}) collective-permute-start(f32[32,1408]{1,0:T(8,128)S(1)} %fusion.4), channel_id=1, source_target_pairs={{0,8},{1,9},{2,10},{3,11},{4,12},{5,13},{6,14},{7,15},{8,0},{9,1},... | collective-permute-start | bytes 540680 | tf_op jit(solution)/shard_map/ppermute | solution.py:22
  58.8 6.8 %collective-permute-start.13 = (f32[32,1024]{1,0:T(8,128)S(1)}, f32[32,1024]{1,0:T(8,128)S(1)}, u32[]{:S(2)}, u32[]{:S(2)}) collective-permute-start(f32[32,1024]{1,0:T(8,128)S(1)} %fusion.15), channel_id=1, source_target_pairs={{0,8},{1,9},{2,10},{3,11},{4,12},{5,13},{6,14},{7,15},{8,0},{9,1},... | collective-permute-start | bytes 393224 | tf_op jit(solution)/shard_map/ppermute | solution.py:22
  67.8 13.8 %copy-start = (f32[32,2048]{1,0:T(8,128)}, f32[32,2048]{1,0:T(8,128)S(1)}, u32[]{:S(2)}) copy-start(f32[32,2048]{1,0:T(8,128)S(1)} %reshape.485) | copy-start | bytes 786436
  67.9 1.9 %collective-permute-start.16 = (f32[2048]{0:T(1024)S(1)}, f32[2048]{0:T(1024)S(1)}, u32[]{:S(2)}, u32[]{:S(2)}) collective-permute-start(f32[2048]{0:T(1024)S(1)} %reduce_max.19), channel_id=1, source_target_pairs={{0,1},{1,0},{2,3},{3,2},{4,5},{5,4},{6,7},{7,6},{8,9},{9,8},{10,11... | collective-permute-start | bytes 24584 | tf_op jit(solution)/shard_map/ppermute | solution.py:27
  67.9 3.7 %collective-permute-start.15 = (f32[2048]{0:T(1024)S(1)}, f32[2048]{0:T(1024)S(1)}, u32[]{:S(2)}, u32[]{:S(2)}) collective-permute-start(f32[2048]{0:T(1024)S(1)} %reduce_max.19), channel_id=1, source_target_pairs={{0,2},{1,3},{2,0},{3,1},{4,6},{5,7},{6,4},{7,5},{8,10},{9,11},{10,... | collective-permute-start | bytes 24584 | tf_op jit(solution)/shard_map/ppermute | solution.py:27
  69.3 3.1 %collective-permute-start.14 = (f32[2048]{0:T(1024)S(1)}, f32[2048]{0:T(1024)S(1)}, u32[]{:S(2)}, u32[]{:S(2)}) collective-permute-start(f32[2048]{0:T(1024)S(1)} %reduce_max.19), channel_id=1, source_target_pairs={{0,3},{1,2},{2,1},{3,0},{4,7},{5,6},{6,5},{7,4},{8,11},{9,10},{10,... | collective-permute-start | bytes 24584 | tf_op jit(solution)/shard_map/ppermute | solution.py:27
  72.4 4.5 %collective-permute-start.19 = (f32[2048]{0:T(1024)S(1)}, f32[2048]{0:T(1024)S(1)}, u32[]{:S(2)}, u32[]{:S(2)}) collective-permute-start(f32[2048]{0:T(1024)S(1)} %maximum_maximum_fusion.1), channel_id=1, source_target_pairs={{0,4},{1,5},{2,6},{3,7},{4,0},{5,1},{6,2},{7,3},{8,12},{9,13},{10,... | collective-permute-start | bytes 24584 | tf_op jit(solution)/shard_map/ppermute | solution.py:27
  72.5 4.7 %collective-permute-start.18 = (f32[2048]{0:T(1024)S(1)}, f32[2048]{0:T(1024)S(1)}, u32[]{:S(2)}, u32[]{:S(2)}) collective-permute-start(f32[2048]{0:T(1024)S(1)} %maximum_maximum_fusion.1), channel_id=1, source_target_pairs={{0,8},{1,9},{2,10},{3,11},{4,12},{5,13},{6,14},{7,15},{8,0},{9,1},... | collective-permute-start | bytes 24584 | tf_op jit(solution)/shard_map/ppermute | solution.py:27
  75.6 5.4 %collective-permute-start.17 = (f32[2048]{0:T(1024)S(1)}, f32[2048]{0:T(1024)S(1)}, u32[]{:S(2)}, u32[]{:S(2)}) collective-permute-start(f32[2048]{0:T(1024)S(1)} %maximum_maximum_fusion.1), channel_id=1, source_target_pairs={{0,12},{1,13},{2,14},{3,15},{4,8},{5,9},{6,10},{7,11},{8,4},{9,5},... | collective-permute-start | bytes 24584 | tf_op jit(solution)/shard_map/ppermute | solution.py:27

commit v12 on v9

--- a/solution.py
+++ b/solution.py
@@ -183,9 +183,11 @@
         lower_head, upper_head = halves(head, partner_head, bit_index)
         head_width = head.shape[1] - SHIFT
         new_head = lower_head[:, :head_width] + shift_rows(upper_head, amounts, head_width)
+        if bit_index + 1 < bit_count:
+            next_partner_head = from_partner(new_head, "band", bit_index + 1)
+            tail, new_head = lax.optimization_barrier((tail, new_head))
         partner_tail = from_partner(tail, "band", bit_index)
         if bit_index + 1 < bit_count:
-            next_partner_head = from_partner(new_head, "band", bit_index + 1)
             partner_tail, next_partner_head = lax.optimization_barrier((partner_tail, next_partner_head))
             partner_head = next_partner_head
         lower_tail, upper_tail = halves(tail, partner_tail, bit_index)

time: 79.8 us -> 79.8 us (level)
  starting transfers between devices: 16.7 us -> 17.5 us
  waiting for transfers between devices: 42.3 us -> 41.5 us
  transfers between devices with their start and end apart: 20 -> 20, of which waited for: 16 -> 16; matrix products, arithmetic and copies ran while one was open for 4% -> 2% of each run, Pallas kernels for 0% -> 0%
where the time goes in v12:
time: 79.8 us; the launch traced here: 79.6 us
  waiting for transfers between devices  41.5 us (52%)
  starting transfers between devices  17.5 us (22%)
  other arithmetic  10.5 us (13%)
  Pallas kernels  6.8 us (9%)
  between operations  1.34 us (2%)
  matrix products  1.03 us (1%)
  local copies, waits for them, and re-layouts  0.94 us (1%)
    ppermute x8, waiting for transfers between devices, from_partner(): return lax.ppermute(value, axis, pairs)  27.2 us
    ppermute x12, waiting for transfers between devices, from_xor(): return lax.ppermute(value, axis, pairs)  14.3 us
    ppermute x12, starting transfers between devices, from_xor(): return lax.ppermute(value, axis, pairs)  14 us
    pallas_call x1, Pallas kernels, local_tree(): pl.pallas_call(functools.partial(local_tree_kernel, tuple(widths_seq), fl...  6.8 us
    select_n x56, other arithmetic, shift_rows(): jnp.where(chosen, current[:, span:span + keep_len], current[:, :keep_len])  6.19 us
    ppermute x8, starting transfers between devices, from_partner(): return lax.ppermute(value, axis, pairs)  3.49 us
  transfers between devices with their start and end apart: 20, of which 16 were waited for; matrix products, arithmetic and copies ran while one was open for 2% of the time, Pallas kernels for 0%

profile of v12, /device:TPU:0, one launch (start us, length us, event | category | flops | bytes accessed | tf_op | source)
XLA Modules:
  0.0 79.6 jit_solution(9347424010114835148)
XLA Ops:
  0.6 1.1 %slice_reduce_fusion = f32[4480]{0:T(1024)S(1)} fusion(f32[32,6144]{1,0:T(8,128)} %x_ref.1), kind=kLoop, calls=%fused_computation.4 | loop fusion | flops 138880 | bytes 591360 | tf_op jit(solution)/shard_map/reduce_sum | solution.py:167
  1.8 0.5 collective-permute-start.2
  2.3 2.6 %collective-permute-start.1 = (f32[4480]{0:T(1024)S(1)}, f32[4480]{0:T(1024)S(1)}, u32[]{:S(2)}, u32[]{:S(2)}) collective-permute-start(f32[4480]{0:T(1024)S(1)} %slice_reduce_fusion), channel_id=1, source_target_pairs={{0,2},{1,3},{2,0},{3,1},{4,6},{5,7},{6,4},{7,5},{8,10},{9,11},{10,... | collective-permute-start | bytes 53768 | tf_op jit(solution)/shard_map/ppermute | solution.py:27
  4.9 1.7 %collective-permute-done.1 = f32[4480]{0:T(1024)S(1)} collective-permute-done((f32[4480]{0:T(1024)S(1)}, f32[4480]{0:T(1024)S(1)}, u32[]{:S(2)}, u32[]{:S(2)}) %collective-permute-start.1) | collective-permute-done | bytes 17952 | tf_op jit(solution)/shard_map/ppermute | solution.py:27
  6.6 1.4 %collective-permute-done = f32[4480]{0:T(1024)S(1)} collective-permute-done((f32[4480]{0:T(1024)S(1)}, f32[4480]{0:T(1024)S(1)}, u32[]{:S(2)}, u32[]{:S(2)}) %collective-permute-start) | collective-permute-done | bytes 17952 | tf_op jit(solution)/shard_map/ppermute | solution.py:27
  8.1 1.6 %collective-permute-start.5 = (f32[4480]{0:T(1024)S(1)}, f32[4480]{0:T(1024)S(1)}, u32[]{:S(2)}, u32[]{:S(2)}) collective-permute-start(f32[4480]{0:T(1024)S(1)} %add_add_fusion.1), channel_id=1, source_target_pairs={{0,4},{1,5},{2,6},{3,7},{4,0},{5,1},{6,2},{7,3},{8,12},{9,13},{10,... | collective-permute-start | bytes 53768 | tf_op jit(solution)/shard_map/ppermute | solution.py:27
  9.7 2.6 %collective-permute-start.4 = (f32[4480]{0:T(1024)S(1)}, f32[4480]{0:T(1024)S(1)}, u32[]{:S(2)}, u32[]{:S(2)}) collective-permute-start(f32[4480]{0:T(1024)S(1)} %add_add_fusion.1), channel_id=1, source_target_pairs={{0,8},{1,9},{2,10},{3,11},{4,12},{5,13},{6,14},{7,15},{8,0},{9,1},... | collective-permute-start | bytes 53768 | tf_op jit(solution)/shard_map/ppermute | solution.py:27
  12.5 2.1 %collective-permute-done.4 = f32[4480]{0:T(1024)S(1)} collective-permute-done((f32[4480]{0:T(1024)S(1)}, f32[4480]{0:T(1024)S(1)}, u32[]{:S(2)}, u32[]{:S(2)}) %collective-permute-start.4) | collective-permute-done | bytes 17952 | tf_op jit(solution)/shard_map/ppermute | solution.py:27
  14.6 3.3 %collective-permute-done.3 = f32[4480]{0:T(1024)S(1)} collective-permute-done((f32[4480]{0:T(1024)S(1)}, f32[4480]{0:T(1024)S(1)}, u32[]{:S(2)}, u32[]{:S(2)}) %collective-permute-start.3) | collective-permute-done | bytes 17952 | tf_op jit(solution)/shard_map/ppermute | solution.py:27
  17.9 0.6 broadcast_in_dim.527.total_ref
  18.5 6.8 %shard_map.50 = (f32[32,2048]{1,0:T(8,128)}, f32[32,1152]{1,0:T(8,128)}) custom-call(f32[32,6144]{1,0:T(8,128)} %x_ref.1, f32[1,4480]{1,0:T(1,128)} %broadcast_in_dim.527.total_ref, s32[9,32]{1,0:T(8,128)} %offsets_ref.1), custom_call_target="tpu_custom_call" | custom-call | flops 25395200 | bytes 983040 | tf_op jit(solution)/shard_map/pallas_call | solution.py:97
  25.4 1.7 %collective-permute-done.6 = f32[32,2048]{1,0:T(8,128)S(1)} collective-permute-done((f32[32,2048]{1,0:T(8,128)}, f32[32,2048]{1,0:T(8,128)S(1)}, u32[]{:S(2)}, u32[]{:S(2)}) %collective-permute-start.6) | collective-permute-done | bytes 262176 | tf_op jit(solution)/shard_map/ppermute | solution.py:22
  27.1 1.0 %broadcast_select_fusion.1 = (f32[32,2048]{1,0:T(8,128)S(1)}, f32[32,2048]{1,0:T(8,128)S(1)}) fusion(f32[32,2048]{1,0:T(8,128)S(1)} %collective-permute-done.6, f32[32,2048]{1,0:T(8,128)} %get-tuple-element.25, pred[]{:T(512)S(6)} %eq.508), kind=kLoop, calls=%fused_computation.101 | loop fusion | flops 131072 | bytes 1048577 | tf_op jit(solution)/shard_map/jit(_where)/select_n | solution.py:177
  29.1 0.8 %collective-permute-start.8 = (f32[32,1792]{1,0:T(8,128)S(1)}, f32[32,1792]{1,0:T(8,128)S(1)}, u32[]{:S(2)}, u32[]{:S(2)}) collective-permute-start(f32[32,1792]{1,0:T(8,128)S(1)} %fusion.2), channel_id=1, source_target_pairs={{0,2},{1,3},{2,0},{3,1},{4,6},{5,7},{6,4},{7,5},{8,10},{9,11},{10,... | collective-permute-start | bytes 688136 | tf_op jit(solution)/shard_map/ppermute | solution.py:22
  30.1 1.3 %collective-permute-done.7 = f32[32,1152]{1,0:T(8,128)S(1)} collective-permute-done((f32[32,1152]{1,0:T(8,128)S(1)}, f32[32,1152]{1,0:T(8,128)S(1)}, u32[]{:S(2)}, u32[]{:S(2)}) %collective-permute-start.7) | collective-permute-done | bytes 147488 | tf_op jit(solution)/shard_map/ppermute | solution.py:22
  31.4 5.4 %collective-permute-done.8 = f32[32,1792]{1,0:T(8,128)S(1)} collective-permute-done((f32[32,1792]{1,0:T(8,128)S(1)}, f32[32,1792]{1,0:T(8,128)S(1)}, u32[]{:S(2)}, u32[]{:S(2)}) %collective-permute-start.8) | collective-permute-done | bytes 229408 | tf_op jit(solution)/shard_map/ppermute | solution.py:22
  38.9 0.8 %collective-permute-start.9 = (f32[32,1152]{1,0:T(8,128)S(1)}, f32[32,1152]{1,0:T(8,128)S(1)}, u32[]{:S(2)}, u32[]{:S(2)}) collective-permute-start(f32[32,1152]{1,0:T(8,128)S(1)} %fusion.16), channel_id=1, source_target_pairs={{0,2},{1,3},{2,0},{3,1},{4,6},{5,7},{6,4},{7,5},{8,10},{9,11},{10,... | collective-permute-start | bytes 442376 | tf_op jit(solution)/shard_map/ppermute | solution.py:22
  39.8 4.3 %collective-permute-done.9 = f32[32,1152]{1,0:T(8,128)S(1)} collective-permute-done((f32[32,1152]{1,0:T(8,128)S(1)}, f32[32,1152]{1,0:T(8,128)S(1)}, u32[]{:S(2)}, u32[]{:S(2)}) %collective-permute-start.9) | collective-permute-done | bytes 147488 | tf_op jit(solution)/shard_map/ppermute | solution.py:22
  44.1 0.9 %collective-permute-done.10 = f32[32,1536]{1,0:T(8,128)S(1)} collective-permute-done((f32[32,1536]{1,0:T(8,128)S(1)}, f32[32,1536]{1,0:T(8,128)S(1)}, u32[]{:S(2)}, u32[]{:S(2)}) %collective-permute-start.10) | collective-permute-done | bytes 196640 | tf_op jit(solution)/shard_map/ppermute | solution.py:22
  47.0 1.1 %collective-permute-start.11 = (f32[32,1152]{1,0:T(8,128)S(1)}, f32[32,1152]{1,0:T(8,128)S(1)}, u32[]{:S(2)}, u32[]{:S(2)}) collective-permute-start(f32[32,1152]{1,0:T(8,128)S(1)} %fusion.15), channel_id=1, source_target_pairs={{0,4},{1,5},{2,6},{3,7},{4,0},{5,1},{6,2},{7,3},{8,12},{9,13},{10,... | collective-permute-start | bytes 442376 | tf_op jit(solution)/shard_map/ppermute | solution.py:22
  48.5 5.1 %collective-permute-done.11 = f32[32,1152]{1,0:T(8,128)S(1)} collective-permute-done((f32[32,1152]{1,0:T(8,128)S(1)}, f32[32,1152]{1,0:T(8,128)S(1)}, u32[]{:S(2)}, u32[]{:S(2)}) %collective-permute-start.11) | collective-permute-done | bytes 147488 | tf_op jit(solution)/shard_map/ppermute | solution.py:22
  53.7 2.2 %collective-permute-done.12 = f32[32,1280]{1,0:T(8,128)S(1)} collective-permute-done((f32[32,1280]{1,0:T(8,128)S(1)}, f32[32,1280]{1,0:T(8,128)S(1)}, u32[]{:S(2)}, u32[]{:S(2)}) %collective-permute-start.12) | collective-permute-done | bytes 163872 | tf_op jit(solution)/shard_map/ppermute | solution.py:22
  57.0 0.6 collective-permute-start.13
  58.3 6.2 %collective-permute-done.13 = f32[32,1152]{1,0:T(8,128)S(1)} collective-permute-done((f32[32,1152]{1,0:T(8,128)S(1)}, f32[32,1152]{1,0:T(8,128)S(1)}, u32[]{:S(2)}, u32[]{:S(2)}) %collective-permute-start.13) | collective-permute-done | bytes 147488 | tf_op jit(solution)/shard_map/ppermute | solution.py:22
  65.6 1.0 %convolution_reduce_fusion = f32[512,128]{1,0:T(8,128)S(1)} fusion(f32[512,256,1]{1,0,2:T(8,128)S(1)} %bitcast.85, f32[8,128,256]{2,1,0:T(8,128)S(1)} %bitcast.84), kind=kOutput, calls=%fused_computation | convolution fusion | flops 805765120 | bytes 1835008 | tf_op jit(solution)/shard_map/dot_general | solution.py:146
  66.8 0.8 %collective-permute-start.15 = (f32[2048]{0:T(1024)S(1)}, f32[2048]{0:T(1024)S(1)}, u32[]{:S(2)}, u32[]{:S(2)}) collective-permute-start(f32[2048]{0:T(1024)S(1)} %reduce_max.19), channel_id=1, source_target_pairs={{0,2},{1,3},{2,0},{3,1},{4,6},{5,7},{6,4},{7,5},{8,10},{9,11},{10,... | collective-permute-start | bytes 24584 | tf_op jit(solution)/shard_map/ppermute | solution.py:27
  67.6 1.0 %collective-permute-start.14 = (f32[2048]{0:T(1024)S(1)}, f32[2048]{0:T(1024)S(1)}, u32[]{:S(2)}, u32[]{:S(2)}) collective-permute-start(f32[2048]{0:T(1024)S(1)} %reduce_max.19), channel_id=1, source_target_pairs={{0,3},{1,2},{2,1},{3,0},{4,7},{5,6},{6,5},{7,4},{8,11},{9,10},{10,... | collective-permute-start | bytes 24584 | tf_op jit(solution)/shard_map/ppermute | solution.py:27
  68.7 1.9 %collective-permute-done.15 = f32[2048]{0:T(1024)S(1)} collective-permute-done((f32[2048]{0:T(1024)S(1)}, f32[2048]{0:T(1024)S(1)}, u32[]{:S(2)}, u32[]{:S(2)}) %collective-permute-start.15) | collective-permute-done | bytes 8224 | tf_op jit(solution)/shard_map/ppermute | solution.py:27
  70.8 2.7 %collective-permute-start.18 = (f32[2048]{0:T(1024)S(1)}, f32[2048]{0:T(1024)S(1)}, u32[]{:S(2)}, u32[]{:S(2)}) collective-permute-start(f32[2048]{0:T(1024)S(1)} %maximum_maximum_fusion.1), channel_id=1, source_target_pairs={{0,8},{1,9},{2,10},{3,11},{4,12},{5,13},{6,14},{7,15},{8,0},{9,1},... | collective-permute-start | bytes 24584 | tf_op jit(solution)/shard_map/ppermute | solution.py:27
  73.5 1.7 %collective-permute-start.17 = (f32[2048]{0:T(1024)S(1)}, f32[2048]{0:T(1024)S(1)}, u32[]{:S(2)}, u32[]{:S(2)}) collective-permute-start(f32[2048]{0:T(1024)S(1)} %maximum_maximum_fusion.1), channel_id=1, source_target_pairs={{0,12},{1,13},{2,14},{3,15},{4,8},{5,9},{6,10},{7,11},{8,4},{9,5},... | collective-permute-start | bytes 24584 | tf_op jit(solution)/shard_map/ppermute | solution.py:27
  75.4 3.6 %collective-permute-done.17 = f32[2048]{0:T(1024)S(1)} collective-permute-done((f32[2048]{0:T(1024)S(1)}, f32[2048]{0:T(1024)S(1)}, u32[]{:S(2)}, u32[]{:S(2)}) %collective-permute-start.17) | collective-permute-done | bytes 8224 | tf_op jit(solution)/shard_map/ppermute | solution.py:27
  79.0 0.6 maximum_maximum_fusion
  (118 shorter events, 9.2 us)
Async XLA Ops:
  0.6 24.7 %copy-start.2 = (s32[9,32]{1,0:T(8,128)S(1)}, s32[9,32]{1,0:T(8,128)}, u32[]{:S(2)}) copy-start(s32[9,32]{1,0:T(8,128)} %offsets_ref.1) | copy-start | bytes 3460
  1.8 3.2 %collective-permute-start.2 = (f32[4480]{0:T(1024)S(1)}, f32[4480]{0:T(1024)S(1)}, u32[]{:S(2)}, u32[]{:S(2)}) collective-permute-start(f32[4480]{0:T(1024)S(1)} %slice_reduce_fusion), channel_id=1, source_target_pairs={{0,1},{1,0},{2,3},{3,2},{4,5},{5,4},{6,7},{7,6},{8,9},{9,8},{10,11... | collective-permute-start | bytes 53768 | tf_op jit(solution)/shard_map/ppermute | solution.py:27
  2.3 4.3 %collective-permute-start.1 = (f32[4480]{0:T(1024)S(1)}, f32[4480]{0:T(1024)S(1)}, u32[]{:S(2)}, u32[]{:S(2)}) collective-permute-start(f32[4480]{0:T(1024)S(1)} %slice_reduce_fusion), channel_id=1, source_target_pairs={{0,2},{1,3},{2,0},{3,1},{4,6},{5,7},{6,4},{7,5},{8,10},{9,11},{10,... | collective-permute-start | bytes 53768 | tf_op jit(solution)/shard_map/ppermute | solution.py:27
  4.8 3.2 %collective-permute-start = (f32[4480]{0:T(1024)S(1)}, f32[4480]{0:T(1024)S(1)}, u32[]{:S(2)}, u32[]{:S(2)}) collective-permute-start(f32[4480]{0:T(1024)S(1)} %slice_reduce_fusion), channel_id=1, source_target_pairs={{0,3},{1,2},{2,1},{3,0},{4,7},{5,6},{6,5},{7,4},{8,11},{9,10},{10,... | collective-permute-start | bytes 53768 | tf_op jit(solution)/shard_map/ppermute | solution.py:27
  8.1 4.5 %collective-permute-start.5 = (f32[4480]{0:T(1024)S(1)}, f32[4480]{0:T(1024)S(1)}, u32[]{:S(2)}, u32[]{:S(2)}) collective-permute-start(f32[4480]{0:T(1024)S(1)} %add_add_fusion.1), channel_id=1, source_target_pairs={{0,4},{1,5},{2,6},{3,7},{4,0},{5,1},{6,2},{7,3},{8,12},{9,13},{10,... | collective-permute-start | bytes 53768 | tf_op jit(solution)/shard_map/ppermute | solution.py:27
  9.7 4.9 %collective-permute-start.4 = (f32[4480]{0:T(1024)S(1)}, f32[4480]{0:T(1024)S(1)}, u32[]{:S(2)}, u32[]{:S(2)}) collective-permute-start(f32[4480]{0:T(1024)S(1)} %add_add_fusion.1), channel_id=1, source_target_pairs={{0,8},{1,9},{2,10},{3,11},{4,12},{5,13},{6,14},{7,15},{8,0},{9,1},... | collective-permute-start | bytes 53768 | tf_op jit(solution)/shard_map/ppermute | solution.py:27
  12.3 5.6 %collective-permute-start.3 = (f32[4480]{0:T(1024)S(1)}, f32[4480]{0:T(1024)S(1)}, u32[]{:S(2)}, u32[]{:S(2)}) collective-permute-start(f32[4480]{0:T(1024)S(1)} %add_add_fusion.1), channel_id=1, source_target_pairs={{0,12},{1,13},{2,14},{3,15},{4,8},{5,9},{6,10},{7,11},{8,4},{9,5},... | collective-permute-start | bytes 53768 | tf_op jit(solution)/shard_map/ppermute | solution.py:27
  25.3 1.7 %collective-permute-start.6 = (f32[32,2048]{1,0:T(8,128)}, f32[32,2048]{1,0:T(8,128)S(1)}, u32[]{:S(2)}, u32[]{:S(2)}) collective-permute-start(f32[32,2048]{1,0:T(8,128)} %get-tuple-element.25), channel_id=1, source_target_pairs={{0,1},{1,0},{2,3},{3,2},{4,5},{5,4},{6,7},{7,6},{8,9},{9,8},{10,11... | collective-permute-start | bytes 786440 | tf_op jit(solution)/shard_map/ppermute | solution.py:22
  28.7 1.3 %copy-start.3 = (s32[8]{0:T(128)S(1)}, s32[8]{0:T(128)}, u32[]{:S(2)}) copy-start(s32[8]{0:T(128)} %param.5) | copy-start | bytes 100
  28.9 1.2 %copy-start.1 = (f32[32,1152]{1,0:T(8,128)S(1)}, f32[32,1152]{1,0:T(8,128)}, u32[]{:S(2)}) copy-start(f32[32,1152]{1,0:T(8,128)} %get-tuple-element.28) | copy-start | bytes 442372
  29.1 7.7 %collective-permute-start.8 = (f32[32,1792]{1,0:T(8,128)S(1)}, f32[32,1792]{1,0:T(8,128)S(1)}, u32[]{:S(2)}, u32[]{:S(2)}) collective-permute-start(f32[32,1792]{1,0:T(8,128)S(1)} %fusion.2), channel_id=1, source_target_pairs={{0,2},{1,3},{2,0},{3,1},{4,6},{5,7},{6,4},{7,5},{8,10},{9,11},{10,... | collective-permute-start | bytes 688136 | tf_op jit(solution)/shard_map/ppermute | solution.py:22
  30.0 1.4 %collective-permute-start.7 = (f32[32,1152]{1,0:T(8,128)S(1)}, f32[32,1152]{1,0:T(8,128)S(1)}, u32[]{:S(2)}, u32[]{:S(2)}) collective-permute-start(f32[32,1152]{1,0:T(8,128)S(1)} %copy-done.1), channel_id=1, source_target_pairs={{0,1},{1,0},{2,3},{3,2},{4,5},{5,4},{6,7},{7,6},{8,9},{9,8},{10,11... | collective-permute-start | bytes 442376 | tf_op jit(solution)/shard_map/ppermute | solution.py:22
  38.8 6.2 %collective-permute-start.10 = (f32[32,1536]{1,0:T(8,128)S(1)}, f32[32,1536]{1,0:T(8,128)S(1)}, u32[]{:S(2)}, u32[]{:S(2)}) collective-permute-start(f32[32,1536]{1,0:T(8,128)S(1)} %fusion.3), channel_id=1, source_target_pairs={{0,4},{1,5},{2,6},{3,7},{4,0},{5,1},{6,2},{7,3},{8,12},{9,13},{10,... | collective-permute-start | bytes 589832 | tf_op jit(solution)/shard_map/ppermute | solution.py:22
  38.9 5.2 %collective-permute-start.9 = (f32[32,1152]{1,0:T(8,128)S(1)}, f32[32,1152]{1,0:T(8,128)S(1)}, u32[]{:S(2)}, u32[]{:S(2)}) collective-permute-start(f32[32,1152]{1,0:T(8,128)S(1)} %fusion.16), channel_id=1, source_target_pairs={{0,2},{1,3},{2,0},{3,1},{4,6},{5,7},{6,4},{7,5},{8,10},{9,11},{10,... | collective-permute-start | bytes 442376 | tf_op jit(solution)/shard_map/ppermute | solution.py:22
  46.9 9.0 %collective-permute-start.12 = (f32[32,1280]{1,0:T(8,128)S(1)}, f32[32,1280]{1,0:T(8,128)S(1)}, u32[]{:S(2)}, u32[]{:S(2)}) collective-permute-start(f32[32,1280]{1,0:T(8,128)S(1)} %fusion.12), channel_id=1, source_target_pairs={{0,8},{1,9},{2,10},{3,11},{4,12},{5,13},{6,14},{7,15},{8,0},{9,1},... | collective-permute-start | bytes 491528 | tf_op jit(solution)/shard_map/ppermute | solution.py:22
  47.0 6.7 %collective-permute-start.11 = (f32[32,1152]{1,0:T(8,128)S(1)}, f32[32,1152]{1,0:T(8,128)S(1)}, u32[]{:S(2)}, u32[]{:S(2)}) collective-permute-start(f32[32,1152]{1,0:T(8,128)S(1)} %fusion.15), channel_id=1, source_target_pairs={{0,4},{1,5},{2,6},{3,7},{4,0},{5,1},{6,2},{7,3},{8,12},{9,13},{10,... | collective-permute-start | bytes 442376 | tf_op jit(solution)/shard_map/ppermute | solution.py:22
  57.0 7.5 %collective-permute-start.13 = (f32[32,1152]{1,0:T(8,128)S(1)}, f32[32,1152]{1,0:T(8,128)S(1)}, u32[]{:S(2)}, u32[]{:S(2)}) collective-permute-start(f32[32,1152]{1,0:T(8,128)S(1)} %fusion.14), channel_id=1, source_target_pairs={{0,8},{1,9},{2,10},{3,11},{4,12},{5,13},{6,14},{7,15},{8,0},{9,1},... | collective-permute-start | bytes 442376 | tf_op jit(solution)/shard_map/ppermute | solution.py:22
  66.7 12.9 %copy-start = (f32[32,2048]{1,0:T(8,128)}, f32[32,2048]{1,0:T(8,128)S(1)}, u32[]{:S(2)}) copy-start(f32[32,2048]{1,0:T(8,128)S(1)} %reshape.485) | copy-start | bytes 786436
  66.7 1.9 %collective-permute-start.16 = (f32[2048]{0:T(1024)S(1)}, f32[2048]{0:T(1024)S(1)}, u32[]{:S(2)}, u32[]{:S(2)}) collective-permute-start(f32[2048]{0:T(1024)S(1)} %reduce_max.19), channel_id=1, source_target_pairs={{0,1},{1,0},{2,3},{3,2},{4,5},{5,4},{6,7},{7,6},{8,9},{9,8},{10,11... | collective-permute-start | bytes 24584 | tf_op jit(solution)/shard_map/ppermute | solution.py:27
  66.8 3.7 %collective-permute-start.15 = (f32[2048]{0:T(1024)S(1)}, f32[2048]{0:T(1024)S(1)}, u32[]{:S(2)}, u32[]{:S(2)}) collective-permute-start(f32[2048]{0:T(1024)S(1)} %reduce_max.19), channel_id=1, source_target_pairs={{0,2},{1,3},{2,0},{3,1},{4,6},{5,7},{6,4},{7,5},{8,10},{9,11},{10,... | collective-permute-start | bytes 24584 | tf_op jit(solution)/shard_map/ppermute | solution.py:27
  67.6 3.1 %collective-permute-start.14 = (f32[2048]{0:T(1024)S(1)}, f32[2048]{0:T(1024)S(1)}, u32[]{:S(2)}, u32[]{:S(2)}) collective-permute-start(f32[2048]{0:T(1024)S(1)} %reduce_max.19), channel_id=1, source_target_pairs={{0,3},{1,2},{2,1},{3,0},{4,7},{5,6},{6,5},{7,4},{8,11},{9,10},{10,... | collective-permute-start | bytes 24584 | tf_op jit(solution)/shard_map/ppermute | solution.py:27
  70.7 4.5 %collective-permute-start.19 = (f32[2048]{0:T(1024)S(1)}, f32[2048]{0:T(1024)S(1)}, u32[]{:S(2)}, u32[]{:S(2)}) collective-permute-start(f32[2048]{0:T(1024)S(1)} %maximum_maximum_fusion.1), channel_id=1, source_target_pairs={{0,4},{1,5},{2,6},{3,7},{4,0},{5,1},{6,2},{7,3},{8,12},{9,13},{10,... | collective-permute-start | bytes 24584 | tf_op jit(solution)/shard_map/ppermute | solution.py:27
  70.8 4.6 %collective-permute-start.18 = (f32[2048]{0:T(1024)S(1)}, f32[2048]{0:T(1024)S(1)}, u32[]{:S(2)}, u32[]{:S(2)}) collective-permute-start(f32[2048]{0:T(1024)S(1)} %maximum_maximum_fusion.1), channel_id=1, source_target_pairs={{0,8},{1,9},{2,10},{3,11},{4,12},{5,13},{6,14},{7,15},{8,0},{9,1},... | collective-permute-start | bytes 24584 | tf_op jit(solution)/shard_map/ppermute | solution.py:27
  73.5 5.4 %collective-permute-start.17 = (f32[2048]{0:T(1024)S(1)}, f32[2048]{0:T(1024)S(1)}, u32[]{:S(2)}, u32[]{:S(2)}) collective-permute-start(f32[2048]{0:T(1024)S(1)} %maximum_maximum_fusion.1), channel_id=1, source_target_pairs={{0,12},{1,13},{2,14},{3,15},{4,8},{5,9},{6,10},{7,11},{8,4},{9,5},... | collective-permute-start | bytes 24584 | tf_op jit(solution)/shard_map/ppermute | solution.py:27

commit v13 on v12

--- a/solution.py
+++ b/solution.py
@@ -29,22 +29,13 @@
 
 def butterfly(value, axis, combine):
     bit_count = lax.axis_size(axis).bit_length() - 1
-    position = lax.axis_index(axis)
     low_bit = 0
     while low_bit < bit_count:
         width = min(2, bit_count - low_bit)
-        group = 2**width
-        received = [value] + [from_xor(value, axis, k << low_bit) for k in range(1, group)]
-        mine = position >> low_bit & (group - 1)
-        ordered = []
-        for slot in range(group):
-            chosen = received[0]
-            for k in range(1, group):
-                chosen = jnp.where((mine ^ slot) == k, received[k], chosen)
-            ordered.append(chosen)
-        while len(ordered) > 1:
-            ordered = [combine(ordered[i], ordered[i + 1]) for i in range(0, len(ordered), 2)]
-        value = ordered[0]
+        received = [value] + [from_xor(value, axis, k << low_bit) for k in range(1, 2**width)]
+        while len(received) > 1:
+            received = [combine(received[i], received[i + 1]) for i in range(0, len(received), 2)]
+        value = received[0]
         low_bit += width
     return value
 
@@ -105,7 +96,7 @@
         cost_estimate=pl.CostEstimate(
             flops=40 * work, transcendentals=0, bytes_accessed=4 * (rows * widths_seq[0] + rows * widths_seq[-1])
         ),
-    )(filterbank, channel_total[None, :], offsets)
+    )(filterbank, channel_total, offsets)
 
 
 def merge_section(current, offsets_now, section_index, new_length):
@@ -164,7 +155,7 @@
         needed = -(-needed // 128) * 128
         return min(TIN, needed)
 
-    partial_value = jnp.sum(filterbank[:, : length_after(0)], axis=0)
+    partial_value = jnp.sum(filterbank[:, : length_after(0)], axis=0, keepdims=True)
     channel_total = butterfly(partial_value, "band", jnp.add)
     widths_seq = [length_after(section) for section in range(local_count + 1)]
     head, tail = local_tree(filterbank, channel_total, offsets, widths_seq, channels_all, TAIL_WIDTH)

time: 79.8 us -> 77.2 us (0.967)
  waiting for transfers between devices: 41.5 us -> 37 us
  starting transfers between devices: 17.5 us -> 19.3 us
    ppermute x12, waiting for transfers between devices: 14.3 us -> 10.7 us  [from_xor(): return lax.ppermute(value, axis, pairs)]
    ppermute x8, starting transfers between devices: 3.49 us -> 5.28 us  [from_partner(): return lax.ppermute(value, axis, pairs)]
  transfers between devices with their start and end apart: 20 -> 20, of which waited for: 16 -> 15; matrix products, arithmetic and copies ran while one was open for 2% -> 2% of each run, Pallas kernels for 0% -> 0%
where the time goes in v13:
time: 77.2 us; the launch traced here: 77 us
  waiting for transfers between devices  37 us (48%)
  starting transfers between devices  19.3 us (25%)
  other arithmetic  11.2 us (15%)
  Pallas kernels  6.8 us (9%)
  between operations  1.34 us (2%)
  matrix products  1.02 us (1%)
    ppermute x8, waiting for transfers between devices, from_partner(): return lax.ppermute(value, axis, pairs)  26.4 us
    ppermute x12, starting transfers between devices, from_xor(): return lax.ppermute(value, axis, pairs)  14 us
    ppermute x12, waiting for transfers between devices, from_xor(): return lax.ppermute(value, axis, pairs)  10.7 us
    pallas_call x1, Pallas kernels, local_tree(): pl.pallas_call(functools.partial(local_tree_kernel, tuple(widths_seq), fl...  6.8 us
    select_n x56, other arithmetic, shift_rows(): jnp.where(chosen, current[:, span:span + keep_len], current[:, :keep_len])  6.19 us
    ppermute x8, starting transfers between devices, from_partner(): return lax.ppermute(value, axis, pairs)  5.28 us
  transfers between devices with their start and end apart: 20, of which 15 were waited for; matrix products, arithmetic and copies ran while one was open for 2% of the time, Pallas kernels for 0%

profile of v13, /device:TPU:0, one launch (start us, length us, event | category | flops | bytes accessed | tf_op | source)
XLA Modules:
  0.0 77.0 jit_solution(7460189406250257300)
XLA Ops:
  0.6 1.1 %slice_reduce_fusion = f32[4480]{0:T(1024)S(1)} fusion(f32[32,6144]{1,0:T(8,128)} %x_ref.1), kind=kLoop, calls=%fused_computation.4 | loop fusion | flops 138880 | bytes 591360 | tf_op jit(solution)/shard_map/reduce_sum | solution.py:158
  1.8 3.0 %collective-permute-start.1 = (f32[1,4480]{1,0:T(1,128)S(1)}, f32[1,4480]{1,0:T(1,128)S(1)}, u32[]{:S(2)}, u32[]{:S(2)}) collective-permute-start(f32[1,4480]{1,0:T(1,128)S(1)} %broadcast_in_dim.527), channel_id=1, source_target_pairs={{0,2},{1,3},{2,0},{3,1},{4,6},{5,7},{6,4},{7,5},{8,10},{9,11},{10,... | collective-permute-start | bytes 53768 | tf_op jit(solution)/shard_map/ppermute | solution.py:27
  5.0 1.5 %collective-permute-done.1 = f32[1,4480]{1,0:T(1,128)S(1)} collective-permute-done((f32[1,4480]{1,0:T(1,128)S(1)}, f32[1,4480]{1,0:T(1,128)S(1)}, u32[]{:S(2)}, u32[]{:S(2)}) %collective-permute-start.1) | collective-permute-done | bytes 17952 | tf_op jit(solution)/shard_map/ppermute | solution.py:27
  6.5 1.4 %collective-permute-done.2 = f32[1,4480]{1,0:T(1,128)S(1)} collective-permute-done((f32[1,4480]{1,0:T(1,128)S(1)}, f32[1,4480]{1,0:T(1,128)S(1)}, u32[]{:S(2)}, u32[]{:S(2)}) %collective-permute-start.2) | collective-permute-done | bytes 17952 | tf_op jit(solution)/shard_map/ppermute | solution.py:27
  8.0 3.7 %collective-permute-start.5 = (f32[1,4480]{1,0:T(1,128)S(1)}, f32[1,4480]{1,0:T(1,128)S(1)}, u32[]{:S(2)}, u32[]{:S(2)}) collective-permute-start(f32[1,4480]{1,0:T(1,128)S(1)} %add_add_fusion.1), channel_id=1, source_target_pairs={{0,12},{1,13},{2,14},{3,15},{4,8},{5,9},{6,10},{7,11},{8,4},{9,5},... | collective-permute-start | bytes 53768 | tf_op jit(solution)/shard_map/ppermute | solution.py:27
  11.7 0.8 %collective-permute-start.3 = (f32[1,4480]{1,0:T(1,128)S(1)}, f32[1,4480]{1,0:T(1,128)S(1)}, u32[]{:S(2)}, u32[]{:S(2)}) collective-permute-start(f32[1,4480]{1,0:T(1,128)S(1)} %add_add_fusion.1), channel_id=1, source_target_pairs={{0,4},{1,5},{2,6},{3,7},{4,0},{5,1},{6,2},{7,3},{8,12},{9,13},{10,... | collective-permute-start | bytes 53768 | tf_op jit(solution)/shard_map/ppermute | solution.py:27
  12.5 1.4 %collective-permute-done.5 = f32[1,4480]{1,0:T(1,128)S(1)} collective-permute-done((f32[1,4480]{1,0:T(1,128)S(1)}, f32[1,4480]{1,0:T(1,128)S(1)}, u32[]{:S(2)}, u32[]{:S(2)}) %collective-permute-start.5) | collective-permute-done | bytes 17952 | tf_op jit(solution)/shard_map/ppermute | solution.py:27
  13.8 2.5 %collective-permute-done.4 = f32[1,4480]{1,0:T(1,128)S(1)} collective-permute-done((f32[1,4480]{1,0:T(1,128)S(1)}, f32[1,4480]{1,0:T(1,128)S(1)}, u32[]{:S(2)}, u32[]{:S(2)}) %collective-permute-start.4) | collective-permute-done | bytes 17952 | tf_op jit(solution)/shard_map/ppermute | solution.py:27
  16.3 0.6 add_add_fusion.total_ref
  17.0 6.8 %shard_map.50 = (f32[32,2048]{1,0:T(8,128)}, f32[32,1152]{1,0:T(8,128)}) custom-call(f32[32,6144]{1,0:T(8,128)} %x_ref.1, f32[1,4480]{1,0:T(1,128)} %add_add_fusion.total_ref, s32[9,32]{1,0:T(8,128)} %offsets_ref.1), custom_call_target="tpu_custom_call" | custom-call | flops 25395200 | bytes 983040 | tf_op jit(solution)/shard_map/pallas_call | solution.py:88
  23.8 1.7 %collective-permute-done.6 = f32[32,2048]{1,0:T(8,128)S(1)} collective-permute-done((f32[32,2048]{1,0:T(8,128)}, f32[32,2048]{1,0:T(8,128)S(1)}, u32[]{:S(2)}, u32[]{:S(2)}) %collective-permute-start.6) | collective-permute-done | bytes 262176 | tf_op jit(solution)/shard_map/ppermute | solution.py:22
  25.5 1.0 %broadcast_select_fusion.1 = (f32[32,2048]{1,0:T(8,128)S(1)}, f32[32,2048]{1,0:T(8,128)S(1)}) fusion(f32[32,2048]{1,0:T(8,128)S(1)} %collective-permute-done.6, f32[32,2048]{1,0:T(8,128)} %get-tuple-element.25, pred[]{:T(512)S(6)} %eq.412), kind=kLoop, calls=%fused_computation.101 | loop fusion | flops 131072 | bytes 1048577 | tf_op jit(solution)/shard_map/jit(_where)/select_n | solution.py:168
  27.6 0.8 %collective-permute-start.8 = (f32[32,1792]{1,0:T(8,128)S(1)}, f32[32,1792]{1,0:T(8,128)S(1)}, u32[]{:S(2)}, u32[]{:S(2)}) collective-permute-start(f32[32,1792]{1,0:T(8,128)S(1)} %fusion.2), channel_id=1, source_target_pairs={{0,2},{1,3},{2,0},{3,1},{4,6},{5,7},{6,4},{7,5},{8,10},{9,11},{10,... | collective-permute-start | bytes 688136 | tf_op jit(solution)/shard_map/ppermute | solution.py:22
  28.5 1.3 %collective-permute-done.7 = f32[32,1152]{1,0:T(8,128)S(1)} collective-permute-done((f32[32,1152]{1,0:T(8,128)S(1)}, f32[32,1152]{1,0:T(8,128)S(1)}, u32[]{:S(2)}, u32[]{:S(2)}) %collective-permute-start.7) | collective-permute-done | bytes 147488 | tf_op jit(solution)/shard_map/ppermute | solution.py:22
  29.8 5.5 %collective-permute-done.8 = f32[32,1792]{1,0:T(8,128)S(1)} collective-permute-done((f32[32,1792]{1,0:T(8,128)S(1)}, f32[32,1792]{1,0:T(8,128)S(1)}, u32[]{:S(2)}, u32[]{:S(2)}) %collective-permute-start.8) | collective-permute-done | bytes 229408 | tf_op jit(solution)/shard_map/ppermute | solution.py:22
  37.3 0.8 %collective-permute-start.9 = (f32[32,1152]{1,0:T(8,128)S(1)}, f32[32,1152]{1,0:T(8,128)S(1)}, u32[]{:S(2)}, u32[]{:S(2)}) collective-permute-start(f32[32,1152]{1,0:T(8,128)S(1)} %fusion.16), channel_id=1, source_target_pairs={{0,2},{1,3},{2,0},{3,1},{4,6},{5,7},{6,4},{7,5},{8,10},{9,11},{10,... | collective-permute-start | bytes 442376 | tf_op jit(solution)/shard_map/ppermute | solution.py:22
  38.2 4.3 %collective-permute-done.9 = f32[32,1152]{1,0:T(8,128)S(1)} collective-permute-done((f32[32,1152]{1,0:T(8,128)S(1)}, f32[32,1152]{1,0:T(8,128)S(1)}, u32[]{:S(2)}, u32[]{:S(2)}) %collective-permute-start.9) | collective-permute-done | bytes 147488 | tf_op jit(solution)/shard_map/ppermute | solution.py:22
  42.6 0.9 %collective-permute-done.10 = f32[32,1536]{1,0:T(8,128)S(1)} collective-permute-done((f32[32,1536]{1,0:T(8,128)S(1)}, f32[32,1536]{1,0:T(8,128)S(1)}, u32[]{:S(2)}, u32[]{:S(2)}) %collective-permute-start.10) | collective-permute-done | bytes 196640 | tf_op jit(solution)/shard_map/ppermute | solution.py:22
  45.4 2.1 %collective-permute-start.12 = (f32[32,1280]{1,0:T(8,128)S(1)}, f32[32,1280]{1,0:T(8,128)S(1)}, u32[]{:S(2)}, u32[]{:S(2)}) collective-permute-start(f32[32,1280]{1,0:T(8,128)S(1)} %fusion.12), channel_id=1, source_target_pairs={{0,8},{1,9},{2,10},{3,11},{4,12},{5,13},{6,14},{7,15},{8,0},{9,1},... | collective-permute-start | bytes 491528 | tf_op jit(solution)/shard_map/ppermute | solution.py:22
  47.4 1.1 %collective-permute-start.11 = (f32[32,1152]{1,0:T(8,128)S(1)}, f32[32,1152]{1,0:T(8,128)S(1)}, u32[]{:S(2)}, u32[]{:S(2)}) collective-permute-start(f32[32,1152]{1,0:T(8,128)S(1)} %fusion.15), channel_id=1, source_target_pairs={{0,4},{1,5},{2,6},{3,7},{4,0},{5,1},{6,2},{7,3},{8,12},{9,13},{10,... | collective-permute-start | bytes 442376 | tf_op jit(solution)/shard_map/ppermute | solution.py:22
  48.9 5.5 %collective-permute-done.11 = f32[32,1152]{1,0:T(8,128)S(1)} collective-permute-done((f32[32,1152]{1,0:T(8,128)S(1)}, f32[32,1152]{1,0:T(8,128)S(1)}, u32[]{:S(2)}, u32[]{:S(2)}) %collective-permute-start.11) | collective-permute-done | bytes 147488 | tf_op jit(solution)/shard_map/ppermute | solution.py:22
  56.8 7.2 %collective-permute-done.13 = f32[32,1152]{1,0:T(8,128)S(1)} collective-permute-done((f32[32,1152]{1,0:T(8,128)S(1)}, f32[32,1152]{1,0:T(8,128)S(1)}, u32[]{:S(2)}, u32[]{:S(2)}) %collective-permute-start.13) | collective-permute-done | bytes 147488 | tf_op jit(solution)/shard_map/ppermute | solution.py:22
  65.0 1.0 %convolution_reduce_fusion = f32[512,128]{1,0:T(8,128)S(1)} fusion(f32[512,256,1]{1,0,2:T(8,128)S(1)} %bitcast.85, f32[8,128,256]{2,1,0:T(8,128)S(1)} %bitcast.84), kind=kOutput, calls=%fused_computation | convolution fusion | flops 805765120 | bytes 1835008 | tf_op jit(solution)/shard_map/dot_general | solution.py:137
  66.3 0.8 %collective-permute-start.15 = (f32[2048]{0:T(1024)S(1)}, f32[2048]{0:T(1024)S(1)}, u32[]{:S(2)}, u32[]{:S(2)}) collective-permute-start(f32[2048]{0:T(1024)S(1)} %reduce_max.19), channel_id=1, source_target_pairs={{0,2},{1,3},{2,0},{3,1},{4,6},{5,7},{6,4},{7,5},{8,10},{9,11},{10,... | collective-permute-start | bytes 24584 | tf_op jit(solution)/shard_map/ppermute | solution.py:27
  67.1 1.0 %collective-permute-start.14 = (f32[2048]{0:T(1024)S(1)}, f32[2048]{0:T(1024)S(1)}, u32[]{:S(2)}, u32[]{:S(2)}) collective-permute-start(f32[2048]{0:T(1024)S(1)} %reduce_max.19), channel_id=1, source_target_pairs={{0,1},{1,0},{2,3},{3,2},{4,5},{5,4},{6,7},{7,6},{8,9},{9,8},{10,11... | collective-permute-start | bytes 24584 | tf_op jit(solution)/shard_map/ppermute | solution.py:27
  68.1 1.2 %collective-permute-done.16 = f32[2048]{0:T(1024)S(1)} collective-permute-done((f32[2048]{0:T(1024)S(1)}, f32[2048]{0:T(1024)S(1)}, u32[]{:S(2)}, u32[]{:S(2)}) %collective-permute-start.16) | collective-permute-done | bytes 8224 | tf_op jit(solution)/shard_map/ppermute | solution.py:27
  69.3 0.7 collective-permute-done.15
  70.0 1.8 %collective-permute-start.19 = (f32[2048]{0:T(1024)S(1)}, f32[2048]{0:T(1024)S(1)}, u32[]{:S(2)}, u32[]{:S(2)}) collective-permute-start(f32[2048]{0:T(1024)S(1)} %maximum_maximum_fusion.1), channel_id=1, source_target_pairs={{0,12},{1,13},{2,14},{3,15},{4,8},{5,9},{6,10},{7,11},{8,4},{9,5},... | collective-permute-start | bytes 24584 | tf_op jit(solution)/shard_map/ppermute | solution.py:27
  71.8 2.6 %collective-permute-start.17 = (f32[2048]{0:T(1024)S(1)}, f32[2048]{0:T(1024)S(1)}, u32[]{:S(2)}, u32[]{:S(2)}) collective-permute-start(f32[2048]{0:T(1024)S(1)} %maximum_maximum_fusion.1), channel_id=1, source_target_pairs={{0,4},{1,5},{2,6},{3,7},{4,0},{5,1},{6,2},{7,3},{8,12},{9,13},{10,... | collective-permute-start | bytes 24584 | tf_op jit(solution)/shard_map/ppermute | solution.py:27
  74.4 1.1 %collective-permute-done.19 = f32[2048]{0:T(1024)S(1)} collective-permute-done((f32[2048]{0:T(1024)S(1)}, f32[2048]{0:T(1024)S(1)}, u32[]{:S(2)}, u32[]{:S(2)}) %collective-permute-start.19) | collective-permute-done | bytes 8224 | tf_op jit(solution)/shard_map/ppermute | solution.py:27
  75.5 0.9 %collective-permute-done.18 = f32[2048]{0:T(1024)S(1)} collective-permute-done((f32[2048]{0:T(1024)S(1)}, f32[2048]{0:T(1024)S(1)}, u32[]{:S(2)}, u32[]{:S(2)}) %collective-permute-start.18) | collective-permute-done | bytes 8224 | tf_op jit(solution)/shard_map/ppermute | solution.py:27
  76.4 0.6 maximum_maximum_fusion
  (118 shorter events, 9.0 us)
Async XLA Ops:
  0.6 23.1 %copy-start.2 = (s32[9,32]{1,0:T(8,128)S(1)}, s32[9,32]{1,0:T(8,128)}, u32[]{:S(2)}) copy-start(s32[9,32]{1,0:T(8,128)} %offsets_ref.1) | copy-start | bytes 3460
  1.8 4.7 %collective-permute-start.1 = (f32[1,4480]{1,0:T(1,128)S(1)}, f32[1,4480]{1,0:T(1,128)S(1)}, u32[]{:S(2)}, u32[]{:S(2)}) collective-permute-start(f32[1,4480]{1,0:T(1,128)S(1)} %broadcast_in_dim.527), channel_id=1, source_target_pairs={{0,2},{1,3},{2,0},{3,1},{4,6},{5,7},{6,4},{7,5},{8,10},{9,11},{10,... | collective-permute-start | bytes 53768 | tf_op jit(solution)/shard_map/ppermute | solution.py:27
  4.8 3.2 %collective-permute-start.2 = (f32[1,4480]{1,0:T(1,128)S(1)}, f32[1,4480]{1,0:T(1,128)S(1)}, u32[]{:S(2)}, u32[]{:S(2)}) collective-permute-start(f32[1,4480]{1,0:T(1,128)S(1)} %broadcast_in_dim.527), channel_id=1, source_target_pairs={{0,3},{1,2},{2,1},{3,0},{4,7},{5,6},{6,5},{7,4},{8,11},{9,10},{10,... | collective-permute-start | bytes 53768 | tf_op jit(solution)/shard_map/ppermute | solution.py:27
  4.8 3.2 %collective-permute-start = (f32[1,4480]{1,0:T(1,128)S(1)}, f32[1,4480]{1,0:T(1,128)S(1)}, u32[]{:S(2)}, u32[]{:S(2)}) collective-permute-start(f32[1,4480]{1,0:T(1,128)S(1)} %broadcast_in_dim.527), channel_id=1, source_target_pairs={{0,1},{1,0},{2,3},{3,2},{4,5},{5,4},{6,7},{7,6},{8,9},{9,8},{10,11... | collective-permute-start | bytes 53768 | tf_op jit(solution)/shard_map/ppermute | solution.py:27
  8.0 5.8 %collective-permute-start.5 = (f32[1,4480]{1,0:T(1,128)S(1)}, f32[1,4480]{1,0:T(1,128)S(1)}, u32[]{:S(2)}, u32[]{:S(2)}) collective-permute-start(f32[1,4480]{1,0:T(1,128)S(1)} %add_add_fusion.1), channel_id=1, source_target_pairs={{0,12},{1,13},{2,14},{3,15},{4,8},{5,9},{6,10},{7,11},{8,4},{9,5},... | collective-permute-start | bytes 53768 | tf_op jit(solution)/shard_map/ppermute | solution.py:27
  11.7 4.7 %collective-permute-start.4 = (f32[1,4480]{1,0:T(1,128)S(1)}, f32[1,4480]{1,0:T(1,128)S(1)}, u32[]{:S(2)}, u32[]{:S(2)}) collective-permute-start(f32[1,4480]{1,0:T(1,128)S(1)} %add_add_fusion.1), channel_id=1, source_target_pairs={{0,8},{1,9},{2,10},{3,11},{4,12},{5,13},{6,14},{7,15},{8,0},{9,1},... | collective-permute-start | bytes 53768 | tf_op jit(solution)/shard_map/ppermute | solution.py:27
  11.7 4.7 %collective-permute-start.3 = (f32[1,4480]{1,0:T(1,128)S(1)}, f32[1,4480]{1,0:T(1,128)S(1)}, u32[]{:S(2)}, u32[]{:S(2)}) collective-permute-start(f32[1,4480]{1,0:T(1,128)S(1)} %add_add_fusion.1), channel_id=1, source_target_pairs={{0,4},{1,5},{2,6},{3,7},{4,0},{5,1},{6,2},{7,3},{8,12},{9,13},{10,... | collective-permute-start | bytes 53768 | tf_op jit(solution)/shard_map/ppermute | solution.py:27
  23.8 1.7 %collective-permute-start.6 = (f32[32,2048]{1,0:T(8,128)}, f32[32,2048]{1,0:T(8,128)S(1)}, u32[]{:S(2)}, u32[]{:S(2)}) collective-permute-start(f32[32,2048]{1,0:T(8,128)} %get-tuple-element.25), channel_id=1, source_target_pairs={{0,1},{1,0},{2,3},{3,2},{4,5},{5,4},{6,7},{7,6},{8,9},{9,8},{10,11... | collective-permute-start | bytes 786440 | tf_op jit(solution)/shard_map/ppermute | solution.py:22
  27.2 1.2 %copy-start.3 = (s32[8]{0:T(128)S(1)}, s32[8]{0:T(128)}, u32[]{:S(2)}) copy-start(s32[8]{0:T(128)} %param.5) | copy-start | bytes 100
  27.3 1.2 %copy-start.1 = (f32[32,1152]{1,0:T(8,128)S(1)}, f32[32,1152]{1,0:T(8,128)}, u32[]{:S(2)}) copy-start(f32[32,1152]{1,0:T(8,128)} %get-tuple-element.28) | copy-start | bytes 442372
  27.6 7.7 %collective-permute-start.8 = (f32[32,1792]{1,0:T(8,128)S(1)}, f32[32,1792]{1,0:T(8,128)S(1)}, u32[]{:S(2)}, u32[]{:S(2)}) collective-permute-start(f32[32,1792]{1,0:T(8,128)S(1)} %fusion.2), channel_id=1, source_target_pairs={{0,2},{1,3},{2,0},{3,1},{4,6},{5,7},{6,4},{7,5},{8,10},{9,11},{10,... | collective-permute-start | bytes 688136 | tf_op jit(solution)/shard_map/ppermute | solution.py:22
  28.5 1.4 %collective-permute-start.7 = (f32[32,1152]{1,0:T(8,128)S(1)}, f32[32,1152]{1,0:T(8,128)S(1)}, u32[]{:S(2)}, u32[]{:S(2)}) collective-permute-start(f32[32,1152]{1,0:T(8,128)S(1)} %copy-done.1), channel_id=1, source_target_pairs={{0,1},{1,0},{2,3},{3,2},{4,5},{5,4},{6,7},{7,6},{8,9},{9,8},{10,11... | collective-permute-start | bytes 442376 | tf_op jit(solution)/shard_map/ppermute | solution.py:22
  37.3 6.2 %collective-permute-start.10 = (f32[32,1536]{1,0:T(8,128)S(1)}, f32[32,1536]{1,0:T(8,128)S(1)}, u32[]{:S(2)}, u32[]{:S(2)}) collective-permute-start(f32[32,1536]{1,0:T(8,128)S(1)} %fusion.3), channel_id=1, source_target_pairs={{0,4},{1,5},{2,6},{3,7},{4,0},{5,1},{6,2},{7,3},{8,12},{9,13},{10,... | collective-permute-start | bytes 589832 | tf_op jit(solution)/shard_map/ppermute | solution.py:22
  37.3 5.2 %collective-permute-start.9 = (f32[32,1152]{1,0:T(8,128)S(1)}, f32[32,1152]{1,0:T(8,128)S(1)}, u32[]{:S(2)}, u32[]{:S(2)}) collective-permute-start(f32[32,1152]{1,0:T(8,128)S(1)} %fusion.16), channel_id=1, source_target_pairs={{0,2},{1,3},{2,0},{3,1},{4,6},{5,7},{6,4},{7,5},{8,10},{9,11},{10,... | collective-permute-start | bytes 442376 | tf_op jit(solution)/shard_map/ppermute | solution.py:22
  45.4 9.1 %collective-permute-start.12 = (f32[32,1280]{1,0:T(8,128)S(1)}, f32[32,1280]{1,0:T(8,128)S(1)}, u32[]{:S(2)}, u32[]{:S(2)}) collective-permute-start(f32[32,1280]{1,0:T(8,128)S(1)} %fusion.12), channel_id=1, source_target_pairs={{0,8},{1,9},{2,10},{3,11},{4,12},{5,13},{6,14},{7,15},{8,0},{9,1},... | collective-permute-start | bytes 491528 | tf_op jit(solution)/shard_map/ppermute | solution.py:22
  47.4 7.0 %collective-permute-start.11 = (f32[32,1152]{1,0:T(8,128)S(1)}, f32[32,1152]{1,0:T(8,128)S(1)}, u32[]{:S(2)}, u32[]{:S(2)}) collective-permute-start(f32[32,1152]{1,0:T(8,128)S(1)} %fusion.15), channel_id=1, source_target_pairs={{0,4},{1,5},{2,6},{3,7},{4,0},{5,1},{6,2},{7,3},{8,12},{9,13},{10,... | collective-permute-start | bytes 442376 | tf_op jit(solution)/shard_map/ppermute | solution.py:22
  55.5 8.4 %collective-permute-start.13 = (f32[32,1152]{1,0:T(8,128)S(1)}, f32[32,1152]{1,0:T(8,128)S(1)}, u32[]{:S(2)}, u32[]{:S(2)}) collective-permute-start(f32[32,1152]{1,0:T(8,128)S(1)} %fusion.14), channel_id=1, source_target_pairs={{0,8},{1,9},{2,10},{3,11},{4,12},{5,13},{6,14},{7,15},{8,0},{9,1},... | collective-permute-start | bytes 442376 | tf_op jit(solution)/shard_map/ppermute | solution.py:22
  66.1 10.9 %copy-start = (f32[32,2048]{1,0:T(8,128)}, f32[32,2048]{1,0:T(8,128)S(1)}, u32[]{:S(2)}) copy-start(f32[32,2048]{1,0:T(8,128)S(1)} %reshape.485) | copy-start | bytes 786436
  66.2 3.1 %collective-permute-start.16 = (f32[2048]{0:T(1024)S(1)}, f32[2048]{0:T(1024)S(1)}, u32[]{:S(2)}, u32[]{:S(2)}) collective-permute-start(f32[2048]{0:T(1024)S(1)} %reduce_max.19), channel_id=1, source_target_pairs={{0,3},{1,2},{2,1},{3,0},{4,7},{5,6},{6,5},{7,4},{8,11},{9,10},{10,... | collective-permute-start | bytes 24584 | tf_op jit(solution)/shard_map/ppermute | solution.py:27
  66.3 3.7 %collective-permute-start.15 = (f32[2048]{0:T(1024)S(1)}, f32[2048]{0:T(1024)S(1)}, u32[]{:S(2)}, u32[]{:S(2)}) collective-permute-start(f32[2048]{0:T(1024)S(1)} %reduce_max.19), channel_id=1, source_target_pairs={{0,2},{1,3},{2,0},{3,1},{4,6},{5,7},{6,4},{7,5},{8,10},{9,11},{10,... | collective-permute-start | bytes 24584 | tf_op jit(solution)/shard_map/ppermute | solution.py:27
  67.1 2.9 %collective-permute-start.14 = (f32[2048]{0:T(1024)S(1)}, f32[2048]{0:T(1024)S(1)}, u32[]{:S(2)}, u32[]{:S(2)}) collective-permute-start(f32[2048]{0:T(1024)S(1)} %reduce_max.19), channel_id=1, source_target_pairs={{0,1},{1,0},{2,3},{3,2},{4,5},{5,4},{6,7},{7,6},{8,9},{9,8},{10,11... | collective-permute-start | bytes 24584 | tf_op jit(solution)/shard_map/ppermute | solution.py:27
  70.0 5.5 %collective-permute-start.19 = (f32[2048]{0:T(1024)S(1)}, f32[2048]{0:T(1024)S(1)}, u32[]{:S(2)}, u32[]{:S(2)}) collective-permute-start(f32[2048]{0:T(1024)S(1)} %maximum_maximum_fusion.1), channel_id=1, source_target_pairs={{0,12},{1,13},{2,14},{3,15},{4,8},{5,9},{6,10},{7,11},{8,4},{9,5},... | collective-permute-start | bytes 24584 | tf_op jit(solution)/shard_map/ppermute | solution.py:27
  71.8 4.5 %collective-permute-start.18 = (f32[2048]{0:T(1024)S(1)}, f32[2048]{0:T(1024)S(1)}, u32[]{:S(2)}, u32[]{:S(2)}) collective-permute-start(f32[2048]{0:T(1024)S(1)} %maximum_maximum_fusion.1), channel_id=1, source_target_pairs={{0,8},{1,9},{2,10},{3,11},{4,12},{5,13},{6,14},{7,15},{8,0},{9,1},... | collective-permute-start | bytes 24584 | tf_op jit(solution)/shard_map/ppermute | solution.py:27
  71.8 4.5 %collective-permute-start.17 = (f32[2048]{0:T(1024)S(1)}, f32[2048]{0:T(1024)S(1)}, u32[]{:S(2)}, u32[]{:S(2)}) collective-permute-start(f32[2048]{0:T(1024)S(1)} %maximum_maximum_fusion.1), channel_id=1, source_target_pairs={{0,4},{1,5},{2,6},{3,7},{4,0},{5,1},{6,2},{7,3},{8,12},{9,13},{10,... | collective-permute-start | bytes 24584 | tf_op jit(solution)/shard_map/ppermute | solution.py:27

commit v14 on v13

--- a/solution.py
+++ b/solution.py
@@ -167,25 +167,33 @@
         upper_half = band_index // 2**bit_index % 2 == 1
         return jnp.where(upper_half, partner, own), jnp.where(upper_half, own, partner)
 
+    def finish_tail(pending):
+        own_tail, partner_tail, lower_edge, upper_edge, amounts, bit_index = pending
+        lower_tail, upper_tail = halves(own_tail, partner_tail, bit_index)
+        lower_window = jnp.concatenate([lower_edge, lower_tail], axis=1)
+        upper_window = jnp.concatenate([upper_edge, upper_tail], axis=1)
+        return lower_window[:, :tail_width] + shift_rows(upper_window, amounts, tail_width)
+
     partner_head = from_partner(head, "band", 0)
+    tail, partner_head = lax.optimization_barrier((tail, partner_head))
+    pending = None
     for bit_index in range(bit_count):
         amounts = offsets[local_count + bit_index]
-        tail, partner_head = lax.optimization_barrier((tail, partner_head))
         lower_head, upper_head = halves(head, partner_head, bit_index)
         head_width = head.shape[1] - SHIFT
         new_head = lower_head[:, :head_width] + shift_rows(upper_head, amounts, head_width)
         if bit_index + 1 < bit_count:
             next_partner_head = from_partner(new_head, "band", bit_index + 1)
-            tail, new_head = lax.optimization_barrier((tail, new_head))
+        if pending is not None:
+            waiting, ordered_head = lax.optimization_barrier((pending[1], new_head))
+            tail = finish_tail(pending[:1] + (waiting,) + pending[2:])
         partner_tail = from_partner(tail, "band", bit_index)
         if bit_index + 1 < bit_count:
             partner_tail, next_partner_head = lax.optimization_barrier((partner_tail, next_partner_head))
             partner_head = next_partner_head
-        lower_tail, upper_tail = halves(tail, partner_tail, bit_index)
-        lower_window = jnp.concatenate([lower_head[:, head_width:], lower_tail], axis=1)
-        upper_window = jnp.concatenate([upper_head[:, head_width:], upper_tail], axis=1)
-        tail = lower_window[:, :tail_width] + shift_rows(upper_window, amounts, tail_width)
+        pending = (tail, partner_tail, lower_head[:, head_width:], upper_head[:, head_width:], amounts, bit_index)
         head = new_head
+    tail = finish_tail(pending)
     current = jnp.concatenate([head, tail], axis=1)
     dedispersed = current * (1.0 / math.sqrt(channels_all))
     detection = boxcar_max(dedispersed, widths)

time: 77.2 us -> 76.1 us (0.986)
  waiting for transfers between devices: 37 us -> 34 us
  starting transfers between devices: 19.3 us -> 21.3 us
    ppermute x8, waiting for transfers between devices: 26.4 us -> 22.8 us  [from_partner(): return lax.ppermute(value, axis, pairs)]
    ppermute x8, starting transfers between devices: 5.28 us -> 7.3 us  [from_partner(): return lax.ppermute(value, axis, pairs)]
  transfers between devices with their start and end apart: 20 -> 20, of which waited for: 15 -> 14; matrix products, arithmetic and copies ran while one was open for 2% -> 3% of each run, Pallas kernels for 0% -> 0%
where the time goes in v14:
time: 76.1 us; the launch traced here: 75.9 us
  waiting for transfers between devices  34 us (45%)
  starting transfers between devices  21.3 us (28%)
  other arithmetic  11.2 us (15%)
  Pallas kernels  6.8 us (9%)
  between operations  1.26 us (2%)
  matrix products  1.03 us (1%)
    ppermute x8, waiting for transfers between devices, from_partner(): return lax.ppermute(value, axis, pairs)  22.8 us
    ppermute x12, starting transfers between devices, from_xor(): return lax.ppermute(value, axis, pairs)  14 us
    ppermute x12, waiting for transfers between devices, from_xor(): return lax.ppermute(value, axis, pairs)  11.2 us
    ppermute x8, starting transfers between devices, from_partner(): return lax.ppermute(value, axis, pairs)  7.3 us
    pallas_call x1, Pallas kernels, local_tree(): pl.pallas_call(functools.partial(local_tree_kernel, tuple(widths_seq), fl...  6.8 us
    select_n x56, other arithmetic, shift_rows(): jnp.where(chosen, current[:, span:span + keep_len], current[:, :keep_len])  6.19 us
  transfers between devices with their start and end apart: 20, of which 14 were waited for; matrix products, arithmetic and copies ran while one was open for 3% of the time, Pallas kernels for 0%

profile of v14, /device:TPU:0, one launch (start us, length us, event | category | flops | bytes accessed | tf_op | source)
XLA Modules:
  0.0 75.9 jit_solution(11922282733043542044)
XLA Ops:
  0.6 1.1 %slice_reduce_fusion = f32[4480]{0:T(1024)S(1)} fusion(f32[32,6144]{1,0:T(8,128)} %x_ref.1), kind=kLoop, calls=%fused_computation.4 | loop fusion | flops 138880 | bytes 591360 | tf_op jit(solution)/shard_map/reduce_sum | solution.py:158
  1.8 3.0 %collective-permute-start.1 = (f32[1,4480]{1,0:T(1,128)S(1)}, f32[1,4480]{1,0:T(1,128)S(1)}, u32[]{:S(2)}, u32[]{:S(2)}) collective-permute-start(f32[1,4480]{1,0:T(1,128)S(1)} %broadcast_in_dim.527), channel_id=1, source_target_pairs={{0,2},{1,3},{2,0},{3,1},{4,6},{5,7},{6,4},{7,5},{8,10},{9,11},{10,... | collective-permute-start | bytes 53768 | tf_op jit(solution)/shard_map/ppermute | solution.py:27
  5.0 1.5 %collective-permute-done.1 = f32[1,4480]{1,0:T(1,128)S(1)} collective-permute-done((f32[1,4480]{1,0:T(1,128)S(1)}, f32[1,4480]{1,0:T(1,128)S(1)}, u32[]{:S(2)}, u32[]{:S(2)}) %collective-permute-start.1) | collective-permute-done | bytes 17952 | tf_op jit(solution)/shard_map/ppermute | solution.py:27
  6.5 1.4 %collective-permute-done.2 = f32[1,4480]{1,0:T(1,128)S(1)} collective-permute-done((f32[1,4480]{1,0:T(1,128)S(1)}, f32[1,4480]{1,0:T(1,128)S(1)}, u32[]{:S(2)}, u32[]{:S(2)}) %collective-permute-start.2) | collective-permute-done | bytes 17952 | tf_op jit(solution)/shard_map/ppermute | solution.py:27
  8.0 3.7 %collective-permute-start.5 = (f32[1,4480]{1,0:T(1,128)S(1)}, f32[1,4480]{1,0:T(1,128)S(1)}, u32[]{:S(2)}, u32[]{:S(2)}) collective-permute-start(f32[1,4480]{1,0:T(1,128)S(1)} %add_add_fusion.1), channel_id=1, source_target_pairs={{0,12},{1,13},{2,14},{3,15},{4,8},{5,9},{6,10},{7,11},{8,4},{9,5},... | collective-permute-start | bytes 53768 | tf_op jit(solution)/shard_map/ppermute | solution.py:27
  11.7 0.8 %collective-permute-start.3 = (f32[1,4480]{1,0:T(1,128)S(1)}, f32[1,4480]{1,0:T(1,128)S(1)}, u32[]{:S(2)}, u32[]{:S(2)}) collective-permute-start(f32[1,4480]{1,0:T(1,128)S(1)} %add_add_fusion.1), channel_id=1, source_target_pairs={{0,4},{1,5},{2,6},{3,7},{4,0},{5,1},{6,2},{7,3},{8,12},{9,13},{10,... | collective-permute-start | bytes 53768 | tf_op jit(solution)/shard_map/ppermute | solution.py:27
  12.5 1.4 %collective-permute-done.5 = f32[1,4480]{1,0:T(1,128)S(1)} collective-permute-done((f32[1,4480]{1,0:T(1,128)S(1)}, f32[1,4480]{1,0:T(1,128)S(1)}, u32[]{:S(2)}, u32[]{:S(2)}) %collective-permute-start.5) | collective-permute-done | bytes 17952 | tf_op jit(solution)/shard_map/ppermute | solution.py:27
  13.8 2.5 %collective-permute-done.4 = f32[1,4480]{1,0:T(1,128)S(1)} collective-permute-done((f32[1,4480]{1,0:T(1,128)S(1)}, f32[1,4480]{1,0:T(1,128)S(1)}, u32[]{:S(2)}, u32[]{:S(2)}) %collective-permute-start.4) | collective-permute-done | bytes 17952 | tf_op jit(solution)/shard_map/ppermute | solution.py:27
  16.3 0.6 add_add_fusion.total_ref
  17.0 6.8 %shard_map.50 = (f32[32,2048]{1,0:T(8,128)}, f32[32,1152]{1,0:T(8,128)}) custom-call(f32[32,6144]{1,0:T(8,128)} %x_ref.1, f32[1,4480]{1,0:T(1,128)} %add_add_fusion.total_ref, s32[9,32]{1,0:T(8,128)} %offsets_ref.1), custom_call_target="tpu_custom_call" | custom-call | flops 25395200 | bytes 983040 | tf_op jit(solution)/shard_map/pallas_call | solution.py:88
  23.8 1.7 %collective-permute-done.6 = f32[32,2048]{1,0:T(8,128)S(1)} collective-permute-done((f32[32,2048]{1,0:T(8,128)}, f32[32,2048]{1,0:T(8,128)S(1)}, u32[]{:S(2)}, u32[]{:S(2)}) %collective-permute-start.6) | collective-permute-done | bytes 262176 | tf_op jit(solution)/shard_map/ppermute | solution.py:22
  25.5 1.0 %broadcast_select_fusion.1 = (f32[32,2048]{1,0:T(8,128)S(1)}, f32[32,2048]{1,0:T(8,128)S(1)}) fusion(f32[32,2048]{1,0:T(8,128)S(1)} %collective-permute-done.6, f32[32,2048]{1,0:T(8,128)} %get-tuple-element.16, pred[]{:T(512)S(6)} %eq.411), kind=kLoop, calls=%fused_computation.101 | loop fusion | flops 131072 | bytes 1048577 | tf_op jit(solution)/shard_map/jit(_where)/select_n | solution.py:168
  27.6 0.8 %collective-permute-start.8 = (f32[32,1792]{1,0:T(8,128)S(1)}, f32[32,1792]{1,0:T(8,128)S(1)}, u32[]{:S(2)}, u32[]{:S(2)}) collective-permute-start(f32[32,1792]{1,0:T(8,128)S(1)} %fusion.2), channel_id=1, source_target_pairs={{0,2},{1,3},{2,0},{3,1},{4,6},{5,7},{6,4},{7,5},{8,10},{9,11},{10,... | collective-permute-start | bytes 688136 | tf_op jit(solution)/shard_map/ppermute | solution.py:22
  28.5 1.3 %collective-permute-done.7 = f32[32,1152]{1,0:T(8,128)S(1)} collective-permute-done((f32[32,1152]{1,0:T(8,128)S(1)}, f32[32,1152]{1,0:T(8,128)S(1)}, u32[]{:S(2)}, u32[]{:S(2)}) %collective-permute-start.7) | collective-permute-done | bytes 147488 | tf_op jit(solution)/shard_map/ppermute | solution.py:22
  29.8 5.5 %collective-permute-done.8 = f32[32,1792]{1,0:T(8,128)S(1)} collective-permute-done((f32[32,1792]{1,0:T(8,128)S(1)}, f32[32,1792]{1,0:T(8,128)S(1)}, u32[]{:S(2)}, u32[]{:S(2)}) %collective-permute-start.8) | collective-permute-done | bytes 229408 | tf_op jit(solution)/shard_map/ppermute | solution.py:22
  37.3 0.8 %collective-permute-start.9 = (f32[32,1152]{1,0:T(8,128)S(1)}, f32[32,1152]{1,0:T(8,128)S(1)}, u32[]{:S(2)}, u32[]{:S(2)}) collective-permute-start(f32[32,1152]{1,0:T(8,128)S(1)} %fusion.16), channel_id=1, source_target_pairs={{0,2},{1,3},{2,0},{3,1},{4,6},{5,7},{6,4},{7,5},{8,10},{9,11},{10,... | collective-permute-start | bytes 442376 | tf_op jit(solution)/shard_map/ppermute | solution.py:22
  38.2 4.4 %collective-permute-done.9 = f32[32,1152]{1,0:T(8,128)S(1)} collective-permute-done((f32[32,1152]{1,0:T(8,128)S(1)}, f32[32,1152]{1,0:T(8,128)S(1)}, u32[]{:S(2)}, u32[]{:S(2)}) %collective-permute-start.9) | collective-permute-done | bytes 147488 | tf_op jit(solution)/shard_map/ppermute | solution.py:22
  43.5 2.1 %collective-permute-start.12 = (f32[32,1280]{1,0:T(8,128)S(1)}, f32[32,1280]{1,0:T(8,128)S(1)}, u32[]{:S(2)}, u32[]{:S(2)}) collective-permute-start(f32[32,1280]{1,0:T(8,128)S(1)} %fusion.12), channel_id=1, source_target_pairs={{0,8},{1,9},{2,10},{3,11},{4,12},{5,13},{6,14},{7,15},{8,0},{9,1},... | collective-permute-start | bytes 491528 | tf_op jit(solution)/shard_map/ppermute | solution.py:22
  46.5 2.1 %collective-permute-start.11 = (f32[32,1152]{1,0:T(8,128)S(1)}, f32[32,1152]{1,0:T(8,128)S(1)}, u32[]{:S(2)}, u32[]{:S(2)}) collective-permute-start(f32[32,1152]{1,0:T(8,128)S(1)} %fusion.15), channel_id=1, source_target_pairs={{0,4},{1,5},{2,6},{3,7},{4,0},{5,1},{6,2},{7,3},{8,12},{9,13},{10,... | collective-permute-start | bytes 442376 | tf_op jit(solution)/shard_map/ppermute | solution.py:22
  48.7 4.1 %collective-permute-done.11 = f32[32,1152]{1,0:T(8,128)S(1)} collective-permute-done((f32[32,1152]{1,0:T(8,128)S(1)}, f32[32,1152]{1,0:T(8,128)S(1)}, u32[]{:S(2)}, u32[]{:S(2)}) %collective-permute-start.11) | collective-permute-done | bytes 147488 | tf_op jit(solution)/shard_map/ppermute | solution.py:22
  54.6 1.5 %collective-permute-start.13 = (f32[32,1152]{1,0:T(8,128)S(1)}, f32[32,1152]{1,0:T(8,128)S(1)}, u32[]{:S(2)}, u32[]{:S(2)}) collective-permute-start(f32[32,1152]{1,0:T(8,128)S(1)} %fusion.14), channel_id=1, source_target_pairs={{0,8},{1,9},{2,10},{3,11},{4,12},{5,13},{6,14},{7,15},{8,0},{9,1},... | collective-permute-start | bytes 442376 | tf_op jit(solution)/shard_map/ppermute | solution.py:22
  56.5 5.8 %collective-permute-done.13 = f32[32,1152]{1,0:T(8,128)S(1)} collective-permute-done((f32[32,1152]{1,0:T(8,128)S(1)}, f32[32,1152]{1,0:T(8,128)S(1)}, u32[]{:S(2)}, u32[]{:S(2)}) %collective-permute-start.13) | collective-permute-done | bytes 147488 | tf_op jit(solution)/shard_map/ppermute | solution.py:22
  63.4 1.0 %convolution_reduce_fusion = f32[512,128]{1,0:T(8,128)S(1)} fusion(f32[512,256,1]{1,0,2:T(8,128)S(1)} %bitcast.85, f32[8,128,256]{2,1,0:T(8,128)S(1)} %bitcast.84), kind=kOutput, calls=%fused_computation | convolution fusion | flops 805765120 | bytes 1835008 | tf_op jit(solution)/shard_map/dot_general | solution.py:137
  64.6 0.8 %collective-permute-start.15 = (f32[2048]{0:T(1024)S(1)}, f32[2048]{0:T(1024)S(1)}, u32[]{:S(2)}, u32[]{:S(2)}) collective-permute-start(f32[2048]{0:T(1024)S(1)} %reduce_max.19), channel_id=1, source_target_pairs={{0,2},{1,3},{2,0},{3,1},{4,6},{5,7},{6,4},{7,5},{8,10},{9,11},{10,... | collective-permute-start | bytes 24584 | tf_op jit(solution)/shard_map/ppermute | solution.py:27
  65.4 1.1 %collective-permute-start.14 = (f32[2048]{0:T(1024)S(1)}, f32[2048]{0:T(1024)S(1)}, u32[]{:S(2)}, u32[]{:S(2)}) collective-permute-start(f32[2048]{0:T(1024)S(1)} %reduce_max.19), channel_id=1, source_target_pairs={{0,1},{1,0},{2,3},{3,2},{4,5},{5,4},{6,7},{7,6},{8,9},{9,8},{10,11... | collective-permute-start | bytes 24584 | tf_op jit(solution)/shard_map/ppermute | solution.py:27
  66.5 1.2 %collective-permute-done.16 = f32[2048]{0:T(1024)S(1)} collective-permute-done((f32[2048]{0:T(1024)S(1)}, f32[2048]{0:T(1024)S(1)}, u32[]{:S(2)}, u32[]{:S(2)}) %collective-permute-start.16) | collective-permute-done | bytes 8224 | tf_op jit(solution)/shard_map/ppermute | solution.py:27
  67.7 0.7 collective-permute-done.15
  68.4 2.4 %collective-permute-start.19 = (f32[2048]{0:T(1024)S(1)}, f32[2048]{0:T(1024)S(1)}, u32[]{:S(2)}, u32[]{:S(2)}) collective-permute-start(f32[2048]{0:T(1024)S(1)} %maximum_maximum_fusion.1), channel_id=1, source_target_pairs={{0,12},{1,13},{2,14},{3,15},{4,8},{5,9},{6,10},{7,11},{8,4},{9,5},... | collective-permute-start | bytes 24584 | tf_op jit(solution)/shard_map/ppermute | solution.py:27
  70.8 2.1 %collective-permute-start.17 = (f32[2048]{0:T(1024)S(1)}, f32[2048]{0:T(1024)S(1)}, u32[]{:S(2)}, u32[]{:S(2)}) collective-permute-start(f32[2048]{0:T(1024)S(1)} %maximum_maximum_fusion.1), channel_id=1, source_target_pairs={{0,4},{1,5},{2,6},{3,7},{4,0},{5,1},{6,2},{7,3},{8,12},{9,13},{10,... | collective-permute-start | bytes 24584 | tf_op jit(solution)/shard_map/ppermute | solution.py:27
  72.8 1.1 %collective-permute-done.19 = f32[2048]{0:T(1024)S(1)} collective-permute-done((f32[2048]{0:T(1024)S(1)}, f32[2048]{0:T(1024)S(1)}, u32[]{:S(2)}, u32[]{:S(2)}) %collective-permute-start.19) | collective-permute-done | bytes 8224 | tf_op jit(solution)/shard_map/ppermute | solution.py:27
  73.9 1.4 %collective-permute-done.18 = f32[2048]{0:T(1024)S(1)} collective-permute-done((f32[2048]{0:T(1024)S(1)}, f32[2048]{0:T(1024)S(1)}, u32[]{:S(2)}, u32[]{:S(2)}) %collective-permute-start.18) | collective-permute-done | bytes 8224 | tf_op jit(solution)/shard_map/ppermute | solution.py:27
  75.3 0.6 maximum_maximum_fusion
  (118 shorter events, 8.5 us)
Async XLA Ops:
  0.6 23.1 %copy-start.2 = (s32[9,32]{1,0:T(8,128)S(1)}, s32[9,32]{1,0:T(8,128)}, u32[]{:S(2)}) copy-start(s32[9,32]{1,0:T(8,128)} %offsets_ref.1) | copy-start | bytes 3460
  1.8 4.7 %collective-permute-start.1 = (f32[1,4480]{1,0:T(1,128)S(1)}, f32[1,4480]{1,0:T(1,128)S(1)}, u32[]{:S(2)}, u32[]{:S(2)}) collective-permute-start(f32[1,4480]{1,0:T(1,128)S(1)} %broadcast_in_dim.527), channel_id=1, source_target_pairs={{0,2},{1,3},{2,0},{3,1},{4,6},{5,7},{6,4},{7,5},{8,10},{9,11},{10,... | collective-permute-start | bytes 53768 | tf_op jit(solution)/shard_map/ppermute | solution.py:27
  4.8 3.2 %collective-permute-start.2 = (f32[1,4480]{1,0:T(1,128)S(1)}, f32[1,4480]{1,0:T(1,128)S(1)}, u32[]{:S(2)}, u32[]{:S(2)}) collective-permute-start(f32[1,4480]{1,0:T(1,128)S(1)} %broadcast_in_dim.527), channel_id=1, source_target_pairs={{0,3},{1,2},{2,1},{3,0},{4,7},{5,6},{6,5},{7,4},{8,11},{9,10},{10,... | collective-permute-start | bytes 53768 | tf_op jit(solution)/shard_map/ppermute | solution.py:27
  4.8 3.2 %collective-permute-start = (f32[1,4480]{1,0:T(1,128)S(1)}, f32[1,4480]{1,0:T(1,128)S(1)}, u32[]{:S(2)}, u32[]{:S(2)}) collective-permute-start(f32[1,4480]{1,0:T(1,128)S(1)} %broadcast_in_dim.527), channel_id=1, source_target_pairs={{0,1},{1,0},{2,3},{3,2},{4,5},{5,4},{6,7},{7,6},{8,9},{9,8},{10,11... | collective-permute-start | bytes 53768 | tf_op jit(solution)/shard_map/ppermute | solution.py:27
  8.0 5.8 %collective-permute-start.5 = (f32[1,4480]{1,0:T(1,128)S(1)}, f32[1,4480]{1,0:T(1,128)S(1)}, u32[]{:S(2)}, u32[]{:S(2)}) collective-permute-start(f32[1,4480]{1,0:T(1,128)S(1)} %add_add_fusion.1), channel_id=1, source_target_pairs={{0,12},{1,13},{2,14},{3,15},{4,8},{5,9},{6,10},{7,11},{8,4},{9,5},... | collective-permute-start | bytes 53768 | tf_op jit(solution)/shard_map/ppermute | solution.py:27
  11.7 4.7 %collective-permute-start.4 = (f32[1,4480]{1,0:T(1,128)S(1)}, f32[1,4480]{1,0:T(1,128)S(1)}, u32[]{:S(2)}, u32[]{:S(2)}) collective-permute-start(f32[1,4480]{1,0:T(1,128)S(1)} %add_add_fusion.1), channel_id=1, source_target_pairs={{0,8},{1,9},{2,10},{3,11},{4,12},{5,13},{6,14},{7,15},{8,0},{9,1},... | collective-permute-start | bytes 53768 | tf_op jit(solution)/shard_map/ppermute | solution.py:27
  11.7 4.7 %collective-permute-start.3 = (f32[1,4480]{1,0:T(1,128)S(1)}, f32[1,4480]{1,0:T(1,128)S(1)}, u32[]{:S(2)}, u32[]{:S(2)}) collective-permute-start(f32[1,4480]{1,0:T(1,128)S(1)} %add_add_fusion.1), channel_id=1, source_target_pairs={{0,4},{1,5},{2,6},{3,7},{4,0},{5,1},{6,2},{7,3},{8,12},{9,13},{10,... | collective-permute-start | bytes 53768 | tf_op jit(solution)/shard_map/ppermute | solution.py:27
  23.8 1.7 %collective-permute-start.6 = (f32[32,2048]{1,0:T(8,128)}, f32[32,2048]{1,0:T(8,128)S(1)}, u32[]{:S(2)}, u32[]{:S(2)}) collective-permute-start(f32[32,2048]{1,0:T(8,128)} %get-tuple-element.16), channel_id=1, source_target_pairs={{0,1},{1,0},{2,3},{3,2},{4,5},{5,4},{6,7},{7,6},{8,9},{9,8},{10,11... | collective-permute-start | bytes 786440 | tf_op jit(solution)/shard_map/ppermute | solution.py:22
  27.3 1.1 %copy-start.1 = (f32[32,1152]{1,0:T(8,128)S(1)}, f32[32,1152]{1,0:T(8,128)}, u32[]{:S(2)}) copy-start(f32[32,1152]{1,0:T(8,128)} %get-tuple-element.17) | copy-start | bytes 442372
  27.3 1.1 %copy-start.3 = (s32[8]{0:T(128)S(1)}, s32[8]{0:T(128)}, u32[]{:S(2)}) copy-start(s32[8]{0:T(128)} %param.5) | copy-start | bytes 100
  27.6 7.7 %collective-permute-start.8 = (f32[32,1792]{1,0:T(8,128)S(1)}, f32[32,1792]{1,0:T(8,128)S(1)}, u32[]{:S(2)}, u32[]{:S(2)}) collective-permute-start(f32[32,1792]{1,0:T(8,128)S(1)} %fusion.2), channel_id=1, source_target_pairs={{0,2},{1,3},{2,0},{3,1},{4,6},{5,7},{6,4},{7,5},{8,10},{9,11},{10,... | collective-permute-start | bytes 688136 | tf_op jit(solution)/shard_map/ppermute | solution.py:22
  28.4 1.4 %collective-permute-start.7 = (f32[32,1152]{1,0:T(8,128)S(1)}, f32[32,1152]{1,0:T(8,128)S(1)}, u32[]{:S(2)}, u32[]{:S(2)}) collective-permute-start(f32[32,1152]{1,0:T(8,128)S(1)} %copy-done.1), channel_id=1, source_target_pairs={{0,1},{1,0},{2,3},{3,2},{4,5},{5,4},{6,7},{7,6},{8,9},{9,8},{10,11... | collective-permute-start | bytes 442376 | tf_op jit(solution)/shard_map/ppermute | solution.py:22
  36.3 6.2 %collective-permute-start.10 = (f32[32,1536]{1,0:T(8,128)S(1)}, f32[32,1536]{1,0:T(8,128)S(1)}, u32[]{:S(2)}, u32[]{:S(2)}) collective-permute-start(f32[32,1536]{1,0:T(8,128)S(1)} %fusion.3), channel_id=1, source_target_pairs={{0,4},{1,5},{2,6},{3,7},{4,0},{5,1},{6,2},{7,3},{8,12},{9,13},{10,... | collective-permute-start | bytes 589832 | tf_op jit(solution)/shard_map/ppermute | solution.py:22
  37.3 5.2 %collective-permute-start.9 = (f32[32,1152]{1,0:T(8,128)S(1)}, f32[32,1152]{1,0:T(8,128)S(1)}, u32[]{:S(2)}, u32[]{:S(2)}) collective-permute-start(f32[32,1152]{1,0:T(8,128)S(1)} %fusion.16), channel_id=1, source_target_pairs={{0,2},{1,3},{2,0},{3,1},{4,6},{5,7},{6,4},{7,5},{8,10},{9,11},{10,... | collective-permute-start | bytes 442376 | tf_op jit(solution)/shard_map/ppermute | solution.py:22
  43.5 9.3 %collective-permute-start.12 = (f32[32,1280]{1,0:T(8,128)S(1)}, f32[32,1280]{1,0:T(8,128)S(1)}, u32[]{:S(2)}, u32[]{:S(2)}) collective-permute-start(f32[32,1280]{1,0:T(8,128)S(1)} %fusion.12), channel_id=1, source_target_pairs={{0,8},{1,9},{2,10},{3,11},{4,12},{5,13},{6,14},{7,15},{8,0},{9,1},... | collective-permute-start | bytes 491528 | tf_op jit(solution)/shard_map/ppermute | solution.py:22
  46.5 6.2 %collective-permute-start.11 = (f32[32,1152]{1,0:T(8,128)S(1)}, f32[32,1152]{1,0:T(8,128)S(1)}, u32[]{:S(2)}, u32[]{:S(2)}) collective-permute-start(f32[32,1152]{1,0:T(8,128)S(1)} %fusion.15), channel_id=1, source_target_pairs={{0,4},{1,5},{2,6},{3,7},{4,0},{5,1},{6,2},{7,3},{8,12},{9,13},{10,... | collective-permute-start | bytes 442376 | tf_op jit(solution)/shard_map/ppermute | solution.py:22
  54.6 7.7 %collective-permute-start.13 = (f32[32,1152]{1,0:T(8,128)S(1)}, f32[32,1152]{1,0:T(8,128)S(1)}, u32[]{:S(2)}, u32[]{:S(2)}) collective-permute-start(f32[32,1152]{1,0:T(8,128)S(1)} %fusion.14), channel_id=1, source_target_pairs={{0,8},{1,9},{2,10},{3,11},{4,12},{5,13},{6,14},{7,15},{8,0},{9,1},... | collective-permute-start | bytes 442376 | tf_op jit(solution)/shard_map/ppermute | solution.py:22
  64.5 11.4 %copy-start = (f32[32,2048]{1,0:T(8,128)}, f32[32,2048]{1,0:T(8,128)S(1)}, u32[]{:S(2)}) copy-start(f32[32,2048]{1,0:T(8,128)S(1)} %reshape.485) | copy-start | bytes 786436
  64.6 3.1 %collective-permute-start.16 = (f32[2048]{0:T(1024)S(1)}, f32[2048]{0:T(1024)S(1)}, u32[]{:S(2)}, u32[]{:S(2)}) collective-permute-start(f32[2048]{0:T(1024)S(1)} %reduce_max.19), channel_id=1, source_target_pairs={{0,3},{1,2},{2,1},{3,0},{4,7},{5,6},{6,5},{7,4},{8,11},{9,10},{10,... | collective-permute-start | bytes 24584 | tf_op jit(solution)/shard_map/ppermute | solution.py:27
  64.6 3.7 %collective-permute-start.15 = (f32[2048]{0:T(1024)S(1)}, f32[2048]{0:T(1024)S(1)}, u32[]{:S(2)}, u32[]{:S(2)}) collective-permute-start(f32[2048]{0:T(1024)S(1)} %reduce_max.19), channel_id=1, source_target_pairs={{0,2},{1,3},{2,0},{3,1},{4,6},{5,7},{6,4},{7,5},{8,10},{9,11},{10,... | collective-permute-start | bytes 24584 | tf_op jit(solution)/shard_map/ppermute | solution.py:27
  65.4 2.9 %collective-permute-start.14 = (f32[2048]{0:T(1024)S(1)}, f32[2048]{0:T(1024)S(1)}, u32[]{:S(2)}, u32[]{:S(2)}) collective-permute-start(f32[2048]{0:T(1024)S(1)} %reduce_max.19), channel_id=1, source_target_pairs={{0,1},{1,0},{2,3},{3,2},{4,5},{5,4},{6,7},{7,6},{8,9},{9,8},{10,11... | collective-permute-start | bytes 24584 | tf_op jit(solution)/shard_map/ppermute | solution.py:27
  68.4 5.5 %collective-permute-start.19 = (f32[2048]{0:T(1024)S(1)}, f32[2048]{0:T(1024)S(1)}, u32[]{:S(2)}, u32[]{:S(2)}) collective-permute-start(f32[2048]{0:T(1024)S(1)} %maximum_maximum_fusion.1), channel_id=1, source_target_pairs={{0,12},{1,13},{2,14},{3,15},{4,8},{5,9},{6,10},{7,11},{8,4},{9,5},... | collective-permute-start | bytes 24584 | tf_op jit(solution)/shard_map/ppermute | solution.py:27
  70.8 4.5 %collective-permute-start.18 = (f32[2048]{0:T(1024)S(1)}, f32[2048]{0:T(1024)S(1)}, u32[]{:S(2)}, u32[]{:S(2)}) collective-permute-start(f32[2048]{0:T(1024)S(1)} %maximum_maximum_fusion.1), channel_id=1, source_target_pairs={{0,8},{1,9},{2,10},{3,11},{4,12},{5,13},{6,14},{7,15},{8,0},{9,1},... | collective-permute-start | bytes 24584 | tf_op jit(solution)/shard_map/ppermute | solution.py:27
  70.8 4.5 %collective-permute-start.17 = (f32[2048]{0:T(1024)S(1)}, f32[2048]{0:T(1024)S(1)}, u32[]{:S(2)}, u32[]{:S(2)}) collective-permute-start(f32[2048]{0:T(1024)S(1)} %maximum_maximum_fusion.1), channel_id=1, source_target_pairs={{0,4},{1,5},{2,6},{3,7},{4,0},{5,1},{6,2},{7,3},{8,12},{9,13},{10,... | collective-permute-start | bytes 24584 | tf_op jit(solution)/shard_map/ppermute | solution.py:27

commit v15 on v13

--- a/solution.py
+++ b/solution.py
@@ -13,7 +13,7 @@
 SHIFT = 256
 TAPS = 128
 TEMPLATES = 8
-TAIL_WIDTH = 1152
+LATER_WIDTHS = (768, 1024)
 
 
 def from_partner(value, axis, distance):
@@ -51,7 +51,7 @@
     return current
 
 
-def local_tree_kernel(widths_seq, channels_all, x_ref, total_ref, offsets_ref, head_ref, tail_ref):
+def local_tree_kernel(widths_seq, channels_all, x_ref, total_ref, offsets_ref, *chunk_refs):
     rows = x_ref.shape[0]
     cur = x_ref[:, : widths_seq[0]] - total_ref[:, : widths_seq[0]] / channels_all
     row_id = lax.broadcasted_iota(jnp.int32, (rows, 1), 0)
@@ -75,24 +75,22 @@
             chosen = (amount >> bit_index & 1) == 1
             shifted = jnp.where(chosen, pltpu.roll(shifted, width - span, axis=1), shifted)
         cur = lower[:, :new_width] + shifted[:, :new_width]
-    head_width = head_ref.shape[1]
-    head_ref[...] = cur[:, :head_width]
-    tail_ref[...] = cur[:, head_width:]
-
-
-def local_tree(filterbank, channel_total, offsets, widths_seq, channels_all, tail_width):
+    start = 0
+    for chunk_ref in chunk_refs:
+        chunk_ref[...] = cur[:, start : start + chunk_ref.shape[1]]
+        start += chunk_ref.shape[1]
+
+
+def local_tree(filterbank, channel_total, offsets, widths_seq, channels_all, later_widths):
     rows = filterbank.shape[0]
     vmem = pl.BlockSpec(memory_space=pltpu.VMEM)
     work = rows * sum(widths_seq[:-1])
-    head_width = widths_seq[-1] - tail_width
+    chunk_widths = (widths_seq[-1] - sum(later_widths),) + tuple(later_widths)
     return pl.pallas_call(
         functools.partial(local_tree_kernel, tuple(widths_seq), float(channels_all)),
-        out_shape=(
-            jax.ShapeDtypeStruct((rows, head_width), jnp.float32),
-            jax.ShapeDtypeStruct((rows, tail_width), jnp.float32),
-        ),
+        out_shape=tuple(jax.ShapeDtypeStruct((rows, width), jnp.float32) for width in chunk_widths),
         in_specs=[vmem, vmem, vmem],
-        out_specs=(vmem, vmem),
+        out_specs=tuple(vmem for _ in chunk_widths),
         cost_estimate=pl.CostEstimate(
             flops=40 * work, transcendentals=0, bytes_accessed=4 * (rows * widths_seq[0] + rows * widths_seq[-1])
         ),
@@ -158,35 +156,51 @@
     partial_value = jnp.sum(filterbank[:, : length_after(0)], axis=0, keepdims=True)
     channel_total = butterfly(partial_value, "band", jnp.add)
     widths_seq = [length_after(section) for section in range(local_count + 1)]
-    head, tail = local_tree(filterbank, channel_total, offsets, widths_seq, channels_all, TAIL_WIDTH)
+    chunks = list(local_tree(filterbank, channel_total, offsets, widths_seq, channels_all, LATER_WIDTHS))
     band_index = lax.axis_index("band")
     bit_count = band_count.bit_length() - 1
-    tail_width = TAIL_WIDTH
+    chunk_count = len(chunks)
 
     def halves(own, partner, bit_index):
         upper_half = band_index // 2**bit_index % 2 == 1
         return jnp.where(upper_half, partner, own), jnp.where(upper_half, own, partner)
 
-    partner_head = from_partner(head, "band", 0)
-    for bit_index in range(bit_count):
-        amounts = offsets[local_count + bit_index]
-        tail, partner_head = lax.optimization_barrier((tail, partner_head))
-        lower_head, upper_head = halves(head, partner_head, bit_index)
-        head_width = head.shape[1] - SHIFT
-        new_head = lower_head[:, :head_width] + shift_rows(upper_head, amounts, head_width)
-        if bit_index + 1 < bit_count:
-            next_partner_head = from_partner(new_head, "band", bit_index + 1)
-            tail, new_head = lax.optimization_barrier((tail, new_head))
-        partner_tail = from_partner(tail, "band", bit_index)
-        if bit_index + 1 < bit_count:
-            partner_tail, next_partner_head = lax.optimization_barrier((partner_tail, next_partner_head))
-            partner_head = next_partner_head
-        lower_tail, upper_tail = halves(tail, partner_tail, bit_index)
-        lower_window = jnp.concatenate([lower_head[:, head_width:], lower_tail], axis=1)
-        upper_window = jnp.concatenate([upper_head[:, head_width:], upper_tail], axis=1)
-        tail = lower_window[:, :tail_width] + shift_rows(upper_window, amounts, tail_width)
-        head = new_head
-    current = jnp.concatenate([head, tail], axis=1)
+    own = {(0, k): chunks[k] for k in range(chunk_count)}
+    received = {}
+    edges = {}
+    final = {}
+    for wave in range(bit_count + chunk_count - 1):
+        cells = [(wave - k, k) for k in range(chunk_count) if 0 <= wave - k < bit_count]
+        for level, k in cells:
+            value = own[(level, k)]
+            if level == 0 and k > 0:
+                value, earlier = lax.optimization_barrier((value, received[(0, k - 1)]))
+                received[(0, k - 1)] = earlier
+            received[(level, k)] = from_partner(value, "band", level)
+        if len(cells) > 1:
+            grouped = lax.optimization_barrier(tuple(received[cell] for cell in cells))
+            for cell, value in zip(cells, grouped):
+                received[cell] = value
+        for level, k in cells:
+            amounts = offsets[local_count + level]
+            lower, upper = halves(own[(level, k)], received[(level, k)], level)
+            if k == 0:
+                width = lower.shape[1] - SHIFT
+                merged = lower[:, :width] + shift_rows(upper, amounts, width)
+                edge_lower, edge_upper = lower[:, width:], upper[:, width:]
+            else:
+                width = lower.shape[1]
+                prior_lower, prior_upper = edges[(level, k - 1)]
+                lower_window = jnp.concatenate([prior_lower, lower], axis=1)
+                upper_window = jnp.concatenate([prior_upper, upper], axis=1)
+                merged = lower_window[:, :width] + shift_rows(upper_window, amounts, width)
+                edge_lower, edge_upper = lower[:, width - SHIFT :], upper[:, width - SHIFT :]
+            edges[(level, k)] = (edge_lower, edge_upper)
+            if level + 1 < bit_count:
+                own[(level + 1, k)] = merged
+            else:
+                final[k] = merged
+    current = jnp.concatenate([final[k] for k in range(chunk_count)], axis=1)
     dedispersed = current * (1.0 / math.sqrt(channels_all))
     detection = boxcar_max(dedispersed, widths)
     peak_series = butterfly(jnp.max(detection, axis=0), "band", jnp.maximum)

time: 77.2 us -> 83.4 us (1.080)
  other arithmetic: 11.2 us -> 15 us
  starting transfers between devices: 19.3 us -> 22.5 us
  waiting for transfers between devices: 37 us -> 35.3 us
    ppermute x8 -> x12, starting transfers between devices: 5.28 us -> 8.46 us  [from_partner(): return lax.ppermute(value, axis, pairs)]
    select_n x56 -> x84, other arithmetic: 6.19 us -> 8.18 us  [shift_rows(): jnp.where(chosen, current[:, span:span + keep_len], current[:, :keep_len])]
    eq x2, other arithmetic: 0.04 us -> 1.64 us  [shift_rows(): chosen = (amounts >> bit_index & 1)[:, None] == 1]
    ppermute x12, waiting for transfers between devices: 10.7 us -> 9.33 us  [from_xor(): return lax.ppermute(value, axis, pairs)]
    ppermute x8 -> x12, waiting for transfers between devices: 26.4 us -> 25.9 us  [from_partner(): return lax.ppermute(value, axis, pairs)]
  transfers between devices with their start and end apart: 20 -> 24, of which waited for: 15 -> 16; matrix products, arithmetic and copies ran while one was open for 2% -> 10% of each run, Pallas kernels for 0% -> 0%
where the time goes in v15:
time: 83.4 us; the launch traced here: 83.1 us
  waiting for transfers between devices  35.3 us (42%)
  starting transfers between devices  22.5 us (27%)
  other arithmetic  15 us (18%)
  Pallas kernels  6.75 us (8%)
  between operations  1.6 us (2%)
  local copies, waits for them, and re-layouts  1.02 us (1%)
  matrix products  1.02 us (1%)
    ppermute x12, waiting for transfers between devices, from_partner(): return lax.ppermute(value, axis, pairs)  25.9 us
    ppermute x12, starting transfers between devices, from_xor(): return lax.ppermute(value, axis, pairs)  14 us
    ppermute x12, waiting for transfers between devices, from_xor(): return lax.ppermute(value, axis, pairs)  9.33 us
    ppermute x12, starting transfers between devices, from_partner(): return lax.ppermute(value, axis, pairs)  8.46 us
    select_n x84, other arithmetic, shift_rows(): jnp.where(chosen, current[:, span:span + keep_len], current[:, :keep_len])  8.18 us
    pallas_call x1, Pallas kernels, local_tree(): pl.pallas_call(functools.partial(local_tree_kernel, tuple(widths_seq), fl...  6.75 us
  transfers between devices with their start and end apart: 24, of which 16 were waited for; matrix products, arithmetic and copies ran while one was open for 10% of the time, Pallas kernels for 0%

profile of v15, /device:TPU:0, one launch (start us, length us, event | category | flops | bytes accessed | tf_op | source)
XLA Modules:
  0.0 83.1 jit_solution(12876090027307044560)
XLA Ops:
  0.6 1.1 %slice_reduce_fusion = f32[4480]{0:T(1024)S(1)} fusion(f32[32,6144]{1,0:T(8,128)} %x_ref.1), kind=kLoop, calls=%fused_computation.4 | loop fusion | flops 138880 | bytes 591360 | tf_op jit(solution)/shard_map/reduce_sum | solution.py:156
  1.8 3.0 %collective-permute-start.1 = (f32[1,4480]{1,0:T(1,128)S(1)}, f32[1,4480]{1,0:T(1,128)S(1)}, u32[]{:S(2)}, u32[]{:S(2)}) collective-permute-start(f32[1,4480]{1,0:T(1,128)S(1)} %broadcast_in_dim.743), channel_id=1, source_target_pairs={{0,2},{1,3},{2,0},{3,1},{4,6},{5,7},{6,4},{7,5},{8,10},{9,11},{10,... | collective-permute-start | bytes 53768 | tf_op jit(solution)/shard_map/ppermute | solution.py:27
  5.0 0.8 compare_bitcast_fusion.7
  5.8 0.8 compare_bitcast_fusion.6
  6.6 1.3 %collective-permute-done.2 = f32[1,4480]{1,0:T(1,128)S(1)} collective-permute-done((f32[1,4480]{1,0:T(1,128)S(1)}, f32[1,4480]{1,0:T(1,128)S(1)}, u32[]{:S(2)}, u32[]{:S(2)}) %collective-permute-start.2) | collective-permute-done | bytes 17952 | tf_op jit(solution)/shard_map/ppermute | solution.py:27
  8.0 3.7 %collective-permute-start.5 = (f32[1,4480]{1,0:T(1,128)S(1)}, f32[1,4480]{1,0:T(1,128)S(1)}, u32[]{:S(2)}, u32[]{:S(2)}) collective-permute-start(f32[1,4480]{1,0:T(1,128)S(1)} %add_add_fusion.1), channel_id=1, source_target_pairs={{0,12},{1,13},{2,14},{3,15},{4,8},{5,9},{6,10},{7,11},{8,4},{9,5},... | collective-permute-start | bytes 53768 | tf_op jit(solution)/shard_map/ppermute | solution.py:27
  11.7 0.8 collective-permute-start.3
  13.8 2.5 %collective-permute-done.4 = f32[1,4480]{1,0:T(1,128)S(1)} collective-permute-done((f32[1,4480]{1,0:T(1,128)S(1)}, f32[1,4480]{1,0:T(1,128)S(1)}, u32[]{:S(2)}, u32[]{:S(2)}) %collective-permute-start.4) | collective-permute-done | bytes 17952 | tf_op jit(solution)/shard_map/ppermute | solution.py:27
  17.0 6.8 %shard_map.50 = (f32[32,1408]{1,0:T(8,128)}, f32[32,768]{1,0:T(8,128)}, f32[32,1024]{1,0:T(8,128)}) custom-call(f32[32,6144]{1,0:T(8,128)} %x_ref.1, f32[1,4480]{1,0:T(1,128)} %add_add_fusion.total_ref, s32[9,32]{1,0:T(8,128)} %offsets_ref.1), custom_call_target="tpu_custom_call" | custom-call | flops 25395200 | bytes 983040 | tf_op jit(solution)/shard_map/pallas_call | solution.py:89
  23.7 1.6 %collective-permute-done.6 = f32[32,1408]{1,0:T(8,128)S(1)} collective-permute-done((f32[32,1408]{1,0:T(8,128)}, f32[32,1408]{1,0:T(8,128)S(1)}, u32[]{:S(2)}, u32[]{:S(2)}) %collective-permute-start.6) | collective-permute-done | bytes 180256 | tf_op jit(solution)/shard_map/ppermute | solution.py:22
  25.5 0.9 %broadcast_select_fusion.1 = (f32[32,1408]{1,0:T(8,128)S(1)}, f32[32,1408]{1,0:T(8,128)S(1)}) fusion(f32[32,1408]{1,0:T(8,128)S(1)} %collective-permute-done.6, f32[32,1408]{1,0:T(8,128)} %get-tuple-element.17, pred[]{:T(512)S(6)} %eq.452), kind=kLoop, calls=%fused_computation.146 | loop fusion | flops 90112 | bytes 720897 | tf_op jit(solution)/shard_map/jit(_where)/select_n | solution.py:166
  27.4 0.8 collective-permute-start.7
  28.3 5.3 %collective-permute-done.7 = f32[32,1152]{1,0:T(8,128)S(1)} collective-permute-done((f32[32,1152]{1,0:T(8,128)S(1)}, f32[32,1152]{1,0:T(8,128)S(1)}, u32[]{:S(2)}, u32[]{:S(2)}) %collective-permute-start.7) | collective-permute-done | bytes 147488 | tf_op jit(solution)/shard_map/ppermute | solution.py:22
  34.4 0.8 collective-permute-start.10
  36.2 2.9 %collective-permute-done.10 = f32[32,768]{1,0:T(8,128)S(1)} collective-permute-done((f32[32,768]{1,0:T(8,128)S(1)}, f32[32,768]{1,0:T(8,128)S(1)}, u32[]{:S(2)}, u32[]{:S(2)}) %collective-permute-start.10) | collective-permute-done | bytes 98336 | tf_op jit(solution)/shard_map/ppermute | solution.py:22
  39.1 2.6 %collective-permute-done.9 = f32[32,896]{1,0:T(8,128)S(1)} collective-permute-done((f32[32,896]{1,0:T(8,128)S(1)}, f32[32,896]{1,0:T(8,128)S(1)}, u32[]{:S(2)}, u32[]{:S(2)}) %collective-permute-start.9) | collective-permute-done | bytes 114720 | tf_op jit(solution)/shard_map/ppermute | solution.py:22
  42.5 2.1 %collective-permute-start.12 = (f32[32,640]{1,0:T(8,128)S(1)}, f32[32,640]{1,0:T(8,128)S(1)}, u32[]{:S(2)}, u32[]{:S(2)}) collective-permute-start(f32[32,640]{1,0:T(8,128)S(1)} %fusion.28), channel_id=1, source_target_pairs={{0,8},{1,9},{2,10},{3,11},{4,12},{5,13},{6,14},{7,15},{8,0},{9,1},... | collective-permute-start | bytes 245768 | tf_op jit(solution)/shard_map/ppermute | solution.py:22
  46.2 1.4 %collective-permute-start.14 = (f32[32,1024]{1,0:T(8,128)S(1)}, f32[32,1024]{1,0:T(8,128)S(1)}, u32[]{:S(2)}, u32[]{:S(2)}) collective-permute-start(f32[32,1024]{1,0:T(8,128)S(1)} %fusion.14), channel_id=1, source_target_pairs={{0,2},{1,3},{2,0},{3,1},{4,6},{5,7},{6,4},{7,5},{8,10},{9,11},{10,... | collective-permute-start | bytes 393224 | tf_op jit(solution)/shard_map/ppermute | solution.py:22
  48.4 0.8 collective-permute-done.12
  49.2 3.1 %collective-permute-done.13 = f32[32,768]{1,0:T(8,128)S(1)} collective-permute-done((f32[32,768]{1,0:T(8,128)S(1)}, f32[32,768]{1,0:T(8,128)S(1)}, u32[]{:S(2)}, u32[]{:S(2)}) %collective-permute-start.13) | collective-permute-done | bytes 98336 | tf_op jit(solution)/shard_map/ppermute | solution.py:22
  53.2 1.0 %collective-permute-start.15 = (f32[32,768]{1,0:T(8,128)S(1)}, f32[32,768]{1,0:T(8,128)S(1)}, u32[]{:S(2)}, u32[]{:S(2)}) collective-permute-start(f32[32,768]{1,0:T(8,128)S(1)} %fusion.25), channel_id=1, source_target_pairs={{0,8},{1,9},{2,10},{3,11},{4,12},{5,13},{6,14},{7,15},{8,0},{9,1},... | collective-permute-start | bytes 294920 | tf_op jit(solution)/shard_map/ppermute | solution.py:22
  56.2 3.6 %collective-permute-done.15 = f32[32,768]{1,0:T(8,128)S(1)} collective-permute-done((f32[32,768]{1,0:T(8,128)S(1)}, f32[32,768]{1,0:T(8,128)S(1)}, u32[]{:S(2)}, u32[]{:S(2)}) %collective-permute-start.15) | collective-permute-done | bytes 98336 | tf_op jit(solution)/shard_map/ppermute | solution.py:22
  59.8 0.9 %collective-permute-done.16 = f32[32,1024]{1,0:T(8,128)S(1)} collective-permute-done((f32[32,1024]{1,0:T(8,128)S(1)}, f32[32,1024]{1,0:T(8,128)S(1)}, u32[]{:S(2)}, u32[]{:S(2)}) %collective-permute-start.16) | collective-permute-done | bytes 131104 | tf_op jit(solution)/shard_map/ppermute | solution.py:22
  62.3 1.5 %collective-permute-start.17 = (f32[32,1024]{1,0:T(8,128)S(1)}, f32[32,1024]{1,0:T(8,128)S(1)}, u32[]{:S(2)}, u32[]{:S(2)}) collective-permute-start(f32[32,1024]{1,0:T(8,128)S(1)} %fusion.12), channel_id=1, source_target_pairs={{0,8},{1,9},{2,10},{3,11},{4,12},{5,13},{6,14},{7,15},{8,0},{9,1},... | collective-permute-start | bytes 393224 | tf_op jit(solution)/shard_map/ppermute | solution.py:22
  63.9 5.2 %collective-permute-done.17 = f32[32,1024]{1,0:T(8,128)S(1)} collective-permute-done((f32[32,1024]{1,0:T(8,128)S(1)}, f32[32,1024]{1,0:T(8,128)S(1)}, u32[]{:S(2)}, u32[]{:S(2)}) %collective-permute-start.17) | collective-permute-done | bytes 131104 | tf_op jit(solution)/shard_map/ppermute | solution.py:22
  70.2 1.0 %convolution_reduce_fusion = f32[512,128]{1,0:T(8,128)S(1)} fusion(f32[512,256,1]{1,0,2:T(8,128)S(1)} %bitcast.85, f32[8,128,256]{2,1,0:T(8,128)S(1)} %bitcast.84), kind=kOutput, calls=%fused_computation | convolution fusion | flops 805765120 | bytes 1835008 | tf_op jit(solution)/shard_map/dot_general | solution.py:135
  71.4 1.3 %collective-permute-start.19 = (f32[2048]{0:T(1024)S(1)}, f32[2048]{0:T(1024)S(1)}, u32[]{:S(2)}, u32[]{:S(2)}) collective-permute-start(f32[2048]{0:T(1024)S(1)} %reduce_max.19), channel_id=1, source_target_pairs={{0,2},{1,3},{2,0},{3,1},{4,6},{5,7},{6,4},{7,5},{8,10},{9,11},{10,... | collective-permute-start | bytes 24584 | tf_op jit(solution)/shard_map/ppermute | solution.py:27
  73.2 1.2 %collective-permute-done.20 = f32[2048]{0:T(1024)S(1)} collective-permute-done((f32[2048]{0:T(1024)S(1)}, f32[2048]{0:T(1024)S(1)}, u32[]{:S(2)}, u32[]{:S(2)}) %collective-permute-start.20) | collective-permute-done | bytes 8224 | tf_op jit(solution)/shard_map/ppermute | solution.py:27
  75.1 2.9 %collective-permute-start.23 = (f32[2048]{0:T(1024)S(1)}, f32[2048]{0:T(1024)S(1)}, u32[]{:S(2)}, u32[]{:S(2)}) collective-permute-start(f32[2048]{0:T(1024)S(1)} %maximum_maximum_fusion.1), channel_id=1, source_target_pairs={{0,12},{1,13},{2,14},{3,15},{4,8},{5,9},{6,10},{7,11},{8,4},{9,5},... | collective-permute-start | bytes 24584 | tf_op jit(solution)/shard_map/ppermute | solution.py:27
  78.0 1.6 %collective-permute-start.21 = (f32[2048]{0:T(1024)S(1)}, f32[2048]{0:T(1024)S(1)}, u32[]{:S(2)}, u32[]{:S(2)}) collective-permute-start(f32[2048]{0:T(1024)S(1)} %maximum_maximum_fusion.1), channel_id=1, source_target_pairs={{0,4},{1,5},{2,6},{3,7},{4,0},{5,1},{6,2},{7,3},{8,12},{9,13},{10,... | collective-permute-start | bytes 24584 | tf_op jit(solution)/shard_map/ppermute | solution.py:27
  79.6 1.1 %collective-permute-done.23 = f32[2048]{0:T(1024)S(1)} collective-permute-done((f32[2048]{0:T(1024)S(1)}, f32[2048]{0:T(1024)S(1)}, u32[]{:S(2)}, u32[]{:S(2)}) %collective-permute-start.23) | collective-permute-done | bytes 8224 | tf_op jit(solution)/shard_map/ppermute | solution.py:27
  80.6 1.9 %collective-permute-done.22 = f32[2048]{0:T(1024)S(1)} collective-permute-done((f32[2048]{0:T(1024)S(1)}, f32[2048]{0:T(1024)S(1)}, u32[]{:S(2)}, u32[]{:S(2)}) %collective-permute-start.22) | collective-permute-done | bytes 8224 | tf_op jit(solution)/shard_map/ppermute | solution.py:27
  (170 shorter events, 15.4 us)
Async XLA Ops:
  0.6 23.1 %copy-start.3 = (s32[8]{0:T(128)S(1)}, s32[8]{0:T(128)}, u32[]{:S(2)}) copy-start(s32[8]{0:T(128)} %param.5) | copy-start | bytes 100
  1.8 4.8 %collective-permute-start.1 = (f32[1,4480]{1,0:T(1,128)S(1)}, f32[1,4480]{1,0:T(1,128)S(1)}, u32[]{:S(2)}, u32[]{:S(2)}) collective-permute-start(f32[1,4480]{1,0:T(1,128)S(1)} %broadcast_in_dim.743), channel_id=1, source_target_pairs={{0,2},{1,3},{2,0},{3,1},{4,6},{5,7},{6,4},{7,5},{8,10},{9,11},{10,... | collective-permute-start | bytes 53768 | tf_op jit(solution)/shard_map/ppermute | solution.py:27
  4.8 3.2 %collective-permute-start.2 = (f32[1,4480]{1,0:T(1,128)S(1)}, f32[1,4480]{1,0:T(1,128)S(1)}, u32[]{:S(2)}, u32[]{:S(2)}) collective-permute-start(f32[1,4480]{1,0:T(1,128)S(1)} %broadcast_in_dim.743), channel_id=1, source_target_pairs={{0,3},{1,2},{2,1},{3,0},{4,7},{5,6},{6,5},{7,4},{8,11},{9,10},{10,... | collective-permute-start | bytes 53768 | tf_op jit(solution)/shard_map/ppermute | solution.py:27
  4.8 3.2 %collective-permute-start = (f32[1,4480]{1,0:T(1,128)S(1)}, f32[1,4480]{1,0:T(1,128)S(1)}, u32[]{:S(2)}, u32[]{:S(2)}) collective-permute-start(f32[1,4480]{1,0:T(1,128)S(1)} %broadcast_in_dim.743), channel_id=1, source_target_pairs={{0,1},{1,0},{2,3},{3,2},{4,5},{5,4},{6,7},{7,6},{8,9},{9,8},{10,11... | collective-permute-start | bytes 53768 | tf_op jit(solution)/shard_map/ppermute | solution.py:27
  8.0 5.8 %collective-permute-start.5 = (f32[1,4480]{1,0:T(1,128)S(1)}, f32[1,4480]{1,0:T(1,128)S(1)}, u32[]{:S(2)}, u32[]{:S(2)}) collective-permute-start(f32[1,4480]{1,0:T(1,128)S(1)} %add_add_fusion.1), channel_id=1, source_target_pairs={{0,12},{1,13},{2,14},{3,15},{4,8},{5,9},{6,10},{7,11},{8,4},{9,5},... | collective-permute-start | bytes 53768 | tf_op jit(solution)/shard_map/ppermute | solution.py:27
  11.7 4.7 %collective-permute-start.4 = (f32[1,4480]{1,0:T(1,128)S(1)}, f32[1,4480]{1,0:T(1,128)S(1)}, u32[]{:S(2)}, u32[]{:S(2)}) collective-permute-start(f32[1,4480]{1,0:T(1,128)S(1)} %add_add_fusion.1), channel_id=1, source_target_pairs={{0,8},{1,9},{2,10},{3,11},{4,12},{5,13},{6,14},{7,15},{8,0},{9,1},... | collective-permute-start | bytes 53768 | tf_op jit(solution)/shard_map/ppermute | solution.py:27
  11.7 4.7 %collective-permute-start.3 = (f32[1,4480]{1,0:T(1,128)S(1)}, f32[1,4480]{1,0:T(1,128)S(1)}, u32[]{:S(2)}, u32[]{:S(2)}) collective-permute-start(f32[1,4480]{1,0:T(1,128)S(1)} %add_add_fusion.1), channel_id=1, source_target_pairs={{0,4},{1,5},{2,6},{3,7},{4,0},{5,1},{6,2},{7,3},{8,12},{9,13},{10,... | collective-permute-start | bytes 53768 | tf_op jit(solution)/shard_map/ppermute | solution.py:27
  23.7 1.6 %collective-permute-start.6 = (f32[32,1408]{1,0:T(8,128)}, f32[32,1408]{1,0:T(8,128)S(1)}, u32[]{:S(2)}, u32[]{:S(2)}) collective-permute-start(f32[32,1408]{1,0:T(8,128)} %get-tuple-element.17), channel_id=1, source_target_pairs={{0,1},{1,0},{2,3},{3,2},{4,5},{5,4},{6,7},{7,6},{8,9},{9,8},{10,11... | collective-permute-start | bytes 540680 | tf_op jit(solution)/shard_map/ppermute | solution.py:22
  25.4 2.9 %collective-permute-start.8 = (f32[32,768]{1,0:T(8,128)}, f32[32,768]{1,0:T(8,128)S(1)}, u32[]{:S(2)}, u32[]{:S(2)}) collective-permute-start(f32[32,768]{1,0:T(8,128)} %get-tuple-element.19), channel_id=1, source_target_pairs={{0,1},{1,0},{2,3},{3,2},{4,5},{5,4},{6,7},{7,6},{8,9},{9,8},{10,11... | collective-permute-start | bytes 294920 | tf_op jit(solution)/shard_map/ppermute | solution.py:22
  26.9 6.7 %copy-start.2 = (f32[32,768]{1,0:T(8,128)S(1)}, f32[32,768]{1,0:T(8,128)}, u32[]{:S(2)}) copy-start(f32[32,768]{1,0:T(8,128)} %get-tuple-element.19) | copy-start | bytes 294916
  27.4 6.2 %collective-permute-start.7 = (f32[32,1152]{1,0:T(8,128)S(1)}, f32[32,1152]{1,0:T(8,128)S(1)}, u32[]{:S(2)}, u32[]{:S(2)}) collective-permute-start(f32[32,1152]{1,0:T(8,128)S(1)} %fusion.10), channel_id=1, source_target_pairs={{0,2},{1,3},{2,0},{3,1},{4,6},{5,7},{6,4},{7,5},{8,10},{9,11},{10,... | collective-permute-start | bytes 442376 | tf_op jit(solution)/shard_map/ppermute | solution.py:22
  33.8 1.4 %copy-start.1 = (f32[32,1024]{1,0:T(8,128)S(1)}, f32[32,1024]{1,0:T(8,128)}, u32[]{:S(2)}) copy-start(f32[32,1024]{1,0:T(8,128)} %get-tuple-element.23) | copy-start | bytes 393220
  34.4 4.7 %collective-permute-start.10 = (f32[32,768]{1,0:T(8,128)S(1)}, f32[32,768]{1,0:T(8,128)S(1)}, u32[]{:S(2)}, u32[]{:S(2)}) collective-permute-start(f32[32,768]{1,0:T(8,128)S(1)} %fusion.27), channel_id=1, source_target_pairs={{0,2},{1,3},{2,0},{3,1},{4,6},{5,7},{6,4},{7,5},{8,10},{9,11},{10,... | collective-permute-start | bytes 294920 | tf_op jit(solution)/shard_map/ppermute | solution.py:22
  35.2 6.5 %collective-permute-start.11 = (f32[32,1024]{1,0:T(8,128)S(1)}, f32[32,1024]{1,0:T(8,128)S(1)}, u32[]{:S(2)}, u32[]{:S(2)}) collective-permute-start(f32[32,1024]{1,0:T(8,128)S(1)} %copy-done.1), channel_id=1, source_target_pairs={{0,1},{1,0},{2,3},{3,2},{4,5},{5,4},{6,7},{7,6},{8,9},{9,8},{10,11... | collective-permute-start | bytes 393224 | tf_op jit(solution)/shard_map/ppermute | solution.py:22
  36.1 5.6 %collective-permute-start.9 = (f32[32,896]{1,0:T(8,128)S(1)}, f32[32,896]{1,0:T(8,128)S(1)}, u32[]{:S(2)}, u32[]{:S(2)}) collective-permute-start(f32[32,896]{1,0:T(8,128)S(1)} %fusion.23), channel_id=1, source_target_pairs={{0,4},{1,5},{2,6},{3,7},{4,0},{5,1},{6,2},{7,3},{8,12},{9,13},{10,... | collective-permute-start | bytes 344072 | tf_op jit(solution)/shard_map/ppermute | solution.py:22
  42.5 6.7 %collective-permute-start.12 = (f32[32,640]{1,0:T(8,128)S(1)}, f32[32,640]{1,0:T(8,128)S(1)}, u32[]{:S(2)}, u32[]{:S(2)}) collective-permute-start(f32[32,640]{1,0:T(8,128)S(1)} %fusion.28), channel_id=1, source_target_pairs={{0,8},{1,9},{2,10},{3,11},{4,12},{5,13},{6,14},{7,15},{8,0},{9,1},... | collective-permute-start | bytes 245768 | tf_op jit(solution)/shard_map/ppermute | solution.py:22
  46.2 6.1 %collective-permute-start.14 = (f32[32,1024]{1,0:T(8,128)S(1)}, f32[32,1024]{1,0:T(8,128)S(1)}, u32[]{:S(2)}, u32[]{:S(2)}) collective-permute-start(f32[32,1024]{1,0:T(8,128)S(1)} %fusion.14), channel_id=1, source_target_pairs={{0,2},{1,3},{2,0},{3,1},{4,6},{5,7},{6,4},{7,5},{8,10},{9,11},{10,... | collective-permute-start | bytes 393224 | tf_op jit(solution)/shard_map/ppermute | solution.py:22
  47.7 4.7 %collective-permute-start.13 = (f32[32,768]{1,0:T(8,128)S(1)}, f32[32,768]{1,0:T(8,128)S(1)}, u32[]{:S(2)}, u32[]{:S(2)}) collective-permute-start(f32[32,768]{1,0:T(8,128)S(1)} %fusion.26), channel_id=1, source_target_pairs={{0,4},{1,5},{2,6},{3,7},{4,0},{5,1},{6,2},{7,3},{8,12},{9,13},{10,... | collective-permute-start | bytes 294920 | tf_op jit(solution)/shard_map/ppermute | solution.py:22
  53.2 6.6 %collective-permute-start.15 = (f32[32,768]{1,0:T(8,128)S(1)}, f32[32,768]{1,0:T(8,128)S(1)}, u32[]{:S(2)}, u32[]{:S(2)}) collective-permute-start(f32[32,768]{1,0:T(8,128)S(1)} %fusion.25), channel_id=1, source_target_pairs={{0,8},{1,9},{2,10},{3,11},{4,12},{5,13},{6,14},{7,15},{8,0},{9,1},... | collective-permute-start | bytes 294920 | tf_op jit(solution)/shard_map/ppermute | solution.py:22
  55.0 5.6 %collective-permute-start.16 = (f32[32,1024]{1,0:T(8,128)S(1)}, f32[32,1024]{1,0:T(8,128)S(1)}, u32[]{:S(2)}, u32[]{:S(2)}) collective-permute-start(f32[32,1024]{1,0:T(8,128)S(1)} %fusion.13), channel_id=1, source_target_pairs={{0,4},{1,5},{2,6},{3,7},{4,0},{5,1},{6,2},{7,3},{8,12},{9,13},{10,... | collective-permute-start | bytes 393224 | tf_op jit(solution)/shard_map/ppermute | solution.py:22
  62.3 6.8 %collective-permute-start.17 = (f32[32,1024]{1,0:T(8,128)S(1)}, f32[32,1024]{1,0:T(8,128)S(1)}, u32[]{:S(2)}, u32[]{:S(2)}) collective-permute-start(f32[32,1024]{1,0:T(8,128)S(1)} %fusion.12), channel_id=1, source_target_pairs={{0,8},{1,9},{2,10},{3,11},{4,12},{5,13},{6,14},{7,15},{8,0},{9,1},... | collective-permute-start | bytes 393224 | tf_op jit(solution)/shard_map/ppermute | solution.py:22
  71.2 11.9 %copy-start = (f32[32,2048]{1,0:T(8,128)}, f32[32,2048]{1,0:T(8,128)S(1)}, u32[]{:S(2)}) copy-start(f32[32,2048]{1,0:T(8,128)S(1)} %reshape.485) | copy-start | bytes 786436
  71.3 3.1 %collective-permute-start.20 = (f32[2048]{0:T(1024)S(1)}, f32[2048]{0:T(1024)S(1)}, u32[]{:S(2)}, u32[]{:S(2)}) collective-permute-start(f32[2048]{0:T(1024)S(1)} %reduce_max.19), channel_id=1, source_target_pairs={{0,3},{1,2},{2,1},{3,0},{4,7},{5,6},{6,5},{7,4},{8,11},{9,10},{10,... | collective-permute-start | bytes 24584 | tf_op jit(solution)/shard_map/ppermute | solution.py:27
  71.4 3.7 %collective-permute-start.19 = (f32[2048]{0:T(1024)S(1)}, f32[2048]{0:T(1024)S(1)}, u32[]{:S(2)}, u32[]{:S(2)}) collective-permute-start(f32[2048]{0:T(1024)S(1)} %reduce_max.19), channel_id=1, source_target_pairs={{0,2},{1,3},{2,0},{3,1},{4,6},{5,7},{6,4},{7,5},{8,10},{9,11},{10,... | collective-permute-start | bytes 24584 | tf_op jit(solution)/shard_map/ppermute | solution.py:27
  72.6 2.5 %collective-permute-start.18 = (f32[2048]{0:T(1024)S(1)}, f32[2048]{0:T(1024)S(1)}, u32[]{:S(2)}, u32[]{:S(2)}) collective-permute-start(f32[2048]{0:T(1024)S(1)} %reduce_max.19), channel_id=1, source_target_pairs={{0,1},{1,0},{2,3},{3,2},{4,5},{5,4},{6,7},{7,6},{8,9},{9,8},{10,11... | collective-permute-start | bytes 24584 | tf_op jit(solution)/shard_map/ppermute | solution.py:27
  75.1 5.5 %collective-permute-start.23 = (f32[2048]{0:T(1024)S(1)}, f32[2048]{0:T(1024)S(1)}, u32[]{:S(2)}, u32[]{:S(2)}) collective-permute-start(f32[2048]{0:T(1024)S(1)} %maximum_maximum_fusion.1), channel_id=1, source_target_pairs={{0,12},{1,13},{2,14},{3,15},{4,8},{5,9},{6,10},{7,11},{8,4},{9,5},... | collective-permute-start | bytes 24584 | tf_op jit(solution)/shard_map/ppermute | solution.py:27
  78.0 4.5 %collective-permute-start.22 = (f32[2048]{0:T(1024)S(1)}, f32[2048]{0:T(1024)S(1)}, u32[]{:S(2)}, u32[]{:S(2)}) collective-permute-start(f32[2048]{0:T(1024)S(1)} %maximum_maximum_fusion.1), channel_id=1, source_target_pairs={{0,8},{1,9},{2,10},{3,11},{4,12},{5,13},{6,14},{7,15},{8,0},{9,1},... | collective-permute-start | bytes 24584 | tf_op jit(solution)/shard_map/ppermute | solution.py:27
  78.0 4.5 %collective-permute-start.21 = (f32[2048]{0:T(1024)S(1)}, f32[2048]{0:T(1024)S(1)}, u32[]{:S(2)}, u32[]{:S(2)}) collective-permute-start(f32[2048]{0:T(1024)S(1)} %maximum_maximum_fusion.1), channel_id=1, source_target_pairs={{0,4},{1,5},{2,6},{3,7},{4,0},{5,1},{6,2},{7,3},{8,12},{9,13},{10,... | collective-permute-start | bytes 24584 | tf_op jit(solution)/shard_map/ppermute | solution.py:27

commit v16 on v14

--- a/solution.py
+++ b/solution.py
@@ -99,6 +99,39 @@
     )(filterbank, channel_total, offsets)
 
 
+def merge_head_kernel(level, flag_ref, own_ref, partner_ref, offsets_ref, out_ref):
+    rows, width = own_ref.shape
+    upper_half = flag_ref[0] == 1
+    own = own_ref[...]
+    partner = partner_ref[...]
+    lower = jnp.where(upper_half, partner, own)
+    shifted = jnp.where(upper_half, own, partner)
+    diagonal = lax.broadcasted_iota(jnp.int32, (rows, rows), 0) == lax.broadcasted_iota(
+        jnp.int32, (rows, rows), 1
+    )
+    amount_row = jnp.broadcast_to(offsets_ref[level : level + 1, :], (rows, rows))
+    amount = jnp.sum(jnp.where(diagonal, amount_row, 0), axis=1, keepdims=True)
+    for bit_index in range((SHIFT - 1).bit_length()):
+        span = 2**bit_index
+        chosen = (amount >> bit_index & 1) == 1
+        shifted = jnp.where(chosen, pltpu.roll(shifted, width - span, axis=1), shifted)
+    new_width = out_ref.shape[1]
+    out_ref[...] = lower[:, :new_width] + shifted[:, :new_width]
+
+
+def merge_head(own, partner, offsets, level, upper_half):
+    rows, width = own.shape
+    vmem = pl.BlockSpec(memory_space=pltpu.VMEM)
+    flag = jnp.where(upper_half, 1, 0).astype(jnp.int32).reshape(1)
+    return pl.pallas_call(
+        functools.partial(merge_head_kernel, level),
+        out_shape=jax.ShapeDtypeStruct((rows, width - SHIFT), jnp.float32),
+        in_specs=[pl.BlockSpec(memory_space=pltpu.SMEM), vmem, vmem, vmem],
+        out_specs=vmem,
+        cost_estimate=pl.CostEstimate(flops=40 * rows * width, transcendentals=0, bytes_accessed=12 * rows * width),
+    )(flag, own, partner, offsets)
+
+
 def merge_section(current, offsets_now, section_index, new_length):
     group_trials = 2**section_index
     total_rows = current.shape[0]
@@ -179,9 +212,10 @@
     pending = None
     for bit_index in range(bit_count):
         amounts = offsets[local_count + bit_index]
-        lower_head, upper_head = halves(head, partner_head, bit_index)
         head_width = head.shape[1] - SHIFT
-        new_head = lower_head[:, :head_width] + shift_rows(upper_head, amounts, head_width)
+        upper_half = band_index // 2**bit_index % 2 == 1
+        new_head = merge_head(head, partner_head, offsets, local_count + bit_index, upper_half)
+        lower_edge, upper_edge = halves(head[:, head_width:], partner_head[:, head_width:], bit_index)
         if bit_index + 1 < bit_count:
             next_partner_head = from_partner(new_head, "band", bit_index + 1)
         if pending is not None:
@@ -191,7 +225,7 @@
         if bit_index + 1 < bit_count:
             partner_tail, next_partner_head = lax.optimization_barrier((partner_tail, next_partner_head))
             partner_head = next_partner_head
-        pending = (tail, partner_tail, lower_head[:, head_width:], upper_head[:, head_width:], amounts, bit_index)
+        pending = (tail, partner_tail, lower_edge, upper_edge, amounts, bit_index)
         head = new_head
     tail = finish_tail(pending)
     current = jnp.concatenate([head, tail], axis=1)

time: 76.1 us -> 84.2 us (1.11)
  Pallas kernels: 6.8 us -> 15.9 us
  waiting for transfers between devices: 34 us -> 27.7 us
  local copies, waits for them, and re-layouts: 0.33 us -> 4.12 us
    pallas_call x0 -> x4, Pallas kernels: none -> 9.12 us  [merge_head(): pl.pallas_call(functools.partial(merge_head_kernel, level), out_shape=jax...]
    ppermute x8, waiting for transfers between devices: 22.8 us -> 18.6 us  [from_partner(): return lax.ppermute(value, axis, pairs)]
    select_n x56 -> x28, other arithmetic: 6.19 us -> 2.99 us  [shift_rows(): jnp.where(chosen, current[:, span:span + keep_len], current[:, :keep_len])]
    unnamed x8 -> x14, local copies, waits for them, and re-layouts: 0.02 us -> 3.18 us
    ppermute x12, waiting for transfers between devices: 11.2 us -> 9.05 us  [from_xor(): return lax.ppermute(value, axis, pairs)]
    select_n x8, other arithmetic: 1.17 us -> 3.22 us  [halves(): jnp.where(upper_half, partner, own)]
    eq x2, other arithmetic: 0.04 us -> 1.64 us  [shift_rows(): chosen = (amounts >> bit_index & 1)[:, None] == 1]
  transfers between devices with their start and end apart: 20 -> 20, of which waited for: 14 -> 14; matrix products, arithmetic and copies ran while one was open for 3% -> 10% of each run, Pallas kernels for 0% -> 0%
where the time goes in v16:
time: 84.2 us; the launch traced here: 83.6 us
  waiting for transfers between devices  27.7 us (33%)
  starting transfers between devices  22 us (26%)
  Pallas kernels  15.9 us (19%)
  other arithmetic  11.8 us (14%)
  local copies, waits for them, and re-layouts  4.12 us (5%)
  between operations  1.05 us (1%)
  matrix products  1.03 us (1%)
    ppermute x8, waiting for transfers between devices, from_partner(): return lax.ppermute(value, axis, pairs)  18.6 us
    ppermute x12, starting transfers between devices, from_xor(): return lax.ppermute(value, axis, pairs)  14 us
    pallas_call x4, Pallas kernels, merge_head(): pl.pallas_call(functools.partial(merge_head_kernel, level), out_shape=jax...  9.12 us
    ppermute x12, waiting for transfers between devices, from_xor(): return lax.ppermute(value, axis, pairs)  9.05 us
    ppermute x8, starting transfers between devices, from_partner(): return lax.ppermute(value, axis, pairs)  7.97 us
    pallas_call x1, Pallas kernels, local_tree(): pl.pallas_call(functools.partial(local_tree_kernel, tuple(widths_seq), fl...  6.79 us
    select_n x8, other arithmetic, halves(): jnp.where(upper_half, partner, own)  3.22 us
    unnamed x14, local copies, waits for them, and re-layouts  3.18 us
  transfers between devices with their start and end apart: 20, of which 14 were waited for; matrix products, arithmetic and copies ran while one was open for 10% of the time, Pallas kernels for 0%

profile of v16, /device:TPU:0, one launch (start us, length us, event | category | flops | bytes accessed | tf_op | source)
XLA Modules:
  0.0 83.6 jit_solution(16473489122411928762)
XLA Ops:
  0.6 1.1 %slice_reduce_fusion = f32[4480]{0:T(1024)S(1)} fusion(f32[32,6144]{1,0:T(8,128)} %x_ref.1), kind=kLoop, calls=%fused_computation.4 | loop fusion | flops 138880 | bytes 591360 | tf_op jit(solution)/shard_map/reduce_sum | solution.py:191
  1.8 3.0 %collective-permute-start.1 = (f32[1,4480]{1,0:T(1,128)S(1)}, f32[1,4480]{1,0:T(1,128)S(1)}, u32[]{:S(2)}, u32[]{:S(2)}) collective-permute-start(f32[1,4480]{1,0:T(1,128)S(1)} %broadcast_in_dim.239), channel_id=1, source_target_pairs={{0,2},{1,3},{2,0},{3,1},{4,6},{5,7},{6,4},{7,5},{8,10},{9,11},{10,... | collective-permute-start | bytes 53768 | tf_op jit(solution)/shard_map/ppermute | solution.py:27
  6.4 0.8 compare_bitcast_fusion.6
  8.0 3.7 %collective-permute-start.5 = (f32[1,4480]{1,0:T(1,128)S(1)}, f32[1,4480]{1,0:T(1,128)S(1)}, u32[]{:S(2)}, u32[]{:S(2)}) collective-permute-start(f32[1,4480]{1,0:T(1,128)S(1)} %add_add_fusion.1), channel_id=1, source_target_pairs={{0,12},{1,13},{2,14},{3,15},{4,8},{5,9},{6,10},{7,11},{8,4},{9,5},... | collective-permute-start | bytes 53768 | tf_op jit(solution)/shard_map/ppermute | solution.py:27
  11.7 0.8 collective-permute-start.3
  12.5 1.1 %collective-permute-done.5 = f32[1,4480]{1,0:T(1,128)S(1)} collective-permute-done((f32[1,4480]{1,0:T(1,128)S(1)}, f32[1,4480]{1,0:T(1,128)S(1)}, u32[]{:S(2)}, u32[]{:S(2)}) %collective-permute-start.5) | collective-permute-done | bytes 17952 | tf_op jit(solution)/shard_map/ppermute | solution.py:27
  13.6 2.7 %collective-permute-done.4 = f32[1,4480]{1,0:T(1,128)S(1)} collective-permute-done((f32[1,4480]{1,0:T(1,128)S(1)}, f32[1,4480]{1,0:T(1,128)S(1)}, u32[]{:S(2)}, u32[]{:S(2)}) %collective-permute-start.4) | collective-permute-done | bytes 17952 | tf_op jit(solution)/shard_map/ppermute | solution.py:27
  17.0 6.8 %shard_map.50 = (f32[32,2048]{1,0:T(8,128)}, f32[32,1152]{1,0:T(8,128)}) custom-call(f32[32,6144]{1,0:T(8,128)} %x_ref.1, f32[1,4480]{1,0:T(1,128)} %add_add_fusion.total_ref, s32[9,32]{1,0:T(8,128)} %offsets_ref.9), custom_call_target="tpu_custom_call" | custom-call | flops 25395200 | bytes 983040 | tf_op jit(solution)/shard_map/pallas_call | solution.py:88
  23.8 0.8 compare_bitcast_fusion.7
  24.7 0.8 collective-permute-done.6.partner_ref
  26.2 2.3 %shard_map.51.own_ref = f32[32,1792]{1,0:T(8,128)} custom-call(s32[1]{0:T(128)} %bitcast.3.flag_ref, f32[32,2048]{1,0:T(8,128)} %get-tuple-element.15.own_ref, f32[32,2048]{1,0:T(8,128)} %copy-done.2, s32[9,32]{1,0:T(8,128)} %offsets_ref.9), custom_call_target="tpu_custom_call" | custom-call | flops 2621440 | bytes 786432 | tf_op jit(solution)/shard_map/pallas_call | solution.py:126
  28.5 1.2 %collective-permute-start.8 = (f32[32,1792]{1,0:T(8,128)}, f32[32,1792]{1,0:T(8,128)S(1)}, u32[]{:S(2)}, u32[]{:S(2)}) collective-permute-start(f32[32,1792]{1,0:T(8,128)} %shard_map.51.own_ref), channel_id=1, source_target_pairs={{0,2},{1,3},{2,0},{3,1},{4,6},{5,7},{6,4},{7,5},{8,10},{9,11},{10,... | collective-permute-start | bytes 688136 | tf_op jit(solution)/shard_map/ppermute | solution.py:22
  30.2 0.8 slice_select_fusion.35
  31.6 4.8 %collective-permute-done.8.partner_ref = f32[32,1792]{1,0:T(8,128)S(1)} collective-permute-done((f32[32,1792]{1,0:T(8,128)}, f32[32,1792]{1,0:T(8,128)S(1)}, u32[]{:S(2)}, u32[]{:S(2)}) %collective-permute-start.8) | collective-permute-done | bytes 229408 | tf_op jit(solution)/shard_map/ppermute | solution.py:22
  37.1 2.3 %shard_map.52.own_ref = f32[32,1536]{1,0:T(8,128)} custom-call(s32[1]{0:T(128)} %bitcast.2.flag_ref, f32[32,1792]{1,0:T(8,128)} %shard_map.51.own_ref, f32[32,1792]{1,0:T(8,128)} %copy-done.3, s32[9,32]{1,0:T(8,128)} %offsets_ref.9), custom_call_target="tpu_custom_call" | custom-call | flops 2293760 | bytes 688128 | tf_op jit(solution)/shard_map/pallas_call | solution.py:126
  40.3 1.3 %collective-permute-start.9 = (f32[32,1152]{1,0:T(8,128)S(1)}, f32[32,1152]{1,0:T(8,128)S(1)}, u32[]{:S(2)}, u32[]{:S(2)}) collective-permute-start(f32[32,1152]{1,0:T(8,128)S(1)} %fusion.13), channel_id=1, source_target_pairs={{0,2},{1,3},{2,0},{3,1},{4,6},{5,7},{6,4},{7,5},{8,10},{9,11},{10,... | collective-permute-start | bytes 442376 | tf_op jit(solution)/shard_map/ppermute | solution.py:22
  42.4 3.1 %collective-permute-done.9 = f32[32,1152]{1,0:T(8,128)S(1)} collective-permute-done((f32[32,1152]{1,0:T(8,128)S(1)}, f32[32,1152]{1,0:T(8,128)S(1)}, u32[]{:S(2)}, u32[]{:S(2)}) %collective-permute-start.9) | collective-permute-done | bytes 147488 | tf_op jit(solution)/shard_map/ppermute | solution.py:22
  46.4 2.3 %shard_map.53.own_ref = f32[32,1280]{1,0:T(8,128)} custom-call(s32[1]{0:T(128)} %bitcast.1.flag_ref, f32[32,1536]{1,0:T(8,128)} %shard_map.52.own_ref, f32[32,1536]{1,0:T(8,128)} %copy-done.4, s32[9,32]{1,0:T(8,128)} %offsets_ref.9), custom_call_target="tpu_custom_call" | custom-call | flops 1966080 | bytes 589824 | tf_op jit(solution)/shard_map/pallas_call | solution.py:126
  48.7 2.0 %collective-permute-start.12 = (f32[32,1280]{1,0:T(8,128)}, f32[32,1280]{1,0:T(8,128)S(1)}, u32[]{:S(2)}, u32[]{:S(2)}) collective-permute-start(f32[32,1280]{1,0:T(8,128)} %shard_map.53.own_ref), channel_id=1, source_target_pairs={{0,8},{1,9},{2,10},{3,11},{4,12},{5,13},{6,14},{7,15},{8,0},{9,1},... | collective-permute-start | bytes 491528 | tf_op jit(solution)/shard_map/ppermute | solution.py:22
  51.6 1.9 %collective-permute-start.11 = (f32[32,1152]{1,0:T(8,128)S(1)}, f32[32,1152]{1,0:T(8,128)S(1)}, u32[]{:S(2)}, u32[]{:S(2)}) collective-permute-start(f32[32,1152]{1,0:T(8,128)S(1)} %fusion.12), channel_id=1, source_target_pairs={{0,4},{1,5},{2,6},{3,7},{4,0},{5,1},{6,2},{7,3},{8,12},{9,13},{10,... | collective-permute-start | bytes 442376 | tf_op jit(solution)/shard_map/ppermute | solution.py:22
  53.5 0.8 slice_select_fusion.29
  54.3 3.6 %collective-permute-done.11 = f32[32,1152]{1,0:T(8,128)S(1)} collective-permute-done((f32[32,1152]{1,0:T(8,128)S(1)}, f32[32,1152]{1,0:T(8,128)S(1)}, u32[]{:S(2)}, u32[]{:S(2)}) %collective-permute-start.11) | collective-permute-done | bytes 147488 | tf_op jit(solution)/shard_map/ppermute | solution.py:22
  58.6 2.2 %shard_map.54 = f32[32,1024]{1,0:T(8,128)} custom-call(s32[1]{0:T(128)} %bitcast.flag_ref, f32[32,1280]{1,0:T(8,128)} %shard_map.53.own_ref, f32[32,1280]{1,0:T(8,128)} %copy-done.5, s32[9,32]{1,0:T(8,128)} %offsets_ref.9), custom_call_target="tpu_custom_call" | custom-call | flops 1638400 | bytes 491520 | tf_op jit(solution)/shard_map/pallas_call | solution.py:126
  61.7 1.4 %collective-permute-start.13 = (f32[32,1152]{1,0:T(8,128)S(1)}, f32[32,1152]{1,0:T(8,128)S(1)}, u32[]{:S(2)}, u32[]{:S(2)}) collective-permute-start(f32[32,1152]{1,0:T(8,128)S(1)} %fusion.11), channel_id=1, source_target_pairs={{0,8},{1,9},{2,10},{3,11},{4,12},{5,13},{6,14},{7,15},{8,0},{9,1},... | collective-permute-start | bytes 442376 | tf_op jit(solution)/shard_map/ppermute | solution.py:22
  63.9 5.5 %collective-permute-done.13 = f32[32,1152]{1,0:T(8,128)S(1)} collective-permute-done((f32[32,1152]{1,0:T(8,128)S(1)}, f32[32,1152]{1,0:T(8,128)S(1)}, u32[]{:S(2)}, u32[]{:S(2)}) %collective-permute-start.13) | collective-permute-done | bytes 147488 | tf_op jit(solution)/shard_map/ppermute | solution.py:22
  71.0 1.0 %convolution_reduce_fusion = f32[512,128]{1,0:T(8,128)S(1)} fusion(f32[512,256,1]{1,0,2:T(8,128)S(1)} %bitcast.89, f32[8,128,256]{2,1,0:T(8,128)S(1)} %bitcast.88), kind=kOutput, calls=%fused_computation | convolution fusion | flops 805765120 | bytes 1835008 | tf_op jit(solution)/shard_map/dot_general | solution.py:170
  72.2 1.3 %collective-permute-start.15 = (f32[2048]{0:T(1024)S(1)}, f32[2048]{0:T(1024)S(1)}, u32[]{:S(2)}, u32[]{:S(2)}) collective-permute-start(f32[2048]{0:T(1024)S(1)} %reduce_max.19), channel_id=1, source_target_pairs={{0,2},{1,3},{2,0},{3,1},{4,6},{5,7},{6,4},{7,5},{8,10},{9,11},{10,... | collective-permute-start | bytes 24584 | tf_op jit(solution)/shard_map/ppermute | solution.py:27
  74.0 1.2 %collective-permute-done.16 = f32[2048]{0:T(1024)S(1)} collective-permute-done((f32[2048]{0:T(1024)S(1)}, f32[2048]{0:T(1024)S(1)}, u32[]{:S(2)}, u32[]{:S(2)}) %collective-permute-start.16) | collective-permute-done | bytes 8224 | tf_op jit(solution)/shard_map/ppermute | solution.py:27
  75.9 2.5 %collective-permute-start.19 = (f32[2048]{0:T(1024)S(1)}, f32[2048]{0:T(1024)S(1)}, u32[]{:S(2)}, u32[]{:S(2)}) collective-permute-start(f32[2048]{0:T(1024)S(1)} %maximum_maximum_fusion.1), channel_id=1, source_target_pairs={{0,12},{1,13},{2,14},{3,15},{4,8},{5,9},{6,10},{7,11},{8,4},{9,5},... | collective-permute-start | bytes 24584 | tf_op jit(solution)/shard_map/ppermute | solution.py:27
  78.4 1.9 %collective-permute-start.17 = (f32[2048]{0:T(1024)S(1)}, f32[2048]{0:T(1024)S(1)}, u32[]{:S(2)}, u32[]{:S(2)}) collective-permute-start(f32[2048]{0:T(1024)S(1)} %maximum_maximum_fusion.1), channel_id=1, source_target_pairs={{0,4},{1,5},{2,6},{3,7},{4,0},{5,1},{6,2},{7,3},{8,12},{9,13},{10,... | collective-permute-start | bytes 24584 | tf_op jit(solution)/shard_map/ppermute | solution.py:27
  80.4 1.1 %collective-permute-done.19 = f32[2048]{0:T(1024)S(1)} collective-permute-done((f32[2048]{0:T(1024)S(1)}, f32[2048]{0:T(1024)S(1)}, u32[]{:S(2)}, u32[]{:S(2)}) %collective-permute-start.19) | collective-permute-done | bytes 8224 | tf_op jit(solution)/shard_map/ppermute | solution.py:27
  81.4 1.6 %collective-permute-done.18 = f32[2048]{0:T(1024)S(1)} collective-permute-done((f32[2048]{0:T(1024)S(1)}, f32[2048]{0:T(1024)S(1)}, u32[]{:S(2)}, u32[]{:S(2)}) %collective-permute-start.18) | collective-permute-done | bytes 8224 | tf_op jit(solution)/shard_map/ppermute | solution.py:27
  (88 shorter events, 14.6 us)
Async XLA Ops:
  1.8 5.5 %collective-permute-start.1 = (f32[1,4480]{1,0:T(1,128)S(1)}, f32[1,4480]{1,0:T(1,128)S(1)}, u32[]{:S(2)}, u32[]{:S(2)}) collective-permute-start(f32[1,4480]{1,0:T(1,128)S(1)} %broadcast_in_dim.239), channel_id=1, source_target_pairs={{0,2},{1,3},{2,0},{3,1},{4,6},{5,7},{6,4},{7,5},{8,10},{9,11},{10,... | collective-permute-start | bytes 53768 | tf_op jit(solution)/shard_map/ppermute | solution.py:27
  4.8 3.2 %collective-permute-start.2 = (f32[1,4480]{1,0:T(1,128)S(1)}, f32[1,4480]{1,0:T(1,128)S(1)}, u32[]{:S(2)}, u32[]{:S(2)}) collective-permute-start(f32[1,4480]{1,0:T(1,128)S(1)} %broadcast_in_dim.239), channel_id=1, source_target_pairs={{0,3},{1,2},{2,1},{3,0},{4,7},{5,6},{6,5},{7,4},{8,11},{9,10},{10,... | collective-permute-start | bytes 53768 | tf_op jit(solution)/shard_map/ppermute | solution.py:27
  4.8 3.2 %collective-permute-start = (f32[1,4480]{1,0:T(1,128)S(1)}, f32[1,4480]{1,0:T(1,128)S(1)}, u32[]{:S(2)}, u32[]{:S(2)}) collective-permute-start(f32[1,4480]{1,0:T(1,128)S(1)} %broadcast_in_dim.239), channel_id=1, source_target_pairs={{0,1},{1,0},{2,3},{3,2},{4,5},{5,4},{6,7},{7,6},{8,9},{9,8},{10,11... | collective-permute-start | bytes 53768 | tf_op jit(solution)/shard_map/ppermute | solution.py:27
  8.0 5.6 %collective-permute-start.5 = (f32[1,4480]{1,0:T(1,128)S(1)}, f32[1,4480]{1,0:T(1,128)S(1)}, u32[]{:S(2)}, u32[]{:S(2)}) collective-permute-start(f32[1,4480]{1,0:T(1,128)S(1)} %add_add_fusion.1), channel_id=1, source_target_pairs={{0,12},{1,13},{2,14},{3,15},{4,8},{5,9},{6,10},{7,11},{8,4},{9,5},... | collective-permute-start | bytes 53768 | tf_op jit(solution)/shard_map/ppermute | solution.py:27
  11.7 4.7 %collective-permute-start.4 = (f32[1,4480]{1,0:T(1,128)S(1)}, f32[1,4480]{1,0:T(1,128)S(1)}, u32[]{:S(2)}, u32[]{:S(2)}) collective-permute-start(f32[1,4480]{1,0:T(1,128)S(1)} %add_add_fusion.1), channel_id=1, source_target_pairs={{0,8},{1,9},{2,10},{3,11},{4,12},{5,13},{6,14},{7,15},{8,0},{9,1},... | collective-permute-start | bytes 53768 | tf_op jit(solution)/shard_map/ppermute | solution.py:27
  11.7 4.7 %collective-permute-start.3 = (f32[1,4480]{1,0:T(1,128)S(1)}, f32[1,4480]{1,0:T(1,128)S(1)}, u32[]{:S(2)}, u32[]{:S(2)}) collective-permute-start(f32[1,4480]{1,0:T(1,128)S(1)} %add_add_fusion.1), channel_id=1, source_target_pairs={{0,4},{1,5},{2,6},{3,7},{4,0},{5,1},{6,2},{7,3},{8,12},{9,13},{10,... | collective-permute-start | bytes 53768 | tf_op jit(solution)/shard_map/ppermute | solution.py:27
  23.8 1.7 %collective-permute-start.6 = (f32[32,2048]{1,0:T(8,128)}, f32[32,2048]{1,0:T(8,128)S(1)}, u32[]{:S(2)}, u32[]{:S(2)}) collective-permute-start(f32[32,2048]{1,0:T(8,128)} %get-tuple-element.15.own_ref), channel_id=1, source_target_pairs={{0,1},{1,0},{2,3},{3,2},{4,5},{5,4},{6,7},{7,6},{8,9},{9,8},{10,11... | collective-permute-start | bytes 786440 | tf_op jit(solution)/shard_map/ppermute | solution.py:22
  23.8 6.3 %copy-start.6 = (f32[32,1152]{1,0:T(8,128)S(1)}, f32[32,1152]{1,0:T(8,128)}, u32[]{:S(2)}) copy-start(f32[32,1152]{1,0:T(8,128)} %get-tuple-element.18) | copy-start | bytes 442372
  25.5 0.7 copy-start.2
  28.5 7.9 %collective-permute-start.8 = (f32[32,1792]{1,0:T(8,128)}, f32[32,1792]{1,0:T(8,128)S(1)}, u32[]{:S(2)}, u32[]{:S(2)}) collective-permute-start(f32[32,1792]{1,0:T(8,128)} %shard_map.51.own_ref), channel_id=1, source_target_pairs={{0,2},{1,3},{2,0},{3,1},{4,6},{5,7},{6,4},{7,5},{8,10},{9,11},{10,... | collective-permute-start | bytes 688136 | tf_op jit(solution)/shard_map/ppermute | solution.py:22
  30.1 1.4 %collective-permute-start.7 = (f32[32,1152]{1,0:T(8,128)S(1)}, f32[32,1152]{1,0:T(8,128)S(1)}, u32[]{:S(2)}, u32[]{:S(2)}) collective-permute-start(f32[32,1152]{1,0:T(8,128)S(1)} %copy-done.6), channel_id=1, source_target_pairs={{0,1},{1,0},{2,3},{3,2},{4,5},{5,4},{6,7},{7,6},{8,9},{9,8},{10,11... | collective-permute-start | bytes 442376 | tf_op jit(solution)/shard_map/ppermute | solution.py:22
  36.4 0.7 copy-start.3
  39.4 6.3 %collective-permute-start.10 = (f32[32,1536]{1,0:T(8,128)}, f32[32,1536]{1,0:T(8,128)S(1)}, u32[]{:S(2)}, u32[]{:S(2)}) collective-permute-start(f32[32,1536]{1,0:T(8,128)} %shard_map.52.own_ref), channel_id=1, source_target_pairs={{0,4},{1,5},{2,6},{3,7},{4,0},{5,1},{6,2},{7,3},{8,12},{9,13},{10,... | collective-permute-start | bytes 589832 | tf_op jit(solution)/shard_map/ppermute | solution.py:22
  40.3 5.2 %collective-permute-start.9 = (f32[32,1152]{1,0:T(8,128)S(1)}, f32[32,1152]{1,0:T(8,128)S(1)}, u32[]{:S(2)}, u32[]{:S(2)}) collective-permute-start(f32[32,1152]{1,0:T(8,128)S(1)} %fusion.13), channel_id=1, source_target_pairs={{0,2},{1,3},{2,0},{3,1},{4,6},{5,7},{6,4},{7,5},{8,10},{9,11},{10,... | collective-permute-start | bytes 442376 | tf_op jit(solution)/shard_map/ppermute | solution.py:22
  45.7 0.7 copy-start.4
  48.7 9.3 %collective-permute-start.12 = (f32[32,1280]{1,0:T(8,128)}, f32[32,1280]{1,0:T(8,128)S(1)}, u32[]{:S(2)}, u32[]{:S(2)}) collective-permute-start(f32[32,1280]{1,0:T(8,128)} %shard_map.53.own_ref), channel_id=1, source_target_pairs={{0,8},{1,9},{2,10},{3,11},{4,12},{5,13},{6,14},{7,15},{8,0},{9,1},... | collective-permute-start | bytes 491528 | tf_op jit(solution)/shard_map/ppermute | solution.py:22
  51.6 6.3 %collective-permute-start.11 = (f32[32,1152]{1,0:T(8,128)S(1)}, f32[32,1152]{1,0:T(8,128)S(1)}, u32[]{:S(2)}, u32[]{:S(2)}) collective-permute-start(f32[32,1152]{1,0:T(8,128)S(1)} %fusion.12), channel_id=1, source_target_pairs={{0,4},{1,5},{2,6},{3,7},{4,0},{5,1},{6,2},{7,3},{8,12},{9,13},{10,... | collective-permute-start | bytes 442376 | tf_op jit(solution)/shard_map/ppermute | solution.py:22
  57.9 0.7 copy-start.5
  61.7 7.7 %collective-permute-start.13 = (f32[32,1152]{1,0:T(8,128)S(1)}, f32[32,1152]{1,0:T(8,128)S(1)}, u32[]{:S(2)}, u32[]{:S(2)}) collective-permute-start(f32[32,1152]{1,0:T(8,128)S(1)} %fusion.11), channel_id=1, source_target_pairs={{0,8},{1,9},{2,10},{3,11},{4,12},{5,13},{6,14},{7,15},{8,0},{9,1},... | collective-permute-start | bytes 442376 | tf_op jit(solution)/shard_map/ppermute | solution.py:22
  69.9 0.9 %copy-start.1 = (f32[32,1024]{1,0:T(8,128)S(1)}, f32[32,1024]{1,0:T(8,128)}, u32[]{:S(2)}) copy-start(f32[32,1024]{1,0:T(8,128)} %shard_map.54) | copy-start | bytes 393220
  72.1 11.5 %copy-start = (f32[32,2048]{1,0:T(8,128)}, f32[32,2048]{1,0:T(8,128)S(1)}, u32[]{:S(2)}) copy-start(f32[32,2048]{1,0:T(8,128)S(1)} %reshape.501) | copy-start | bytes 786436
  72.1 3.1 %collective-permute-start.16 = (f32[2048]{0:T(1024)S(1)}, f32[2048]{0:T(1024)S(1)}, u32[]{:S(2)}, u32[]{:S(2)}) collective-permute-start(f32[2048]{0:T(1024)S(1)} %reduce_max.19), channel_id=1, source_target_pairs={{0,3},{1,2},{2,1},{3,0},{4,7},{5,6},{6,5},{7,4},{8,11},{9,10},{10,... | collective-permute-start | bytes 24584 | tf_op jit(solution)/shard_map/ppermute | solution.py:27
  72.2 3.7 %collective-permute-start.15 = (f32[2048]{0:T(1024)S(1)}, f32[2048]{0:T(1024)S(1)}, u32[]{:S(2)}, u32[]{:S(2)}) collective-permute-start(f32[2048]{0:T(1024)S(1)} %reduce_max.19), channel_id=1, source_target_pairs={{0,2},{1,3},{2,0},{3,1},{4,6},{5,7},{6,4},{7,5},{8,10},{9,11},{10,... | collective-permute-start | bytes 24584 | tf_op jit(solution)/shard_map/ppermute | solution.py:27
  73.5 2.4 %collective-permute-start.14 = (f32[2048]{0:T(1024)S(1)}, f32[2048]{0:T(1024)S(1)}, u32[]{:S(2)}, u32[]{:S(2)}) collective-permute-start(f32[2048]{0:T(1024)S(1)} %reduce_max.19), channel_id=1, source_target_pairs={{0,1},{1,0},{2,3},{3,2},{4,5},{5,4},{6,7},{7,6},{8,9},{9,8},{10,11... | collective-permute-start | bytes 24584 | tf_op jit(solution)/shard_map/ppermute | solution.py:27
  75.9 5.5 %collective-permute-start.19 = (f32[2048]{0:T(1024)S(1)}, f32[2048]{0:T(1024)S(1)}, u32[]{:S(2)}, u32[]{:S(2)}) collective-permute-start(f32[2048]{0:T(1024)S(1)} %maximum_maximum_fusion.1), channel_id=1, source_target_pairs={{0,12},{1,13},{2,14},{3,15},{4,8},{5,9},{6,10},{7,11},{8,4},{9,5},... | collective-permute-start | bytes 24584 | tf_op jit(solution)/shard_map/ppermute | solution.py:27
  78.4 4.5 %collective-permute-start.18 = (f32[2048]{0:T(1024)S(1)}, f32[2048]{0:T(1024)S(1)}, u32[]{:S(2)}, u32[]{:S(2)}) collective-permute-start(f32[2048]{0:T(1024)S(1)} %maximum_maximum_fusion.1), channel_id=1, source_target_pairs={{0,8},{1,9},{2,10},{3,11},{4,12},{5,13},{6,14},{7,15},{8,0},{9,1},... | collective-permute-start | bytes 24584 | tf_op jit(solution)/shard_map/ppermute | solution.py:27
  78.4 4.5 %collective-permute-start.17 = (f32[2048]{0:T(1024)S(1)}, f32[2048]{0:T(1024)S(1)}, u32[]{:S(2)}, u32[]{:S(2)}) collective-permute-start(f32[2048]{0:T(1024)S(1)} %maximum_maximum_fusion.1), channel_id=1, source_target_pairs={{0,4},{1,5},{2,6},{3,7},{4,0},{5,1},{6,2},{7,3},{8,12},{9,13},{10,... | collective-permute-start | bytes 24584 | tf_op jit(solution)/shard_map/ppermute | solution.py:27

commit v17 on v14

--- a/solution.py
+++ b/solution.py
@@ -27,17 +27,28 @@
     return lax.ppermute(value, axis, pairs)
 
 
-def butterfly(value, axis, combine):
+def butterfly_terms(value, axis, combine):
     bit_count = lax.axis_size(axis).bit_length() - 1
     low_bit = 0
+    received = [value]
     while low_bit < bit_count:
-        width = min(2, bit_count - low_bit)
-        received = [value] + [from_xor(value, axis, k << low_bit) for k in range(1, 2**width)]
         while len(received) > 1:
             received = [combine(received[i], received[i + 1]) for i in range(0, len(received), 2)]
         value = received[0]
+        width = min(2, bit_count - low_bit)
+        received = [value] + [from_xor(value, axis, k << low_bit) for k in range(1, 2**width)]
         low_bit += width
-    return value
+    return received
+
+
+def combine_terms(terms, combine):
+    while len(terms) > 1:
+        terms = [combine(terms[i], terms[i + 1]) for i in range(0, len(terms), 2)]
+    return terms[0]
+
+
+def butterfly(value, axis, combine):
+    return combine_terms(butterfly_terms(value, axis, combine), combine)
 
 
 def shift_rows(trial_rows, amounts, length):
@@ -51,9 +62,12 @@
     return current
 
 
-def local_tree_kernel(widths_seq, channels_all, x_ref, total_ref, offsets_ref, head_ref, tail_ref):
+def local_tree_kernel(widths_seq, channels_all, term_count, x_ref, *refs):
+    term_refs = refs[:term_count]
+    offsets_ref, head_ref, tail_ref = refs[term_count:]
     rows = x_ref.shape[0]
-    cur = x_ref[:, : widths_seq[0]] - total_ref[:, : widths_seq[0]] / channels_all
+    total = combine_terms([ref[:, : widths_seq[0]] for ref in term_refs], jnp.add)
+    cur = x_ref[:, : widths_seq[0]] - total / channels_all
     row_id = lax.broadcasted_iota(jnp.int32, (rows, 1), 0)
     diagonal = lax.broadcasted_iota(jnp.int32, (rows, rows), 0) == lax.broadcasted_iota(
         jnp.int32, (rows, rows), 1
@@ -80,23 +94,23 @@
     tail_ref[...] = cur[:, head_width:]
 
 
-def local_tree(filterbank, channel_total, offsets, widths_seq, channels_all, tail_width):
+def local_tree(filterbank, total_terms, offsets, widths_seq, channels_all, tail_width):
     rows = filterbank.shape[0]
     vmem = pl.BlockSpec(memory_space=pltpu.VMEM)
     work = rows * sum(widths_seq[:-1])
     head_width = widths_seq[-1] - tail_width
     return pl.pallas_call(
-        functools.partial(local_tree_kernel, tuple(widths_seq), float(channels_all)),
+        functools.partial(local_tree_kernel, tuple(widths_seq), float(channels_all), len(total_terms)),
         out_shape=(
             jax.ShapeDtypeStruct((rows, head_width), jnp.float32),
             jax.ShapeDtypeStruct((rows, tail_width), jnp.float32),
         ),
-        in_specs=[vmem, vmem, vmem],
+        in_specs=[vmem] * (len(total_terms) + 2),
         out_specs=(vmem, vmem),
         cost_estimate=pl.CostEstimate(
             flops=40 * work, transcendentals=0, bytes_accessed=4 * (rows * widths_seq[0] + rows * widths_seq[-1])
         ),
-    )(filterbank, channel_total, offsets)
+    )(filterbank, *total_terms, offsets)
 
 
 def merge_section(current, offsets_now, section_index, new_length):
@@ -156,9 +170,9 @@
         return min(TIN, needed)
 
     partial_value = jnp.sum(filterbank[:, : length_after(0)], axis=0, keepdims=True)
-    channel_total = butterfly(partial_value, "band", jnp.add)
+    total_terms = butterfly_terms(partial_value, "band", jnp.add)
     widths_seq = [length_after(section) for section in range(local_count + 1)]
-    head, tail = local_tree(filterbank, channel_total, offsets, widths_seq, channels_all, TAIL_WIDTH)
+    head, tail = local_tree(filterbank, total_terms, offsets, widths_seq, channels_all, TAIL_WIDTH)
     band_index = lax.axis_index("band")
     bit_count = band_count.bit_length() - 1
     tail_width = TAIL_WIDTH

time: 76.1 us -> 76.6 us (level)
  local copies, waits for them, and re-layouts: 0.33 us -> 1.52 us
    unnamed x8 -> x16, local copies, waits for them, and re-layouts: 0.02 us -> 1.21 us
  transfers between devices with their start and end apart: 20 -> 20, of which waited for: 14 -> 15; matrix products, arithmetic and copies ran while one was open for 3% -> 3% of each run, Pallas kernels for 0% -> 0%
where the time goes in v17:
time: 76.6 us; the launch traced here: 76.4 us
  waiting for transfers between devices  34.3 us (45%)
  starting transfers between devices  20.9 us (27%)
  other arithmetic  10.5 us (14%)
  Pallas kernels  6.82 us (9%)
  local copies, waits for them, and re-layouts  1.52 us (2%)
  between operations  1.29 us (2%)
  matrix products  1.03 us (1%)
    ppermute x8, waiting for transfers between devices, from_partner(): return lax.ppermute(value, axis, pairs)  23 us
    ppermute x12, starting transfers between devices, from_xor(): return lax.ppermute(value, axis, pairs)  14 us
    ppermute x12, waiting for transfers between devices, from_xor(): return lax.ppermute(value, axis, pairs)  11.3 us
    ppermute x8, starting transfers between devices, from_partner(): return lax.ppermute(value, axis, pairs)  6.85 us
    pallas_call x1, Pallas kernels, local_tree(): pl.pallas_call(functools.partial(local_tree_kernel, tuple(widths_seq), fl...  6.82 us
    select_n x56, other arithmetic, shift_rows(): jnp.where(chosen, current[:, span:span + keep_len], current[:, :keep_len])  6.19 us
  transfers between devices with their start and end apart: 20, of which 15 were waited for; matrix products, arithmetic and copies ran while one was open for 3% of the time, Pallas kernels for 0%

profile of v17, /device:TPU:0, one launch (start us, length us, event | category | flops | bytes accessed | tf_op | source)
XLA Modules:
  0.0 76.4 jit_solution(18005293859009397517)
XLA Ops:
  0.6 1.1 %slice_reduce_fusion = f32[4480]{0:T(1024)S(1)} fusion(f32[32,6144]{1,0:T(8,128)} %x_ref.1), kind=kLoop, calls=%fused_computation.4 | loop fusion | flops 138880 | bytes 591360 | tf_op jit(solution)/shard_map/reduce_sum | solution.py:172
  1.8 3.0 %collective-permute-start.1 = (f32[1,4480]{1,0:T(1,128)S(1)}, f32[1,4480]{1,0:T(1,128)S(1)}, u32[]{:S(2)}, u32[]{:S(2)}) collective-permute-start(f32[1,4480]{1,0:T(1,128)S(1)} %broadcast_in_dim.527), channel_id=1, source_target_pairs={{0,2},{1,3},{2,0},{3,1},{4,6},{5,7},{6,4},{7,5},{8,10},{9,11},{10,... | collective-permute-start | bytes 53768 | tf_op jit(solution)/shard_map/ppermute | solution.py:27
  5.0 1.5 %collective-permute-done.1 = f32[1,4480]{1,0:T(1,128)S(1)} collective-permute-done((f32[1,4480]{1,0:T(1,128)S(1)}, f32[1,4480]{1,0:T(1,128)S(1)}, u32[]{:S(2)}, u32[]{:S(2)}) %collective-permute-start.1) | collective-permute-done | bytes 17952 | tf_op jit(solution)/shard_map/ppermute | solution.py:27
  6.5 1.4 %collective-permute-done.2 = f32[1,4480]{1,0:T(1,128)S(1)} collective-permute-done((f32[1,4480]{1,0:T(1,128)S(1)}, f32[1,4480]{1,0:T(1,128)S(1)}, u32[]{:S(2)}, u32[]{:S(2)}) %collective-permute-start.2) | collective-permute-done | bytes 17952 | tf_op jit(solution)/shard_map/ppermute | solution.py:27
  8.0 3.7 %collective-permute-start.5 = (f32[1,4480]{1,0:T(1,128)S(1)}, f32[1,4480]{1,0:T(1,128)S(1)}, u32[]{:S(2)}, u32[]{:S(2)}) collective-permute-start(f32[1,4480]{1,0:T(1,128)S(1)} %add_add_fusion.refs_0_), channel_id=1, source_target_pairs={{0,12},{1,13},{2,14},{3,15},{4,8},{5,9},{6,10},{7,11},{8,4},{9,5},... | collective-permute-start | bytes 53768 | tf_op jit(solution)/shard_map/ppermute | solution.py:27
  11.7 0.8 %collective-permute-start.3 = (f32[1,4480]{1,0:T(1,128)S(1)}, f32[1,4480]{1,0:T(1,128)S(1)}, u32[]{:S(2)}, u32[]{:S(2)}) collective-permute-start(f32[1,4480]{1,0:T(1,128)S(1)} %add_add_fusion.refs_0_), channel_id=1, source_target_pairs={{0,4},{1,5},{2,6},{3,7},{4,0},{5,1},{6,2},{7,3},{8,12},{9,13},{10,... | collective-permute-start | bytes 53768 | tf_op jit(solution)/shard_map/ppermute | solution.py:27
  12.5 1.4 %collective-permute-done.5.refs_3_ = f32[1,4480]{1,0:T(1,128)S(1)} collective-permute-done((f32[1,4480]{1,0:T(1,128)S(1)}, f32[1,4480]{1,0:T(1,128)S(1)}, u32[]{:S(2)}, u32[]{:S(2)}) %collective-permute-start.5) | collective-permute-done | bytes 17952 | tf_op jit(solution)/shard_map/ppermute | solution.py:27
  13.8 2.5 %collective-permute-done.4.refs_2_ = f32[1,4480]{1,0:T(1,128)S(1)} collective-permute-done((f32[1,4480]{1,0:T(1,128)S(1)}, f32[1,4480]{1,0:T(1,128)S(1)}, u32[]{:S(2)}, u32[]{:S(2)}) %collective-permute-start.4) | collective-permute-done | bytes 17952 | tf_op jit(solution)/shard_map/ppermute | solution.py:27
  17.5 6.8 %shard_map.50 = (f32[32,2048]{1,0:T(8,128)}, f32[32,1152]{1,0:T(8,128)}) custom-call(f32[32,6144]{1,0:T(8,128)} %x_ref.1, f32[1,4480]{1,0:T(1,128)} %copy-done.2, f32[1,4480]{1,0:T(1,128)} %copy-done.6, f32[1,4480]{1,0:T(1,128)} %copy-done.5, f32[1,4480]{1,0:T(1,128)} %copy-done.4, s32[9,32]{1,0:T(8,128)} %refs_4_.1), custom_call_target="tpu_custom_call" | custom-call | flops 25395200 | bytes 983040 | tf_op jit(solution)/shard_map/pallas_call | solution.py:102
  24.5 1.7 %collective-permute-done.6 = f32[32,2048]{1,0:T(8,128)S(1)} collective-permute-done((f32[32,2048]{1,0:T(8,128)}, f32[32,2048]{1,0:T(8,128)S(1)}, u32[]{:S(2)}, u32[]{:S(2)}) %collective-permute-start.6) | collective-permute-done | bytes 262176 | tf_op jit(solution)/shard_map/ppermute | solution.py:22
  26.1 1.0 %broadcast_select_fusion.1 = (f32[32,2048]{1,0:T(8,128)S(1)}, f32[32,2048]{1,0:T(8,128)S(1)}) fusion(f32[32,2048]{1,0:T(8,128)S(1)} %collective-permute-done.6, f32[32,2048]{1,0:T(8,128)} %get-tuple-element.16, pred[]{:T(512)S(6)} %eq.411), kind=kLoop, calls=%fused_computation.101 | loop fusion | flops 131072 | bytes 1048577 | tf_op jit(solution)/shard_map/jit(_where)/select_n | solution.py:182
  28.2 0.8 %collective-permute-start.8 = (f32[32,1792]{1,0:T(8,128)S(1)}, f32[32,1792]{1,0:T(8,128)S(1)}, u32[]{:S(2)}, u32[]{:S(2)}) collective-permute-start(f32[32,1792]{1,0:T(8,128)S(1)} %fusion.2), channel_id=1, source_target_pairs={{0,2},{1,3},{2,0},{3,1},{4,6},{5,7},{6,4},{7,5},{8,10},{9,11},{10,... | collective-permute-start | bytes 688136 | tf_op jit(solution)/shard_map/ppermute | solution.py:22
  29.1 1.3 %collective-permute-done.7 = f32[32,1152]{1,0:T(8,128)S(1)} collective-permute-done((f32[32,1152]{1,0:T(8,128)S(1)}, f32[32,1152]{1,0:T(8,128)S(1)}, u32[]{:S(2)}, u32[]{:S(2)}) %collective-permute-start.7) | collective-permute-done | bytes 147488 | tf_op jit(solution)/shard_map/ppermute | solution.py:22
  30.4 5.5 %collective-permute-done.8 = f32[32,1792]{1,0:T(8,128)S(1)} collective-permute-done((f32[32,1792]{1,0:T(8,128)S(1)}, f32[32,1792]{1,0:T(8,128)S(1)}, u32[]{:S(2)}, u32[]{:S(2)}) %collective-permute-start.8) | collective-permute-done | bytes 229408 | tf_op jit(solution)/shard_map/ppermute | solution.py:22
  37.9 0.8 %collective-permute-start.9 = (f32[32,1152]{1,0:T(8,128)S(1)}, f32[32,1152]{1,0:T(8,128)S(1)}, u32[]{:S(2)}, u32[]{:S(2)}) collective-permute-start(f32[32,1152]{1,0:T(8,128)S(1)} %fusion.16), channel_id=1, source_target_pairs={{0,2},{1,3},{2,0},{3,1},{4,6},{5,7},{6,4},{7,5},{8,10},{9,11},{10,... | collective-permute-start | bytes 442376 | tf_op jit(solution)/shard_map/ppermute | solution.py:22
  38.8 4.4 %collective-permute-done.9 = f32[32,1152]{1,0:T(8,128)S(1)} collective-permute-done((f32[32,1152]{1,0:T(8,128)S(1)}, f32[32,1152]{1,0:T(8,128)S(1)}, u32[]{:S(2)}, u32[]{:S(2)}) %collective-permute-start.9) | collective-permute-done | bytes 147488 | tf_op jit(solution)/shard_map/ppermute | solution.py:22
  44.1 1.5 %collective-permute-start.12 = (f32[32,1280]{1,0:T(8,128)S(1)}, f32[32,1280]{1,0:T(8,128)S(1)}, u32[]{:S(2)}, u32[]{:S(2)}) collective-permute-start(f32[32,1280]{1,0:T(8,128)S(1)} %fusion.12), channel_id=1, source_target_pairs={{0,8},{1,9},{2,10},{3,11},{4,12},{5,13},{6,14},{7,15},{8,0},{9,1},... | collective-permute-start | bytes 491528 | tf_op jit(solution)/shard_map/ppermute | solution.py:22
  46.6 2.1 %collective-permute-start.11 = (f32[32,1152]{1,0:T(8,128)S(1)}, f32[32,1152]{1,0:T(8,128)S(1)}, u32[]{:S(2)}, u32[]{:S(2)}) collective-permute-start(f32[32,1152]{1,0:T(8,128)S(1)} %fusion.15), channel_id=1, source_target_pairs={{0,4},{1,5},{2,6},{3,7},{4,0},{5,1},{6,2},{7,3},{8,12},{9,13},{10,... | collective-permute-start | bytes 442376 | tf_op jit(solution)/shard_map/ppermute | solution.py:22
  48.7 3.7 %collective-permute-done.11 = f32[32,1152]{1,0:T(8,128)S(1)} collective-permute-done((f32[32,1152]{1,0:T(8,128)S(1)}, f32[32,1152]{1,0:T(8,128)S(1)}, u32[]{:S(2)}, u32[]{:S(2)}) %collective-permute-start.11) | collective-permute-done | bytes 147488 | tf_op jit(solution)/shard_map/ppermute | solution.py:22
  52.4 0.8 %collective-permute-done.12 = f32[32,1280]{1,0:T(8,128)S(1)} collective-permute-done((f32[32,1280]{1,0:T(8,128)S(1)}, f32[32,1280]{1,0:T(8,128)S(1)}, u32[]{:S(2)}, u32[]{:S(2)}) %collective-permute-start.12) | collective-permute-done | bytes 163872 | tf_op jit(solution)/shard_map/ppermute | solution.py:22
  55.0 1.6 %collective-permute-start.13 = (f32[32,1152]{1,0:T(8,128)S(1)}, f32[32,1152]{1,0:T(8,128)S(1)}, u32[]{:S(2)}, u32[]{:S(2)}) collective-permute-start(f32[32,1152]{1,0:T(8,128)S(1)} %fusion.14), channel_id=1, source_target_pairs={{0,8},{1,9},{2,10},{3,11},{4,12},{5,13},{6,14},{7,15},{8,0},{9,1},... | collective-permute-start | bytes 442376 | tf_op jit(solution)/shard_map/ppermute | solution.py:22
  57.0 5.7 %collective-permute-done.13 = f32[32,1152]{1,0:T(8,128)S(1)} collective-permute-done((f32[32,1152]{1,0:T(8,128)S(1)}, f32[32,1152]{1,0:T(8,128)S(1)}, u32[]{:S(2)}, u32[]{:S(2)}) %collective-permute-start.13) | collective-permute-done | bytes 147488 | tf_op jit(solution)/shard_map/ppermute | solution.py:22
  63.8 1.0 %convolution_reduce_fusion = f32[512,128]{1,0:T(8,128)S(1)} fusion(f32[512,256,1]{1,0,2:T(8,128)S(1)} %bitcast.85, f32[8,128,256]{2,1,0:T(8,128)S(1)} %bitcast.84), kind=kOutput, calls=%fused_computation | convolution fusion | flops 805765120 | bytes 1835008 | tf_op jit(solution)/shard_map/dot_general | solution.py:151
  65.0 0.8 %collective-permute-start.15 = (f32[2048]{0:T(1024)S(1)}, f32[2048]{0:T(1024)S(1)}, u32[]{:S(2)}, u32[]{:S(2)}) collective-permute-start(f32[2048]{0:T(1024)S(1)} %reduce_max.19), channel_id=1, source_target_pairs={{0,2},{1,3},{2,0},{3,1},{4,6},{5,7},{6,4},{7,5},{8,10},{9,11},{10,... | collective-permute-start | bytes 24584 | tf_op jit(solution)/shard_map/ppermute | solution.py:27
  65.8 1.1 %collective-permute-start.14 = (f32[2048]{0:T(1024)S(1)}, f32[2048]{0:T(1024)S(1)}, u32[]{:S(2)}, u32[]{:S(2)}) collective-permute-start(f32[2048]{0:T(1024)S(1)} %reduce_max.19), channel_id=1, source_target_pairs={{0,1},{1,0},{2,3},{3,2},{4,5},{5,4},{6,7},{7,6},{8,9},{9,8},{10,11... | collective-permute-start | bytes 24584 | tf_op jit(solution)/shard_map/ppermute | solution.py:27
  66.9 1.2 %collective-permute-done.16 = f32[2048]{0:T(1024)S(1)} collective-permute-done((f32[2048]{0:T(1024)S(1)}, f32[2048]{0:T(1024)S(1)}, u32[]{:S(2)}, u32[]{:S(2)}) %collective-permute-start.16) | collective-permute-done | bytes 8224 | tf_op jit(solution)/shard_map/ppermute | solution.py:27
  68.1 0.7 collective-permute-done.15
  68.7 2.5 %collective-permute-start.19 = (f32[2048]{0:T(1024)S(1)}, f32[2048]{0:T(1024)S(1)}, u32[]{:S(2)}, u32[]{:S(2)}) collective-permute-start(f32[2048]{0:T(1024)S(1)} %maximum_maximum_fusion.1), channel_id=1, source_target_pairs={{0,12},{1,13},{2,14},{3,15},{4,8},{5,9},{6,10},{7,11},{8,4},{9,5},... | collective-permute-start | bytes 24584 | tf_op jit(solution)/shard_map/ppermute | solution.py:27
  71.2 1.9 %collective-permute-start.17 = (f32[2048]{0:T(1024)S(1)}, f32[2048]{0:T(1024)S(1)}, u32[]{:S(2)}, u32[]{:S(2)}) collective-permute-start(f32[2048]{0:T(1024)S(1)} %maximum_maximum_fusion.1), channel_id=1, source_target_pairs={{0,4},{1,5},{2,6},{3,7},{4,0},{5,1},{6,2},{7,3},{8,12},{9,13},{10,... | collective-permute-start | bytes 24584 | tf_op jit(solution)/shard_map/ppermute | solution.py:27
  73.2 1.1 %collective-permute-done.19 = f32[2048]{0:T(1024)S(1)} collective-permute-done((f32[2048]{0:T(1024)S(1)}, f32[2048]{0:T(1024)S(1)}, u32[]{:S(2)}, u32[]{:S(2)}) %collective-permute-start.19) | collective-permute-done | bytes 8224 | tf_op jit(solution)/shard_map/ppermute | solution.py:27
  74.3 1.5 %collective-permute-done.18 = f32[2048]{0:T(1024)S(1)} collective-permute-done((f32[2048]{0:T(1024)S(1)}, f32[2048]{0:T(1024)S(1)}, u32[]{:S(2)}, u32[]{:S(2)}) %collective-permute-start.18) | collective-permute-done | bytes 8224 | tf_op jit(solution)/shard_map/ppermute | solution.py:27
  75.8 0.6 maximum_maximum_fusion
  (125 shorter events, 9.7 us)
Async XLA Ops:
  0.6 23.7 %copy-start.3 = (s32[9,32]{1,0:T(8,128)S(1)}, s32[9,32]{1,0:T(8,128)}, u32[]{:S(2)}) copy-start(s32[9,32]{1,0:T(8,128)} %refs_4_.1) | copy-start | bytes 3460
  1.8 4.7 %collective-permute-start.1 = (f32[1,4480]{1,0:T(1,128)S(1)}, f32[1,4480]{1,0:T(1,128)S(1)}, u32[]{:S(2)}, u32[]{:S(2)}) collective-permute-start(f32[1,4480]{1,0:T(1,128)S(1)} %broadcast_in_dim.527), channel_id=1, source_target_pairs={{0,2},{1,3},{2,0},{3,1},{4,6},{5,7},{6,4},{7,5},{8,10},{9,11},{10,... | collective-permute-start | bytes 53768 | tf_op jit(solution)/shard_map/ppermute | solution.py:27
  4.8 3.2 %collective-permute-start.2 = (f32[1,4480]{1,0:T(1,128)S(1)}, f32[1,4480]{1,0:T(1,128)S(1)}, u32[]{:S(2)}, u32[]{:S(2)}) collective-permute-start(f32[1,4480]{1,0:T(1,128)S(1)} %broadcast_in_dim.527), channel_id=1, source_target_pairs={{0,3},{1,2},{2,1},{3,0},{4,7},{5,6},{6,5},{7,4},{8,11},{9,10},{10,... | collective-permute-start | bytes 53768 | tf_op jit(solution)/shard_map/ppermute | solution.py:27
  4.8 3.2 %collective-permute-start = (f32[1,4480]{1,0:T(1,128)S(1)}, f32[1,4480]{1,0:T(1,128)S(1)}, u32[]{:S(2)}, u32[]{:S(2)}) collective-permute-start(f32[1,4480]{1,0:T(1,128)S(1)} %broadcast_in_dim.527), channel_id=1, source_target_pairs={{0,1},{1,0},{2,3},{3,2},{4,5},{5,4},{6,7},{7,6},{8,9},{9,8},{10,11... | collective-permute-start | bytes 53768 | tf_op jit(solution)/shard_map/ppermute | solution.py:27
  8.0 8.3 %copy-start.2 = (f32[1,4480]{1,0:T(1,128)}, f32[1,4480]{1,0:T(1,128)S(1)}, u32[]{:S(2)}) copy-start(f32[1,4480]{1,0:T(1,128)S(1)} %add_add_fusion.refs_0_) | copy-start | bytes 53764
  8.0 5.8 %collective-permute-start.5 = (f32[1,4480]{1,0:T(1,128)S(1)}, f32[1,4480]{1,0:T(1,128)S(1)}, u32[]{:S(2)}, u32[]{:S(2)}) collective-permute-start(f32[1,4480]{1,0:T(1,128)S(1)} %add_add_fusion.refs_0_), channel_id=1, source_target_pairs={{0,12},{1,13},{2,14},{3,15},{4,8},{5,9},{6,10},{7,11},{8,4},{9,5},... | collective-permute-start | bytes 53768 | tf_op jit(solution)/shard_map/ppermute | solution.py:27
  11.7 4.7 %collective-permute-start.4 = (f32[1,4480]{1,0:T(1,128)S(1)}, f32[1,4480]{1,0:T(1,128)S(1)}, u32[]{:S(2)}, u32[]{:S(2)}) collective-permute-start(f32[1,4480]{1,0:T(1,128)S(1)} %add_add_fusion.refs_0_), channel_id=1, source_target_pairs={{0,8},{1,9},{2,10},{3,11},{4,12},{5,13},{6,14},{7,15},{8,0},{9,1},... | collective-permute-start | bytes 53768 | tf_op jit(solution)/shard_map/ppermute | solution.py:27
  11.7 4.7 %collective-permute-start.3 = (f32[1,4480]{1,0:T(1,128)S(1)}, f32[1,4480]{1,0:T(1,128)S(1)}, u32[]{:S(2)}, u32[]{:S(2)}) collective-permute-start(f32[1,4480]{1,0:T(1,128)S(1)} %add_add_fusion.refs_0_), channel_id=1, source_target_pairs={{0,4},{1,5},{2,6},{3,7},{4,0},{5,1},{6,2},{7,3},{8,12},{9,13},{10,... | collective-permute-start | bytes 53768 | tf_op jit(solution)/shard_map/ppermute | solution.py:27
  13.8 2.5 %copy-start.4 = (f32[1,4480]{1,0:T(1,128)}, f32[1,4480]{1,0:T(1,128)S(1)}, u32[]{:S(2)}) copy-start(f32[1,4480]{1,0:T(1,128)S(1)} %collective-permute-done.5.refs_3_) | copy-start | bytes 53764
  16.3 0.6 copy-start.5
  16.9 0.6 copy-start.6
  24.4 1.7 %collective-permute-start.6 = (f32[32,2048]{1,0:T(8,128)}, f32[32,2048]{1,0:T(8,128)S(1)}, u32[]{:S(2)}, u32[]{:S(2)}) collective-permute-start(f32[32,2048]{1,0:T(8,128)} %get-tuple-element.16), channel_id=1, source_target_pairs={{0,1},{1,0},{2,3},{3,2},{4,5},{5,4},{6,7},{7,6},{8,9},{9,8},{10,11... | collective-permute-start | bytes 786440 | tf_op jit(solution)/shard_map/ppermute | solution.py:22
  27.9 1.1 %copy-start.1 = (f32[32,1152]{1,0:T(8,128)S(1)}, f32[32,1152]{1,0:T(8,128)}, u32[]{:S(2)}) copy-start(f32[32,1152]{1,0:T(8,128)} %get-tuple-element.17) | copy-start | bytes 442372
  27.9 1.1 %copy-start.7 = (s32[8]{0:T(128)S(1)}, s32[8]{0:T(128)}, u32[]{:S(2)}) copy-start(s32[8]{0:T(128)} %param.5) | copy-start | bytes 100
  28.2 7.7 %collective-permute-start.8 = (f32[32,1792]{1,0:T(8,128)S(1)}, f32[32,1792]{1,0:T(8,128)S(1)}, u32[]{:S(2)}, u32[]{:S(2)}) collective-permute-start(f32[32,1792]{1,0:T(8,128)S(1)} %fusion.2), channel_id=1, source_target_pairs={{0,2},{1,3},{2,0},{3,1},{4,6},{5,7},{6,4},{7,5},{8,10},{9,11},{10,... | collective-permute-start | bytes 688136 | tf_op jit(solution)/shard_map/ppermute | solution.py:22
  29.0 1.4 %collective-permute-start.7 = (f32[32,1152]{1,0:T(8,128)S(1)}, f32[32,1152]{1,0:T(8,128)S(1)}, u32[]{:S(2)}, u32[]{:S(2)}) collective-permute-start(f32[32,1152]{1,0:T(8,128)S(1)} %copy-done.1), channel_id=1, source_target_pairs={{0,1},{1,0},{2,3},{3,2},{4,5},{5,4},{6,7},{7,6},{8,9},{9,8},{10,11... | collective-permute-start | bytes 442376 | tf_op jit(solution)/shard_map/ppermute | solution.py:22
  36.9 6.2 %collective-permute-start.10 = (f32[32,1536]{1,0:T(8,128)S(1)}, f32[32,1536]{1,0:T(8,128)S(1)}, u32[]{:S(2)}, u32[]{:S(2)}) collective-permute-start(f32[32,1536]{1,0:T(8,128)S(1)} %fusion.3), channel_id=1, source_target_pairs={{0,4},{1,5},{2,6},{3,7},{4,0},{5,1},{6,2},{7,3},{8,12},{9,13},{10,... | collective-permute-start | bytes 589832 | tf_op jit(solution)/shard_map/ppermute | solution.py:22
  37.9 5.2 %collective-permute-start.9 = (f32[32,1152]{1,0:T(8,128)S(1)}, f32[32,1152]{1,0:T(8,128)S(1)}, u32[]{:S(2)}, u32[]{:S(2)}) collective-permute-start(f32[32,1152]{1,0:T(8,128)S(1)} %fusion.16), channel_id=1, source_target_pairs={{0,2},{1,3},{2,0},{3,1},{4,6},{5,7},{6,4},{7,5},{8,10},{9,11},{10,... | collective-permute-start | bytes 442376 | tf_op jit(solution)/shard_map/ppermute | solution.py:22
  44.1 9.0 %collective-permute-start.12 = (f32[32,1280]{1,0:T(8,128)S(1)}, f32[32,1280]{1,0:T(8,128)S(1)}, u32[]{:S(2)}, u32[]{:S(2)}) collective-permute-start(f32[32,1280]{1,0:T(8,128)S(1)} %fusion.12), channel_id=1, source_target_pairs={{0,8},{1,9},{2,10},{3,11},{4,12},{5,13},{6,14},{7,15},{8,0},{9,1},... | collective-permute-start | bytes 491528 | tf_op jit(solution)/shard_map/ppermute | solution.py:22
  46.6 5.8 %collective-permute-start.11 = (f32[32,1152]{1,0:T(8,128)S(1)}, f32[32,1152]{1,0:T(8,128)S(1)}, u32[]{:S(2)}, u32[]{:S(2)}) collective-permute-start(f32[32,1152]{1,0:T(8,128)S(1)} %fusion.15), channel_id=1, source_target_pairs={{0,4},{1,5},{2,6},{3,7},{4,0},{5,1},{6,2},{7,3},{8,12},{9,13},{10,... | collective-permute-start | bytes 442376 | tf_op jit(solution)/shard_map/ppermute | solution.py:22
  55.0 7.7 %collective-permute-start.13 = (f32[32,1152]{1,0:T(8,128)S(1)}, f32[32,1152]{1,0:T(8,128)S(1)}, u32[]{:S(2)}, u32[]{:S(2)}) collective-permute-start(f32[32,1152]{1,0:T(8,128)S(1)} %fusion.14), channel_id=1, source_target_pairs={{0,8},{1,9},{2,10},{3,11},{4,12},{5,13},{6,14},{7,15},{8,0},{9,1},... | collective-permute-start | bytes 442376 | tf_op jit(solution)/shard_map/ppermute | solution.py:22
  64.9 11.5 %copy-start = (f32[32,2048]{1,0:T(8,128)}, f32[32,2048]{1,0:T(8,128)S(1)}, u32[]{:S(2)}) copy-start(f32[32,2048]{1,0:T(8,128)S(1)} %reshape.485) | copy-start | bytes 786436
  64.9 3.1 %collective-permute-start.16 = (f32[2048]{0:T(1024)S(1)}, f32[2048]{0:T(1024)S(1)}, u32[]{:S(2)}, u32[]{:S(2)}) collective-permute-start(f32[2048]{0:T(1024)S(1)} %reduce_max.19), channel_id=1, source_target_pairs={{0,3},{1,2},{2,1},{3,0},{4,7},{5,6},{6,5},{7,4},{8,11},{9,10},{10,... | collective-permute-start | bytes 24584 | tf_op jit(solution)/shard_map/ppermute | solution.py:27
  65.0 3.7 %collective-permute-start.15 = (f32[2048]{0:T(1024)S(1)}, f32[2048]{0:T(1024)S(1)}, u32[]{:S(2)}, u32[]{:S(2)}) collective-permute-start(f32[2048]{0:T(1024)S(1)} %reduce_max.19), channel_id=1, source_target_pairs={{0,2},{1,3},{2,0},{3,1},{4,6},{5,7},{6,4},{7,5},{8,10},{9,11},{10,... | collective-permute-start | bytes 24584 | tf_op jit(solution)/shard_map/ppermute | solution.py:27
  65.8 2.9 %collective-permute-start.14 = (f32[2048]{0:T(1024)S(1)}, f32[2048]{0:T(1024)S(1)}, u32[]{:S(2)}, u32[]{:S(2)}) collective-permute-start(f32[2048]{0:T(1024)S(1)} %reduce_max.19), channel_id=1, source_target_pairs={{0,1},{1,0},{2,3},{3,2},{4,5},{5,4},{6,7},{7,6},{8,9},{9,8},{10,11... | collective-permute-start | bytes 24584 | tf_op jit(solution)/shard_map/ppermute | solution.py:27
  68.7 5.5 %collective-permute-start.19 = (f32[2048]{0:T(1024)S(1)}, f32[2048]{0:T(1024)S(1)}, u32[]{:S(2)}, u32[]{:S(2)}) collective-permute-start(f32[2048]{0:T(1024)S(1)} %maximum_maximum_fusion.1), channel_id=1, source_target_pairs={{0,12},{1,13},{2,14},{3,15},{4,8},{5,9},{6,10},{7,11},{8,4},{9,5},... | collective-permute-start | bytes 24584 | tf_op jit(solution)/shard_map/ppermute | solution.py:27
  71.2 4.5 %collective-permute-start.18 = (f32[2048]{0:T(1024)S(1)}, f32[2048]{0:T(1024)S(1)}, u32[]{:S(2)}, u32[]{:S(2)}) collective-permute-start(f32[2048]{0:T(1024)S(1)} %maximum_maximum_fusion.1), channel_id=1, source_target_pairs={{0,8},{1,9},{2,10},{3,11},{4,12},{5,13},{6,14},{7,15},{8,0},{9,1},... | collective-permute-start | bytes 24584 | tf_op jit(solution)/shard_map/ppermute | solution.py:27
  71.2 4.5 %collective-permute-start.17 = (f32[2048]{0:T(1024)S(1)}, f32[2048]{0:T(1024)S(1)}, u32[]{:S(2)}, u32[]{:S(2)}) collective-permute-start(f32[2048]{0:T(1024)S(1)} %maximum_maximum_fusion.1), channel_id=1, source_target_pairs={{0,4},{1,5},{2,6},{3,7},{4,0},{5,1},{6,2},{7,3},{8,12},{9,13},{10,... | collective-permute-start | bytes 24584 | tf_op jit(solution)/shard_map/ppermute | solution.py:27

commit v18 on v17

--- a/solution.py
+++ b/solution.py
@@ -169,7 +169,10 @@
         needed = -(-needed // 128) * 128
         return min(TIN, needed)
 
-    partial_value = jnp.sum(filterbank[:, : length_after(0)], axis=0, keepdims=True)
+    needed = filterbank[:, : length_after(0)]
+    stage = jnp.sum(needed.reshape(-1, 8, needed.shape[1]), axis=0)
+    stage = lax.optimization_barrier(stage)
+    partial_value = jnp.sum(stage, axis=0, keepdims=True)
     total_terms = butterfly_terms(partial_value, "band", jnp.add)
     widths_seq = [length_after(section) for section in range(local_count + 1)]
     head, tail = local_tree(filterbank, total_terms, offsets, widths_seq, channels_all, TAIL_WIDTH)

time: 76.6 us -> 76.6 us (level)
  no operation moved by 1% of the time
where the time goes in v18:
time: 76.6 us; the launch traced here: 76.4 us
  waiting for transfers between devices  34.3 us (45%)
  starting transfers between devices  20.9 us (27%)
  other arithmetic  10.6 us (14%)
  Pallas kernels  6.82 us (9%)
  local copies, waits for them, and re-layouts  1.52 us (2%)
  between operations  1.29 us (2%)
  matrix products  1.03 us (1%)
    ppermute x8, waiting for transfers between devices, from_partner(): return lax.ppermute(value, axis, pairs)  23 us
    ppermute x12, starting transfers between devices, from_xor(): return lax.ppermute(value, axis, pairs)  14 us
    ppermute x12, waiting for transfers between devices, from_xor(): return lax.ppermute(value, axis, pairs)  11.3 us
    ppermute x8, starting transfers between devices, from_partner(): return lax.ppermute(value, axis, pairs)  6.85 us
    pallas_call x1, Pallas kernels, local_tree(): pl.pallas_call(functools.partial(local_tree_kernel, tuple(widths_seq), fl...  6.82 us
    select_n x56, other arithmetic, shift_rows(): jnp.where(chosen, current[:, span:span + keep_len], current[:, :keep_len])  6.19 us
  transfers between devices with their start and end apart: 20, of which 15 were waited for; matrix products, arithmetic and copies ran while one was open for 3% of the time, Pallas kernels for 0%

profile of v18, /device:TPU:0, one launch (start us, length us, event | category | flops | bytes accessed | tf_op | source)
XLA Modules:
  0.0 76.4 jit_solution(12898785393754203283)
XLA Ops:
  0.6 1.1 %bitcast_reduce_fusion = f32[8,4480]{1,0:T(8,128)S(1)} fusion(f32[32,6144]{1,0:T(8,128)} %x_ref.1), kind=kLoop, calls=%fused_computation.4 | loop fusion | flops 107520 | bytes 716800 | tf_op jit(solution)/shard_map/reduce_sum | solution.py:173
  1.8 3.0 %collective-permute-start.1 = (f32[1,4480]{1,0:T(1,128)S(1)}, f32[1,4480]{1,0:T(1,128)S(1)}, u32[]{:S(2)}, u32[]{:S(2)}) collective-permute-start(f32[1,4480]{1,0:T(1,128)S(1)} %broadcast_in_dim.527), channel_id=1, source_target_pairs={{0,2},{1,3},{2,0},{3,1},{4,6},{5,7},{6,4},{7,5},{8,10},{9,11},{10,... | collective-permute-start | bytes 53768 | tf_op jit(solution)/shard_map/ppermute | solution.py:27
  5.0 1.5 %collective-permute-done.1 = f32[1,4480]{1,0:T(1,128)S(1)} collective-permute-done((f32[1,4480]{1,0:T(1,128)S(1)}, f32[1,4480]{1,0:T(1,128)S(1)}, u32[]{:S(2)}, u32[]{:S(2)}) %collective-permute-start.1) | collective-permute-done | bytes 17952 | tf_op jit(solution)/shard_map/ppermute | solution.py:27
  6.6 1.4 %collective-permute-done.2 = f32[1,4480]{1,0:T(1,128)S(1)} collective-permute-done((f32[1,4480]{1,0:T(1,128)S(1)}, f32[1,4480]{1,0:T(1,128)S(1)}, u32[]{:S(2)}, u32[]{:S(2)}) %collective-permute-start.2) | collective-permute-done | bytes 17952 | tf_op jit(solution)/shard_map/ppermute | solution.py:27
  8.1 3.7 %collective-permute-start.5 = (f32[1,4480]{1,0:T(1,128)S(1)}, f32[1,4480]{1,0:T(1,128)S(1)}, u32[]{:S(2)}, u32[]{:S(2)}) collective-permute-start(f32[1,4480]{1,0:T(1,128)S(1)} %add_add_fusion.refs_0_), channel_id=1, source_target_pairs={{0,12},{1,13},{2,14},{3,15},{4,8},{5,9},{6,10},{7,11},{8,4},{9,5},... | collective-permute-start | bytes 53768 | tf_op jit(solution)/shard_map/ppermute | solution.py:27
  11.7 0.8 %collective-permute-start.3 = (f32[1,4480]{1,0:T(1,128)S(1)}, f32[1,4480]{1,0:T(1,128)S(1)}, u32[]{:S(2)}, u32[]{:S(2)}) collective-permute-start(f32[1,4480]{1,0:T(1,128)S(1)} %add_add_fusion.refs_0_), channel_id=1, source_target_pairs={{0,4},{1,5},{2,6},{3,7},{4,0},{5,1},{6,2},{7,3},{8,12},{9,13},{10,... | collective-permute-start | bytes 53768 | tf_op jit(solution)/shard_map/ppermute | solution.py:27
  12.5 1.4 %collective-permute-done.5.refs_3_ = f32[1,4480]{1,0:T(1,128)S(1)} collective-permute-done((f32[1,4480]{1,0:T(1,128)S(1)}, f32[1,4480]{1,0:T(1,128)S(1)}, u32[]{:S(2)}, u32[]{:S(2)}) %collective-permute-start.5) | collective-permute-done | bytes 17952 | tf_op jit(solution)/shard_map/ppermute | solution.py:27
  13.9 2.5 %collective-permute-done.4.refs_2_ = f32[1,4480]{1,0:T(1,128)S(1)} collective-permute-done((f32[1,4480]{1,0:T(1,128)S(1)}, f32[1,4480]{1,0:T(1,128)S(1)}, u32[]{:S(2)}, u32[]{:S(2)}) %collective-permute-start.4) | collective-permute-done | bytes 17952 | tf_op jit(solution)/shard_map/ppermute | solution.py:27
  17.6 6.8 %shard_map.50 = (f32[32,2048]{1,0:T(8,128)}, f32[32,1152]{1,0:T(8,128)}) custom-call(f32[32,6144]{1,0:T(8,128)} %x_ref.1, f32[1,4480]{1,0:T(1,128)} %copy-done.2, f32[1,4480]{1,0:T(1,128)} %copy-done.6, f32[1,4480]{1,0:T(1,128)} %copy-done.5, f32[1,4480]{1,0:T(1,128)} %copy-done.4, s32[9,32]{1,0:T(8,128)} %refs_4_.1), custom_call_target="tpu_custom_call" | custom-call | flops 25395200 | bytes 983040 | tf_op jit(solution)/shard_map/pallas_call | solution.py:102
  24.5 1.7 %collective-permute-done.6 = f32[32,2048]{1,0:T(8,128)S(1)} collective-permute-done((f32[32,2048]{1,0:T(8,128)}, f32[32,2048]{1,0:T(8,128)S(1)}, u32[]{:S(2)}, u32[]{:S(2)}) %collective-permute-start.6) | collective-permute-done | bytes 262176 | tf_op jit(solution)/shard_map/ppermute | solution.py:22
  26.1 1.0 %broadcast_select_fusion.1 = (f32[32,2048]{1,0:T(8,128)S(1)}, f32[32,2048]{1,0:T(8,128)S(1)}) fusion(f32[32,2048]{1,0:T(8,128)S(1)} %collective-permute-done.6, f32[32,2048]{1,0:T(8,128)} %get-tuple-element.16, pred[]{:T(512)S(6)} %eq.411), kind=kLoop, calls=%fused_computation.101 | loop fusion | flops 131072 | bytes 1048577 | tf_op jit(solution)/shard_map/jit(_where)/select_n | solution.py:185
  28.2 0.8 %collective-permute-start.8 = (f32[32,1792]{1,0:T(8,128)S(1)}, f32[32,1792]{1,0:T(8,128)S(1)}, u32[]{:S(2)}, u32[]{:S(2)}) collective-permute-start(f32[32,1792]{1,0:T(8,128)S(1)} %fusion.2), channel_id=1, source_target_pairs={{0,2},{1,3},{2,0},{3,1},{4,6},{5,7},{6,4},{7,5},{8,10},{9,11},{10,... | collective-permute-start | bytes 688136 | tf_op jit(solution)/shard_map/ppermute | solution.py:22
  29.1 1.3 %collective-permute-done.7 = f32[32,1152]{1,0:T(8,128)S(1)} collective-permute-done((f32[32,1152]{1,0:T(8,128)S(1)}, f32[32,1152]{1,0:T(8,128)S(1)}, u32[]{:S(2)}, u32[]{:S(2)}) %collective-permute-start.7) | collective-permute-done | bytes 147488 | tf_op jit(solution)/shard_map/ppermute | solution.py:22
  30.4 5.5 %collective-permute-done.8 = f32[32,1792]{1,0:T(8,128)S(1)} collective-permute-done((f32[32,1792]{1,0:T(8,128)S(1)}, f32[32,1792]{1,0:T(8,128)S(1)}, u32[]{:S(2)}, u32[]{:S(2)}) %collective-permute-start.8) | collective-permute-done | bytes 229408 | tf_op jit(solution)/shard_map/ppermute | solution.py:22
  38.0 0.8 %collective-permute-start.9 = (f32[32,1152]{1,0:T(8,128)S(1)}, f32[32,1152]{1,0:T(8,128)S(1)}, u32[]{:S(2)}, u32[]{:S(2)}) collective-permute-start(f32[32,1152]{1,0:T(8,128)S(1)} %fusion.16), channel_id=1, source_target_pairs={{0,2},{1,3},{2,0},{3,1},{4,6},{5,7},{6,4},{7,5},{8,10},{9,11},{10,... | collective-permute-start | bytes 442376 | tf_op jit(solution)/shard_map/ppermute | solution.py:22
  38.8 4.4 %collective-permute-done.9 = f32[32,1152]{1,0:T(8,128)S(1)} collective-permute-done((f32[32,1152]{1,0:T(8,128)S(1)}, f32[32,1152]{1,0:T(8,128)S(1)}, u32[]{:S(2)}, u32[]{:S(2)}) %collective-permute-start.9) | collective-permute-done | bytes 147488 | tf_op jit(solution)/shard_map/ppermute | solution.py:22
  44.2 1.5 %collective-permute-start.12 = (f32[32,1280]{1,0:T(8,128)S(1)}, f32[32,1280]{1,0:T(8,128)S(1)}, u32[]{:S(2)}, u32[]{:S(2)}) collective-permute-start(f32[32,1280]{1,0:T(8,128)S(1)} %fusion.12), channel_id=1, source_target_pairs={{0,8},{1,9},{2,10},{3,11},{4,12},{5,13},{6,14},{7,15},{8,0},{9,1},... | collective-permute-start | bytes 491528 | tf_op jit(solution)/shard_map/ppermute | solution.py:22
  46.6 2.1 %collective-permute-start.11 = (f32[32,1152]{1,0:T(8,128)S(1)}, f32[32,1152]{1,0:T(8,128)S(1)}, u32[]{:S(2)}, u32[]{:S(2)}) collective-permute-start(f32[32,1152]{1,0:T(8,128)S(1)} %fusion.15), channel_id=1, source_target_pairs={{0,4},{1,5},{2,6},{3,7},{4,0},{5,1},{6,2},{7,3},{8,12},{9,13},{10,... | collective-permute-start | bytes 442376 | tf_op jit(solution)/shard_map/ppermute | solution.py:22
  48.7 3.7 %collective-permute-done.11 = f32[32,1152]{1,0:T(8,128)S(1)} collective-permute-done((f32[32,1152]{1,0:T(8,128)S(1)}, f32[32,1152]{1,0:T(8,128)S(1)}, u32[]{:S(2)}, u32[]{:S(2)}) %collective-permute-start.11) | collective-permute-done | bytes 147488 | tf_op jit(solution)/shard_map/ppermute | solution.py:22
  52.4 0.8 %collective-permute-done.12 = f32[32,1280]{1,0:T(8,128)S(1)} collective-permute-done((f32[32,1280]{1,0:T(8,128)S(1)}, f32[32,1280]{1,0:T(8,128)S(1)}, u32[]{:S(2)}, u32[]{:S(2)}) %collective-permute-start.12) | collective-permute-done | bytes 163872 | tf_op jit(solution)/shard_map/ppermute | solution.py:22
  55.0 1.6 %collective-permute-start.13 = (f32[32,1152]{1,0:T(8,128)S(1)}, f32[32,1152]{1,0:T(8,128)S(1)}, u32[]{:S(2)}, u32[]{:S(2)}) collective-permute-start(f32[32,1152]{1,0:T(8,128)S(1)} %fusion.14), channel_id=1, source_target_pairs={{0,8},{1,9},{2,10},{3,11},{4,12},{5,13},{6,14},{7,15},{8,0},{9,1},... | collective-permute-start | bytes 442376 | tf_op jit(solution)/shard_map/ppermute | solution.py:22
  57.0 5.7 %collective-permute-done.13 = f32[32,1152]{1,0:T(8,128)S(1)} collective-permute-done((f32[32,1152]{1,0:T(8,128)S(1)}, f32[32,1152]{1,0:T(8,128)S(1)}, u32[]{:S(2)}, u32[]{:S(2)}) %collective-permute-start.13) | collective-permute-done | bytes 147488 | tf_op jit(solution)/shard_map/ppermute | solution.py:22
  63.8 1.0 %convolution_reduce_fusion = f32[512,128]{1,0:T(8,128)S(1)} fusion(f32[512,256,1]{1,0,2:T(8,128)S(1)} %bitcast.87, f32[8,128,256]{2,1,0:T(8,128)S(1)} %bitcast.86), kind=kOutput, calls=%fused_computation | convolution fusion | flops 805765120 | bytes 1835008 | tf_op jit(solution)/shard_map/dot_general | solution.py:151
  65.0 0.8 %collective-permute-start.15 = (f32[2048]{0:T(1024)S(1)}, f32[2048]{0:T(1024)S(1)}, u32[]{:S(2)}, u32[]{:S(2)}) collective-permute-start(f32[2048]{0:T(1024)S(1)} %reduce_max.19), channel_id=1, source_target_pairs={{0,2},{1,3},{2,0},{3,1},{4,6},{5,7},{6,4},{7,5},{8,10},{9,11},{10,... | collective-permute-start | bytes 24584 | tf_op jit(solution)/shard_map/ppermute | solution.py:27
  65.8 1.1 %collective-permute-start.14 = (f32[2048]{0:T(1024)S(1)}, f32[2048]{0:T(1024)S(1)}, u32[]{:S(2)}, u32[]{:S(2)}) collective-permute-start(f32[2048]{0:T(1024)S(1)} %reduce_max.19), channel_id=1, source_target_pairs={{0,1},{1,0},{2,3},{3,2},{4,5},{5,4},{6,7},{7,6},{8,9},{9,8},{10,11... | collective-permute-start | bytes 24584 | tf_op jit(solution)/shard_map/ppermute | solution.py:27
  66.9 1.2 %collective-permute-done.16 = f32[2048]{0:T(1024)S(1)} collective-permute-done((f32[2048]{0:T(1024)S(1)}, f32[2048]{0:T(1024)S(1)}, u32[]{:S(2)}, u32[]{:S(2)}) %collective-permute-start.16) | collective-permute-done | bytes 8224 | tf_op jit(solution)/shard_map/ppermute | solution.py:27
  68.1 0.7 collective-permute-done.15
  68.8 2.5 %collective-permute-start.19 = (f32[2048]{0:T(1024)S(1)}, f32[2048]{0:T(1024)S(1)}, u32[]{:S(2)}, u32[]{:S(2)}) collective-permute-start(f32[2048]{0:T(1024)S(1)} %maximum_maximum_fusion.1), channel_id=1, source_target_pairs={{0,12},{1,13},{2,14},{3,15},{4,8},{5,9},{6,10},{7,11},{8,4},{9,5},... | collective-permute-start | bytes 24584 | tf_op jit(solution)/shard_map/ppermute | solution.py:27
  71.3 1.9 %collective-permute-start.17 = (f32[2048]{0:T(1024)S(1)}, f32[2048]{0:T(1024)S(1)}, u32[]{:S(2)}, u32[]{:S(2)}) collective-permute-start(f32[2048]{0:T(1024)S(1)} %maximum_maximum_fusion.1), channel_id=1, source_target_pairs={{0,4},{1,5},{2,6},{3,7},{4,0},{5,1},{6,2},{7,3},{8,12},{9,13},{10,... | collective-permute-start | bytes 24584 | tf_op jit(solution)/shard_map/ppermute | solution.py:27
  73.2 1.1 %collective-permute-done.19 = f32[2048]{0:T(1024)S(1)} collective-permute-done((f32[2048]{0:T(1024)S(1)}, f32[2048]{0:T(1024)S(1)}, u32[]{:S(2)}, u32[]{:S(2)}) %collective-permute-start.19) | collective-permute-done | bytes 8224 | tf_op jit(solution)/shard_map/ppermute | solution.py:27
  74.3 1.5 %collective-permute-done.18 = f32[2048]{0:T(1024)S(1)} collective-permute-done((f32[2048]{0:T(1024)S(1)}, f32[2048]{0:T(1024)S(1)}, u32[]{:S(2)}, u32[]{:S(2)}) %collective-permute-start.18) | collective-permute-done | bytes 8224 | tf_op jit(solution)/shard_map/ppermute | solution.py:27
  75.8 0.6 maximum_maximum_fusion
  (126 shorter events, 9.7 us)
Async XLA Ops:
  0.6 23.8 %copy-start.3 = (s32[9,32]{1,0:T(8,128)S(1)}, s32[9,32]{1,0:T(8,128)}, u32[]{:S(2)}) copy-start(s32[9,32]{1,0:T(8,128)} %refs_4_.1) | copy-start | bytes 3460
  1.8 4.7 %collective-permute-start.1 = (f32[1,4480]{1,0:T(1,128)S(1)}, f32[1,4480]{1,0:T(1,128)S(1)}, u32[]{:S(2)}, u32[]{:S(2)}) collective-permute-start(f32[1,4480]{1,0:T(1,128)S(1)} %broadcast_in_dim.527), channel_id=1, source_target_pairs={{0,2},{1,3},{2,0},{3,1},{4,6},{5,7},{6,4},{7,5},{8,10},{9,11},{10,... | collective-permute-start | bytes 53768 | tf_op jit(solution)/shard_map/ppermute | solution.py:27
  4.8 3.2 %collective-permute-start.2 = (f32[1,4480]{1,0:T(1,128)S(1)}, f32[1,4480]{1,0:T(1,128)S(1)}, u32[]{:S(2)}, u32[]{:S(2)}) collective-permute-start(f32[1,4480]{1,0:T(1,128)S(1)} %broadcast_in_dim.527), channel_id=1, source_target_pairs={{0,3},{1,2},{2,1},{3,0},{4,7},{5,6},{6,5},{7,4},{8,11},{9,10},{10,... | collective-permute-start | bytes 53768 | tf_op jit(solution)/shard_map/ppermute | solution.py:27
  4.8 3.2 %collective-permute-start = (f32[1,4480]{1,0:T(1,128)S(1)}, f32[1,4480]{1,0:T(1,128)S(1)}, u32[]{:S(2)}, u32[]{:S(2)}) collective-permute-start(f32[1,4480]{1,0:T(1,128)S(1)} %broadcast_in_dim.527), channel_id=1, source_target_pairs={{0,1},{1,0},{2,3},{3,2},{4,5},{5,4},{6,7},{7,6},{8,9},{9,8},{10,11... | collective-permute-start | bytes 53768 | tf_op jit(solution)/shard_map/ppermute | solution.py:27
  8.0 8.3 %copy-start.2 = (f32[1,4480]{1,0:T(1,128)}, f32[1,4480]{1,0:T(1,128)S(1)}, u32[]{:S(2)}) copy-start(f32[1,4480]{1,0:T(1,128)S(1)} %add_add_fusion.refs_0_) | copy-start | bytes 53764
  8.1 5.8 %collective-permute-start.5 = (f32[1,4480]{1,0:T(1,128)S(1)}, f32[1,4480]{1,0:T(1,128)S(1)}, u32[]{:S(2)}, u32[]{:S(2)}) collective-permute-start(f32[1,4480]{1,0:T(1,128)S(1)} %add_add_fusion.refs_0_), channel_id=1, source_target_pairs={{0,12},{1,13},{2,14},{3,15},{4,8},{5,9},{6,10},{7,11},{8,4},{9,5},... | collective-permute-start | bytes 53768 | tf_op jit(solution)/shard_map/ppermute | solution.py:27
  11.7 4.7 %collective-permute-start.4 = (f32[1,4480]{1,0:T(1,128)S(1)}, f32[1,4480]{1,0:T(1,128)S(1)}, u32[]{:S(2)}, u32[]{:S(2)}) collective-permute-start(f32[1,4480]{1,0:T(1,128)S(1)} %add_add_fusion.refs_0_), channel_id=1, source_target_pairs={{0,8},{1,9},{2,10},{3,11},{4,12},{5,13},{6,14},{7,15},{8,0},{9,1},... | collective-permute-start | bytes 53768 | tf_op jit(solution)/shard_map/ppermute | solution.py:27
  11.7 4.7 %collective-permute-start.3 = (f32[1,4480]{1,0:T(1,128)S(1)}, f32[1,4480]{1,0:T(1,128)S(1)}, u32[]{:S(2)}, u32[]{:S(2)}) collective-permute-start(f32[1,4480]{1,0:T(1,128)S(1)} %add_add_fusion.refs_0_), channel_id=1, source_target_pairs={{0,4},{1,5},{2,6},{3,7},{4,0},{5,1},{6,2},{7,3},{8,12},{9,13},{10,... | collective-permute-start | bytes 53768 | tf_op jit(solution)/shard_map/ppermute | solution.py:27
  13.9 2.5 %copy-start.4 = (f32[1,4480]{1,0:T(1,128)}, f32[1,4480]{1,0:T(1,128)S(1)}, u32[]{:S(2)}) copy-start(f32[1,4480]{1,0:T(1,128)S(1)} %collective-permute-done.5.refs_3_) | copy-start | bytes 53764
  16.4 0.6 copy-start.5
  17.0 0.6 copy-start.6
  24.4 1.7 %collective-permute-start.6 = (f32[32,2048]{1,0:T(8,128)}, f32[32,2048]{1,0:T(8,128)S(1)}, u32[]{:S(2)}, u32[]{:S(2)}) collective-permute-start(f32[32,2048]{1,0:T(8,128)} %get-tuple-element.16), channel_id=1, source_target_pairs={{0,1},{1,0},{2,3},{3,2},{4,5},{5,4},{6,7},{7,6},{8,9},{9,8},{10,11... | collective-permute-start | bytes 786440 | tf_op jit(solution)/shard_map/ppermute | solution.py:22
  27.9 1.1 %copy-start.1 = (f32[32,1152]{1,0:T(8,128)S(1)}, f32[32,1152]{1,0:T(8,128)}, u32[]{:S(2)}) copy-start(f32[32,1152]{1,0:T(8,128)} %get-tuple-element.17) | copy-start | bytes 442372
  27.9 1.1 %copy-start.7 = (s32[8]{0:T(128)S(1)}, s32[8]{0:T(128)}, u32[]{:S(2)}) copy-start(s32[8]{0:T(128)} %param.5) | copy-start | bytes 100
  28.2 7.7 %collective-permute-start.8 = (f32[32,1792]{1,0:T(8,128)S(1)}, f32[32,1792]{1,0:T(8,128)S(1)}, u32[]{:S(2)}, u32[]{:S(2)}) collective-permute-start(f32[32,1792]{1,0:T(8,128)S(1)} %fusion.2), channel_id=1, source_target_pairs={{0,2},{1,3},{2,0},{3,1},{4,6},{5,7},{6,4},{7,5},{8,10},{9,11},{10,... | collective-permute-start | bytes 688136 | tf_op jit(solution)/shard_map/ppermute | solution.py:22
  29.0 1.4 %collective-permute-start.7 = (f32[32,1152]{1,0:T(8,128)S(1)}, f32[32,1152]{1,0:T(8,128)S(1)}, u32[]{:S(2)}, u32[]{:S(2)}) collective-permute-start(f32[32,1152]{1,0:T(8,128)S(1)} %copy-done.1), channel_id=1, source_target_pairs={{0,1},{1,0},{2,3},{3,2},{4,5},{5,4},{6,7},{7,6},{8,9},{9,8},{10,11... | collective-permute-start | bytes 442376 | tf_op jit(solution)/shard_map/ppermute | solution.py:22
  37.0 6.2 %collective-permute-start.10 = (f32[32,1536]{1,0:T(8,128)S(1)}, f32[32,1536]{1,0:T(8,128)S(1)}, u32[]{:S(2)}, u32[]{:S(2)}) collective-permute-start(f32[32,1536]{1,0:T(8,128)S(1)} %fusion.3), channel_id=1, source_target_pairs={{0,4},{1,5},{2,6},{3,7},{4,0},{5,1},{6,2},{7,3},{8,12},{9,13},{10,... | collective-permute-start | bytes 589832 | tf_op jit(solution)/shard_map/ppermute | solution.py:22
  38.0 5.2 %collective-permute-start.9 = (f32[32,1152]{1,0:T(8,128)S(1)}, f32[32,1152]{1,0:T(8,128)S(1)}, u32[]{:S(2)}, u32[]{:S(2)}) collective-permute-start(f32[32,1152]{1,0:T(8,128)S(1)} %fusion.16), channel_id=1, source_target_pairs={{0,2},{1,3},{2,0},{3,1},{4,6},{5,7},{6,4},{7,5},{8,10},{9,11},{10,... | collective-permute-start | bytes 442376 | tf_op jit(solution)/shard_map/ppermute | solution.py:22
  44.2 9.0 %collective-permute-start.12 = (f32[32,1280]{1,0:T(8,128)S(1)}, f32[32,1280]{1,0:T(8,128)S(1)}, u32[]{:S(2)}, u32[]{:S(2)}) collective-permute-start(f32[32,1280]{1,0:T(8,128)S(1)} %fusion.12), channel_id=1, source_target_pairs={{0,8},{1,9},{2,10},{3,11},{4,12},{5,13},{6,14},{7,15},{8,0},{9,1},... | collective-permute-start | bytes 491528 | tf_op jit(solution)/shard_map/ppermute | solution.py:22
  46.6 5.8 %collective-permute-start.11 = (f32[32,1152]{1,0:T(8,128)S(1)}, f32[32,1152]{1,0:T(8,128)S(1)}, u32[]{:S(2)}, u32[]{:S(2)}) collective-permute-start(f32[32,1152]{1,0:T(8,128)S(1)} %fusion.15), channel_id=1, source_target_pairs={{0,4},{1,5},{2,6},{3,7},{4,0},{5,1},{6,2},{7,3},{8,12},{9,13},{10,... | collective-permute-start | bytes 442376 | tf_op jit(solution)/shard_map/ppermute | solution.py:22
  55.0 7.7 %collective-permute-start.13 = (f32[32,1152]{1,0:T(8,128)S(1)}, f32[32,1152]{1,0:T(8,128)S(1)}, u32[]{:S(2)}, u32[]{:S(2)}) collective-permute-start(f32[32,1152]{1,0:T(8,128)S(1)} %fusion.14), channel_id=1, source_target_pairs={{0,8},{1,9},{2,10},{3,11},{4,12},{5,13},{6,14},{7,15},{8,0},{9,1},... | collective-permute-start | bytes 442376 | tf_op jit(solution)/shard_map/ppermute | solution.py:22
  64.9 11.5 %copy-start = (f32[32,2048]{1,0:T(8,128)}, f32[32,2048]{1,0:T(8,128)S(1)}, u32[]{:S(2)}) copy-start(f32[32,2048]{1,0:T(8,128)S(1)} %reshape.489) | copy-start | bytes 786436
  65.0 3.1 %collective-permute-start.16 = (f32[2048]{0:T(1024)S(1)}, f32[2048]{0:T(1024)S(1)}, u32[]{:S(2)}, u32[]{:S(2)}) collective-permute-start(f32[2048]{0:T(1024)S(1)} %reduce_max.19), channel_id=1, source_target_pairs={{0,3},{1,2},{2,1},{3,0},{4,7},{5,6},{6,5},{7,4},{8,11},{9,10},{10,... | collective-permute-start | bytes 24584 | tf_op jit(solution)/shard_map/ppermute | solution.py:27
  65.0 3.7 %collective-permute-start.15 = (f32[2048]{0:T(1024)S(1)}, f32[2048]{0:T(1024)S(1)}, u32[]{:S(2)}, u32[]{:S(2)}) collective-permute-start(f32[2048]{0:T(1024)S(1)} %reduce_max.19), channel_id=1, source_target_pairs={{0,2},{1,3},{2,0},{3,1},{4,6},{5,7},{6,4},{7,5},{8,10},{9,11},{10,... | collective-permute-start | bytes 24584 | tf_op jit(solution)/shard_map/ppermute | solution.py:27
  65.8 2.9 %collective-permute-start.14 = (f32[2048]{0:T(1024)S(1)}, f32[2048]{0:T(1024)S(1)}, u32[]{:S(2)}, u32[]{:S(2)}) collective-permute-start(f32[2048]{0:T(1024)S(1)} %reduce_max.19), channel_id=1, source_target_pairs={{0,1},{1,0},{2,3},{3,2},{4,5},{5,4},{6,7},{7,6},{8,9},{9,8},{10,11... | collective-permute-start | bytes 24584 | tf_op jit(solution)/shard_map/ppermute | solution.py:27
  68.8 5.5 %collective-permute-start.19 = (f32[2048]{0:T(1024)S(1)}, f32[2048]{0:T(1024)S(1)}, u32[]{:S(2)}, u32[]{:S(2)}) collective-permute-start(f32[2048]{0:T(1024)S(1)} %maximum_maximum_fusion.1), channel_id=1, source_target_pairs={{0,12},{1,13},{2,14},{3,15},{4,8},{5,9},{6,10},{7,11},{8,4},{9,5},... | collective-permute-start | bytes 24584 | tf_op jit(solution)/shard_map/ppermute | solution.py:27
  71.3 4.5 %collective-permute-start.18 = (f32[2048]{0:T(1024)S(1)}, f32[2048]{0:T(1024)S(1)}, u32[]{:S(2)}, u32[]{:S(2)}) collective-permute-start(f32[2048]{0:T(1024)S(1)} %maximum_maximum_fusion.1), channel_id=1, source_target_pairs={{0,8},{1,9},{2,10},{3,11},{4,12},{5,13},{6,14},{7,15},{8,0},{9,1},... | collective-permute-start | bytes 24584 | tf_op jit(solution)/shard_map/ppermute | solution.py:27
  71.3 4.5 %collective-permute-start.17 = (f32[2048]{0:T(1024)S(1)}, f32[2048]{0:T(1024)S(1)}, u32[]{:S(2)}, u32[]{:S(2)}) collective-permute-start(f32[2048]{0:T(1024)S(1)} %maximum_maximum_fusion.1), channel_id=1, source_target_pairs={{0,4},{1,5},{2,6},{3,7},{4,0},{5,1},{6,2},{7,3},{8,12},{9,13},{10,... | collective-permute-start | bytes 24584 | tf_op jit(solution)/shard_map/ppermute | solution.py:27

commit v19 on v17

--- a/solution.py
+++ b/solution.py
@@ -62,12 +62,13 @@
     return current
 
 
-def local_tree_kernel(widths_seq, channels_all, term_count, x_ref, *refs):
+def local_tree_kernel(widths_seq, channels_all, term_count, column, x_ref, *refs):
     term_refs = refs[:term_count]
-    offsets_ref, head_ref, tail_ref = refs[term_count:]
+    offsets_ref, out_ref = refs[term_count:]
     rows = x_ref.shape[0]
-    total = combine_terms([ref[:, : widths_seq[0]] for ref in term_refs], jnp.add)
-    cur = x_ref[:, : widths_seq[0]] - total / channels_all
+    window = pl.ds(column, widths_seq[0])
+    total = combine_terms([ref[:, window] for ref in term_refs], jnp.add)
+    cur = x_ref[:, window] - total / channels_all
     row_id = lax.broadcasted_iota(jnp.int32, (rows, 1), 0)
     diagonal = lax.broadcasted_iota(jnp.int32, (rows, rows), 0) == lax.broadcasted_iota(
         jnp.int32, (rows, rows), 1
@@ -89,24 +90,18 @@
             chosen = (amount >> bit_index & 1) == 1
             shifted = jnp.where(chosen, pltpu.roll(shifted, width - span, axis=1), shifted)
         cur = lower[:, :new_width] + shifted[:, :new_width]
-    head_width = head_ref.shape[1]
-    head_ref[...] = cur[:, :head_width]
-    tail_ref[...] = cur[:, head_width:]
-
-
-def local_tree(filterbank, total_terms, offsets, widths_seq, channels_all, tail_width):
+    out_ref[...] = cur
+
+
+def local_tree(filterbank, total_terms, offsets, widths_seq, channels_all, column):
     rows = filterbank.shape[0]
     vmem = pl.BlockSpec(memory_space=pltpu.VMEM)
     work = rows * sum(widths_seq[:-1])
-    head_width = widths_seq[-1] - tail_width
     return pl.pallas_call(
-        functools.partial(local_tree_kernel, tuple(widths_seq), float(channels_all), len(total_terms)),
-        out_shape=(
-            jax.ShapeDtypeStruct((rows, head_width), jnp.float32),
-            jax.ShapeDtypeStruct((rows, tail_width), jnp.float32),
-        ),
+        functools.partial(local_tree_kernel, tuple(widths_seq), float(channels_all), len(total_terms), column),
+        out_shape=jax.ShapeDtypeStruct((rows, widths_seq[-1]), jnp.float32),
         in_specs=[vmem] * (len(total_terms) + 2),
-        out_specs=(vmem, vmem),
+        out_specs=vmem,
         cost_estimate=pl.CostEstimate(
             flops=40 * work, transcendentals=0, bytes_accessed=4 * (rows * widths_seq[0] + rows * widths_seq[-1])
         ),
@@ -172,7 +167,9 @@
     partial_value = jnp.sum(filterbank[:, : length_after(0)], axis=0, keepdims=True)
     total_terms = butterfly_terms(partial_value, "band", jnp.add)
     widths_seq = [length_after(section) for section in range(local_count + 1)]
-    head, tail = local_tree(filterbank, total_terms, offsets, widths_seq, channels_all, TAIL_WIDTH)
+    head_widths = [width - widths_seq[-1] + (widths_seq[-1] - TAIL_WIDTH) for width in widths_seq]
+    tail_widths = [width - (widths_seq[-1] - TAIL_WIDTH) for width in widths_seq]
+    head = local_tree(filterbank, total_terms, offsets, head_widths, channels_all, 0)
     band_index = lax.axis_index("band")
     bit_count = band_count.bit_length() - 1
     tail_width = TAIL_WIDTH
@@ -189,7 +186,6 @@
         return lower_window[:, :tail_width] + shift_rows(upper_window, amounts, tail_width)
 
     partner_head = from_partner(head, "band", 0)
-    tail, partner_head = lax.optimization_barrier((tail, partner_head))
     pending = None
     for bit_index in range(bit_count):
         amounts = offsets[local_count + bit_index]
@@ -198,6 +194,11 @@
         new_head = lower_head[:, :head_width] + shift_rows(upper_head, amounts, head_width)
         if bit_index + 1 < bit_count:
             next_partner_head = from_partner(new_head, "band", bit_index + 1)
+        if bit_index == 0:
+            late_input, new_head = lax.optimization_barrier((filterbank, new_head))
+            tail = local_tree(
+                late_input, total_terms, offsets, tail_widths, channels_all, widths_seq[-1] - TAIL_WIDTH
+            )
         if pending is not None:
             waiting, ordered_head = lax.optimization_barrier((pending[1], new_head))
             tail = finish_tail(pending[:1] + (waiting,) + pending[2:])

time: 76.6 us -> 77.6 us (1.013)
  Pallas kernels: 6.82 us -> 10 us
  waiting for transfers between devices: 34.3 us -> 32.5 us
  starting transfers between devices: 20.9 us -> 20 us
    pallas_call x1 -> x2, Pallas kernels: 6.82 us -> 10 us  [local_tree(): pl.pallas_call(functools.partial(local_tree_kernel, tuple(widths_seq), fl...]
    ppermute x8, waiting for transfers between devices: 23 us -> 20.5 us  [from_partner(): return lax.ppermute(value, axis, pairs)]
    ppermute x8, starting transfers between devices: 6.85 us -> 5.77 us  [from_partner(): return lax.ppermute(value, axis, pairs)]
  transfers between devices with their start and end apart: 20 -> 20, of which waited for: 15 -> 15; matrix products, arithmetic and copies ran while one was open for 3% -> 3% of each run, Pallas kernels for 0% -> 6%
where the time goes in v19:
time: 77.6 us; the launch traced here: 77.3 us
  waiting for transfers between devices  32.5 us (42%)
  starting transfers between devices  20 us (26%)
  other arithmetic  10.5 us (14%)
  Pallas kernels  10 us (13%)
  local copies, waits for them, and re-layouts  1.97 us (3%)
  between operations  1.27 us (2%)
  matrix products  1.03 us (1%)
    ppermute x8, waiting for transfers between devices, from_partner(): return lax.ppermute(value, axis, pairs)  20.5 us
    ppermute x12, starting transfers between devices, from_xor(): return lax.ppermute(value, axis, pairs)  14.2 us
    ppermute x12, waiting for transfers between devices, from_xor(): return lax.ppermute(value, axis, pairs)  12.1 us
    pallas_call x2, Pallas kernels, local_tree(): pl.pallas_call(functools.partial(local_tree_kernel, tuple(widths_seq), fl...  10 us
    select_n x56, other arithmetic, shift_rows(): jnp.where(chosen, current[:, span:span + keep_len], current[:, :keep_len])  6.19 us
    ppermute x8, starting transfers between devices, from_partner(): return lax.ppermute(value, axis, pairs)  5.77 us
    unnamed x16, local copies, waits for them, and re-layouts  1.66 us
  transfers between devices with their start and end apart: 20, of which 15 were waited for; matrix products, arithmetic and copies ran while one was open for 3% of the time, Pallas kernels for 6%

profile of v19, /device:TPU:0, one launch (start us, length us, event | category | flops | bytes accessed | tf_op | source)
XLA Modules:
  0.0 77.3 jit_solution(12252897060914699298)
XLA Ops:
  0.6 1.1 %slice_reduce_fusion = f32[4480]{0:T(1024)S(1)} fusion(f32[32,6144]{1,0:T(8,128)} %x_ref.2), kind=kLoop, calls=%fused_computation.4 | loop fusion | flops 138880 | bytes 591360 | tf_op jit(solution)/shard_map/reduce_sum | solution.py:167
  1.8 3.0 %collective-permute-start.1 = (f32[1,4480]{1,0:T(1,128)S(1)}, f32[1,4480]{1,0:T(1,128)S(1)}, u32[]{:S(2)}, u32[]{:S(2)}) collective-permute-start(f32[1,4480]{1,0:T(1,128)S(1)} %broadcast_in_dim.527), channel_id=1, source_target_pairs={{0,2},{1,3},{2,0},{3,1},{4,6},{5,7},{6,4},{7,5},{8,10},{9,11},{10,... | collective-permute-start | bytes 53768 | tf_op jit(solution)/shard_map/ppermute | solution.py:27
  5.0 1.5 %collective-permute-done.1 = f32[1,4480]{1,0:T(1,128)S(1)} collective-permute-done((f32[1,4480]{1,0:T(1,128)S(1)}, f32[1,4480]{1,0:T(1,128)S(1)}, u32[]{:S(2)}, u32[]{:S(2)}) %collective-permute-start.1) | collective-permute-done | bytes 17952 | tf_op jit(solution)/shard_map/ppermute | solution.py:27
  6.5 1.4 %collective-permute-done.2 = f32[1,4480]{1,0:T(1,128)S(1)} collective-permute-done((f32[1,4480]{1,0:T(1,128)S(1)}, f32[1,4480]{1,0:T(1,128)S(1)}, u32[]{:S(2)}, u32[]{:S(2)}) %collective-permute-start.2) | collective-permute-done | bytes 17952 | tf_op jit(solution)/shard_map/ppermute | solution.py:27
  8.0 3.7 %collective-permute-start.5 = (f32[1,4480]{1,0:T(1,128)S(1)}, f32[1,4480]{1,0:T(1,128)S(1)}, u32[]{:S(2)}, u32[]{:S(2)}) collective-permute-start(f32[1,4480]{1,0:T(1,128)S(1)} %add_add_fusion.refs_0_), channel_id=1, source_target_pairs={{0,12},{1,13},{2,14},{3,15},{4,8},{5,9},{6,10},{7,11},{8,4},{9,5},... | collective-permute-start | bytes 53768 | tf_op jit(solution)/shard_map/ppermute | solution.py:27
  11.7 0.8 %collective-permute-start.3 = (f32[1,4480]{1,0:T(1,128)S(1)}, f32[1,4480]{1,0:T(1,128)S(1)}, u32[]{:S(2)}, u32[]{:S(2)}) collective-permute-start(f32[1,4480]{1,0:T(1,128)S(1)} %add_add_fusion.refs_0_), channel_id=1, source_target_pairs={{0,4},{1,5},{2,6},{3,7},{4,0},{5,1},{6,2},{7,3},{8,12},{9,13},{10,... | collective-permute-start | bytes 53768 | tf_op jit(solution)/shard_map/ppermute | solution.py:27
  12.5 1.4 %collective-permute-done.5.refs_3_ = f32[1,4480]{1,0:T(1,128)S(1)} collective-permute-done((f32[1,4480]{1,0:T(1,128)S(1)}, f32[1,4480]{1,0:T(1,128)S(1)}, u32[]{:S(2)}, u32[]{:S(2)}) %collective-permute-start.5) | collective-permute-done | bytes 17952 | tf_op jit(solution)/shard_map/ppermute | solution.py:27
  13.8 2.5 %collective-permute-done.4.refs_2_ = f32[1,4480]{1,0:T(1,128)S(1)} collective-permute-done((f32[1,4480]{1,0:T(1,128)S(1)}, f32[1,4480]{1,0:T(1,128)S(1)}, u32[]{:S(2)}, u32[]{:S(2)}) %collective-permute-start.4) | collective-permute-done | bytes 17952 | tf_op jit(solution)/shard_map/ppermute | solution.py:27
  17.6 5.4 %shard_map.50 = f32[32,2048]{1,0:T(8,128)} custom-call(f32[32,6144]{1,0:T(8,128)} %x_ref.2, f32[1,4480]{1,0:T(1,128)} %copy-done.2, f32[1,4480]{1,0:T(1,128)} %copy-done.5, f32[1,4480]{1,0:T(1,128)} %copy-done.4, f32[1,4480]{1,0:T(1,128)} %copy-done.3, s32[9,32]{1,0:T(8,128)} %refs_4_.3), custom_call_target="tpu_custom_call" | custom-call | flops 18022400 | bytes 688128 | tf_op jit(solution)/shard_map/pallas_call | solution.py:100
  23.0 1.7 %collective-permute-done.6 = f32[32,2048]{1,0:T(8,128)S(1)} collective-permute-done((f32[32,2048]{1,0:T(8,128)}, f32[32,2048]{1,0:T(8,128)S(1)}, u32[]{:S(2)}, u32[]{:S(2)}) %collective-permute-start.6) | collective-permute-done | bytes 262176 | tf_op jit(solution)/shard_map/ppermute | solution.py:22
  24.7 1.0 %broadcast_select_fusion.1 = (f32[32,2048]{1,0:T(8,128)S(1)}, f32[32,2048]{1,0:T(8,128)S(1)}) fusion(f32[32,2048]{1,0:T(8,128)S(1)} %collective-permute-done.6, f32[32,2048]{1,0:T(8,128)} %shard_map.50, pred[]{:T(512)S(6)} %eq.411), kind=kLoop, calls=%fused_computation.101 | loop fusion | flops 131072 | bytes 1048577 | tf_op jit(solution)/shard_map/jit(_where)/select_n | solution.py:179
  26.8 0.8 %collective-permute-start.8 = (f32[32,1792]{1,0:T(8,128)S(1)}, f32[32,1792]{1,0:T(8,128)S(1)}, u32[]{:S(2)}, u32[]{:S(2)}) collective-permute-start(f32[32,1792]{1,0:T(8,128)S(1)} %fusion.2), channel_id=1, source_target_pairs={{0,2},{1,3},{2,0},{3,1},{4,6},{5,7},{6,4},{7,5},{8,10},{9,11},{10,... | collective-permute-start | bytes 688136 | tf_op jit(solution)/shard_map/ppermute | solution.py:22
  27.6 4.6 %shard_map.51 = f32[32,1152]{1,0:T(8,128)} custom-call(f32[32,6144]{1,0:T(8,128)} %x_ref.2, f32[1,4480]{1,0:T(1,128)} %copy-done.2, f32[1,4480]{1,0:T(1,128)} %copy-done.5, f32[1,4480]{1,0:T(1,128)} %copy-done.4, f32[1,4480]{1,0:T(1,128)} %copy-done.3, s32[9,32]{1,0:T(8,128)} %refs_4_.3), custom_call_target="tpu_custom_call" | custom-call | flops 12288000 | bytes 458752 | tf_op jit(solution)/shard_map/pallas_call | solution.py:100
  32.3 1.5 %collective-permute-done.7 = f32[32,1152]{1,0:T(8,128)S(1)} collective-permute-done((f32[32,1152]{1,0:T(8,128)}, f32[32,1152]{1,0:T(8,128)S(1)}, u32[]{:S(2)}, u32[]{:S(2)}) %collective-permute-start.7) | collective-permute-done | bytes 147488 | tf_op jit(solution)/shard_map/ppermute | solution.py:22
  33.8 0.7 collective-permute-done.8
  37.0 0.8 %collective-permute-start.9 = (f32[32,1152]{1,0:T(8,128)S(1)}, f32[32,1152]{1,0:T(8,128)S(1)}, u32[]{:S(2)}, u32[]{:S(2)}) collective-permute-start(f32[32,1152]{1,0:T(8,128)S(1)} %fusion.16), channel_id=1, source_target_pairs={{0,2},{1,3},{2,0},{3,1},{4,6},{5,7},{6,4},{7,5},{8,10},{9,11},{10,... | collective-permute-start | bytes 442376 | tf_op jit(solution)/shard_map/ppermute | solution.py:22
  37.8 4.5 %collective-permute-done.9 = f32[32,1152]{1,0:T(8,128)S(1)} collective-permute-done((f32[32,1152]{1,0:T(8,128)S(1)}, f32[32,1152]{1,0:T(8,128)S(1)}, u32[]{:S(2)}, u32[]{:S(2)}) %collective-permute-start.9) | collective-permute-done | bytes 147488 | tf_op jit(solution)/shard_map/ppermute | solution.py:22
  43.2 1.5 %collective-permute-start.12 = (f32[32,1280]{1,0:T(8,128)S(1)}, f32[32,1280]{1,0:T(8,128)S(1)}, u32[]{:S(2)}, u32[]{:S(2)}) collective-permute-start(f32[32,1280]{1,0:T(8,128)S(1)} %fusion.12), channel_id=1, source_target_pairs={{0,8},{1,9},{2,10},{3,11},{4,12},{5,13},{6,14},{7,15},{8,0},{9,1},... | collective-permute-start | bytes 491528 | tf_op jit(solution)/shard_map/ppermute | solution.py:22
  45.6 1.6 %collective-permute-start.11 = (f32[32,1152]{1,0:T(8,128)S(1)}, f32[32,1152]{1,0:T(8,128)S(1)}, u32[]{:S(2)}, u32[]{:S(2)}) collective-permute-start(f32[32,1152]{1,0:T(8,128)S(1)} %fusion.15), channel_id=1, source_target_pairs={{0,4},{1,5},{2,6},{3,7},{4,0},{5,1},{6,2},{7,3},{8,12},{9,13},{10,... | collective-permute-start | bytes 442376 | tf_op jit(solution)/shard_map/ppermute | solution.py:22
  47.3 4.1 %collective-permute-done.11 = f32[32,1152]{1,0:T(8,128)S(1)} collective-permute-done((f32[32,1152]{1,0:T(8,128)S(1)}, f32[32,1152]{1,0:T(8,128)S(1)}, u32[]{:S(2)}, u32[]{:S(2)}) %collective-permute-start.11) | collective-permute-done | bytes 147488 | tf_op jit(solution)/shard_map/ppermute | solution.py:22
  51.4 1.0 %collective-permute-done.12 = f32[32,1280]{1,0:T(8,128)S(1)} collective-permute-done((f32[32,1280]{1,0:T(8,128)S(1)}, f32[32,1280]{1,0:T(8,128)S(1)}, u32[]{:S(2)}, u32[]{:S(2)}) %collective-permute-start.12) | collective-permute-done | bytes 163872 | tf_op jit(solution)/shard_map/ppermute | solution.py:22
  54.2 1.0 %collective-permute-start.13 = (f32[32,1152]{1,0:T(8,128)S(1)}, f32[32,1152]{1,0:T(8,128)S(1)}, u32[]{:S(2)}, u32[]{:S(2)}) collective-permute-start(f32[32,1152]{1,0:T(8,128)S(1)} %fusion.14), channel_id=1, source_target_pairs={{0,8},{1,9},{2,10},{3,11},{4,12},{5,13},{6,14},{7,15},{8,0},{9,1},... | collective-permute-start | bytes 442376 | tf_op jit(solution)/shard_map/ppermute | solution.py:22
  55.7 7.0 %collective-permute-done.13 = f32[32,1152]{1,0:T(8,128)S(1)} collective-permute-done((f32[32,1152]{1,0:T(8,128)S(1)}, f32[32,1152]{1,0:T(8,128)S(1)}, u32[]{:S(2)}, u32[]{:S(2)}) %collective-permute-start.13) | collective-permute-done | bytes 147488 | tf_op jit(solution)/shard_map/ppermute | solution.py:22
  63.8 1.0 %convolution_reduce_fusion = f32[512,128]{1,0:T(8,128)S(1)} fusion(f32[512,256,1]{1,0,2:T(8,128)S(1)} %bitcast.85, f32[8,128,256]{2,1,0:T(8,128)S(1)} %bitcast.84), kind=kOutput, calls=%fused_computation | convolution fusion | flops 805765120 | bytes 1835008 | tf_op jit(solution)/shard_map/dot_general | solution.py:146
  65.0 1.3 %collective-permute-start.16 = (f32[2048]{0:T(1024)S(1)}, f32[2048]{0:T(1024)S(1)}, u32[]{:S(2)}, u32[]{:S(2)}) collective-permute-start(f32[2048]{0:T(1024)S(1)} %reduce_max.19), channel_id=1, source_target_pairs={{0,3},{1,2},{2,1},{3,0},{4,7},{5,6},{6,5},{7,4},{8,11},{9,10},{10,... | collective-permute-start | bytes 24584 | tf_op jit(solution)/shard_map/ppermute | solution.py:27
  66.2 0.8 %collective-permute-start.15 = (f32[2048]{0:T(1024)S(1)}, f32[2048]{0:T(1024)S(1)}, u32[]{:S(2)}, u32[]{:S(2)}) collective-permute-start(f32[2048]{0:T(1024)S(1)} %reduce_max.19), channel_id=1, source_target_pairs={{0,2},{1,3},{2,0},{3,1},{4,6},{5,7},{6,4},{7,5},{8,10},{9,11},{10,... | collective-permute-start | bytes 24584 | tf_op jit(solution)/shard_map/ppermute | solution.py:27
  67.1 1.0 %collective-permute-done.16 = f32[2048]{0:T(1024)S(1)} collective-permute-done((f32[2048]{0:T(1024)S(1)}, f32[2048]{0:T(1024)S(1)}, u32[]{:S(2)}, u32[]{:S(2)}) %collective-permute-start.16) | collective-permute-done | bytes 8224 | tf_op jit(solution)/shard_map/ppermute | solution.py:27
  68.1 1.8 %collective-permute-done.15 = f32[2048]{0:T(1024)S(1)} collective-permute-done((f32[2048]{0:T(1024)S(1)}, f32[2048]{0:T(1024)S(1)}, u32[]{:S(2)}, u32[]{:S(2)}) %collective-permute-start.15) | collective-permute-done | bytes 8224 | tf_op jit(solution)/shard_map/ppermute | solution.py:27
  69.9 2.3 %collective-permute-start.19 = (f32[2048]{0:T(1024)S(1)}, f32[2048]{0:T(1024)S(1)}, u32[]{:S(2)}, u32[]{:S(2)}) collective-permute-start(f32[2048]{0:T(1024)S(1)} %maximum_maximum_fusion.1), channel_id=1, source_target_pairs={{0,12},{1,13},{2,14},{3,15},{4,8},{5,9},{6,10},{7,11},{8,4},{9,5},... | collective-permute-start | bytes 24584 | tf_op jit(solution)/shard_map/ppermute | solution.py:27
  72.2 2.2 %collective-permute-start.17 = (f32[2048]{0:T(1024)S(1)}, f32[2048]{0:T(1024)S(1)}, u32[]{:S(2)}, u32[]{:S(2)}) collective-permute-start(f32[2048]{0:T(1024)S(1)} %maximum_maximum_fusion.1), channel_id=1, source_target_pairs={{0,4},{1,5},{2,6},{3,7},{4,0},{5,1},{6,2},{7,3},{8,12},{9,13},{10,... | collective-permute-start | bytes 24584 | tf_op jit(solution)/shard_map/ppermute | solution.py:27
  74.4 1.1 %collective-permute-done.19 = f32[2048]{0:T(1024)S(1)} collective-permute-done((f32[2048]{0:T(1024)S(1)}, f32[2048]{0:T(1024)S(1)}, u32[]{:S(2)}, u32[]{:S(2)}) %collective-permute-start.19) | collective-permute-done | bytes 8224 | tf_op jit(solution)/shard_map/ppermute | solution.py:27
  75.4 1.3 %collective-permute-done.18 = f32[2048]{0:T(1024)S(1)} collective-permute-done((f32[2048]{0:T(1024)S(1)}, f32[2048]{0:T(1024)S(1)}, u32[]{:S(2)}, u32[]{:S(2)}) %collective-permute-start.18) | collective-permute-done | bytes 8224 | tf_op jit(solution)/shard_map/ppermute | solution.py:27
  (126 shorter events, 10.7 us)
Async XLA Ops:
  0.6 22.3 %copy-start.6 = (s32[9,32]{1,0:T(8,128)S(1)}, s32[9,32]{1,0:T(8,128)}, u32[]{:S(2)}) copy-start(s32[9,32]{1,0:T(8,128)} %refs_4_.3) | copy-start | bytes 3460
  1.8 4.7 %collective-permute-start.1 = (f32[1,4480]{1,0:T(1,128)S(1)}, f32[1,4480]{1,0:T(1,128)S(1)}, u32[]{:S(2)}, u32[]{:S(2)}) collective-permute-start(f32[1,4480]{1,0:T(1,128)S(1)} %broadcast_in_dim.527), channel_id=1, source_target_pairs={{0,2},{1,3},{2,0},{3,1},{4,6},{5,7},{6,4},{7,5},{8,10},{9,11},{10,... | collective-permute-start | bytes 53768 | tf_op jit(solution)/shard_map/ppermute | solution.py:27
  4.8 3.2 %collective-permute-start.2 = (f32[1,4480]{1,0:T(1,128)S(1)}, f32[1,4480]{1,0:T(1,128)S(1)}, u32[]{:S(2)}, u32[]{:S(2)}) collective-permute-start(f32[1,4480]{1,0:T(1,128)S(1)} %broadcast_in_dim.527), channel_id=1, source_target_pairs={{0,3},{1,2},{2,1},{3,0},{4,7},{5,6},{6,5},{7,4},{8,11},{9,10},{10,... | collective-permute-start | bytes 53768 | tf_op jit(solution)/shard_map/ppermute | solution.py:27
  4.8 3.2 %collective-permute-start = (f32[1,4480]{1,0:T(1,128)S(1)}, f32[1,4480]{1,0:T(1,128)S(1)}, u32[]{:S(2)}, u32[]{:S(2)}) collective-permute-start(f32[1,4480]{1,0:T(1,128)S(1)} %broadcast_in_dim.527), channel_id=1, source_target_pairs={{0,1},{1,0},{2,3},{3,2},{4,5},{5,4},{6,7},{7,6},{8,9},{9,8},{10,11... | collective-permute-start | bytes 53768 | tf_op jit(solution)/shard_map/ppermute | solution.py:27
  8.0 8.3 %copy-start.2 = (f32[1,4480]{1,0:T(1,128)}, f32[1,4480]{1,0:T(1,128)S(1)}, u32[]{:S(2)}) copy-start(f32[1,4480]{1,0:T(1,128)S(1)} %add_add_fusion.refs_0_) | copy-start | bytes 53764
  8.0 5.8 %collective-permute-start.5 = (f32[1,4480]{1,0:T(1,128)S(1)}, f32[1,4480]{1,0:T(1,128)S(1)}, u32[]{:S(2)}, u32[]{:S(2)}) collective-permute-start(f32[1,4480]{1,0:T(1,128)S(1)} %add_add_fusion.refs_0_), channel_id=1, source_target_pairs={{0,12},{1,13},{2,14},{3,15},{4,8},{5,9},{6,10},{7,11},{8,4},{9,5},... | collective-permute-start | bytes 53768 | tf_op jit(solution)/shard_map/ppermute | solution.py:27
  11.7 4.7 %collective-permute-start.4 = (f32[1,4480]{1,0:T(1,128)S(1)}, f32[1,4480]{1,0:T(1,128)S(1)}, u32[]{:S(2)}, u32[]{:S(2)}) collective-permute-start(f32[1,4480]{1,0:T(1,128)S(1)} %add_add_fusion.refs_0_), channel_id=1, source_target_pairs={{0,8},{1,9},{2,10},{3,11},{4,12},{5,13},{6,14},{7,15},{8,0},{9,1},... | collective-permute-start | bytes 53768 | tf_op jit(solution)/shard_map/ppermute | solution.py:27
  11.7 4.7 %collective-permute-start.3 = (f32[1,4480]{1,0:T(1,128)S(1)}, f32[1,4480]{1,0:T(1,128)S(1)}, u32[]{:S(2)}, u32[]{:S(2)}) collective-permute-start(f32[1,4480]{1,0:T(1,128)S(1)} %add_add_fusion.refs_0_), channel_id=1, source_target_pairs={{0,4},{1,5},{2,6},{3,7},{4,0},{5,1},{6,2},{7,3},{8,12},{9,13},{10,... | collective-permute-start | bytes 53768 | tf_op jit(solution)/shard_map/ppermute | solution.py:27
  13.8 2.5 %copy-start.3 = (f32[1,4480]{1,0:T(1,128)}, f32[1,4480]{1,0:T(1,128)S(1)}, u32[]{:S(2)}) copy-start(f32[1,4480]{1,0:T(1,128)S(1)} %collective-permute-done.5.refs_3_) | copy-start | bytes 53764
  16.3 0.6 copy-start.4
  17.0 0.6 copy-start.5
  23.0 1.7 %collective-permute-start.6 = (f32[32,2048]{1,0:T(8,128)}, f32[32,2048]{1,0:T(8,128)S(1)}, u32[]{:S(2)}, u32[]{:S(2)}) collective-permute-start(f32[32,2048]{1,0:T(8,128)} %shard_map.50), channel_id=1, source_target_pairs={{0,1},{1,0},{2,3},{3,2},{4,5},{5,4},{6,7},{7,6},{8,9},{9,8},{10,11... | collective-permute-start | bytes 786440 | tf_op jit(solution)/shard_map/ppermute | solution.py:22
  26.6 5.6 %copy-start.7 = (s32[8]{0:T(128)S(1)}, s32[8]{0:T(128)}, u32[]{:S(2)}) copy-start(s32[8]{0:T(128)} %param.5) | copy-start | bytes 100
  26.8 7.7 %collective-permute-start.8 = (f32[32,1792]{1,0:T(8,128)S(1)}, f32[32,1792]{1,0:T(8,128)S(1)}, u32[]{:S(2)}, u32[]{:S(2)}) collective-permute-start(f32[32,1792]{1,0:T(8,128)S(1)} %fusion.2), channel_id=1, source_target_pairs={{0,2},{1,3},{2,0},{3,1},{4,6},{5,7},{6,4},{7,5},{8,10},{9,11},{10,... | collective-permute-start | bytes 688136 | tf_op jit(solution)/shard_map/ppermute | solution.py:22
  32.2 1.6 %collective-permute-start.7 = (f32[32,1152]{1,0:T(8,128)}, f32[32,1152]{1,0:T(8,128)S(1)}, u32[]{:S(2)}, u32[]{:S(2)}) collective-permute-start(f32[32,1152]{1,0:T(8,128)} %shard_map.51), channel_id=1, source_target_pairs={{0,1},{1,0},{2,3},{3,2},{4,5},{5,4},{6,7},{7,6},{8,9},{9,8},{10,11... | collective-permute-start | bytes 442376 | tf_op jit(solution)/shard_map/ppermute | solution.py:22
  35.1 0.9 %copy-start.1 = (f32[32,1152]{1,0:T(8,128)S(1)}, f32[32,1152]{1,0:T(8,128)}, u32[]{:S(2)}) copy-start(f32[32,1152]{1,0:T(8,128)} %shard_map.51) | copy-start | bytes 442372
  35.5 6.7 %collective-permute-start.10 = (f32[32,1536]{1,0:T(8,128)S(1)}, f32[32,1536]{1,0:T(8,128)S(1)}, u32[]{:S(2)}, u32[]{:S(2)}) collective-permute-start(f32[32,1536]{1,0:T(8,128)S(1)} %fusion.3), channel_id=1, source_target_pairs={{0,4},{1,5},{2,6},{3,7},{4,0},{5,1},{6,2},{7,3},{8,12},{9,13},{10,... | collective-permute-start | bytes 589832 | tf_op jit(solution)/shard_map/ppermute | solution.py:22
  37.0 5.3 %collective-permute-start.9 = (f32[32,1152]{1,0:T(8,128)S(1)}, f32[32,1152]{1,0:T(8,128)S(1)}, u32[]{:S(2)}, u32[]{:S(2)}) collective-permute-start(f32[32,1152]{1,0:T(8,128)S(1)} %fusion.16), channel_id=1, source_target_pairs={{0,2},{1,3},{2,0},{3,1},{4,6},{5,7},{6,4},{7,5},{8,10},{9,11},{10,... | collective-permute-start | bytes 442376 | tf_op jit(solution)/shard_map/ppermute | solution.py:22
  43.2 9.2 %collective-permute-start.12 = (f32[32,1280]{1,0:T(8,128)S(1)}, f32[32,1280]{1,0:T(8,128)S(1)}, u32[]{:S(2)}, u32[]{:S(2)}) collective-permute-start(f32[32,1280]{1,0:T(8,128)S(1)} %fusion.12), channel_id=1, source_target_pairs={{0,8},{1,9},{2,10},{3,11},{4,12},{5,13},{6,14},{7,15},{8,0},{9,1},... | collective-permute-start | bytes 491528 | tf_op jit(solution)/shard_map/ppermute | solution.py:22
  45.6 5.7 %collective-permute-start.11 = (f32[32,1152]{1,0:T(8,128)S(1)}, f32[32,1152]{1,0:T(8,128)S(1)}, u32[]{:S(2)}, u32[]{:S(2)}) collective-permute-start(f32[32,1152]{1,0:T(8,128)S(1)} %fusion.15), channel_id=1, source_target_pairs={{0,4},{1,5},{2,6},{3,7},{4,0},{5,1},{6,2},{7,3},{8,12},{9,13},{10,... | collective-permute-start | bytes 442376 | tf_op jit(solution)/shard_map/ppermute | solution.py:22
  54.2 8.5 %collective-permute-start.13 = (f32[32,1152]{1,0:T(8,128)S(1)}, f32[32,1152]{1,0:T(8,128)S(1)}, u32[]{:S(2)}, u32[]{:S(2)}) collective-permute-start(f32[32,1152]{1,0:T(8,128)S(1)} %fusion.14), channel_id=1, source_target_pairs={{0,8},{1,9},{2,10},{3,11},{4,12},{5,13},{6,14},{7,15},{8,0},{9,1},... | collective-permute-start | bytes 442376 | tf_op jit(solution)/shard_map/ppermute | solution.py:22
  64.9 12.4 %copy-start = (f32[32,2048]{1,0:T(8,128)}, f32[32,2048]{1,0:T(8,128)S(1)}, u32[]{:S(2)}) copy-start(f32[32,2048]{1,0:T(8,128)S(1)} %reshape.485) | copy-start | bytes 786436
  65.0 3.1 %collective-permute-start.16 = (f32[2048]{0:T(1024)S(1)}, f32[2048]{0:T(1024)S(1)}, u32[]{:S(2)}, u32[]{:S(2)}) collective-permute-start(f32[2048]{0:T(1024)S(1)} %reduce_max.19), channel_id=1, source_target_pairs={{0,3},{1,2},{2,1},{3,0},{4,7},{5,6},{6,5},{7,4},{8,11},{9,10},{10,... | collective-permute-start | bytes 24584 | tf_op jit(solution)/shard_map/ppermute | solution.py:27
  66.2 3.7 %collective-permute-start.15 = (f32[2048]{0:T(1024)S(1)}, f32[2048]{0:T(1024)S(1)}, u32[]{:S(2)}, u32[]{:S(2)}) collective-permute-start(f32[2048]{0:T(1024)S(1)} %reduce_max.19), channel_id=1, source_target_pairs={{0,2},{1,3},{2,0},{3,1},{4,6},{5,7},{6,4},{7,5},{8,10},{9,11},{10,... | collective-permute-start | bytes 24584 | tf_op jit(solution)/shard_map/ppermute | solution.py:27
  67.0 2.9 %collective-permute-start.14 = (f32[2048]{0:T(1024)S(1)}, f32[2048]{0:T(1024)S(1)}, u32[]{:S(2)}, u32[]{:S(2)}) collective-permute-start(f32[2048]{0:T(1024)S(1)} %reduce_max.19), channel_id=1, source_target_pairs={{0,1},{1,0},{2,3},{3,2},{4,5},{5,4},{6,7},{7,6},{8,9},{9,8},{10,11... | collective-permute-start | bytes 24584 | tf_op jit(solution)/shard_map/ppermute | solution.py:27
  69.9 5.5 %collective-permute-start.19 = (f32[2048]{0:T(1024)S(1)}, f32[2048]{0:T(1024)S(1)}, u32[]{:S(2)}, u32[]{:S(2)}) collective-permute-start(f32[2048]{0:T(1024)S(1)} %maximum_maximum_fusion.1), channel_id=1, source_target_pairs={{0,12},{1,13},{2,14},{3,15},{4,8},{5,9},{6,10},{7,11},{8,4},{9,5},... | collective-permute-start | bytes 24584 | tf_op jit(solution)/shard_map/ppermute | solution.py:27
  72.2 4.5 %collective-permute-start.18 = (f32[2048]{0:T(1024)S(1)}, f32[2048]{0:T(1024)S(1)}, u32[]{:S(2)}, u32[]{:S(2)}) collective-permute-start(f32[2048]{0:T(1024)S(1)} %maximum_maximum_fusion.1), channel_id=1, source_target_pairs={{0,8},{1,9},{2,10},{3,11},{4,12},{5,13},{6,14},{7,15},{8,0},{9,1},... | collective-permute-start | bytes 24584 | tf_op jit(solution)/shard_map/ppermute | solution.py:27
  72.2 4.5 %collective-permute-start.17 = (f32[2048]{0:T(1024)S(1)}, f32[2048]{0:T(1024)S(1)}, u32[]{:S(2)}, u32[]{:S(2)}) collective-permute-start(f32[2048]{0:T(1024)S(1)} %maximum_maximum_fusion.1), channel_id=1, source_target_pairs={{0,4},{1,5},{2,6},{3,7},{4,0},{5,1},{6,2},{7,3},{8,12},{9,13},{10,... | collective-permute-start | bytes 24584 | tf_op jit(solution)/shard_map/ppermute | solution.py:27

commit v20 on v17

--- a/solution.py
+++ b/solution.py
@@ -13,7 +13,7 @@
 SHIFT = 256
 TAPS = 128
 TEMPLATES = 8
-TAIL_WIDTH = 1152
+TAIL_WIDTH = 1280
 
 
 def from_partner(value, axis, distance):

time: 76.6 us -> 77.6 us (1.013)
  waiting for transfers between devices: 34.3 us -> 36.8 us
  starting transfers between devices: 20.9 us -> 18.9 us
    ppermute x8, waiting for transfers between devices: 23 us -> 26.5 us  [from_partner(): return lax.ppermute(value, axis, pairs)]
    ppermute x8, starting transfers between devices: 6.85 us -> 4.87 us  [from_partner(): return lax.ppermute(value, axis, pairs)]
    ppermute x12, waiting for transfers between devices: 11.3 us -> 10.4 us  [from_xor(): return lax.ppermute(value, axis, pairs)]
  transfers between devices with their start and end apart: 20 -> 20, of which waited for: 15 -> 15; matrix products, arithmetic and copies ran while one was open for 3% -> 6% of each run, Pallas kernels for 0% -> 0%
where the time goes in v20:
time: 77.6 us; the launch traced here: 77.4 us
  waiting for transfers between devices  36.8 us (47%)
  starting transfers between devices  18.9 us (24%)
  other arithmetic  10.5 us (14%)
  Pallas kernels  6.81 us (9%)
  local copies, waits for them, and re-layouts  1.97 us (3%)
  between operations  1.36 us (2%)
  matrix products  1.03 us (1%)
    ppermute x8, waiting for transfers between devices, from_partner(): return lax.ppermute(value, axis, pairs)  26.5 us
    ppermute x12, starting transfers between devices, from_xor(): return lax.ppermute(value, axis, pairs)  14 us
    ppermute x12, waiting for transfers between devices, from_xor(): return lax.ppermute(value, axis, pairs)  10.4 us
    pallas_call x1, Pallas kernels, local_tree(): pl.pallas_call(functools.partial(local_tree_kernel, tuple(widths_seq), fl...  6.81 us
    select_n x56, other arithmetic, shift_rows(): jnp.where(chosen, current[:, span:span + keep_len], current[:, :keep_len])  6.18 us
    ppermute x8, starting transfers between devices, from_partner(): return lax.ppermute(value, axis, pairs)  4.87 us
    unnamed x16, local copies, waits for them, and re-layouts  1.66 us
  transfers between devices with their start and end apart: 20, of which 15 were waited for; matrix products, arithmetic and copies ran while one was open for 6% of the time, Pallas kernels for 0%

profile of v20, /device:TPU:0, one launch (start us, length us, event | category | flops | bytes accessed | tf_op | source)
XLA Modules:
  0.0 77.4 jit_solution(17978183893032377630)
XLA Ops:
  0.6 1.1 %slice_reduce_fusion = f32[4480]{0:T(1024)S(1)} fusion(f32[32,6144]{1,0:T(8,128)} %x_ref.1), kind=kLoop, calls=%fused_computation.4 | loop fusion | flops 138880 | bytes 591360 | tf_op jit(solution)/shard_map/reduce_sum | solution.py:172
  1.8 3.0 %collective-permute-start.1 = (f32[1,4480]{1,0:T(1,128)S(1)}, f32[1,4480]{1,0:T(1,128)S(1)}, u32[]{:S(2)}, u32[]{:S(2)}) collective-permute-start(f32[1,4480]{1,0:T(1,128)S(1)} %broadcast_in_dim.527), channel_id=1, source_target_pairs={{0,2},{1,3},{2,0},{3,1},{4,6},{5,7},{6,4},{7,5},{8,10},{9,11},{10,... | collective-permute-start | bytes 53768 | tf_op jit(solution)/shard_map/ppermute | solution.py:27
  5.0 1.5 %collective-permute-done.1 = f32[1,4480]{1,0:T(1,128)S(1)} collective-permute-done((f32[1,4480]{1,0:T(1,128)S(1)}, f32[1,4480]{1,0:T(1,128)S(1)}, u32[]{:S(2)}, u32[]{:S(2)}) %collective-permute-start.1) | collective-permute-done | bytes 17952 | tf_op jit(solution)/shard_map/ppermute | solution.py:27
  6.5 1.4 %collective-permute-done.2 = f32[1,4480]{1,0:T(1,128)S(1)} collective-permute-done((f32[1,4480]{1,0:T(1,128)S(1)}, f32[1,4480]{1,0:T(1,128)S(1)}, u32[]{:S(2)}, u32[]{:S(2)}) %collective-permute-start.2) | collective-permute-done | bytes 17952 | tf_op jit(solution)/shard_map/ppermute | solution.py:27
  8.0 3.7 %collective-permute-start.5 = (f32[1,4480]{1,0:T(1,128)S(1)}, f32[1,4480]{1,0:T(1,128)S(1)}, u32[]{:S(2)}, u32[]{:S(2)}) collective-permute-start(f32[1,4480]{1,0:T(1,128)S(1)} %add_add_fusion.refs_0_), channel_id=1, source_target_pairs={{0,12},{1,13},{2,14},{3,15},{4,8},{5,9},{6,10},{7,11},{8,4},{9,5},... | collective-permute-start | bytes 53768 | tf_op jit(solution)/shard_map/ppermute | solution.py:27
  11.7 0.8 %collective-permute-start.3 = (f32[1,4480]{1,0:T(1,128)S(1)}, f32[1,4480]{1,0:T(1,128)S(1)}, u32[]{:S(2)}, u32[]{:S(2)}) collective-permute-start(f32[1,4480]{1,0:T(1,128)S(1)} %add_add_fusion.refs_0_), channel_id=1, source_target_pairs={{0,4},{1,5},{2,6},{3,7},{4,0},{5,1},{6,2},{7,3},{8,12},{9,13},{10,... | collective-permute-start | bytes 53768 | tf_op jit(solution)/shard_map/ppermute | solution.py:27
  12.5 1.4 %collective-permute-done.5.refs_3_ = f32[1,4480]{1,0:T(1,128)S(1)} collective-permute-done((f32[1,4480]{1,0:T(1,128)S(1)}, f32[1,4480]{1,0:T(1,128)S(1)}, u32[]{:S(2)}, u32[]{:S(2)}) %collective-permute-start.5) | collective-permute-done | bytes 17952 | tf_op jit(solution)/shard_map/ppermute | solution.py:27
  13.8 2.5 %collective-permute-done.4.refs_2_ = f32[1,4480]{1,0:T(1,128)S(1)} collective-permute-done((f32[1,4480]{1,0:T(1,128)S(1)}, f32[1,4480]{1,0:T(1,128)S(1)}, u32[]{:S(2)}, u32[]{:S(2)}) %collective-permute-start.4) | collective-permute-done | bytes 17952 | tf_op jit(solution)/shard_map/ppermute | solution.py:27
  16.4 0.6 copy-done.5
  16.9 0.6 copy-done.6
  17.5 6.8 %shard_map.50 = (f32[32,1920]{1,0:T(8,128)}, f32[32,1280]{1,0:T(8,128)}) custom-call(f32[32,6144]{1,0:T(8,128)} %x_ref.1, f32[1,4480]{1,0:T(1,128)} %copy-done.2, f32[1,4480]{1,0:T(1,128)} %copy-done.6, f32[1,4480]{1,0:T(1,128)} %copy-done.5, f32[1,4480]{1,0:T(1,128)} %copy-done.4, s32[9,32]{1,0:T(8,128)} %refs_4_.1), custom_call_target="tpu_custom_call" | custom-call | flops 25395200 | bytes 983040 | tf_op jit(solution)/shard_map/pallas_call | solution.py:102
  24.5 1.6 %collective-permute-done.6 = f32[32,1920]{1,0:T(8,128)S(1)} collective-permute-done((f32[32,1920]{1,0:T(8,128)}, f32[32,1920]{1,0:T(8,128)S(1)}, u32[]{:S(2)}, u32[]{:S(2)}) %collective-permute-start.6) | collective-permute-done | bytes 245792 | tf_op jit(solution)/shard_map/ppermute | solution.py:22
  26.2 1.0 %broadcast_select_fusion.1 = (f32[32,1920]{1,0:T(8,128)S(1)}, f32[32,1920]{1,0:T(8,128)S(1)}) fusion(f32[32,1920]{1,0:T(8,128)S(1)} %collective-permute-done.6, f32[32,1920]{1,0:T(8,128)} %get-tuple-element.16, pred[]{:T(512)S(6)} %eq.411), kind=kLoop, calls=%fused_computation.99 | loop fusion | flops 122880 | bytes 983041 | tf_op jit(solution)/shard_map/jit(_where)/select_n | solution.py:182
  28.2 0.8 %collective-permute-start.8 = (f32[32,1664]{1,0:T(8,128)S(1)}, f32[32,1664]{1,0:T(8,128)S(1)}, u32[]{:S(2)}, u32[]{:S(2)}) collective-permute-start(f32[32,1664]{1,0:T(8,128)S(1)} %fusion.2), channel_id=1, source_target_pairs={{0,2},{1,3},{2,0},{3,1},{4,6},{5,7},{6,4},{7,5},{8,10},{9,11},{10,... | collective-permute-start | bytes 638984 | tf_op jit(solution)/shard_map/ppermute | solution.py:22
  29.1 6.7 %collective-permute-done.8 = f32[32,1664]{1,0:T(8,128)S(1)} collective-permute-done((f32[32,1664]{1,0:T(8,128)S(1)}, f32[32,1664]{1,0:T(8,128)S(1)}, u32[]{:S(2)}, u32[]{:S(2)}) %collective-permute-start.8) | collective-permute-done | bytes 213024 | tf_op jit(solution)/shard_map/ppermute | solution.py:22
  36.9 0.5 copy-done.1
  38.3 0.8 %collective-permute-start.9 = (f32[32,1280]{1,0:T(8,128)S(1)}, f32[32,1280]{1,0:T(8,128)S(1)}, u32[]{:S(2)}, u32[]{:S(2)}) collective-permute-start(f32[32,1280]{1,0:T(8,128)S(1)} %fusion.15), channel_id=1, source_target_pairs={{0,2},{1,3},{2,0},{3,1},{4,6},{5,7},{6,4},{7,5},{8,10},{9,11},{10,... | collective-permute-start | bytes 491528 | tf_op jit(solution)/shard_map/ppermute | solution.py:22
  39.1 4.9 %collective-permute-done.9 = f32[32,1280]{1,0:T(8,128)S(1)} collective-permute-done((f32[32,1280]{1,0:T(8,128)S(1)}, f32[32,1280]{1,0:T(8,128)S(1)}, u32[]{:S(2)}, u32[]{:S(2)}) %collective-permute-start.9) | collective-permute-done | bytes 163872 | tf_op jit(solution)/shard_map/ppermute | solution.py:22
  45.0 1.5 %collective-permute-start.12 = (f32[32,1152]{1,0:T(8,128)S(1)}, f32[32,1152]{1,0:T(8,128)S(1)}, u32[]{:S(2)}, u32[]{:S(2)}) collective-permute-start(f32[32,1152]{1,0:T(8,128)S(1)} %fusion.16), channel_id=1, source_target_pairs={{0,8},{1,9},{2,10},{3,11},{4,12},{5,13},{6,14},{7,15},{8,0},{9,1},... | collective-permute-start | bytes 442376 | tf_op jit(solution)/shard_map/ppermute | solution.py:22
  47.5 1.3 %collective-permute-start.11 = (f32[32,1280]{1,0:T(8,128)S(1)}, f32[32,1280]{1,0:T(8,128)S(1)}, u32[]{:S(2)}, u32[]{:S(2)}) collective-permute-start(f32[32,1280]{1,0:T(8,128)S(1)} %fusion.14), channel_id=1, source_target_pairs={{0,4},{1,5},{2,6},{3,7},{4,0},{5,1},{6,2},{7,3},{8,12},{9,13},{10,... | collective-permute-start | bytes 491528 | tf_op jit(solution)/shard_map/ppermute | solution.py:22
  48.9 4.8 %collective-permute-done.12 = f32[32,1152]{1,0:T(8,128)S(1)} collective-permute-done((f32[32,1152]{1,0:T(8,128)S(1)}, f32[32,1152]{1,0:T(8,128)S(1)}, u32[]{:S(2)}, u32[]{:S(2)}) %collective-permute-start.12) | collective-permute-done | bytes 147488 | tf_op jit(solution)/shard_map/ppermute | solution.py:22
  53.7 1.2 %collective-permute-done.11 = f32[32,1280]{1,0:T(8,128)S(1)} collective-permute-done((f32[32,1280]{1,0:T(8,128)S(1)}, f32[32,1280]{1,0:T(8,128)S(1)}, u32[]{:S(2)}, u32[]{:S(2)}) %collective-permute-start.11) | collective-permute-done | bytes 163872 | tf_op jit(solution)/shard_map/ppermute | solution.py:22
  57.4 7.2 %collective-permute-done.13 = f32[32,1280]{1,0:T(8,128)S(1)} collective-permute-done((f32[32,1280]{1,0:T(8,128)S(1)}, f32[32,1280]{1,0:T(8,128)S(1)}, u32[]{:S(2)}, u32[]{:S(2)}) %collective-permute-start.13) | collective-permute-done | bytes 163872 | tf_op jit(solution)/shard_map/ppermute | solution.py:22
  65.8 1.0 %convolution_reduce_fusion = f32[512,128]{1,0:T(8,128)S(1)} fusion(f32[512,256,1]{1,0,2:T(8,128)S(1)} %bitcast.85, f32[8,128,256]{2,1,0:T(8,128)S(1)} %bitcast.84), kind=kOutput, calls=%fused_computation | convolution fusion | flops 805765120 | bytes 1835008 | tf_op jit(solution)/shard_map/dot_general | solution.py:151
  67.0 0.8 %collective-permute-start.15 = (f32[2048]{0:T(1024)S(1)}, f32[2048]{0:T(1024)S(1)}, u32[]{:S(2)}, u32[]{:S(2)}) collective-permute-start(f32[2048]{0:T(1024)S(1)} %reduce_max.19), channel_id=1, source_target_pairs={{0,2},{1,3},{2,0},{3,1},{4,6},{5,7},{6,4},{7,5},{8,10},{9,11},{10,... | collective-permute-start | bytes 24584 | tf_op jit(solution)/shard_map/ppermute | solution.py:27
  67.8 1.1 %collective-permute-start.14 = (f32[2048]{0:T(1024)S(1)}, f32[2048]{0:T(1024)S(1)}, u32[]{:S(2)}, u32[]{:S(2)}) collective-permute-start(f32[2048]{0:T(1024)S(1)} %reduce_max.19), channel_id=1, source_target_pairs={{0,1},{1,0},{2,3},{3,2},{4,5},{5,4},{6,7},{7,6},{8,9},{9,8},{10,11... | collective-permute-start | bytes 24584 | tf_op jit(solution)/shard_map/ppermute | solution.py:27
  68.8 1.2 %collective-permute-done.16 = f32[2048]{0:T(1024)S(1)} collective-permute-done((f32[2048]{0:T(1024)S(1)}, f32[2048]{0:T(1024)S(1)}, u32[]{:S(2)}, u32[]{:S(2)}) %collective-permute-start.16) | collective-permute-done | bytes 8224 | tf_op jit(solution)/shard_map/ppermute | solution.py:27
  70.0 0.7 collective-permute-done.15
  70.7 1.3 %collective-permute-start.19 = (f32[2048]{0:T(1024)S(1)}, f32[2048]{0:T(1024)S(1)}, u32[]{:S(2)}, u32[]{:S(2)}) collective-permute-start(f32[2048]{0:T(1024)S(1)} %maximum_maximum_fusion.1), channel_id=1, source_target_pairs={{0,12},{1,13},{2,14},{3,15},{4,8},{5,9},{6,10},{7,11},{8,4},{9,5},... | collective-permute-start | bytes 24584 | tf_op jit(solution)/shard_map/ppermute | solution.py:27
  72.0 3.2 %collective-permute-start.17 = (f32[2048]{0:T(1024)S(1)}, f32[2048]{0:T(1024)S(1)}, u32[]{:S(2)}, u32[]{:S(2)}) collective-permute-start(f32[2048]{0:T(1024)S(1)} %maximum_maximum_fusion.1), channel_id=1, source_target_pairs={{0,4},{1,5},{2,6},{3,7},{4,0},{5,1},{6,2},{7,3},{8,12},{9,13},{10,... | collective-permute-start | bytes 24584 | tf_op jit(solution)/shard_map/ppermute | solution.py:27
  75.2 1.1 %collective-permute-done.19 = f32[2048]{0:T(1024)S(1)} collective-permute-done((f32[2048]{0:T(1024)S(1)}, f32[2048]{0:T(1024)S(1)}, u32[]{:S(2)}, u32[]{:S(2)}) %collective-permute-start.19) | collective-permute-done | bytes 8224 | tf_op jit(solution)/shard_map/ppermute | solution.py:27
  76.8 0.6 maximum_maximum_fusion
  (125 shorter events, 9.4 us)
Async XLA Ops:
  0.6 23.7 %copy-start.3 = (s32[9,32]{1,0:T(8,128)S(1)}, s32[9,32]{1,0:T(8,128)}, u32[]{:S(2)}) copy-start(s32[9,32]{1,0:T(8,128)} %refs_4_.1) | copy-start | bytes 3460
  1.8 4.7 %collective-permute-start.1 = (f32[1,4480]{1,0:T(1,128)S(1)}, f32[1,4480]{1,0:T(1,128)S(1)}, u32[]{:S(2)}, u32[]{:S(2)}) collective-permute-start(f32[1,4480]{1,0:T(1,128)S(1)} %broadcast_in_dim.527), channel_id=1, source_target_pairs={{0,2},{1,3},{2,0},{3,1},{4,6},{5,7},{6,4},{7,5},{8,10},{9,11},{10,... | collective-permute-start | bytes 53768 | tf_op jit(solution)/shard_map/ppermute | solution.py:27
  4.8 3.2 %collective-permute-start.2 = (f32[1,4480]{1,0:T(1,128)S(1)}, f32[1,4480]{1,0:T(1,128)S(1)}, u32[]{:S(2)}, u32[]{:S(2)}) collective-permute-start(f32[1,4480]{1,0:T(1,128)S(1)} %broadcast_in_dim.527), channel_id=1, source_target_pairs={{0,3},{1,2},{2,1},{3,0},{4,7},{5,6},{6,5},{7,4},{8,11},{9,10},{10,... | collective-permute-start | bytes 53768 | tf_op jit(solution)/shard_map/ppermute | solution.py:27
  4.8 3.2 %collective-permute-start = (f32[1,4480]{1,0:T(1,128)S(1)}, f32[1,4480]{1,0:T(1,128)S(1)}, u32[]{:S(2)}, u32[]{:S(2)}) collective-permute-start(f32[1,4480]{1,0:T(1,128)S(1)} %broadcast_in_dim.527), channel_id=1, source_target_pairs={{0,1},{1,0},{2,3},{3,2},{4,5},{5,4},{6,7},{7,6},{8,9},{9,8},{10,11... | collective-permute-start | bytes 53768 | tf_op jit(solution)/shard_map/ppermute | solution.py:27
  8.0 8.3 %copy-start.2 = (f32[1,4480]{1,0:T(1,128)}, f32[1,4480]{1,0:T(1,128)S(1)}, u32[]{:S(2)}) copy-start(f32[1,4480]{1,0:T(1,128)S(1)} %add_add_fusion.refs_0_) | copy-start | bytes 53764
  8.0 5.8 %collective-permute-start.5 = (f32[1,4480]{1,0:T(1,128)S(1)}, f32[1,4480]{1,0:T(1,128)S(1)}, u32[]{:S(2)}, u32[]{:S(2)}) collective-permute-start(f32[1,4480]{1,0:T(1,128)S(1)} %add_add_fusion.refs_0_), channel_id=1, source_target_pairs={{0,12},{1,13},{2,14},{3,15},{4,8},{5,9},{6,10},{7,11},{8,4},{9,5},... | collective-permute-start | bytes 53768 | tf_op jit(solution)/shard_map/ppermute | solution.py:27
  11.7 4.7 %collective-permute-start.4 = (f32[1,4480]{1,0:T(1,128)S(1)}, f32[1,4480]{1,0:T(1,128)S(1)}, u32[]{:S(2)}, u32[]{:S(2)}) collective-permute-start(f32[1,4480]{1,0:T(1,128)S(1)} %add_add_fusion.refs_0_), channel_id=1, source_target_pairs={{0,8},{1,9},{2,10},{3,11},{4,12},{5,13},{6,14},{7,15},{8,0},{9,1},... | collective-permute-start | bytes 53768 | tf_op jit(solution)/shard_map/ppermute | solution.py:27
  11.7 4.7 %collective-permute-start.3 = (f32[1,4480]{1,0:T(1,128)S(1)}, f32[1,4480]{1,0:T(1,128)S(1)}, u32[]{:S(2)}, u32[]{:S(2)}) collective-permute-start(f32[1,4480]{1,0:T(1,128)S(1)} %add_add_fusion.refs_0_), channel_id=1, source_target_pairs={{0,4},{1,5},{2,6},{3,7},{4,0},{5,1},{6,2},{7,3},{8,12},{9,13},{10,... | collective-permute-start | bytes 53768 | tf_op jit(solution)/shard_map/ppermute | solution.py:27
  13.8 2.5 %copy-start.4 = (f32[1,4480]{1,0:T(1,128)}, f32[1,4480]{1,0:T(1,128)S(1)}, u32[]{:S(2)}) copy-start(f32[1,4480]{1,0:T(1,128)S(1)} %collective-permute-done.5.refs_3_) | copy-start | bytes 53764
  16.3 0.6 copy-start.5
  16.9 0.6 copy-start.6
  24.4 1.7 %collective-permute-start.6 = (f32[32,1920]{1,0:T(8,128)}, f32[32,1920]{1,0:T(8,128)S(1)}, u32[]{:S(2)}, u32[]{:S(2)}) collective-permute-start(f32[32,1920]{1,0:T(8,128)} %get-tuple-element.16), channel_id=1, source_target_pairs={{0,1},{1,0},{2,3},{3,2},{4,5},{5,4},{6,7},{7,6},{8,9},{9,8},{10,11... | collective-permute-start | bytes 737288 | tf_op jit(solution)/shard_map/ppermute | solution.py:22
  26.1 3.0 %collective-permute-start.7 = (f32[32,1280]{1,0:T(8,128)}, f32[32,1280]{1,0:T(8,128)S(1)}, u32[]{:S(2)}, u32[]{:S(2)}) collective-permute-start(f32[32,1280]{1,0:T(8,128)} %get-tuple-element.17), channel_id=1, source_target_pairs={{0,1},{1,0},{2,3},{3,2},{4,5},{5,4},{6,7},{7,6},{8,9},{9,8},{10,11... | collective-permute-start | bytes 491528 | tf_op jit(solution)/shard_map/ppermute | solution.py:22
  27.8 1.2 %copy-start.7 = (s32[8]{0:T(128)S(1)}, s32[8]{0:T(128)}, u32[]{:S(2)}) copy-start(s32[8]{0:T(128)} %param.5) | copy-start | bytes 100
  28.2 7.6 %collective-permute-start.8 = (f32[32,1664]{1,0:T(8,128)S(1)}, f32[32,1664]{1,0:T(8,128)S(1)}, u32[]{:S(2)}, u32[]{:S(2)}) collective-permute-start(f32[32,1664]{1,0:T(8,128)S(1)} %fusion.2), channel_id=1, source_target_pairs={{0,2},{1,3},{2,0},{3,1},{4,6},{5,7},{6,4},{7,5},{8,10},{9,11},{10,... | collective-permute-start | bytes 638984 | tf_op jit(solution)/shard_map/ppermute | solution.py:22
  36.5 0.9 %copy-start.1 = (f32[32,1280]{1,0:T(8,128)S(1)}, f32[32,1280]{1,0:T(8,128)}, u32[]{:S(2)}) copy-start(f32[32,1280]{1,0:T(8,128)} %get-tuple-element.17) | copy-start | bytes 491524
  36.8 7.2 %collective-permute-start.10 = (f32[32,1408]{1,0:T(8,128)S(1)}, f32[32,1408]{1,0:T(8,128)S(1)}, u32[]{:S(2)}, u32[]{:S(2)}) collective-permute-start(f32[32,1408]{1,0:T(8,128)S(1)} %fusion.11), channel_id=1, source_target_pairs={{0,4},{1,5},{2,6},{3,7},{4,0},{5,1},{6,2},{7,3},{8,12},{9,13},{10,... | collective-permute-start | bytes 540680 | tf_op jit(solution)/shard_map/ppermute | solution.py:22
  38.3 5.7 %collective-permute-start.9 = (f32[32,1280]{1,0:T(8,128)S(1)}, f32[32,1280]{1,0:T(8,128)S(1)}, u32[]{:S(2)}, u32[]{:S(2)}) collective-permute-start(f32[32,1280]{1,0:T(8,128)S(1)} %fusion.15), channel_id=1, source_target_pairs={{0,2},{1,3},{2,0},{3,1},{4,6},{5,7},{6,4},{7,5},{8,10},{9,11},{10,... | collective-permute-start | bytes 491528 | tf_op jit(solution)/shard_map/ppermute | solution.py:22
  45.0 8.7 %collective-permute-start.12 = (f32[32,1152]{1,0:T(8,128)S(1)}, f32[32,1152]{1,0:T(8,128)S(1)}, u32[]{:S(2)}, u32[]{:S(2)}) collective-permute-start(f32[32,1152]{1,0:T(8,128)S(1)} %fusion.16), channel_id=1, source_target_pairs={{0,8},{1,9},{2,10},{3,11},{4,12},{5,13},{6,14},{7,15},{8,0},{9,1},... | collective-permute-start | bytes 442376 | tf_op jit(solution)/shard_map/ppermute | solution.py:22
  47.5 7.5 %collective-permute-start.11 = (f32[32,1280]{1,0:T(8,128)S(1)}, f32[32,1280]{1,0:T(8,128)S(1)}, u32[]{:S(2)}, u32[]{:S(2)}) collective-permute-start(f32[32,1280]{1,0:T(8,128)S(1)} %fusion.14), channel_id=1, source_target_pairs={{0,4},{1,5},{2,6},{3,7},{4,0},{5,1},{6,2},{7,3},{8,12},{9,13},{10,... | collective-permute-start | bytes 491528 | tf_op jit(solution)/shard_map/ppermute | solution.py:22
  56.8 7.9 %collective-permute-start.13 = (f32[32,1280]{1,0:T(8,128)S(1)}, f32[32,1280]{1,0:T(8,128)S(1)}, u32[]{:S(2)}, u32[]{:S(2)}) collective-permute-start(f32[32,1280]{1,0:T(8,128)S(1)} %fusion.13), channel_id=1, source_target_pairs={{0,8},{1,9},{2,10},{3,11},{4,12},{5,13},{6,14},{7,15},{8,0},{9,1},... | collective-permute-start | bytes 491528 | tf_op jit(solution)/shard_map/ppermute | solution.py:22
  66.8 10.5 %copy-start = (f32[32,2048]{1,0:T(8,128)}, f32[32,2048]{1,0:T(8,128)S(1)}, u32[]{:S(2)}) copy-start(f32[32,2048]{1,0:T(8,128)S(1)} %reshape.485) | copy-start | bytes 786436
  66.9 3.1 %collective-permute-start.16 = (f32[2048]{0:T(1024)S(1)}, f32[2048]{0:T(1024)S(1)}, u32[]{:S(2)}, u32[]{:S(2)}) collective-permute-start(f32[2048]{0:T(1024)S(1)} %reduce_max.19), channel_id=1, source_target_pairs={{0,3},{1,2},{2,1},{3,0},{4,7},{5,6},{6,5},{7,4},{8,11},{9,10},{10,... | collective-permute-start | bytes 24584 | tf_op jit(solution)/shard_map/ppermute | solution.py:27
  67.0 3.7 %collective-permute-start.15 = (f32[2048]{0:T(1024)S(1)}, f32[2048]{0:T(1024)S(1)}, u32[]{:S(2)}, u32[]{:S(2)}) collective-permute-start(f32[2048]{0:T(1024)S(1)} %reduce_max.19), channel_id=1, source_target_pairs={{0,2},{1,3},{2,0},{3,1},{4,6},{5,7},{6,4},{7,5},{8,10},{9,11},{10,... | collective-permute-start | bytes 24584 | tf_op jit(solution)/shard_map/ppermute | solution.py:27
  67.8 2.9 %collective-permute-start.14 = (f32[2048]{0:T(1024)S(1)}, f32[2048]{0:T(1024)S(1)}, u32[]{:S(2)}, u32[]{:S(2)}) collective-permute-start(f32[2048]{0:T(1024)S(1)} %reduce_max.19), channel_id=1, source_target_pairs={{0,1},{1,0},{2,3},{3,2},{4,5},{5,4},{6,7},{7,6},{8,9},{9,8},{10,11... | collective-permute-start | bytes 24584 | tf_op jit(solution)/shard_map/ppermute | solution.py:27
  70.7 5.5 %collective-permute-start.19 = (f32[2048]{0:T(1024)S(1)}, f32[2048]{0:T(1024)S(1)}, u32[]{:S(2)}, u32[]{:S(2)}) collective-permute-start(f32[2048]{0:T(1024)S(1)} %maximum_maximum_fusion.1), channel_id=1, source_target_pairs={{0,12},{1,13},{2,14},{3,15},{4,8},{5,9},{6,10},{7,11},{8,4},{9,5},... | collective-permute-start | bytes 24584 | tf_op jit(solution)/shard_map/ppermute | solution.py:27
  72.0 4.5 %collective-permute-start.18 = (f32[2048]{0:T(1024)S(1)}, f32[2048]{0:T(1024)S(1)}, u32[]{:S(2)}, u32[]{:S(2)}) collective-permute-start(f32[2048]{0:T(1024)S(1)} %maximum_maximum_fusion.1), channel_id=1, source_target_pairs={{0,8},{1,9},{2,10},{3,11},{4,12},{5,13},{6,14},{7,15},{8,0},{9,1},... | collective-permute-start | bytes 24584 | tf_op jit(solution)/shard_map/ppermute | solution.py:27
  72.0 4.8 %collective-permute-start.17 = (f32[2048]{0:T(1024)S(1)}, f32[2048]{0:T(1024)S(1)}, u32[]{:S(2)}, u32[]{:S(2)}) collective-permute-start(f32[2048]{0:T(1024)S(1)} %maximum_maximum_fusion.1), channel_id=1, source_target_pairs={{0,4},{1,5},{2,6},{3,7},{4,0},{5,1},{6,2},{7,3},{8,12},{9,13},{10,... | collective-permute-start | bytes 24584 | tf_op jit(solution)/shard_map/ppermute | solution.py:27

commit v21 on v17

--- a/solution.py
+++ b/solution.py
@@ -141,7 +141,7 @@
 
 def boxcar_max(dedispersed, widths):
     total_rows = dedispersed.shape[0]
-    blocks_time = TS // TAPS
+    blocks_time = dedispersed.shape[1] // TAPS - 1
     window = dedispersed.reshape(total_rows, blocks_time + 1, TAPS)
     paired = jnp.concatenate([window[:, :-1], window[:, 1:]], axis=2).reshape(
         total_rows * blocks_time, 2 * TAPS
@@ -155,7 +155,7 @@
         preferred_element_type=jnp.float32,
     )
     best_value = jnp.max(result.reshape(total_rows * blocks_time, TEMPLATES, TAPS), axis=1)
-    return best_value.reshape(total_rows, TS)
+    return best_value.reshape(total_rows, blocks_time * TAPS)
 
 
 def per_device(filterbank, offsets, widths):
@@ -208,9 +208,11 @@
         pending = (tail, partner_tail, lower_head[:, head_width:], upper_head[:, head_width:], amounts, bit_index)
         head = new_head
     tail = finish_tail(pending)
-    current = jnp.concatenate([head, tail], axis=1)
-    dedispersed = current * (1.0 / math.sqrt(channels_all))
-    detection = boxcar_max(dedispersed, widths)
+    scale = 1.0 / math.sqrt(channels_all)
+    head_scaled = head * scale
+    head_detection = boxcar_max(head_scaled, widths)
+    tail_scaled = jnp.concatenate([head_scaled[:, -TAPS:], tail * scale], axis=1)
+    detection = jnp.concatenate([head_detection, boxcar_max(tail_scaled, widths)], axis=1)
     peak_series = butterfly(jnp.max(detection, axis=0), "band", jnp.maximum)
     return (detection, peak_series)
 

time: 76.6 us -> 76.4 us (level)
  waiting for transfers between devices: 34.3 us -> 33.5 us
    ppermute x8, waiting for transfers between devices: 23 us -> 22.2 us  [from_partner(): return lax.ppermute(value, axis, pairs)]
  transfers between devices with their start and end apart: 20 -> 20, of which waited for: 15 -> 15; matrix products, arithmetic and copies ran while one was open for 3% -> 4% of each run, Pallas kernels for 0% -> 0%
where the time goes in v21:
time: 76.4 us; the launch traced here: 76.2 us
  waiting for transfers between devices  33.5 us (44%)
  starting transfers between devices  20.9 us (27%)
  other arithmetic  10.6 us (14%)
  Pallas kernels  6.81 us (9%)
  local copies, waits for them, and re-layouts  1.67 us (2%)
  between operations  1.44 us (2%)
  matrix products  1.34 us (2%)
    ppermute x8, waiting for transfers between devices, from_partner(): return lax.ppermute(value, axis, pairs)  22.2 us
    ppermute x12, starting transfers between devices, from_xor(): return lax.ppermute(value, axis, pairs)  14 us
    ppermute x12, waiting for transfers between devices, from_xor(): return lax.ppermute(value, axis, pairs)  11.3 us
    ppermute x8, starting transfers between devices, from_partner(): return lax.ppermute(value, axis, pairs)  6.86 us
    pallas_call x1, Pallas kernels, local_tree(): pl.pallas_call(functools.partial(local_tree_kernel, tuple(widths_seq), fl...  6.81 us
    select_n x56, other arithmetic, shift_rows(): jnp.where(chosen, current[:, span:span + keep_len], current[:, :keep_len])  6.19 us
  transfers between devices with their start and end apart: 20, of which 15 were waited for; matrix products, arithmetic and copies ran while one was open for 4% of the time, Pallas kernels for 0%

profile of v21, /device:TPU:0, one launch (start us, length us, event | category | flops | bytes accessed | tf_op | source)
XLA Modules:
  0.0 76.2 jit_solution(12840534204618619283)
XLA Ops:
  0.6 1.1 %slice_reduce_fusion = f32[4480]{0:T(1024)S(1)} fusion(f32[32,6144]{1,0:T(8,128)} %x_ref.1), kind=kLoop, calls=%fused_computation.5 | loop fusion | flops 138880 | bytes 591360 | tf_op jit(solution)/shard_map/reduce_sum | solution.py:172
  1.8 3.0 %collective-permute-start.1 = (f32[1,4480]{1,0:T(1,128)S(1)}, f32[1,4480]{1,0:T(1,128)S(1)}, u32[]{:S(2)}, u32[]{:S(2)}) collective-permute-start(f32[1,4480]{1,0:T(1,128)S(1)} %broadcast_in_dim.535), channel_id=1, source_target_pairs={{0,2},{1,3},{2,0},{3,1},{4,6},{5,7},{6,4},{7,5},{8,10},{9,11},{10,... | collective-permute-start | bytes 53768 | tf_op jit(solution)/shard_map/ppermute | solution.py:27
  5.0 1.5 %collective-permute-done.1 = f32[1,4480]{1,0:T(1,128)S(1)} collective-permute-done((f32[1,4480]{1,0:T(1,128)S(1)}, f32[1,4480]{1,0:T(1,128)S(1)}, u32[]{:S(2)}, u32[]{:S(2)}) %collective-permute-start.1) | collective-permute-done | bytes 17952 | tf_op jit(solution)/shard_map/ppermute | solution.py:27
  6.5 1.4 %collective-permute-done.2 = f32[1,4480]{1,0:T(1,128)S(1)} collective-permute-done((f32[1,4480]{1,0:T(1,128)S(1)}, f32[1,4480]{1,0:T(1,128)S(1)}, u32[]{:S(2)}, u32[]{:S(2)}) %collective-permute-start.2) | collective-permute-done | bytes 17952 | tf_op jit(solution)/shard_map/ppermute | solution.py:27
  8.0 3.7 %collective-permute-start.5 = (f32[1,4480]{1,0:T(1,128)S(1)}, f32[1,4480]{1,0:T(1,128)S(1)}, u32[]{:S(2)}, u32[]{:S(2)}) collective-permute-start(f32[1,4480]{1,0:T(1,128)S(1)} %add_add_fusion.refs_0_), channel_id=1, source_target_pairs={{0,12},{1,13},{2,14},{3,15},{4,8},{5,9},{6,10},{7,11},{8,4},{9,5},... | collective-permute-start | bytes 53768 | tf_op jit(solution)/shard_map/ppermute | solution.py:27
  11.7 0.8 %collective-permute-start.3 = (f32[1,4480]{1,0:T(1,128)S(1)}, f32[1,4480]{1,0:T(1,128)S(1)}, u32[]{:S(2)}, u32[]{:S(2)}) collective-permute-start(f32[1,4480]{1,0:T(1,128)S(1)} %add_add_fusion.refs_0_), channel_id=1, source_target_pairs={{0,4},{1,5},{2,6},{3,7},{4,0},{5,1},{6,2},{7,3},{8,12},{9,13},{10,... | collective-permute-start | bytes 53768 | tf_op jit(solution)/shard_map/ppermute | solution.py:27
  12.5 1.4 %collective-permute-done.5.refs_3_ = f32[1,4480]{1,0:T(1,128)S(1)} collective-permute-done((f32[1,4480]{1,0:T(1,128)S(1)}, f32[1,4480]{1,0:T(1,128)S(1)}, u32[]{:S(2)}, u32[]{:S(2)}) %collective-permute-start.5) | collective-permute-done | bytes 17952 | tf_op jit(solution)/shard_map/ppermute | solution.py:27
  13.8 2.5 %collective-permute-done.4.refs_2_ = f32[1,4480]{1,0:T(1,128)S(1)} collective-permute-done((f32[1,4480]{1,0:T(1,128)S(1)}, f32[1,4480]{1,0:T(1,128)S(1)}, u32[]{:S(2)}, u32[]{:S(2)}) %collective-permute-start.4) | collective-permute-done | bytes 17952 | tf_op jit(solution)/shard_map/ppermute | solution.py:27
  17.5 6.8 %shard_map.50 = (f32[32,2048]{1,0:T(8,128)}, f32[32,1152]{1,0:T(8,128)}) custom-call(f32[32,6144]{1,0:T(8,128)} %x_ref.1, f32[1,4480]{1,0:T(1,128)} %copy-done.2, f32[1,4480]{1,0:T(1,128)} %copy-done.6, f32[1,4480]{1,0:T(1,128)} %copy-done.5, f32[1,4480]{1,0:T(1,128)} %copy-done.4, s32[9,32]{1,0:T(8,128)} %refs_4_.1), custom_call_target="tpu_custom_call" | custom-call | flops 25395200 | bytes 983040 | tf_op jit(solution)/shard_map/pallas_call | solution.py:102
  24.4 1.7 %collective-permute-done.6 = f32[32,2048]{1,0:T(8,128)S(1)} collective-permute-done((f32[32,2048]{1,0:T(8,128)}, f32[32,2048]{1,0:T(8,128)S(1)}, u32[]{:S(2)}, u32[]{:S(2)}) %collective-permute-start.6) | collective-permute-done | bytes 262176 | tf_op jit(solution)/shard_map/ppermute | solution.py:22
  26.1 1.0 %broadcast_select_fusion.1 = (f32[32,2048]{1,0:T(8,128)S(1)}, f32[32,2048]{1,0:T(8,128)S(1)}) fusion(f32[32,2048]{1,0:T(8,128)S(1)} %collective-permute-done.6, f32[32,2048]{1,0:T(8,128)} %get-tuple-element.16, pred[]{:T(512)S(6)} %eq.411), kind=kLoop, calls=%fused_computation.104 | loop fusion | flops 131072 | bytes 1048577 | tf_op jit(solution)/shard_map/jit(_where)/select_n | solution.py:182
  28.2 0.8 %collective-permute-start.8 = (f32[32,1792]{1,0:T(8,128)S(1)}, f32[32,1792]{1,0:T(8,128)S(1)}, u32[]{:S(2)}, u32[]{:S(2)}) collective-permute-start(f32[32,1792]{1,0:T(8,128)S(1)} %fusion.2), channel_id=1, source_target_pairs={{0,2},{1,3},{2,0},{3,1},{4,6},{5,7},{6,4},{7,5},{8,10},{9,11},{10,... | collective-permute-start | bytes 688136 | tf_op jit(solution)/shard_map/ppermute | solution.py:22
  29.1 1.3 %collective-permute-done.7 = f32[32,1152]{1,0:T(8,128)S(1)} collective-permute-done((f32[32,1152]{1,0:T(8,128)S(1)}, f32[32,1152]{1,0:T(8,128)S(1)}, u32[]{:S(2)}, u32[]{:S(2)}) %collective-permute-start.7) | collective-permute-done | bytes 147488 | tf_op jit(solution)/shard_map/ppermute | solution.py:22
  30.4 5.5 %collective-permute-done.8 = f32[32,1792]{1,0:T(8,128)S(1)} collective-permute-done((f32[32,1792]{1,0:T(8,128)S(1)}, f32[32,1792]{1,0:T(8,128)S(1)}, u32[]{:S(2)}, u32[]{:S(2)}) %collective-permute-start.8) | collective-permute-done | bytes 229408 | tf_op jit(solution)/shard_map/ppermute | solution.py:22
  37.9 0.8 %collective-permute-start.9 = (f32[32,1152]{1,0:T(8,128)S(1)}, f32[32,1152]{1,0:T(8,128)S(1)}, u32[]{:S(2)}, u32[]{:S(2)}) collective-permute-start(f32[32,1152]{1,0:T(8,128)S(1)} %fusion.17), channel_id=1, source_target_pairs={{0,2},{1,3},{2,0},{3,1},{4,6},{5,7},{6,4},{7,5},{8,10},{9,11},{10,... | collective-permute-start | bytes 442376 | tf_op jit(solution)/shard_map/ppermute | solution.py:22
  38.8 4.3 %collective-permute-done.9 = f32[32,1152]{1,0:T(8,128)S(1)} collective-permute-done((f32[32,1152]{1,0:T(8,128)S(1)}, f32[32,1152]{1,0:T(8,128)S(1)}, u32[]{:S(2)}, u32[]{:S(2)}) %collective-permute-start.9) | collective-permute-done | bytes 147488 | tf_op jit(solution)/shard_map/ppermute | solution.py:22
  44.1 1.5 %collective-permute-start.12 = (f32[32,1280]{1,0:T(8,128)S(1)}, f32[32,1280]{1,0:T(8,128)S(1)}, u32[]{:S(2)}, u32[]{:S(2)}) collective-permute-start(f32[32,1280]{1,0:T(8,128)S(1)} %fusion.12), channel_id=1, source_target_pairs={{0,8},{1,9},{2,10},{3,11},{4,12},{5,13},{6,14},{7,15},{8,0},{9,1},... | collective-permute-start | bytes 491528 | tf_op jit(solution)/shard_map/ppermute | solution.py:22
  46.6 2.1 %collective-permute-start.11 = (f32[32,1152]{1,0:T(8,128)S(1)}, f32[32,1152]{1,0:T(8,128)S(1)}, u32[]{:S(2)}, u32[]{:S(2)}) collective-permute-start(f32[32,1152]{1,0:T(8,128)S(1)} %fusion.16), channel_id=1, source_target_pairs={{0,4},{1,5},{2,6},{3,7},{4,0},{5,1},{6,2},{7,3},{8,12},{9,13},{10,... | collective-permute-start | bytes 442376 | tf_op jit(solution)/shard_map/ppermute | solution.py:22
  49.1 3.3 %collective-permute-done.11 = f32[32,1152]{1,0:T(8,128)S(1)} collective-permute-done((f32[32,1152]{1,0:T(8,128)S(1)}, f32[32,1152]{1,0:T(8,128)S(1)}, u32[]{:S(2)}, u32[]{:S(2)}) %collective-permute-start.11) | collective-permute-done | bytes 147488 | tf_op jit(solution)/shard_map/ppermute | solution.py:22
  52.4 0.8 %collective-permute-done.12 = f32[32,1280]{1,0:T(8,128)S(1)} collective-permute-done((f32[32,1280]{1,0:T(8,128)S(1)}, f32[32,1280]{1,0:T(8,128)S(1)}, u32[]{:S(2)}, u32[]{:S(2)}) %collective-permute-start.12) | collective-permute-done | bytes 163872 | tf_op jit(solution)/shard_map/ppermute | solution.py:22
  55.1 1.6 %collective-permute-start.13 = (f32[32,1152]{1,0:T(8,128)S(1)}, f32[32,1152]{1,0:T(8,128)S(1)}, u32[]{:S(2)}, u32[]{:S(2)}) collective-permute-start(f32[32,1152]{1,0:T(8,128)S(1)} %fusion.15), channel_id=1, source_target_pairs={{0,8},{1,9},{2,10},{3,11},{4,12},{5,13},{6,14},{7,15},{8,0},{9,1},... | collective-permute-start | bytes 442376 | tf_op jit(solution)/shard_map/ppermute | solution.py:22
  56.7 0.7 convolution_reduce_fusion.1
  57.5 5.3 %collective-permute-done.13 = f32[32,1152]{1,0:T(8,128)S(1)} collective-permute-done((f32[32,1152]{1,0:T(8,128)S(1)}, f32[32,1152]{1,0:T(8,128)S(1)}, u32[]{:S(2)}, u32[]{:S(2)}) %collective-permute-start.13) | collective-permute-done | bytes 147488 | tf_op jit(solution)/shard_map/ppermute | solution.py:22
  64.0 0.7 convolution_reduce_fusion
  64.8 0.8 %collective-permute-start.15 = (f32[2048]{0:T(1024)S(1)}, f32[2048]{0:T(1024)S(1)}, u32[]{:S(2)}, u32[]{:S(2)}) collective-permute-start(f32[2048]{0:T(1024)S(1)} %reduce_max.29), channel_id=1, source_target_pairs={{0,2},{1,3},{2,0},{3,1},{4,6},{5,7},{6,4},{7,5},{8,10},{9,11},{10,... | collective-permute-start | bytes 24584 | tf_op jit(solution)/shard_map/ppermute | solution.py:27
  65.6 1.1 %collective-permute-start.14 = (f32[2048]{0:T(1024)S(1)}, f32[2048]{0:T(1024)S(1)}, u32[]{:S(2)}, u32[]{:S(2)}) collective-permute-start(f32[2048]{0:T(1024)S(1)} %reduce_max.29), channel_id=1, source_target_pairs={{0,1},{1,0},{2,3},{3,2},{4,5},{5,4},{6,7},{7,6},{8,9},{9,8},{10,11... | collective-permute-start | bytes 24584 | tf_op jit(solution)/shard_map/ppermute | solution.py:27
  66.7 1.2 %collective-permute-done.16 = f32[2048]{0:T(1024)S(1)} collective-permute-done((f32[2048]{0:T(1024)S(1)}, f32[2048]{0:T(1024)S(1)}, u32[]{:S(2)}, u32[]{:S(2)}) %collective-permute-start.16) | collective-permute-done | bytes 8224 | tf_op jit(solution)/shard_map/ppermute | solution.py:27
  67.9 0.7 collective-permute-done.15
  68.6 2.5 %collective-permute-start.19 = (f32[2048]{0:T(1024)S(1)}, f32[2048]{0:T(1024)S(1)}, u32[]{:S(2)}, u32[]{:S(2)}) collective-permute-start(f32[2048]{0:T(1024)S(1)} %maximum_maximum_fusion.1), channel_id=1, source_target_pairs={{0,12},{1,13},{2,14},{3,15},{4,8},{5,9},{6,10},{7,11},{8,4},{9,5},... | collective-permute-start | bytes 24584 | tf_op jit(solution)/shard_map/ppermute | solution.py:27
  71.1 1.9 %collective-permute-start.17 = (f32[2048]{0:T(1024)S(1)}, f32[2048]{0:T(1024)S(1)}, u32[]{:S(2)}, u32[]{:S(2)}) collective-permute-start(f32[2048]{0:T(1024)S(1)} %maximum_maximum_fusion.1), channel_id=1, source_target_pairs={{0,4},{1,5},{2,6},{3,7},{4,0},{5,1},{6,2},{7,3},{8,12},{9,13},{10,... | collective-permute-start | bytes 24584 | tf_op jit(solution)/shard_map/ppermute | solution.py:27
  73.0 1.1 %collective-permute-done.19 = f32[2048]{0:T(1024)S(1)} collective-permute-done((f32[2048]{0:T(1024)S(1)}, f32[2048]{0:T(1024)S(1)}, u32[]{:S(2)}, u32[]{:S(2)}) %collective-permute-start.19) | collective-permute-done | bytes 8224 | tf_op jit(solution)/shard_map/ppermute | solution.py:27
  74.1 1.5 %collective-permute-done.18 = f32[2048]{0:T(1024)S(1)} collective-permute-done((f32[2048]{0:T(1024)S(1)}, f32[2048]{0:T(1024)S(1)}, u32[]{:S(2)}, u32[]{:S(2)}) %collective-permute-start.18) | collective-permute-done | bytes 8224 | tf_op jit(solution)/shard_map/ppermute | solution.py:27
  (136 shorter events, 10.5 us)
Async XLA Ops:
  0.6 23.7 %copy-start.3 = (s32[9,32]{1,0:T(8,128)S(1)}, s32[9,32]{1,0:T(8,128)}, u32[]{:S(2)}) copy-start(s32[9,32]{1,0:T(8,128)} %refs_4_.1) | copy-start | bytes 3460
  1.8 4.7 %collective-permute-start.1 = (f32[1,4480]{1,0:T(1,128)S(1)}, f32[1,4480]{1,0:T(1,128)S(1)}, u32[]{:S(2)}, u32[]{:S(2)}) collective-permute-start(f32[1,4480]{1,0:T(1,128)S(1)} %broadcast_in_dim.535), channel_id=1, source_target_pairs={{0,2},{1,3},{2,0},{3,1},{4,6},{5,7},{6,4},{7,5},{8,10},{9,11},{10,... | collective-permute-start | bytes 53768 | tf_op jit(solution)/shard_map/ppermute | solution.py:27
  4.8 3.2 %collective-permute-start.2 = (f32[1,4480]{1,0:T(1,128)S(1)}, f32[1,4480]{1,0:T(1,128)S(1)}, u32[]{:S(2)}, u32[]{:S(2)}) collective-permute-start(f32[1,4480]{1,0:T(1,128)S(1)} %broadcast_in_dim.535), channel_id=1, source_target_pairs={{0,3},{1,2},{2,1},{3,0},{4,7},{5,6},{6,5},{7,4},{8,11},{9,10},{10,... | collective-permute-start | bytes 53768 | tf_op jit(solution)/shard_map/ppermute | solution.py:27
  4.8 3.2 %collective-permute-start = (f32[1,4480]{1,0:T(1,128)S(1)}, f32[1,4480]{1,0:T(1,128)S(1)}, u32[]{:S(2)}, u32[]{:S(2)}) collective-permute-start(f32[1,4480]{1,0:T(1,128)S(1)} %broadcast_in_dim.535), channel_id=1, source_target_pairs={{0,1},{1,0},{2,3},{3,2},{4,5},{5,4},{6,7},{7,6},{8,9},{9,8},{10,11... | collective-permute-start | bytes 53768 | tf_op jit(solution)/shard_map/ppermute | solution.py:27
  8.0 8.3 %copy-start.2 = (f32[1,4480]{1,0:T(1,128)}, f32[1,4480]{1,0:T(1,128)S(1)}, u32[]{:S(2)}) copy-start(f32[1,4480]{1,0:T(1,128)S(1)} %add_add_fusion.refs_0_) | copy-start | bytes 53764
  8.0 5.8 %collective-permute-start.5 = (f32[1,4480]{1,0:T(1,128)S(1)}, f32[1,4480]{1,0:T(1,128)S(1)}, u32[]{:S(2)}, u32[]{:S(2)}) collective-permute-start(f32[1,4480]{1,0:T(1,128)S(1)} %add_add_fusion.refs_0_), channel_id=1, source_target_pairs={{0,12},{1,13},{2,14},{3,15},{4,8},{5,9},{6,10},{7,11},{8,4},{9,5},... | collective-permute-start | bytes 53768 | tf_op jit(solution)/shard_map/ppermute | solution.py:27
  11.7 4.7 %collective-permute-start.4 = (f32[1,4480]{1,0:T(1,128)S(1)}, f32[1,4480]{1,0:T(1,128)S(1)}, u32[]{:S(2)}, u32[]{:S(2)}) collective-permute-start(f32[1,4480]{1,0:T(1,128)S(1)} %add_add_fusion.refs_0_), channel_id=1, source_target_pairs={{0,8},{1,9},{2,10},{3,11},{4,12},{5,13},{6,14},{7,15},{8,0},{9,1},... | collective-permute-start | bytes 53768 | tf_op jit(solution)/shard_map/ppermute | solution.py:27
  11.7 4.7 %collective-permute-start.3 = (f32[1,4480]{1,0:T(1,128)S(1)}, f32[1,4480]{1,0:T(1,128)S(1)}, u32[]{:S(2)}, u32[]{:S(2)}) collective-permute-start(f32[1,4480]{1,0:T(1,128)S(1)} %add_add_fusion.refs_0_), channel_id=1, source_target_pairs={{0,4},{1,5},{2,6},{3,7},{4,0},{5,1},{6,2},{7,3},{8,12},{9,13},{10,... | collective-permute-start | bytes 53768 | tf_op jit(solution)/shard_map/ppermute | solution.py:27
  13.8 2.5 %copy-start.4 = (f32[1,4480]{1,0:T(1,128)}, f32[1,4480]{1,0:T(1,128)S(1)}, u32[]{:S(2)}) copy-start(f32[1,4480]{1,0:T(1,128)S(1)} %collective-permute-done.5.refs_3_) | copy-start | bytes 53764
  16.3 0.6 copy-start.5
  16.9 0.6 copy-start.6
  24.3 1.7 %collective-permute-start.6 = (f32[32,2048]{1,0:T(8,128)}, f32[32,2048]{1,0:T(8,128)S(1)}, u32[]{:S(2)}, u32[]{:S(2)}) collective-permute-start(f32[32,2048]{1,0:T(8,128)} %get-tuple-element.16), channel_id=1, source_target_pairs={{0,1},{1,0},{2,3},{3,2},{4,5},{5,4},{6,7},{7,6},{8,9},{9,8},{10,11... | collective-permute-start | bytes 786440 | tf_op jit(solution)/shard_map/ppermute | solution.py:22
  27.7 1.2 %copy-start.7 = (s32[8]{0:T(128)S(1)}, s32[8]{0:T(128)}, u32[]{:S(2)}) copy-start(s32[8]{0:T(128)} %param.5) | copy-start | bytes 100
  27.9 1.2 %copy-start.1 = (f32[32,1152]{1,0:T(8,128)S(1)}, f32[32,1152]{1,0:T(8,128)}, u32[]{:S(2)}) copy-start(f32[32,1152]{1,0:T(8,128)} %get-tuple-element.17) | copy-start | bytes 442372
  28.2 7.7 %collective-permute-start.8 = (f32[32,1792]{1,0:T(8,128)S(1)}, f32[32,1792]{1,0:T(8,128)S(1)}, u32[]{:S(2)}, u32[]{:S(2)}) collective-permute-start(f32[32,1792]{1,0:T(8,128)S(1)} %fusion.2), channel_id=1, source_target_pairs={{0,2},{1,3},{2,0},{3,1},{4,6},{5,7},{6,4},{7,5},{8,10},{9,11},{10,... | collective-permute-start | bytes 688136 | tf_op jit(solution)/shard_map/ppermute | solution.py:22
  29.0 1.4 %collective-permute-start.7 = (f32[32,1152]{1,0:T(8,128)S(1)}, f32[32,1152]{1,0:T(8,128)S(1)}, u32[]{:S(2)}, u32[]{:S(2)}) collective-permute-start(f32[32,1152]{1,0:T(8,128)S(1)} %copy-done.1), channel_id=1, source_target_pairs={{0,1},{1,0},{2,3},{3,2},{4,5},{5,4},{6,7},{7,6},{8,9},{9,8},{10,11... | collective-permute-start | bytes 442376 | tf_op jit(solution)/shard_map/ppermute | solution.py:22
  36.9 6.2 %collective-permute-start.10 = (f32[32,1536]{1,0:T(8,128)S(1)}, f32[32,1536]{1,0:T(8,128)S(1)}, u32[]{:S(2)}, u32[]{:S(2)}) collective-permute-start(f32[32,1536]{1,0:T(8,128)S(1)} %fusion.3), channel_id=1, source_target_pairs={{0,4},{1,5},{2,6},{3,7},{4,0},{5,1},{6,2},{7,3},{8,12},{9,13},{10,... | collective-permute-start | bytes 589832 | tf_op jit(solution)/shard_map/ppermute | solution.py:22
  37.9 5.2 %collective-permute-start.9 = (f32[32,1152]{1,0:T(8,128)S(1)}, f32[32,1152]{1,0:T(8,128)S(1)}, u32[]{:S(2)}, u32[]{:S(2)}) collective-permute-start(f32[32,1152]{1,0:T(8,128)S(1)} %fusion.17), channel_id=1, source_target_pairs={{0,2},{1,3},{2,0},{3,1},{4,6},{5,7},{6,4},{7,5},{8,10},{9,11},{10,... | collective-permute-start | bytes 442376 | tf_op jit(solution)/shard_map/ppermute | solution.py:22
  44.1 9.0 %collective-permute-start.12 = (f32[32,1280]{1,0:T(8,128)S(1)}, f32[32,1280]{1,0:T(8,128)S(1)}, u32[]{:S(2)}, u32[]{:S(2)}) collective-permute-start(f32[32,1280]{1,0:T(8,128)S(1)} %fusion.12), channel_id=1, source_target_pairs={{0,8},{1,9},{2,10},{3,11},{4,12},{5,13},{6,14},{7,15},{8,0},{9,1},... | collective-permute-start | bytes 491528 | tf_op jit(solution)/shard_map/ppermute | solution.py:22
  46.6 5.8 %collective-permute-start.11 = (f32[32,1152]{1,0:T(8,128)S(1)}, f32[32,1152]{1,0:T(8,128)S(1)}, u32[]{:S(2)}, u32[]{:S(2)}) collective-permute-start(f32[32,1152]{1,0:T(8,128)S(1)} %fusion.16), channel_id=1, source_target_pairs={{0,4},{1,5},{2,6},{3,7},{4,0},{5,1},{6,2},{7,3},{8,12},{9,13},{10,... | collective-permute-start | bytes 442376 | tf_op jit(solution)/shard_map/ppermute | solution.py:22
  55.1 7.7 %collective-permute-start.13 = (f32[32,1152]{1,0:T(8,128)S(1)}, f32[32,1152]{1,0:T(8,128)S(1)}, u32[]{:S(2)}, u32[]{:S(2)}) collective-permute-start(f32[32,1152]{1,0:T(8,128)S(1)} %fusion.15), channel_id=1, source_target_pairs={{0,8},{1,9},{2,10},{3,11},{4,12},{5,13},{6,14},{7,15},{8,0},{9,1},... | collective-permute-start | bytes 442376 | tf_op jit(solution)/shard_map/ppermute | solution.py:22
  64.7 11.5 %copy-start = (f32[32,2048]{1,0:T(8,128)}, f32[32,2048]{1,0:T(8,128)S(1)}, u32[]{:S(2)}) copy-start(f32[32,2048]{1,0:T(8,128)S(1)} %constant_dynamic-update-slice_fusion) | copy-start | bytes 786436
  64.8 3.1 %collective-permute-start.16 = (f32[2048]{0:T(1024)S(1)}, f32[2048]{0:T(1024)S(1)}, u32[]{:S(2)}, u32[]{:S(2)}) collective-permute-start(f32[2048]{0:T(1024)S(1)} %reduce_max.29), channel_id=1, source_target_pairs={{0,3},{1,2},{2,1},{3,0},{4,7},{5,6},{6,5},{7,4},{8,11},{9,10},{10,... | collective-permute-start | bytes 24584 | tf_op jit(solution)/shard_map/ppermute | solution.py:27
  64.8 3.7 %collective-permute-start.15 = (f32[2048]{0:T(1024)S(1)}, f32[2048]{0:T(1024)S(1)}, u32[]{:S(2)}, u32[]{:S(2)}) collective-permute-start(f32[2048]{0:T(1024)S(1)} %reduce_max.29), channel_id=1, source_target_pairs={{0,2},{1,3},{2,0},{3,1},{4,6},{5,7},{6,4},{7,5},{8,10},{9,11},{10,... | collective-permute-start | bytes 24584 | tf_op jit(solution)/shard_map/ppermute | solution.py:27
  65.6 2.9 %collective-permute-start.14 = (f32[2048]{0:T(1024)S(1)}, f32[2048]{0:T(1024)S(1)}, u32[]{:S(2)}, u32[]{:S(2)}) collective-permute-start(f32[2048]{0:T(1024)S(1)} %reduce_max.29), channel_id=1, source_target_pairs={{0,1},{1,0},{2,3},{3,2},{4,5},{5,4},{6,7},{7,6},{8,9},{9,8},{10,11... | collective-permute-start | bytes 24584 | tf_op jit(solution)/shard_map/ppermute | solution.py:27
  68.6 5.5 %collective-permute-start.19 = (f32[2048]{0:T(1024)S(1)}, f32[2048]{0:T(1024)S(1)}, u32[]{:S(2)}, u32[]{:S(2)}) collective-permute-start(f32[2048]{0:T(1024)S(1)} %maximum_maximum_fusion.1), channel_id=1, source_target_pairs={{0,12},{1,13},{2,14},{3,15},{4,8},{5,9},{6,10},{7,11},{8,4},{9,5},... | collective-permute-start | bytes 24584 | tf_op jit(solution)/shard_map/ppermute | solution.py:27
  71.1 4.5 %collective-permute-start.18 = (f32[2048]{0:T(1024)S(1)}, f32[2048]{0:T(1024)S(1)}, u32[]{:S(2)}, u32[]{:S(2)}) collective-permute-start(f32[2048]{0:T(1024)S(1)} %maximum_maximum_fusion.1), channel_id=1, source_target_pairs={{0,8},{1,9},{2,10},{3,11},{4,12},{5,13},{6,14},{7,15},{8,0},{9,1},... | collective-permute-start | bytes 24584 | tf_op jit(solution)/shard_map/ppermute | solution.py:27
  71.1 4.5 %collective-permute-start.17 = (f32[2048]{0:T(1024)S(1)}, f32[2048]{0:T(1024)S(1)}, u32[]{:S(2)}, u32[]{:S(2)}) collective-permute-start(f32[2048]{0:T(1024)S(1)} %maximum_maximum_fusion.1), channel_id=1, source_target_pairs={{0,4},{1,5},{2,6},{3,7},{4,0},{5,1},{6,2},{7,3},{8,12},{9,13},{10,... | collective-permute-start | bytes 24584 | tf_op jit(solution)/shard_map/ppermute | solution.py:27

commit v22 on v17

--- a/solution.py
+++ b/solution.py
@@ -102,8 +102,8 @@
     return pl.pallas_call(
         functools.partial(local_tree_kernel, tuple(widths_seq), float(channels_all), len(total_terms)),
         out_shape=(
-            jax.ShapeDtypeStruct((rows, head_width), jnp.float32),
-            jax.ShapeDtypeStruct((rows, tail_width), jnp.float32),
+            pltpu.VMEM((rows, head_width), jnp.float32),
+            pltpu.VMEM((rows, tail_width), jnp.float32),
         ),
         in_specs=[vmem] * (len(total_terms) + 2),
         out_specs=(vmem, vmem),

time: 76.6 us -> 74.7 us (0.975)
  other arithmetic: 10.5 us -> 9.58 us
    select_n x8, other arithmetic: 1.17 us -> 0.21 us  [halves(): jnp.where(upper_half, partner, own)]
where the time goes in v22:
time: 74.7 us; the launch traced here: 74.6 us
  waiting for transfers between devices  34.1 us (46%)
  starting transfers between devices  20.9 us (28%)
  other arithmetic  9.58 us (13%)
  Pallas kernels  6.1 us (8%)
  local copies, waits for them, and re-layouts  1.52 us (2%)
  between operations  1.29 us (2%)
  matrix products  1.03 us (1%)
    ppermute x8, waiting for transfers between devices, from_partner(): return lax.ppermute(value, axis, pairs)  22.8 us
    ppermute x12, starting transfers between devices, from_xor(): return lax.ppermute(value, axis, pairs)  14 us
    ppermute x12, waiting for transfers between devices, from_xor(): return lax.ppermute(value, axis, pairs)  11.3 us
    ppermute x8, starting transfers between devices, from_partner(): return lax.ppermute(value, axis, pairs)  6.91 us
    select_n x56, other arithmetic, shift_rows(): jnp.where(chosen, current[:, span:span + keep_len], current[:, :keep_len])  6.19 us
    pallas_call x1, Pallas kernels, local_tree(): pl.pallas_call(functools.partial(local_tree_kernel, tuple(widths_seq), fl...  6.1 us
  transfers between devices with their start and end apart: 20, of which 15 were waited for; matrix products, arithmetic and copies ran while one was open for 3% of the time, Pallas kernels for 0%

profile of v22, /device:TPU:0, one launch (start us, length us, event | category | flops | bytes accessed | tf_op | source)
XLA Modules:
  0.0 74.6 jit_solution(18253629734022984810)
XLA Ops:
  0.6 1.1 %slice_reduce_fusion = f32[4480]{0:T(1024)S(1)} fusion(f32[32,6144]{1,0:T(8,128)} %x_ref.1), kind=kLoop, calls=%fused_computation.4 | loop fusion | flops 138880 | bytes 591360 | tf_op jit(solution)/shard_map/reduce_sum | solution.py:172
  1.8 3.0 %collective-permute-start.1 = (f32[1,4480]{1,0:T(1,128)S(1)}, f32[1,4480]{1,0:T(1,128)S(1)}, u32[]{:S(2)}, u32[]{:S(2)}) collective-permute-start(f32[1,4480]{1,0:T(1,128)S(1)} %broadcast_in_dim.527), channel_id=1, source_target_pairs={{0,2},{1,3},{2,0},{3,1},{4,6},{5,7},{6,4},{7,5},{8,10},{9,11},{10,... | collective-permute-start | bytes 53768 | tf_op jit(solution)/shard_map/ppermute | solution.py:27
  5.0 1.5 %collective-permute-done.1 = f32[1,4480]{1,0:T(1,128)S(1)} collective-permute-done((f32[1,4480]{1,0:T(1,128)S(1)}, f32[1,4480]{1,0:T(1,128)S(1)}, u32[]{:S(2)}, u32[]{:S(2)}) %collective-permute-start.1) | collective-permute-done | bytes 17952 | tf_op jit(solution)/shard_map/ppermute | solution.py:27
  6.5 1.4 %collective-permute-done.2 = f32[1,4480]{1,0:T(1,128)S(1)} collective-permute-done((f32[1,4480]{1,0:T(1,128)S(1)}, f32[1,4480]{1,0:T(1,128)S(1)}, u32[]{:S(2)}, u32[]{:S(2)}) %collective-permute-start.2) | collective-permute-done | bytes 17952 | tf_op jit(solution)/shard_map/ppermute | solution.py:27
  8.0 3.7 %collective-permute-start.5 = (f32[1,4480]{1,0:T(1,128)S(1)}, f32[1,4480]{1,0:T(1,128)S(1)}, u32[]{:S(2)}, u32[]{:S(2)}) collective-permute-start(f32[1,4480]{1,0:T(1,128)S(1)} %add_add_fusion.refs_0_), channel_id=1, source_target_pairs={{0,12},{1,13},{2,14},{3,15},{4,8},{5,9},{6,10},{7,11},{8,4},{9,5},... | collective-permute-start | bytes 53768 | tf_op jit(solution)/shard_map/ppermute | solution.py:27
  11.7 0.8 %collective-permute-start.3 = (f32[1,4480]{1,0:T(1,128)S(1)}, f32[1,4480]{1,0:T(1,128)S(1)}, u32[]{:S(2)}, u32[]{:S(2)}) collective-permute-start(f32[1,4480]{1,0:T(1,128)S(1)} %add_add_fusion.refs_0_), channel_id=1, source_target_pairs={{0,4},{1,5},{2,6},{3,7},{4,0},{5,1},{6,2},{7,3},{8,12},{9,13},{10,... | collective-permute-start | bytes 53768 | tf_op jit(solution)/shard_map/ppermute | solution.py:27
  12.5 1.4 %collective-permute-done.5.refs_3_ = f32[1,4480]{1,0:T(1,128)S(1)} collective-permute-done((f32[1,4480]{1,0:T(1,128)S(1)}, f32[1,4480]{1,0:T(1,128)S(1)}, u32[]{:S(2)}, u32[]{:S(2)}) %collective-permute-start.5) | collective-permute-done | bytes 17952 | tf_op jit(solution)/shard_map/ppermute | solution.py:27
  13.8 2.5 %collective-permute-done.4.refs_2_ = f32[1,4480]{1,0:T(1,128)S(1)} collective-permute-done((f32[1,4480]{1,0:T(1,128)S(1)}, f32[1,4480]{1,0:T(1,128)S(1)}, u32[]{:S(2)}, u32[]{:S(2)}) %collective-permute-start.4) | collective-permute-done | bytes 17952 | tf_op jit(solution)/shard_map/ppermute | solution.py:27
  16.9 0.6 copy-done.5
  17.6 6.1 %shard_map.50 = (f32[32,2048]{1,0:T(8,128)S(1)}, f32[32,1152]{1,0:T(8,128)S(1)}) custom-call(f32[32,6144]{1,0:T(8,128)} %x_ref.1, f32[1,4480]{1,0:T(1,128)} %copy-done.1, f32[1,4480]{1,0:T(1,128)} %copy-done.5, f32[1,4480]{1,0:T(1,128)} %copy-done.4, f32[1,4480]{1,0:T(1,128)} %copy-done.3, s32[9,32]{1,0:T(8,128)} %refs_4_.1), custom_call_target="tpu_custom_call" | custom-call | flops 25395200 | bytes 983040 | tf_op jit(solution)/shard_map/pallas_call | solution.py:102
  23.8 1.4 %collective-permute-done.6 = f32[32,2048]{1,0:T(8,128)S(1)} collective-permute-done((f32[32,2048]{1,0:T(8,128)S(1)}, f32[32,2048]{1,0:T(8,128)S(1)}, u32[]{:S(2)}, u32[]{:S(2)}) %collective-permute-start.6) | collective-permute-done | bytes 262176 | tf_op jit(solution)/shard_map/ppermute | solution.py:22
  26.4 0.8 %collective-permute-start.8 = (f32[32,1792]{1,0:T(8,128)S(1)}, f32[32,1792]{1,0:T(8,128)S(1)}, u32[]{:S(2)}, u32[]{:S(2)}) collective-permute-start(f32[32,1792]{1,0:T(8,128)S(1)} %fusion.2), channel_id=1, source_target_pairs={{0,2},{1,3},{2,0},{3,1},{4,6},{5,7},{6,4},{7,5},{8,10},{9,11},{10,... | collective-permute-start | bytes 688136 | tf_op jit(solution)/shard_map/ppermute | solution.py:22
  27.3 1.3 %collective-permute-done.7 = f32[32,1152]{1,0:T(8,128)S(1)} collective-permute-done((f32[32,1152]{1,0:T(8,128)S(1)}, f32[32,1152]{1,0:T(8,128)S(1)}, u32[]{:S(2)}, u32[]{:S(2)}) %collective-permute-start.7) | collective-permute-done | bytes 147488 | tf_op jit(solution)/shard_map/ppermute | solution.py:22
  28.5 5.5 %collective-permute-done.8 = f32[32,1792]{1,0:T(8,128)S(1)} collective-permute-done((f32[32,1792]{1,0:T(8,128)S(1)}, f32[32,1792]{1,0:T(8,128)S(1)}, u32[]{:S(2)}, u32[]{:S(2)}) %collective-permute-start.8) | collective-permute-done | bytes 229408 | tf_op jit(solution)/shard_map/ppermute | solution.py:22
  36.1 0.8 %collective-permute-start.9 = (f32[32,1152]{1,0:T(8,128)S(1)}, f32[32,1152]{1,0:T(8,128)S(1)}, u32[]{:S(2)}, u32[]{:S(2)}) collective-permute-start(f32[32,1152]{1,0:T(8,128)S(1)} %fusion.16), channel_id=1, source_target_pairs={{0,2},{1,3},{2,0},{3,1},{4,6},{5,7},{6,4},{7,5},{8,10},{9,11},{10,... | collective-permute-start | bytes 442376 | tf_op jit(solution)/shard_map/ppermute | solution.py:22
  36.9 4.4 %collective-permute-done.9 = f32[32,1152]{1,0:T(8,128)S(1)} collective-permute-done((f32[32,1152]{1,0:T(8,128)S(1)}, f32[32,1152]{1,0:T(8,128)S(1)}, u32[]{:S(2)}, u32[]{:S(2)}) %collective-permute-start.9) | collective-permute-done | bytes 147488 | tf_op jit(solution)/shard_map/ppermute | solution.py:22
  42.3 1.5 %collective-permute-start.12 = (f32[32,1280]{1,0:T(8,128)S(1)}, f32[32,1280]{1,0:T(8,128)S(1)}, u32[]{:S(2)}, u32[]{:S(2)}) collective-permute-start(f32[32,1280]{1,0:T(8,128)S(1)} %fusion.12), channel_id=1, source_target_pairs={{0,8},{1,9},{2,10},{3,11},{4,12},{5,13},{6,14},{7,15},{8,0},{9,1},... | collective-permute-start | bytes 491528 | tf_op jit(solution)/shard_map/ppermute | solution.py:22
  44.8 2.0 %collective-permute-start.11 = (f32[32,1152]{1,0:T(8,128)S(1)}, f32[32,1152]{1,0:T(8,128)S(1)}, u32[]{:S(2)}, u32[]{:S(2)}) collective-permute-start(f32[32,1152]{1,0:T(8,128)S(1)} %fusion.15), channel_id=1, source_target_pairs={{0,4},{1,5},{2,6},{3,7},{4,0},{5,1},{6,2},{7,3},{8,12},{9,13},{10,... | collective-permute-start | bytes 442376 | tf_op jit(solution)/shard_map/ppermute | solution.py:22
  46.9 3.7 %collective-permute-done.11 = f32[32,1152]{1,0:T(8,128)S(1)} collective-permute-done((f32[32,1152]{1,0:T(8,128)S(1)}, f32[32,1152]{1,0:T(8,128)S(1)}, u32[]{:S(2)}, u32[]{:S(2)}) %collective-permute-start.11) | collective-permute-done | bytes 147488 | tf_op jit(solution)/shard_map/ppermute | solution.py:22
  50.6 0.8 %collective-permute-done.12 = f32[32,1280]{1,0:T(8,128)S(1)} collective-permute-done((f32[32,1280]{1,0:T(8,128)S(1)}, f32[32,1280]{1,0:T(8,128)S(1)}, u32[]{:S(2)}, u32[]{:S(2)}) %collective-permute-start.12) | collective-permute-done | bytes 163872 | tf_op jit(solution)/shard_map/ppermute | solution.py:22
  53.2 1.6 %collective-permute-start.13 = (f32[32,1152]{1,0:T(8,128)S(1)}, f32[32,1152]{1,0:T(8,128)S(1)}, u32[]{:S(2)}, u32[]{:S(2)}) collective-permute-start(f32[32,1152]{1,0:T(8,128)S(1)} %fusion.14), channel_id=1, source_target_pairs={{0,8},{1,9},{2,10},{3,11},{4,12},{5,13},{6,14},{7,15},{8,0},{9,1},... | collective-permute-start | bytes 442376 | tf_op jit(solution)/shard_map/ppermute | solution.py:22
  55.2 5.7 %collective-permute-done.13 = f32[32,1152]{1,0:T(8,128)S(1)} collective-permute-done((f32[32,1152]{1,0:T(8,128)S(1)}, f32[32,1152]{1,0:T(8,128)S(1)}, u32[]{:S(2)}, u32[]{:S(2)}) %collective-permute-start.13) | collective-permute-done | bytes 147488 | tf_op jit(solution)/shard_map/ppermute | solution.py:22
  62.0 1.0 %convolution_reduce_fusion = f32[512,128]{1,0:T(8,128)S(1)} fusion(f32[512,256,1]{1,0,2:T(8,128)S(1)} %bitcast.85, f32[8,128,256]{2,1,0:T(8,128)S(1)} %bitcast.84), kind=kOutput, calls=%fused_computation | convolution fusion | flops 805765120 | bytes 1835008 | tf_op jit(solution)/shard_map/dot_general | solution.py:151
  63.2 0.8 %collective-permute-start.15 = (f32[2048]{0:T(1024)S(1)}, f32[2048]{0:T(1024)S(1)}, u32[]{:S(2)}, u32[]{:S(2)}) collective-permute-start(f32[2048]{0:T(1024)S(1)} %reduce_max.19), channel_id=1, source_target_pairs={{0,2},{1,3},{2,0},{3,1},{4,6},{5,7},{6,4},{7,5},{8,10},{9,11},{10,... | collective-permute-start | bytes 24584 | tf_op jit(solution)/shard_map/ppermute | solution.py:27
  64.0 1.1 %collective-permute-start.14 = (f32[2048]{0:T(1024)S(1)}, f32[2048]{0:T(1024)S(1)}, u32[]{:S(2)}, u32[]{:S(2)}) collective-permute-start(f32[2048]{0:T(1024)S(1)} %reduce_max.19), channel_id=1, source_target_pairs={{0,1},{1,0},{2,3},{3,2},{4,5},{5,4},{6,7},{7,6},{8,9},{9,8},{10,11... | collective-permute-start | bytes 24584 | tf_op jit(solution)/shard_map/ppermute | solution.py:27
  65.0 1.2 %collective-permute-done.16 = f32[2048]{0:T(1024)S(1)} collective-permute-done((f32[2048]{0:T(1024)S(1)}, f32[2048]{0:T(1024)S(1)}, u32[]{:S(2)}, u32[]{:S(2)}) %collective-permute-start.16) | collective-permute-done | bytes 8224 | tf_op jit(solution)/shard_map/ppermute | solution.py:27
  66.3 0.7 collective-permute-done.15
  66.9 2.5 %collective-permute-start.19 = (f32[2048]{0:T(1024)S(1)}, f32[2048]{0:T(1024)S(1)}, u32[]{:S(2)}, u32[]{:S(2)}) collective-permute-start(f32[2048]{0:T(1024)S(1)} %maximum_maximum_fusion.1), channel_id=1, source_target_pairs={{0,12},{1,13},{2,14},{3,15},{4,8},{5,9},{6,10},{7,11},{8,4},{9,5},... | collective-permute-start | bytes 24584 | tf_op jit(solution)/shard_map/ppermute | solution.py:27
  69.4 1.9 %collective-permute-start.17 = (f32[2048]{0:T(1024)S(1)}, f32[2048]{0:T(1024)S(1)}, u32[]{:S(2)}, u32[]{:S(2)}) collective-permute-start(f32[2048]{0:T(1024)S(1)} %maximum_maximum_fusion.1), channel_id=1, source_target_pairs={{0,4},{1,5},{2,6},{3,7},{4,0},{5,1},{6,2},{7,3},{8,12},{9,13},{10,... | collective-permute-start | bytes 24584 | tf_op jit(solution)/shard_map/ppermute | solution.py:27
  71.4 1.1 %collective-permute-done.19 = f32[2048]{0:T(1024)S(1)} collective-permute-done((f32[2048]{0:T(1024)S(1)}, f32[2048]{0:T(1024)S(1)}, u32[]{:S(2)}, u32[]{:S(2)}) %collective-permute-start.19) | collective-permute-done | bytes 8224 | tf_op jit(solution)/shard_map/ppermute | solution.py:27
  72.4 1.5 %collective-permute-done.18 = f32[2048]{0:T(1024)S(1)} collective-permute-done((f32[2048]{0:T(1024)S(1)}, f32[2048]{0:T(1024)S(1)}, u32[]{:S(2)}, u32[]{:S(2)}) %collective-permute-start.18) | collective-permute-done | bytes 8224 | tf_op jit(solution)/shard_map/ppermute | solution.py:27
  74.0 0.6 maximum_maximum_fusion
  (123 shorter events, 9.2 us)
Async XLA Ops:
  0.6 23.1 %copy-start.2 = (s32[9,32]{1,0:T(8,128)S(1)}, s32[9,32]{1,0:T(8,128)}, u32[]{:S(2)}) copy-start(s32[9,32]{1,0:T(8,128)} %refs_4_.1) | copy-start | bytes 3460
  1.8 4.7 %collective-permute-start.1 = (f32[1,4480]{1,0:T(1,128)S(1)}, f32[1,4480]{1,0:T(1,128)S(1)}, u32[]{:S(2)}, u32[]{:S(2)}) collective-permute-start(f32[1,4480]{1,0:T(1,128)S(1)} %broadcast_in_dim.527), channel_id=1, source_target_pairs={{0,2},{1,3},{2,0},{3,1},{4,6},{5,7},{6,4},{7,5},{8,10},{9,11},{10,... | collective-permute-start | bytes 53768 | tf_op jit(solution)/shard_map/ppermute | solution.py:27
  4.8 3.2 %collective-permute-start.2 = (f32[1,4480]{1,0:T(1,128)S(1)}, f32[1,4480]{1,0:T(1,128)S(1)}, u32[]{:S(2)}, u32[]{:S(2)}) collective-permute-start(f32[1,4480]{1,0:T(1,128)S(1)} %broadcast_in_dim.527), channel_id=1, source_target_pairs={{0,3},{1,2},{2,1},{3,0},{4,7},{5,6},{6,5},{7,4},{8,11},{9,10},{10,... | collective-permute-start | bytes 53768 | tf_op jit(solution)/shard_map/ppermute | solution.py:27
  4.8 3.2 %collective-permute-start = (f32[1,4480]{1,0:T(1,128)S(1)}, f32[1,4480]{1,0:T(1,128)S(1)}, u32[]{:S(2)}, u32[]{:S(2)}) collective-permute-start(f32[1,4480]{1,0:T(1,128)S(1)} %broadcast_in_dim.527), channel_id=1, source_target_pairs={{0,1},{1,0},{2,3},{3,2},{4,5},{5,4},{6,7},{7,6},{8,9},{9,8},{10,11... | collective-permute-start | bytes 53768 | tf_op jit(solution)/shard_map/ppermute | solution.py:27
  8.0 8.3 %copy-start.1 = (f32[1,4480]{1,0:T(1,128)}, f32[1,4480]{1,0:T(1,128)S(1)}, u32[]{:S(2)}) copy-start(f32[1,4480]{1,0:T(1,128)S(1)} %add_add_fusion.refs_0_) | copy-start | bytes 53764
  8.0 5.8 %collective-permute-start.5 = (f32[1,4480]{1,0:T(1,128)S(1)}, f32[1,4480]{1,0:T(1,128)S(1)}, u32[]{:S(2)}, u32[]{:S(2)}) collective-permute-start(f32[1,4480]{1,0:T(1,128)S(1)} %add_add_fusion.refs_0_), channel_id=1, source_target_pairs={{0,12},{1,13},{2,14},{3,15},{4,8},{5,9},{6,10},{7,11},{8,4},{9,5},... | collective-permute-start | bytes 53768 | tf_op jit(solution)/shard_map/ppermute | solution.py:27
  11.7 4.7 %collective-permute-start.4 = (f32[1,4480]{1,0:T(1,128)S(1)}, f32[1,4480]{1,0:T(1,128)S(1)}, u32[]{:S(2)}, u32[]{:S(2)}) collective-permute-start(f32[1,4480]{1,0:T(1,128)S(1)} %add_add_fusion.refs_0_), channel_id=1, source_target_pairs={{0,8},{1,9},{2,10},{3,11},{4,12},{5,13},{6,14},{7,15},{8,0},{9,1},... | collective-permute-start | bytes 53768 | tf_op jit(solution)/shard_map/ppermute | solution.py:27
  11.7 4.7 %collective-permute-start.3 = (f32[1,4480]{1,0:T(1,128)S(1)}, f32[1,4480]{1,0:T(1,128)S(1)}, u32[]{:S(2)}, u32[]{:S(2)}) collective-permute-start(f32[1,4480]{1,0:T(1,128)S(1)} %add_add_fusion.refs_0_), channel_id=1, source_target_pairs={{0,4},{1,5},{2,6},{3,7},{4,0},{5,1},{6,2},{7,3},{8,12},{9,13},{10,... | collective-permute-start | bytes 53768 | tf_op jit(solution)/shard_map/ppermute | solution.py:27
  13.8 2.5 %copy-start.3 = (f32[1,4480]{1,0:T(1,128)}, f32[1,4480]{1,0:T(1,128)S(1)}, u32[]{:S(2)}) copy-start(f32[1,4480]{1,0:T(1,128)S(1)} %collective-permute-done.5.refs_3_) | copy-start | bytes 53764
  16.3 0.6 copy-start.4
  16.9 0.6 copy-start.5
  23.7 1.6 %collective-permute-start.6 = (f32[32,2048]{1,0:T(8,128)S(1)}, f32[32,2048]{1,0:T(8,128)S(1)}, u32[]{:S(2)}, u32[]{:S(2)}) collective-permute-start(f32[32,2048]{1,0:T(8,128)S(1)} %get-tuple-element.16), channel_id=1, source_target_pairs={{0,1},{1,0},{2,3},{3,2},{4,5},{5,4},{6,7},{7,6},{8,9},{9,8},{10,11... | collective-permute-start | bytes 786440 | tf_op jit(solution)/shard_map/ppermute | solution.py:22
  26.1 1.1 %copy-start.6 = (s32[8]{0:T(128)S(1)}, s32[8]{0:T(128)}, u32[]{:S(2)}) copy-start(s32[8]{0:T(128)} %param.5) | copy-start | bytes 100
  26.4 7.7 %collective-permute-start.8 = (f32[32,1792]{1,0:T(8,128)S(1)}, f32[32,1792]{1,0:T(8,128)S(1)}, u32[]{:S(2)}, u32[]{:S(2)}) collective-permute-start(f32[32,1792]{1,0:T(8,128)S(1)} %fusion.2), channel_id=1, source_target_pairs={{0,2},{1,3},{2,0},{3,1},{4,6},{5,7},{6,4},{7,5},{8,10},{9,11},{10,... | collective-permute-start | bytes 688136 | tf_op jit(solution)/shard_map/ppermute | solution.py:22
  27.2 1.4 %collective-permute-start.7 = (f32[32,1152]{1,0:T(8,128)S(1)}, f32[32,1152]{1,0:T(8,128)S(1)}, u32[]{:S(2)}, u32[]{:S(2)}) collective-permute-start(f32[32,1152]{1,0:T(8,128)S(1)} %get-tuple-element.17), channel_id=1, source_target_pairs={{0,1},{1,0},{2,3},{3,2},{4,5},{5,4},{6,7},{7,6},{8,9},{9,8},{10,11... | collective-permute-start | bytes 442376 | tf_op jit(solution)/shard_map/ppermute | solution.py:22
  35.1 6.2 %collective-permute-start.10 = (f32[32,1536]{1,0:T(8,128)S(1)}, f32[32,1536]{1,0:T(8,128)S(1)}, u32[]{:S(2)}, u32[]{:S(2)}) collective-permute-start(f32[32,1536]{1,0:T(8,128)S(1)} %fusion.3), channel_id=1, source_target_pairs={{0,4},{1,5},{2,6},{3,7},{4,0},{5,1},{6,2},{7,3},{8,12},{9,13},{10,... | collective-permute-start | bytes 589832 | tf_op jit(solution)/shard_map/ppermute | solution.py:22
  36.1 5.2 %collective-permute-start.9 = (f32[32,1152]{1,0:T(8,128)S(1)}, f32[32,1152]{1,0:T(8,128)S(1)}, u32[]{:S(2)}, u32[]{:S(2)}) collective-permute-start(f32[32,1152]{1,0:T(8,128)S(1)} %fusion.16), channel_id=1, source_target_pairs={{0,2},{1,3},{2,0},{3,1},{4,6},{5,7},{6,4},{7,5},{8,10},{9,11},{10,... | collective-permute-start | bytes 442376 | tf_op jit(solution)/shard_map/ppermute | solution.py:22
  42.3 9.0 %collective-permute-start.12 = (f32[32,1280]{1,0:T(8,128)S(1)}, f32[32,1280]{1,0:T(8,128)S(1)}, u32[]{:S(2)}, u32[]{:S(2)}) collective-permute-start(f32[32,1280]{1,0:T(8,128)S(1)} %fusion.12), channel_id=1, source_target_pairs={{0,8},{1,9},{2,10},{3,11},{4,12},{5,13},{6,14},{7,15},{8,0},{9,1},... | collective-permute-start | bytes 491528 | tf_op jit(solution)/shard_map/ppermute | solution.py:22
  44.8 5.8 %collective-permute-start.11 = (f32[32,1152]{1,0:T(8,128)S(1)}, f32[32,1152]{1,0:T(8,128)S(1)}, u32[]{:S(2)}, u32[]{:S(2)}) collective-permute-start(f32[32,1152]{1,0:T(8,128)S(1)} %fusion.15), channel_id=1, source_target_pairs={{0,4},{1,5},{2,6},{3,7},{4,0},{5,1},{6,2},{7,3},{8,12},{9,13},{10,... | collective-permute-start | bytes 442376 | tf_op jit(solution)/shard_map/ppermute | solution.py:22
  53.2 7.7 %collective-permute-start.13 = (f32[32,1152]{1,0:T(8,128)S(1)}, f32[32,1152]{1,0:T(8,128)S(1)}, u32[]{:S(2)}, u32[]{:S(2)}) collective-permute-start(f32[32,1152]{1,0:T(8,128)S(1)} %fusion.14), channel_id=1, source_target_pairs={{0,8},{1,9},{2,10},{3,11},{4,12},{5,13},{6,14},{7,15},{8,0},{9,1},... | collective-permute-start | bytes 442376 | tf_op jit(solution)/shard_map/ppermute | solution.py:22
  63.1 11.5 %copy-start = (f32[32,2048]{1,0:T(8,128)}, f32[32,2048]{1,0:T(8,128)S(1)}, u32[]{:S(2)}) copy-start(f32[32,2048]{1,0:T(8,128)S(1)} %reshape.485) | copy-start | bytes 786436
  63.1 3.1 %collective-permute-start.16 = (f32[2048]{0:T(1024)S(1)}, f32[2048]{0:T(1024)S(1)}, u32[]{:S(2)}, u32[]{:S(2)}) collective-permute-start(f32[2048]{0:T(1024)S(1)} %reduce_max.19), channel_id=1, source_target_pairs={{0,3},{1,2},{2,1},{3,0},{4,7},{5,6},{6,5},{7,4},{8,11},{9,10},{10,... | collective-permute-start | bytes 24584 | tf_op jit(solution)/shard_map/ppermute | solution.py:27
  63.2 3.7 %collective-permute-start.15 = (f32[2048]{0:T(1024)S(1)}, f32[2048]{0:T(1024)S(1)}, u32[]{:S(2)}, u32[]{:S(2)}) collective-permute-start(f32[2048]{0:T(1024)S(1)} %reduce_max.19), channel_id=1, source_target_pairs={{0,2},{1,3},{2,0},{3,1},{4,6},{5,7},{6,4},{7,5},{8,10},{9,11},{10,... | collective-permute-start | bytes 24584 | tf_op jit(solution)/shard_map/ppermute | solution.py:27
  64.0 2.9 %collective-permute-start.14 = (f32[2048]{0:T(1024)S(1)}, f32[2048]{0:T(1024)S(1)}, u32[]{:S(2)}, u32[]{:S(2)}) collective-permute-start(f32[2048]{0:T(1024)S(1)} %reduce_max.19), channel_id=1, source_target_pairs={{0,1},{1,0},{2,3},{3,2},{4,5},{5,4},{6,7},{7,6},{8,9},{9,8},{10,11... | collective-permute-start | bytes 24584 | tf_op jit(solution)/shard_map/ppermute | solution.py:27
  66.9 5.5 %collective-permute-start.19 = (f32[2048]{0:T(1024)S(1)}, f32[2048]{0:T(1024)S(1)}, u32[]{:S(2)}, u32[]{:S(2)}) collective-permute-start(f32[2048]{0:T(1024)S(1)} %maximum_maximum_fusion.1), channel_id=1, source_target_pairs={{0,12},{1,13},{2,14},{3,15},{4,8},{5,9},{6,10},{7,11},{8,4},{9,5},... | collective-permute-start | bytes 24584 | tf_op jit(solution)/shard_map/ppermute | solution.py:27
  69.4 4.5 %collective-permute-start.18 = (f32[2048]{0:T(1024)S(1)}, f32[2048]{0:T(1024)S(1)}, u32[]{:S(2)}, u32[]{:S(2)}) collective-permute-start(f32[2048]{0:T(1024)S(1)} %maximum_maximum_fusion.1), channel_id=1, source_target_pairs={{0,8},{1,9},{2,10},{3,11},{4,12},{5,13},{6,14},{7,15},{8,0},{9,1},... | collective-permute-start | bytes 24584 | tf_op jit(solution)/shard_map/ppermute | solution.py:27
  69.4 4.5 %collective-permute-start.17 = (f32[2048]{0:T(1024)S(1)}, f32[2048]{0:T(1024)S(1)}, u32[]{:S(2)}, u32[]{:S(2)}) collective-permute-start(f32[2048]{0:T(1024)S(1)} %maximum_maximum_fusion.1), channel_id=1, source_target_pairs={{0,4},{1,5},{2,6},{3,7},{4,0},{5,1},{6,2},{7,3},{8,12},{9,13},{10,... | collective-permute-start | bytes 24584 | tf_op jit(solution)/shard_map/ppermute | solution.py:27

commit v23 on v14

--- a/solution.py
+++ b/solution.py
@@ -88,8 +88,8 @@
     return pl.pallas_call(
         functools.partial(local_tree_kernel, tuple(widths_seq), float(channels_all)),
         out_shape=(
-            jax.ShapeDtypeStruct((rows, head_width), jnp.float32),
-            jax.ShapeDtypeStruct((rows, tail_width), jnp.float32),
+            pltpu.VMEM((rows, head_width), jnp.float32),
+            pltpu.VMEM((rows, tail_width), jnp.float32),
         ),
         in_specs=[vmem, vmem, vmem],
         out_specs=(vmem, vmem),

time: 76.1 us -> 74.3 us (0.976)
  other arithmetic: 11.2 us -> 10.2 us
    select_n x8, other arithmetic: 1.17 us -> 0.21 us  [halves(): jnp.where(upper_half, partner, own)]
where the time goes in v23:
time: 74.3 us; the launch traced here: 74.1 us
  waiting for transfers between devices  33.8 us (45%)
  starting transfers between devices  21.4 us (29%)
  other arithmetic  10.2 us (14%)
  Pallas kernels  6.08 us (8%)
  between operations  1.27 us (2%)
  matrix products  1.03 us (1%)
    ppermute x8, waiting for transfers between devices, from_partner(): return lax.ppermute(value, axis, pairs)  22.6 us
    ppermute x12, starting transfers between devices, from_xor(): return lax.ppermute(value, axis, pairs)  14 us
    ppermute x12, waiting for transfers between devices, from_xor(): return lax.ppermute(value, axis, pairs)  11.2 us
    ppermute x8, starting transfers between devices, from_partner(): return lax.ppermute(value, axis, pairs)  7.37 us
    select_n x56, other arithmetic, shift_rows(): jnp.where(chosen, current[:, span:span + keep_len], current[:, :keep_len])  6.19 us
    pallas_call x1, Pallas kernels, local_tree(): pl.pallas_call(functools.partial(local_tree_kernel, tuple(widths_seq), fl...  6.08 us
  transfers between devices with their start and end apart: 20, of which 14 were waited for; matrix products, arithmetic and copies ran while one was open for 3% of the time, Pallas kernels for 0%

profile of v23, /device:TPU:0, one launch (start us, length us, event | category | flops | bytes accessed | tf_op | source)
XLA Modules:
  0.0 74.1 jit_solution(4001695329060133360)
XLA Ops:
  0.6 1.1 %slice_reduce_fusion = f32[4480]{0:T(1024)S(1)} fusion(f32[32,6144]{1,0:T(8,128)} %x_ref.1), kind=kLoop, calls=%fused_computation.4 | loop fusion | flops 138880 | bytes 591360 | tf_op jit(solution)/shard_map/reduce_sum | solution.py:158
  1.8 3.0 %collective-permute-start.1 = (f32[1,4480]{1,0:T(1,128)S(1)}, f32[1,4480]{1,0:T(1,128)S(1)}, u32[]{:S(2)}, u32[]{:S(2)}) collective-permute-start(f32[1,4480]{1,0:T(1,128)S(1)} %broadcast_in_dim.527), channel_id=1, source_target_pairs={{0,2},{1,3},{2,0},{3,1},{4,6},{5,7},{6,4},{7,5},{8,10},{9,11},{10,... | collective-permute-start | bytes 53768 | tf_op jit(solution)/shard_map/ppermute | solution.py:27
  5.0 1.5 %collective-permute-done.1 = f32[1,4480]{1,0:T(1,128)S(1)} collective-permute-done((f32[1,4480]{1,0:T(1,128)S(1)}, f32[1,4480]{1,0:T(1,128)S(1)}, u32[]{:S(2)}, u32[]{:S(2)}) %collective-permute-start.1) | collective-permute-done | bytes 17952 | tf_op jit(solution)/shard_map/ppermute | solution.py:27
  6.5 1.4 %collective-permute-done.2 = f32[1,4480]{1,0:T(1,128)S(1)} collective-permute-done((f32[1,4480]{1,0:T(1,128)S(1)}, f32[1,4480]{1,0:T(1,128)S(1)}, u32[]{:S(2)}, u32[]{:S(2)}) %collective-permute-start.2) | collective-permute-done | bytes 17952 | tf_op jit(solution)/shard_map/ppermute | solution.py:27
  8.0 3.7 %collective-permute-start.5 = (f32[1,4480]{1,0:T(1,128)S(1)}, f32[1,4480]{1,0:T(1,128)S(1)}, u32[]{:S(2)}, u32[]{:S(2)}) collective-permute-start(f32[1,4480]{1,0:T(1,128)S(1)} %add_add_fusion.1), channel_id=1, source_target_pairs={{0,12},{1,13},{2,14},{3,15},{4,8},{5,9},{6,10},{7,11},{8,4},{9,5},... | collective-permute-start | bytes 53768 | tf_op jit(solution)/shard_map/ppermute | solution.py:27
  11.7 0.8 %collective-permute-start.3 = (f32[1,4480]{1,0:T(1,128)S(1)}, f32[1,4480]{1,0:T(1,128)S(1)}, u32[]{:S(2)}, u32[]{:S(2)}) collective-permute-start(f32[1,4480]{1,0:T(1,128)S(1)} %add_add_fusion.1), channel_id=1, source_target_pairs={{0,4},{1,5},{2,6},{3,7},{4,0},{5,1},{6,2},{7,3},{8,12},{9,13},{10,... | collective-permute-start | bytes 53768 | tf_op jit(solution)/shard_map/ppermute | solution.py:27
  12.5 1.4 %collective-permute-done.5 = f32[1,4480]{1,0:T(1,128)S(1)} collective-permute-done((f32[1,4480]{1,0:T(1,128)S(1)}, f32[1,4480]{1,0:T(1,128)S(1)}, u32[]{:S(2)}, u32[]{:S(2)}) %collective-permute-start.5) | collective-permute-done | bytes 17952 | tf_op jit(solution)/shard_map/ppermute | solution.py:27
  13.8 2.5 %collective-permute-done.4 = f32[1,4480]{1,0:T(1,128)S(1)} collective-permute-done((f32[1,4480]{1,0:T(1,128)S(1)}, f32[1,4480]{1,0:T(1,128)S(1)}, u32[]{:S(2)}, u32[]{:S(2)}) %collective-permute-start.4) | collective-permute-done | bytes 17952 | tf_op jit(solution)/shard_map/ppermute | solution.py:27
  16.3 0.6 add_add_fusion.total_ref
  17.0 6.1 %shard_map.50 = (f32[32,2048]{1,0:T(8,128)S(1)}, f32[32,1152]{1,0:T(8,128)S(1)}) custom-call(f32[32,6144]{1,0:T(8,128)} %x_ref.1, f32[1,4480]{1,0:T(1,128)} %add_add_fusion.total_ref, s32[9,32]{1,0:T(8,128)} %offsets_ref.1), custom_call_target="tpu_custom_call" | custom-call | flops 25395200 | bytes 983040 | tf_op jit(solution)/shard_map/pallas_call | solution.py:88
  23.2 1.4 %collective-permute-done.6 = f32[32,2048]{1,0:T(8,128)S(1)} collective-permute-done((f32[32,2048]{1,0:T(8,128)S(1)}, f32[32,2048]{1,0:T(8,128)S(1)}, u32[]{:S(2)}, u32[]{:S(2)}) %collective-permute-start.6) | collective-permute-done | bytes 262176 | tf_op jit(solution)/shard_map/ppermute | solution.py:22
  25.8 0.8 %collective-permute-start.8 = (f32[32,1792]{1,0:T(8,128)S(1)}, f32[32,1792]{1,0:T(8,128)S(1)}, u32[]{:S(2)}, u32[]{:S(2)}) collective-permute-start(f32[32,1792]{1,0:T(8,128)S(1)} %fusion.2), channel_id=1, source_target_pairs={{0,2},{1,3},{2,0},{3,1},{4,6},{5,7},{6,4},{7,5},{8,10},{9,11},{10,... | collective-permute-start | bytes 688136 | tf_op jit(solution)/shard_map/ppermute | solution.py:22
  26.7 1.3 %collective-permute-done.7 = f32[32,1152]{1,0:T(8,128)S(1)} collective-permute-done((f32[32,1152]{1,0:T(8,128)S(1)}, f32[32,1152]{1,0:T(8,128)S(1)}, u32[]{:S(2)}, u32[]{:S(2)}) %collective-permute-start.7) | collective-permute-done | bytes 147488 | tf_op jit(solution)/shard_map/ppermute | solution.py:22
  27.9 5.5 %collective-permute-done.8 = f32[32,1792]{1,0:T(8,128)S(1)} collective-permute-done((f32[32,1792]{1,0:T(8,128)S(1)}, f32[32,1792]{1,0:T(8,128)S(1)}, u32[]{:S(2)}, u32[]{:S(2)}) %collective-permute-start.8) | collective-permute-done | bytes 229408 | tf_op jit(solution)/shard_map/ppermute | solution.py:22
  35.5 0.8 %collective-permute-start.9 = (f32[32,1152]{1,0:T(8,128)S(1)}, f32[32,1152]{1,0:T(8,128)S(1)}, u32[]{:S(2)}, u32[]{:S(2)}) collective-permute-start(f32[32,1152]{1,0:T(8,128)S(1)} %fusion.16), channel_id=1, source_target_pairs={{0,2},{1,3},{2,0},{3,1},{4,6},{5,7},{6,4},{7,5},{8,10},{9,11},{10,... | collective-permute-start | bytes 442376 | tf_op jit(solution)/shard_map/ppermute | solution.py:22
  36.3 4.4 %collective-permute-done.9 = f32[32,1152]{1,0:T(8,128)S(1)} collective-permute-done((f32[32,1152]{1,0:T(8,128)S(1)}, f32[32,1152]{1,0:T(8,128)S(1)}, u32[]{:S(2)}, u32[]{:S(2)}) %collective-permute-start.9) | collective-permute-done | bytes 147488 | tf_op jit(solution)/shard_map/ppermute | solution.py:22
  41.7 2.1 %collective-permute-start.12 = (f32[32,1280]{1,0:T(8,128)S(1)}, f32[32,1280]{1,0:T(8,128)S(1)}, u32[]{:S(2)}, u32[]{:S(2)}) collective-permute-start(f32[32,1280]{1,0:T(8,128)S(1)} %fusion.12), channel_id=1, source_target_pairs={{0,8},{1,9},{2,10},{3,11},{4,12},{5,13},{6,14},{7,15},{8,0},{9,1},... | collective-permute-start | bytes 491528 | tf_op jit(solution)/shard_map/ppermute | solution.py:22
  44.7 2.1 %collective-permute-start.11 = (f32[32,1152]{1,0:T(8,128)S(1)}, f32[32,1152]{1,0:T(8,128)S(1)}, u32[]{:S(2)}, u32[]{:S(2)}) collective-permute-start(f32[32,1152]{1,0:T(8,128)S(1)} %fusion.15), channel_id=1, source_target_pairs={{0,4},{1,5},{2,6},{3,7},{4,0},{5,1},{6,2},{7,3},{8,12},{9,13},{10,... | collective-permute-start | bytes 442376 | tf_op jit(solution)/shard_map/ppermute | solution.py:22
  46.9 4.1 %collective-permute-done.11 = f32[32,1152]{1,0:T(8,128)S(1)} collective-permute-done((f32[32,1152]{1,0:T(8,128)S(1)}, f32[32,1152]{1,0:T(8,128)S(1)}, u32[]{:S(2)}, u32[]{:S(2)}) %collective-permute-start.11) | collective-permute-done | bytes 147488 | tf_op jit(solution)/shard_map/ppermute | solution.py:22
  52.8 1.5 %collective-permute-start.13 = (f32[32,1152]{1,0:T(8,128)S(1)}, f32[32,1152]{1,0:T(8,128)S(1)}, u32[]{:S(2)}, u32[]{:S(2)}) collective-permute-start(f32[32,1152]{1,0:T(8,128)S(1)} %fusion.14), channel_id=1, source_target_pairs={{0,8},{1,9},{2,10},{3,11},{4,12},{5,13},{6,14},{7,15},{8,0},{9,1},... | collective-permute-start | bytes 442376 | tf_op jit(solution)/shard_map/ppermute | solution.py:22
  54.3 0.3 fusion.1
  54.7 5.8 %collective-permute-done.13 = f32[32,1152]{1,0:T(8,128)S(1)} collective-permute-done((f32[32,1152]{1,0:T(8,128)S(1)}, f32[32,1152]{1,0:T(8,128)S(1)}, u32[]{:S(2)}, u32[]{:S(2)}) %collective-permute-start.13) | collective-permute-done | bytes 147488 | tf_op jit(solution)/shard_map/ppermute | solution.py:22
  61.6 1.0 %convolution_reduce_fusion = f32[512,128]{1,0:T(8,128)S(1)} fusion(f32[512,256,1]{1,0,2:T(8,128)S(1)} %bitcast.85, f32[8,128,256]{2,1,0:T(8,128)S(1)} %bitcast.84), kind=kOutput, calls=%fused_computation | convolution fusion | flops 805765120 | bytes 1835008 | tf_op jit(solution)/shard_map/dot_general | solution.py:137
  62.8 0.8 %collective-permute-start.15 = (f32[2048]{0:T(1024)S(1)}, f32[2048]{0:T(1024)S(1)}, u32[]{:S(2)}, u32[]{:S(2)}) collective-permute-start(f32[2048]{0:T(1024)S(1)} %reduce_max.19), channel_id=1, source_target_pairs={{0,2},{1,3},{2,0},{3,1},{4,6},{5,7},{6,4},{7,5},{8,10},{9,11},{10,... | collective-permute-start | bytes 24584 | tf_op jit(solution)/shard_map/ppermute | solution.py:27
  63.6 1.1 %collective-permute-start.14 = (f32[2048]{0:T(1024)S(1)}, f32[2048]{0:T(1024)S(1)}, u32[]{:S(2)}, u32[]{:S(2)}) collective-permute-start(f32[2048]{0:T(1024)S(1)} %reduce_max.19), channel_id=1, source_target_pairs={{0,1},{1,0},{2,3},{3,2},{4,5},{5,4},{6,7},{7,6},{8,9},{9,8},{10,11... | collective-permute-start | bytes 24584 | tf_op jit(solution)/shard_map/ppermute | solution.py:27
  64.7 1.2 %collective-permute-done.16 = f32[2048]{0:T(1024)S(1)} collective-permute-done((f32[2048]{0:T(1024)S(1)}, f32[2048]{0:T(1024)S(1)}, u32[]{:S(2)}, u32[]{:S(2)}) %collective-permute-start.16) | collective-permute-done | bytes 8224 | tf_op jit(solution)/shard_map/ppermute | solution.py:27
  65.9 0.7 collective-permute-done.15
  66.6 2.4 %collective-permute-start.19 = (f32[2048]{0:T(1024)S(1)}, f32[2048]{0:T(1024)S(1)}, u32[]{:S(2)}, u32[]{:S(2)}) collective-permute-start(f32[2048]{0:T(1024)S(1)} %maximum_maximum_fusion.1), channel_id=1, source_target_pairs={{0,12},{1,13},{2,14},{3,15},{4,8},{5,9},{6,10},{7,11},{8,4},{9,5},... | collective-permute-start | bytes 24584 | tf_op jit(solution)/shard_map/ppermute | solution.py:27
  68.9 2.1 %collective-permute-start.17 = (f32[2048]{0:T(1024)S(1)}, f32[2048]{0:T(1024)S(1)}, u32[]{:S(2)}, u32[]{:S(2)}) collective-permute-start(f32[2048]{0:T(1024)S(1)} %maximum_maximum_fusion.1), channel_id=1, source_target_pairs={{0,4},{1,5},{2,6},{3,7},{4,0},{5,1},{6,2},{7,3},{8,12},{9,13},{10,... | collective-permute-start | bytes 24584 | tf_op jit(solution)/shard_map/ppermute | solution.py:27
  71.0 1.1 %collective-permute-done.19 = f32[2048]{0:T(1024)S(1)} collective-permute-done((f32[2048]{0:T(1024)S(1)}, f32[2048]{0:T(1024)S(1)}, u32[]{:S(2)}, u32[]{:S(2)}) %collective-permute-start.19) | collective-permute-done | bytes 8224 | tf_op jit(solution)/shard_map/ppermute | solution.py:27
  72.1 1.4 %collective-permute-done.18 = f32[2048]{0:T(1024)S(1)} collective-permute-done((f32[2048]{0:T(1024)S(1)}, f32[2048]{0:T(1024)S(1)}, u32[]{:S(2)}, u32[]{:S(2)}) %collective-permute-start.18) | collective-permute-done | bytes 8224 | tf_op jit(solution)/shard_map/ppermute | solution.py:27
  73.5 0.6 maximum_maximum_fusion
  (116 shorter events, 8.3 us)
Async XLA Ops:
  0.6 22.5 %copy-start.1 = (s32[9,32]{1,0:T(8,128)S(1)}, s32[9,32]{1,0:T(8,128)}, u32[]{:S(2)}) copy-start(s32[9,32]{1,0:T(8,128)} %offsets_ref.1) | copy-start | bytes 3460
  1.8 4.7 %collective-permute-start.1 = (f32[1,4480]{1,0:T(1,128)S(1)}, f32[1,4480]{1,0:T(1,128)S(1)}, u32[]{:S(2)}, u32[]{:S(2)}) collective-permute-start(f32[1,4480]{1,0:T(1,128)S(1)} %broadcast_in_dim.527), channel_id=1, source_target_pairs={{0,2},{1,3},{2,0},{3,1},{4,6},{5,7},{6,4},{7,5},{8,10},{9,11},{10,... | collective-permute-start | bytes 53768 | tf_op jit(solution)/shard_map/ppermute | solution.py:27
  4.8 3.2 %collective-permute-start.2 = (f32[1,4480]{1,0:T(1,128)S(1)}, f32[1,4480]{1,0:T(1,128)S(1)}, u32[]{:S(2)}, u32[]{:S(2)}) collective-permute-start(f32[1,4480]{1,0:T(1,128)S(1)} %broadcast_in_dim.527), channel_id=1, source_target_pairs={{0,3},{1,2},{2,1},{3,0},{4,7},{5,6},{6,5},{7,4},{8,11},{9,10},{10,... | collective-permute-start | bytes 53768 | tf_op jit(solution)/shard_map/ppermute | solution.py:27
  4.8 3.2 %collective-permute-start = (f32[1,4480]{1,0:T(1,128)S(1)}, f32[1,4480]{1,0:T(1,128)S(1)}, u32[]{:S(2)}, u32[]{:S(2)}) collective-permute-start(f32[1,4480]{1,0:T(1,128)S(1)} %broadcast_in_dim.527), channel_id=1, source_target_pairs={{0,1},{1,0},{2,3},{3,2},{4,5},{5,4},{6,7},{7,6},{8,9},{9,8},{10,11... | collective-permute-start | bytes 53768 | tf_op jit(solution)/shard_map/ppermute | solution.py:27
  8.0 5.8 %collective-permute-start.5 = (f32[1,4480]{1,0:T(1,128)S(1)}, f32[1,4480]{1,0:T(1,128)S(1)}, u32[]{:S(2)}, u32[]{:S(2)}) collective-permute-start(f32[1,4480]{1,0:T(1,128)S(1)} %add_add_fusion.1), channel_id=1, source_target_pairs={{0,12},{1,13},{2,14},{3,15},{4,8},{5,9},{6,10},{7,11},{8,4},{9,5},... | collective-permute-start | bytes 53768 | tf_op jit(solution)/shard_map/ppermute | solution.py:27
  11.7 4.7 %collective-permute-start.4 = (f32[1,4480]{1,0:T(1,128)S(1)}, f32[1,4480]{1,0:T(1,128)S(1)}, u32[]{:S(2)}, u32[]{:S(2)}) collective-permute-start(f32[1,4480]{1,0:T(1,128)S(1)} %add_add_fusion.1), channel_id=1, source_target_pairs={{0,8},{1,9},{2,10},{3,11},{4,12},{5,13},{6,14},{7,15},{8,0},{9,1},... | collective-permute-start | bytes 53768 | tf_op jit(solution)/shard_map/ppermute | solution.py:27
  11.7 4.7 %collective-permute-start.3 = (f32[1,4480]{1,0:T(1,128)S(1)}, f32[1,4480]{1,0:T(1,128)S(1)}, u32[]{:S(2)}, u32[]{:S(2)}) collective-permute-start(f32[1,4480]{1,0:T(1,128)S(1)} %add_add_fusion.1), channel_id=1, source_target_pairs={{0,4},{1,5},{2,6},{3,7},{4,0},{5,1},{6,2},{7,3},{8,12},{9,13},{10,... | collective-permute-start | bytes 53768 | tf_op jit(solution)/shard_map/ppermute | solution.py:27
  23.1 1.6 %collective-permute-start.6 = (f32[32,2048]{1,0:T(8,128)S(1)}, f32[32,2048]{1,0:T(8,128)S(1)}, u32[]{:S(2)}, u32[]{:S(2)}) collective-permute-start(f32[32,2048]{1,0:T(8,128)S(1)} %get-tuple-element.16), channel_id=1, source_target_pairs={{0,1},{1,0},{2,3},{3,2},{4,5},{5,4},{6,7},{7,6},{8,9},{9,8},{10,11... | collective-permute-start | bytes 786440 | tf_op jit(solution)/shard_map/ppermute | solution.py:22
  25.5 1.1 %copy-start.2 = (s32[8]{0:T(128)S(1)}, s32[8]{0:T(128)}, u32[]{:S(2)}) copy-start(s32[8]{0:T(128)} %param.5) | copy-start | bytes 100
  25.8 7.7 %collective-permute-start.8 = (f32[32,1792]{1,0:T(8,128)S(1)}, f32[32,1792]{1,0:T(8,128)S(1)}, u32[]{:S(2)}, u32[]{:S(2)}) collective-permute-start(f32[32,1792]{1,0:T(8,128)S(1)} %fusion.2), channel_id=1, source_target_pairs={{0,2},{1,3},{2,0},{3,1},{4,6},{5,7},{6,4},{7,5},{8,10},{9,11},{10,... | collective-permute-start | bytes 688136 | tf_op jit(solution)/shard_map/ppermute | solution.py:22
  26.6 1.4 %collective-permute-start.7 = (f32[32,1152]{1,0:T(8,128)S(1)}, f32[32,1152]{1,0:T(8,128)S(1)}, u32[]{:S(2)}, u32[]{:S(2)}) collective-permute-start(f32[32,1152]{1,0:T(8,128)S(1)} %get-tuple-element.17), channel_id=1, source_target_pairs={{0,1},{1,0},{2,3},{3,2},{4,5},{5,4},{6,7},{7,6},{8,9},{9,8},{10,11... | collective-permute-start | bytes 442376 | tf_op jit(solution)/shard_map/ppermute | solution.py:22
  34.5 6.2 %collective-permute-start.10 = (f32[32,1536]{1,0:T(8,128)S(1)}, f32[32,1536]{1,0:T(8,128)S(1)}, u32[]{:S(2)}, u32[]{:S(2)}) collective-permute-start(f32[32,1536]{1,0:T(8,128)S(1)} %fusion.3), channel_id=1, source_target_pairs={{0,4},{1,5},{2,6},{3,7},{4,0},{5,1},{6,2},{7,3},{8,12},{9,13},{10,... | collective-permute-start | bytes 589832 | tf_op jit(solution)/shard_map/ppermute | solution.py:22
  35.5 5.2 %collective-permute-start.9 = (f32[32,1152]{1,0:T(8,128)S(1)}, f32[32,1152]{1,0:T(8,128)S(1)}, u32[]{:S(2)}, u32[]{:S(2)}) collective-permute-start(f32[32,1152]{1,0:T(8,128)S(1)} %fusion.16), channel_id=1, source_target_pairs={{0,2},{1,3},{2,0},{3,1},{4,6},{5,7},{6,4},{7,5},{8,10},{9,11},{10,... | collective-permute-start | bytes 442376 | tf_op jit(solution)/shard_map/ppermute | solution.py:22
  41.7 9.3 %collective-permute-start.12 = (f32[32,1280]{1,0:T(8,128)S(1)}, f32[32,1280]{1,0:T(8,128)S(1)}, u32[]{:S(2)}, u32[]{:S(2)}) collective-permute-start(f32[32,1280]{1,0:T(8,128)S(1)} %fusion.12), channel_id=1, source_target_pairs={{0,8},{1,9},{2,10},{3,11},{4,12},{5,13},{6,14},{7,15},{8,0},{9,1},... | collective-permute-start | bytes 491528 | tf_op jit(solution)/shard_map/ppermute | solution.py:22
  44.7 6.2 %collective-permute-start.11 = (f32[32,1152]{1,0:T(8,128)S(1)}, f32[32,1152]{1,0:T(8,128)S(1)}, u32[]{:S(2)}, u32[]{:S(2)}) collective-permute-start(f32[32,1152]{1,0:T(8,128)S(1)} %fusion.15), channel_id=1, source_target_pairs={{0,4},{1,5},{2,6},{3,7},{4,0},{5,1},{6,2},{7,3},{8,12},{9,13},{10,... | collective-permute-start | bytes 442376 | tf_op jit(solution)/shard_map/ppermute | solution.py:22
  52.8 7.7 %collective-permute-start.13 = (f32[32,1152]{1,0:T(8,128)S(1)}, f32[32,1152]{1,0:T(8,128)S(1)}, u32[]{:S(2)}, u32[]{:S(2)}) collective-permute-start(f32[32,1152]{1,0:T(8,128)S(1)} %fusion.14), channel_id=1, source_target_pairs={{0,8},{1,9},{2,10},{3,11},{4,12},{5,13},{6,14},{7,15},{8,0},{9,1},... | collective-permute-start | bytes 442376 | tf_op jit(solution)/shard_map/ppermute | solution.py:22
  62.7 11.4 %copy-start = (f32[32,2048]{1,0:T(8,128)}, f32[32,2048]{1,0:T(8,128)S(1)}, u32[]{:S(2)}) copy-start(f32[32,2048]{1,0:T(8,128)S(1)} %reshape.485) | copy-start | bytes 786436
  62.7 3.1 %collective-permute-start.16 = (f32[2048]{0:T(1024)S(1)}, f32[2048]{0:T(1024)S(1)}, u32[]{:S(2)}, u32[]{:S(2)}) collective-permute-start(f32[2048]{0:T(1024)S(1)} %reduce_max.19), channel_id=1, source_target_pairs={{0,3},{1,2},{2,1},{3,0},{4,7},{5,6},{6,5},{7,4},{8,11},{9,10},{10,... | collective-permute-start | bytes 24584 | tf_op jit(solution)/shard_map/ppermute | solution.py:27
  62.8 3.7 %collective-permute-start.15 = (f32[2048]{0:T(1024)S(1)}, f32[2048]{0:T(1024)S(1)}, u32[]{:S(2)}, u32[]{:S(2)}) collective-permute-start(f32[2048]{0:T(1024)S(1)} %reduce_max.19), channel_id=1, source_target_pairs={{0,2},{1,3},{2,0},{3,1},{4,6},{5,7},{6,4},{7,5},{8,10},{9,11},{10,... | collective-permute-start | bytes 24584 | tf_op jit(solution)/shard_map/ppermute | solution.py:27
  63.6 2.9 %collective-permute-start.14 = (f32[2048]{0:T(1024)S(1)}, f32[2048]{0:T(1024)S(1)}, u32[]{:S(2)}, u32[]{:S(2)}) collective-permute-start(f32[2048]{0:T(1024)S(1)} %reduce_max.19), channel_id=1, source_target_pairs={{0,1},{1,0},{2,3},{3,2},{4,5},{5,4},{6,7},{7,6},{8,9},{9,8},{10,11... | collective-permute-start | bytes 24584 | tf_op jit(solution)/shard_map/ppermute | solution.py:27
  66.6 5.5 %collective-permute-start.19 = (f32[2048]{0:T(1024)S(1)}, f32[2048]{0:T(1024)S(1)}, u32[]{:S(2)}, u32[]{:S(2)}) collective-permute-start(f32[2048]{0:T(1024)S(1)} %maximum_maximum_fusion.1), channel_id=1, source_target_pairs={{0,12},{1,13},{2,14},{3,15},{4,8},{5,9},{6,10},{7,11},{8,4},{9,5},... | collective-permute-start | bytes 24584 | tf_op jit(solution)/shard_map/ppermute | solution.py:27
  68.9 4.5 %collective-permute-start.18 = (f32[2048]{0:T(1024)S(1)}, f32[2048]{0:T(1024)S(1)}, u32[]{:S(2)}, u32[]{:S(2)}) collective-permute-start(f32[2048]{0:T(1024)S(1)} %maximum_maximum_fusion.1), channel_id=1, source_target_pairs={{0,8},{1,9},{2,10},{3,11},{4,12},{5,13},{6,14},{7,15},{8,0},{9,1},... | collective-permute-start | bytes 24584 | tf_op jit(solution)/shard_map/ppermute | solution.py:27
  68.9 4.5 %collective-permute-start.17 = (f32[2048]{0:T(1024)S(1)}, f32[2048]{0:T(1024)S(1)}, u32[]{:S(2)}, u32[]{:S(2)}) collective-permute-start(f32[2048]{0:T(1024)S(1)} %maximum_maximum_fusion.1), channel_id=1, source_target_pairs={{0,4},{1,5},{2,6},{3,7},{4,0},{5,1},{6,2},{7,3},{8,12},{9,13},{10,... | collective-permute-start | bytes 24584 | tf_op jit(solution)/shard_map/ppermute | solution.py:27

commit v24 on v23

--- a/solution.py
+++ b/solution.py
@@ -99,6 +99,24 @@
     )(filterbank, channel_total, offsets)
 
 
+def channel_sum_kernel(x_ref, out_ref):
+    width = out_ref.shape[1]
+    out_ref[...] = jnp.sum(x_ref[:, :width], axis=0, keepdims=True)
+
+
+def channel_sum(filterbank, width):
+    vmem = pl.BlockSpec(memory_space=pltpu.VMEM)
+    return pl.pallas_call(
+        channel_sum_kernel,
+        out_shape=pltpu.VMEM((1, width), jnp.float32),
+        in_specs=[vmem],
+        out_specs=vmem,
+        cost_estimate=pl.CostEstimate(
+            flops=filterbank.shape[0] * width, transcendentals=0, bytes_accessed=4 * filterbank.shape[0] * width
+        ),
+    )(filterbank)
+
+
 def merge_section(current, offsets_now, section_index, new_length):
     group_trials = 2**section_index
     total_rows = current.shape[0]
@@ -155,7 +173,7 @@
         needed = -(-needed // 128) * 128
         return min(TIN, needed)
 
-    partial_value = jnp.sum(filterbank[:, : length_after(0)], axis=0, keepdims=True)
+    partial_value = channel_sum(filterbank, length_after(0))
     channel_total = butterfly(partial_value, "band", jnp.add)
     widths_seq = [length_after(section) for section in range(local_count + 1)]
     head, tail = local_tree(filterbank, channel_total, offsets, widths_seq, channels_all, TAIL_WIDTH)

time: 74.3 us -> 74.3 us (level)
  Pallas kernels: 6.08 us -> 7.28 us
  other arithmetic: 10.2 us -> 9.1 us
    pallas_call x0 -> x1, Pallas kernels: none -> 1.2 us  [channel_sum(): pl.pallas_call(channel_sum_kernel, out_shape=pltpu.VMEM((1, width), jnp.f...]
    reduce_sum x1 -> x0, other arithmetic: 1.12 us -> none  [per_device(): jnp.sum(filterbank[:, :length_after(0)], axis=0, keepdims=True)]
where the time goes in v24:
time: 74.3 us; the launch traced here: 74.2 us
  waiting for transfers between devices  34.1 us (46%)
  starting transfers between devices  21.1 us (28%)
  other arithmetic  9.1 us (12%)
  Pallas kernels  7.28 us (10%)
  between operations  1.27 us (2%)
  matrix products  1.03 us (1%)
    ppermute x8, waiting for transfers between devices, from_partner(): return lax.ppermute(value, axis, pairs)  22.8 us
    ppermute x12, starting transfers between devices, from_xor(): return lax.ppermute(value, axis, pairs)  13.9 us
    ppermute x12, waiting for transfers between devices, from_xor(): return lax.ppermute(value, axis, pairs)  11.3 us
    ppermute x8, starting transfers between devices, from_partner(): return lax.ppermute(value, axis, pairs)  7.18 us
    select_n x56, other arithmetic, shift_rows(): jnp.where(chosen, current[:, span:span + keep_len], current[:, :keep_len])  6.19 us
    pallas_call x1, Pallas kernels, local_tree(): pl.pallas_call(functools.partial(local_tree_kernel, tuple(widths_seq), fl...  6.08 us
  transfers between devices with their start and end apart: 20, of which 14 were waited for; matrix products, arithmetic and copies ran while one was open for 3% of the time, Pallas kernels for 0%

profile of v24, /device:TPU:0, one launch (start us, length us, event | category | flops | bytes accessed | tf_op | source)
XLA Modules:
  0.0 74.2 jit_solution(6745229354304120684)
XLA Ops:
  0.6 1.2 %shard_map.50 = f32[1,4480]{1,0:T(1,128)S(1)} custom-call(f32[32,6144]{1,0:T(8,128)} %x_ref.3), custom_call_target="tpu_custom_call" | custom-call | flops 143360 | bytes 573440 | tf_op jit(solution)/shard_map/pallas_call | solution.py:109
  1.8 2.4 %collective-permute-start.2 = (f32[1,4480]{1,0:T(1,128)S(1)}, f32[1,4480]{1,0:T(1,128)S(1)}, u32[]{:S(2)}, u32[]{:S(2)}) collective-permute-start(f32[1,4480]{1,0:T(1,128)S(1)} %shard_map.50), channel_id=1, source_target_pairs={{0,3},{1,2},{2,1},{3,0},{4,7},{5,6},{6,5},{7,4},{8,11},{9,10},{10,... | collective-permute-start | bytes 53768 | tf_op jit(solution)/shard_map/ppermute | solution.py:27
  4.3 0.6 collective-permute-start.1
  5.0 0.8 %collective-permute-done.2 = f32[1,4480]{1,0:T(1,128)S(1)} collective-permute-done((f32[1,4480]{1,0:T(1,128)S(1)}, f32[1,4480]{1,0:T(1,128)S(1)}, u32[]{:S(2)}, u32[]{:S(2)}) %collective-permute-start.2) | collective-permute-done | bytes 17952 | tf_op jit(solution)/shard_map/ppermute | solution.py:27
  5.7 2.3 %collective-permute-done.1 = f32[1,4480]{1,0:T(1,128)S(1)} collective-permute-done((f32[1,4480]{1,0:T(1,128)S(1)}, f32[1,4480]{1,0:T(1,128)S(1)}, u32[]{:S(2)}, u32[]{:S(2)}) %collective-permute-start.1) | collective-permute-done | bytes 17952 | tf_op jit(solution)/shard_map/ppermute | solution.py:27
  8.1 3.7 %collective-permute-start.5 = (f32[1,4480]{1,0:T(1,128)S(1)}, f32[1,4480]{1,0:T(1,128)S(1)}, u32[]{:S(2)}, u32[]{:S(2)}) collective-permute-start(f32[1,4480]{1,0:T(1,128)S(1)} %add_add_fusion.1), channel_id=1, source_target_pairs={{0,12},{1,13},{2,14},{3,15},{4,8},{5,9},{6,10},{7,11},{8,4},{9,5},... | collective-permute-start | bytes 53768 | tf_op jit(solution)/shard_map/ppermute | solution.py:27
  11.8 0.8 %collective-permute-start.3 = (f32[1,4480]{1,0:T(1,128)S(1)}, f32[1,4480]{1,0:T(1,128)S(1)}, u32[]{:S(2)}, u32[]{:S(2)}) collective-permute-start(f32[1,4480]{1,0:T(1,128)S(1)} %add_add_fusion.1), channel_id=1, source_target_pairs={{0,4},{1,5},{2,6},{3,7},{4,0},{5,1},{6,2},{7,3},{8,12},{9,13},{10,... | collective-permute-start | bytes 53768 | tf_op jit(solution)/shard_map/ppermute | solution.py:27
  12.5 1.4 %collective-permute-done.5 = f32[1,4480]{1,0:T(1,128)S(1)} collective-permute-done((f32[1,4480]{1,0:T(1,128)S(1)}, f32[1,4480]{1,0:T(1,128)S(1)}, u32[]{:S(2)}, u32[]{:S(2)}) %collective-permute-start.5) | collective-permute-done | bytes 17952 | tf_op jit(solution)/shard_map/ppermute | solution.py:27
  13.9 2.5 %collective-permute-done.4 = f32[1,4480]{1,0:T(1,128)S(1)} collective-permute-done((f32[1,4480]{1,0:T(1,128)S(1)}, f32[1,4480]{1,0:T(1,128)S(1)}, u32[]{:S(2)}, u32[]{:S(2)}) %collective-permute-start.4) | collective-permute-done | bytes 17952 | tf_op jit(solution)/shard_map/ppermute | solution.py:27
  16.4 0.6 add_add_fusion.total_ref
  17.0 6.1 %shard_map.51 = (f32[32,2048]{1,0:T(8,128)S(1)}, f32[32,1152]{1,0:T(8,128)S(1)}) custom-call(f32[32,6144]{1,0:T(8,128)} %x_ref.3, f32[1,4480]{1,0:T(1,128)} %add_add_fusion.total_ref, s32[9,32]{1,0:T(8,128)} %offsets_ref.1), custom_call_target="tpu_custom_call" | custom-call | flops 25395200 | bytes 983040 | tf_op jit(solution)/shard_map/pallas_call | solution.py:88
  23.3 1.4 %collective-permute-done.6 = f32[32,2048]{1,0:T(8,128)S(1)} collective-permute-done((f32[32,2048]{1,0:T(8,128)S(1)}, f32[32,2048]{1,0:T(8,128)S(1)}, u32[]{:S(2)}, u32[]{:S(2)}) %collective-permute-start.6) | collective-permute-done | bytes 262176 | tf_op jit(solution)/shard_map/ppermute | solution.py:22
  25.8 0.7 collective-permute-start.8
  26.6 1.3 %collective-permute-done.7 = f32[32,1152]{1,0:T(8,128)S(1)} collective-permute-done((f32[32,1152]{1,0:T(8,128)S(1)}, f32[32,1152]{1,0:T(8,128)S(1)}, u32[]{:S(2)}, u32[]{:S(2)}) %collective-permute-start.7) | collective-permute-done | bytes 147488 | tf_op jit(solution)/shard_map/ppermute | solution.py:22
  27.9 5.6 %collective-permute-done.8 = f32[32,1792]{1,0:T(8,128)S(1)} collective-permute-done((f32[32,1792]{1,0:T(8,128)S(1)}, f32[32,1792]{1,0:T(8,128)S(1)}, u32[]{:S(2)}, u32[]{:S(2)}) %collective-permute-start.8) | collective-permute-done | bytes 229408 | tf_op jit(solution)/shard_map/ppermute | solution.py:22
  35.6 0.7 collective-permute-start.9
  36.3 4.5 %collective-permute-done.9 = f32[32,1152]{1,0:T(8,128)S(1)} collective-permute-done((f32[32,1152]{1,0:T(8,128)S(1)}, f32[32,1152]{1,0:T(8,128)S(1)}, u32[]{:S(2)}, u32[]{:S(2)}) %collective-permute-start.9) | collective-permute-done | bytes 147488 | tf_op jit(solution)/shard_map/ppermute | solution.py:22
  41.8 2.1 %collective-permute-start.12 = (f32[32,1280]{1,0:T(8,128)S(1)}, f32[32,1280]{1,0:T(8,128)S(1)}, u32[]{:S(2)}, u32[]{:S(2)}) collective-permute-start(f32[32,1280]{1,0:T(8,128)S(1)} %fusion.12), channel_id=1, source_target_pairs={{0,8},{1,9},{2,10},{3,11},{4,12},{5,13},{6,14},{7,15},{8,0},{9,1},... | collective-permute-start | bytes 491528 | tf_op jit(solution)/shard_map/ppermute | solution.py:22
  44.8 2.1 %collective-permute-start.11 = (f32[32,1152]{1,0:T(8,128)S(1)}, f32[32,1152]{1,0:T(8,128)S(1)}, u32[]{:S(2)}, u32[]{:S(2)}) collective-permute-start(f32[32,1152]{1,0:T(8,128)S(1)} %fusion.15), channel_id=1, source_target_pairs={{0,4},{1,5},{2,6},{3,7},{4,0},{5,1},{6,2},{7,3},{8,12},{9,13},{10,... | collective-permute-start | bytes 442376 | tf_op jit(solution)/shard_map/ppermute | solution.py:22
  47.0 4.1 %collective-permute-done.11 = f32[32,1152]{1,0:T(8,128)S(1)} collective-permute-done((f32[32,1152]{1,0:T(8,128)S(1)}, f32[32,1152]{1,0:T(8,128)S(1)}, u32[]{:S(2)}, u32[]{:S(2)}) %collective-permute-start.11) | collective-permute-done | bytes 147488 | tf_op jit(solution)/shard_map/ppermute | solution.py:22
  52.9 1.5 %collective-permute-start.13 = (f32[32,1152]{1,0:T(8,128)S(1)}, f32[32,1152]{1,0:T(8,128)S(1)}, u32[]{:S(2)}, u32[]{:S(2)}) collective-permute-start(f32[32,1152]{1,0:T(8,128)S(1)} %fusion.14), channel_id=1, source_target_pairs={{0,8},{1,9},{2,10},{3,11},{4,12},{5,13},{6,14},{7,15},{8,0},{9,1},... | collective-permute-start | bytes 442376 | tf_op jit(solution)/shard_map/ppermute | solution.py:22
  54.8 5.8 %collective-permute-done.13 = f32[32,1152]{1,0:T(8,128)S(1)} collective-permute-done((f32[32,1152]{1,0:T(8,128)S(1)}, f32[32,1152]{1,0:T(8,128)S(1)}, u32[]{:S(2)}, u32[]{:S(2)}) %collective-permute-start.13) | collective-permute-done | bytes 147488 | tf_op jit(solution)/shard_map/ppermute | solution.py:22
  61.7 1.0 %convolution_reduce_fusion = f32[512,128]{1,0:T(8,128)S(1)} fusion(f32[512,256,1]{1,0,2:T(8,128)S(1)} %bitcast.85, f32[8,128,256]{2,1,0:T(8,128)S(1)} %bitcast.84), kind=kOutput, calls=%fused_computation | convolution fusion | flops 805765120 | bytes 1835008 | tf_op jit(solution)/shard_map/dot_general | solution.py:155
  62.9 0.7 collective-permute-start.15
  63.6 1.1 %collective-permute-start.14 = (f32[2048]{0:T(1024)S(1)}, f32[2048]{0:T(1024)S(1)}, u32[]{:S(2)}, u32[]{:S(2)}) collective-permute-start(f32[2048]{0:T(1024)S(1)} %reduce_max.19), channel_id=1, source_target_pairs={{0,1},{1,0},{2,3},{3,2},{4,5},{5,4},{6,7},{7,6},{8,9},{9,8},{10,11... | collective-permute-start | bytes 24584 | tf_op jit(solution)/shard_map/ppermute | solution.py:27
  64.7 1.2 %collective-permute-done.16 = f32[2048]{0:T(1024)S(1)} collective-permute-done((f32[2048]{0:T(1024)S(1)}, f32[2048]{0:T(1024)S(1)}, u32[]{:S(2)}, u32[]{:S(2)}) %collective-permute-start.16) | collective-permute-done | bytes 8224 | tf_op jit(solution)/shard_map/ppermute | solution.py:27
  66.0 0.7 collective-permute-done.15
  66.6 2.4 %collective-permute-start.19 = (f32[2048]{0:T(1024)S(1)}, f32[2048]{0:T(1024)S(1)}, u32[]{:S(2)}, u32[]{:S(2)}) collective-permute-start(f32[2048]{0:T(1024)S(1)} %maximum_maximum_fusion.1), channel_id=1, source_target_pairs={{0,12},{1,13},{2,14},{3,15},{4,8},{5,9},{6,10},{7,11},{8,4},{9,5},... | collective-permute-start | bytes 24584 | tf_op jit(solution)/shard_map/ppermute | solution.py:27
  69.0 2.1 %collective-permute-start.17 = (f32[2048]{0:T(1024)S(1)}, f32[2048]{0:T(1024)S(1)}, u32[]{:S(2)}, u32[]{:S(2)}) collective-permute-start(f32[2048]{0:T(1024)S(1)} %maximum_maximum_fusion.1), channel_id=1, source_target_pairs={{0,4},{1,5},{2,6},{3,7},{4,0},{5,1},{6,2},{7,3},{8,12},{9,13},{10,... | collective-permute-start | bytes 24584 | tf_op jit(solution)/shard_map/ppermute | solution.py:27
  71.1 1.1 %collective-permute-done.19 = f32[2048]{0:T(1024)S(1)} collective-permute-done((f32[2048]{0:T(1024)S(1)}, f32[2048]{0:T(1024)S(1)}, u32[]{:S(2)}, u32[]{:S(2)}) %collective-permute-start.19) | collective-permute-done | bytes 8224 | tf_op jit(solution)/shard_map/ppermute | solution.py:27
  72.1 1.4 %collective-permute-done.18 = f32[2048]{0:T(1024)S(1)} collective-permute-done((f32[2048]{0:T(1024)S(1)}, f32[2048]{0:T(1024)S(1)}, u32[]{:S(2)}, u32[]{:S(2)}) %collective-permute-start.18) | collective-permute-done | bytes 8224 | tf_op jit(solution)/shard_map/ppermute | solution.py:27
  73.6 0.6 maximum_maximum_fusion
  (115 shorter events, 8.4 us)
Async XLA Ops:
  0.6 22.6 %copy-start.1 = (s32[9,32]{1,0:T(8,128)S(1)}, s32[9,32]{1,0:T(8,128)}, u32[]{:S(2)}) copy-start(s32[9,32]{1,0:T(8,128)} %offsets_ref.1) | copy-start | bytes 3460
  1.8 3.9 %collective-permute-start.2 = (f32[1,4480]{1,0:T(1,128)S(1)}, f32[1,4480]{1,0:T(1,128)S(1)}, u32[]{:S(2)}, u32[]{:S(2)}) collective-permute-start(f32[1,4480]{1,0:T(1,128)S(1)} %shard_map.50), channel_id=1, source_target_pairs={{0,3},{1,2},{2,1},{3,0},{4,7},{5,6},{6,5},{7,4},{8,11},{9,10},{10,... | collective-permute-start | bytes 53768 | tf_op jit(solution)/shard_map/ppermute | solution.py:27
  4.3 3.8 %collective-permute-start.1 = (f32[1,4480]{1,0:T(1,128)S(1)}, f32[1,4480]{1,0:T(1,128)S(1)}, u32[]{:S(2)}, u32[]{:S(2)}) collective-permute-start(f32[1,4480]{1,0:T(1,128)S(1)} %shard_map.50), channel_id=1, source_target_pairs={{0,2},{1,3},{2,0},{3,1},{4,6},{5,7},{6,4},{7,5},{8,10},{9,11},{10,... | collective-permute-start | bytes 53768 | tf_op jit(solution)/shard_map/ppermute | solution.py:27
  4.9 3.1 %collective-permute-start = (f32[1,4480]{1,0:T(1,128)S(1)}, f32[1,4480]{1,0:T(1,128)S(1)}, u32[]{:S(2)}, u32[]{:S(2)}) collective-permute-start(f32[1,4480]{1,0:T(1,128)S(1)} %shard_map.50), channel_id=1, source_target_pairs={{0,1},{1,0},{2,3},{3,2},{4,5},{5,4},{6,7},{7,6},{8,9},{9,8},{10,11... | collective-permute-start | bytes 53768 | tf_op jit(solution)/shard_map/ppermute | solution.py:27
  8.1 5.9 %collective-permute-start.5 = (f32[1,4480]{1,0:T(1,128)S(1)}, f32[1,4480]{1,0:T(1,128)S(1)}, u32[]{:S(2)}, u32[]{:S(2)}) collective-permute-start(f32[1,4480]{1,0:T(1,128)S(1)} %add_add_fusion.1), channel_id=1, source_target_pairs={{0,12},{1,13},{2,14},{3,15},{4,8},{5,9},{6,10},{7,11},{8,4},{9,5},... | collective-permute-start | bytes 53768 | tf_op jit(solution)/shard_map/ppermute | solution.py:27
  11.8 4.7 %collective-permute-start.4 = (f32[1,4480]{1,0:T(1,128)S(1)}, f32[1,4480]{1,0:T(1,128)S(1)}, u32[]{:S(2)}, u32[]{:S(2)}) collective-permute-start(f32[1,4480]{1,0:T(1,128)S(1)} %add_add_fusion.1), channel_id=1, source_target_pairs={{0,8},{1,9},{2,10},{3,11},{4,12},{5,13},{6,14},{7,15},{8,0},{9,1},... | collective-permute-start | bytes 53768 | tf_op jit(solution)/shard_map/ppermute | solution.py:27
  11.8 4.7 %collective-permute-start.3 = (f32[1,4480]{1,0:T(1,128)S(1)}, f32[1,4480]{1,0:T(1,128)S(1)}, u32[]{:S(2)}, u32[]{:S(2)}) collective-permute-start(f32[1,4480]{1,0:T(1,128)S(1)} %add_add_fusion.1), channel_id=1, source_target_pairs={{0,4},{1,5},{2,6},{3,7},{4,0},{5,1},{6,2},{7,3},{8,12},{9,13},{10,... | collective-permute-start | bytes 53768 | tf_op jit(solution)/shard_map/ppermute | solution.py:27
  23.1 1.6 %collective-permute-start.6 = (f32[32,2048]{1,0:T(8,128)S(1)}, f32[32,2048]{1,0:T(8,128)S(1)}, u32[]{:S(2)}, u32[]{:S(2)}) collective-permute-start(f32[32,2048]{1,0:T(8,128)S(1)} %get-tuple-element.16), channel_id=1, source_target_pairs={{0,1},{1,0},{2,3},{3,2},{4,5},{5,4},{6,7},{7,6},{8,9},{9,8},{10,11... | collective-permute-start | bytes 786440 | tf_op jit(solution)/shard_map/ppermute | solution.py:22
  25.6 1.0 %copy-start.2 = (s32[8]{0:T(128)S(1)}, s32[8]{0:T(128)}, u32[]{:S(2)}) copy-start(s32[8]{0:T(128)} %param.5) | copy-start | bytes 100
  25.8 7.7 %collective-permute-start.8 = (f32[32,1792]{1,0:T(8,128)S(1)}, f32[32,1792]{1,0:T(8,128)S(1)}, u32[]{:S(2)}, u32[]{:S(2)}) collective-permute-start(f32[32,1792]{1,0:T(8,128)S(1)} %fusion.2), channel_id=1, source_target_pairs={{0,2},{1,3},{2,0},{3,1},{4,6},{5,7},{6,4},{7,5},{8,10},{9,11},{10,... | collective-permute-start | bytes 688136 | tf_op jit(solution)/shard_map/ppermute | solution.py:22
  26.6 1.4 %collective-permute-start.7 = (f32[32,1152]{1,0:T(8,128)S(1)}, f32[32,1152]{1,0:T(8,128)S(1)}, u32[]{:S(2)}, u32[]{:S(2)}) collective-permute-start(f32[32,1152]{1,0:T(8,128)S(1)} %get-tuple-element.17), channel_id=1, source_target_pairs={{0,1},{1,0},{2,3},{3,2},{4,5},{5,4},{6,7},{7,6},{8,9},{9,8},{10,11... | collective-permute-start | bytes 442376 | tf_op jit(solution)/shard_map/ppermute | solution.py:22
  34.6 6.2 %collective-permute-start.10 = (f32[32,1536]{1,0:T(8,128)S(1)}, f32[32,1536]{1,0:T(8,128)S(1)}, u32[]{:S(2)}, u32[]{:S(2)}) collective-permute-start(f32[32,1536]{1,0:T(8,128)S(1)} %fusion.3), channel_id=1, source_target_pairs={{0,4},{1,5},{2,6},{3,7},{4,0},{5,1},{6,2},{7,3},{8,12},{9,13},{10,... | collective-permute-start | bytes 589832 | tf_op jit(solution)/shard_map/ppermute | solution.py:22
  35.6 5.2 %collective-permute-start.9 = (f32[32,1152]{1,0:T(8,128)S(1)}, f32[32,1152]{1,0:T(8,128)S(1)}, u32[]{:S(2)}, u32[]{:S(2)}) collective-permute-start(f32[32,1152]{1,0:T(8,128)S(1)} %fusion.16), channel_id=1, source_target_pairs={{0,2},{1,3},{2,0},{3,1},{4,6},{5,7},{6,4},{7,5},{8,10},{9,11},{10,... | collective-permute-start | bytes 442376 | tf_op jit(solution)/shard_map/ppermute | solution.py:22
  41.8 9.3 %collective-permute-start.12 = (f32[32,1280]{1,0:T(8,128)S(1)}, f32[32,1280]{1,0:T(8,128)S(1)}, u32[]{:S(2)}, u32[]{:S(2)}) collective-permute-start(f32[32,1280]{1,0:T(8,128)S(1)} %fusion.12), channel_id=1, source_target_pairs={{0,8},{1,9},{2,10},{3,11},{4,12},{5,13},{6,14},{7,15},{8,0},{9,1},... | collective-permute-start | bytes 491528 | tf_op jit(solution)/shard_map/ppermute | solution.py:22
  44.8 6.2 %collective-permute-start.11 = (f32[32,1152]{1,0:T(8,128)S(1)}, f32[32,1152]{1,0:T(8,128)S(1)}, u32[]{:S(2)}, u32[]{:S(2)}) collective-permute-start(f32[32,1152]{1,0:T(8,128)S(1)} %fusion.15), channel_id=1, source_target_pairs={{0,4},{1,5},{2,6},{3,7},{4,0},{5,1},{6,2},{7,3},{8,12},{9,13},{10,... | collective-permute-start | bytes 442376 | tf_op jit(solution)/shard_map/ppermute | solution.py:22
  52.9 7.7 %collective-permute-start.13 = (f32[32,1152]{1,0:T(8,128)S(1)}, f32[32,1152]{1,0:T(8,128)S(1)}, u32[]{:S(2)}, u32[]{:S(2)}) collective-permute-start(f32[32,1152]{1,0:T(8,128)S(1)} %fusion.14), channel_id=1, source_target_pairs={{0,8},{1,9},{2,10},{3,11},{4,12},{5,13},{6,14},{7,15},{8,0},{9,1},... | collective-permute-start | bytes 442376 | tf_op jit(solution)/shard_map/ppermute | solution.py:22
  62.8 11.4 %copy-start = (f32[32,2048]{1,0:T(8,128)}, f32[32,2048]{1,0:T(8,128)S(1)}, u32[]{:S(2)}) copy-start(f32[32,2048]{1,0:T(8,128)S(1)} %reshape.485) | copy-start | bytes 786436
  62.8 3.1 %collective-permute-start.16 = (f32[2048]{0:T(1024)S(1)}, f32[2048]{0:T(1024)S(1)}, u32[]{:S(2)}, u32[]{:S(2)}) collective-permute-start(f32[2048]{0:T(1024)S(1)} %reduce_max.19), channel_id=1, source_target_pairs={{0,3},{1,2},{2,1},{3,0},{4,7},{5,6},{6,5},{7,4},{8,11},{9,10},{10,... | collective-permute-start | bytes 24584 | tf_op jit(solution)/shard_map/ppermute | solution.py:27
  62.9 3.7 %collective-permute-start.15 = (f32[2048]{0:T(1024)S(1)}, f32[2048]{0:T(1024)S(1)}, u32[]{:S(2)}, u32[]{:S(2)}) collective-permute-start(f32[2048]{0:T(1024)S(1)} %reduce_max.19), channel_id=1, source_target_pairs={{0,2},{1,3},{2,0},{3,1},{4,6},{5,7},{6,4},{7,5},{8,10},{9,11},{10,... | collective-permute-start | bytes 24584 | tf_op jit(solution)/shard_map/ppermute | solution.py:27
  63.6 3.0 %collective-permute-start.14 = (f32[2048]{0:T(1024)S(1)}, f32[2048]{0:T(1024)S(1)}, u32[]{:S(2)}, u32[]{:S(2)}) collective-permute-start(f32[2048]{0:T(1024)S(1)} %reduce_max.19), channel_id=1, source_target_pairs={{0,1},{1,0},{2,3},{3,2},{4,5},{5,4},{6,7},{7,6},{8,9},{9,8},{10,11... | collective-permute-start | bytes 24584 | tf_op jit(solution)/shard_map/ppermute | solution.py:27
  66.6 5.5 %collective-permute-start.19 = (f32[2048]{0:T(1024)S(1)}, f32[2048]{0:T(1024)S(1)}, u32[]{:S(2)}, u32[]{:S(2)}) collective-permute-start(f32[2048]{0:T(1024)S(1)} %maximum_maximum_fusion.1), channel_id=1, source_target_pairs={{0,12},{1,13},{2,14},{3,15},{4,8},{5,9},{6,10},{7,11},{8,4},{9,5},... | collective-permute-start | bytes 24584 | tf_op jit(solution)/shard_map/ppermute | solution.py:27
  69.0 4.5 %collective-permute-start.18 = (f32[2048]{0:T(1024)S(1)}, f32[2048]{0:T(1024)S(1)}, u32[]{:S(2)}, u32[]{:S(2)}) collective-permute-start(f32[2048]{0:T(1024)S(1)} %maximum_maximum_fusion.1), channel_id=1, source_target_pairs={{0,8},{1,9},{2,10},{3,11},{4,12},{5,13},{6,14},{7,15},{8,0},{9,1},... | collective-permute-start | bytes 24584 | tf_op jit(solution)/shard_map/ppermute | solution.py:27
  69.0 4.5 %collective-permute-start.17 = (f32[2048]{0:T(1024)S(1)}, f32[2048]{0:T(1024)S(1)}, u32[]{:S(2)}, u32[]{:S(2)}) collective-permute-start(f32[2048]{0:T(1024)S(1)} %maximum_maximum_fusion.1), channel_id=1, source_target_pairs={{0,4},{1,5},{2,6},{3,7},{4,0},{5,1},{6,2},{7,3},{8,12},{9,13},{10,... | collective-permute-start | bytes 24584 | tf_op jit(solution)/shard_map/ppermute | solution.py:27

commit v25 on v23

--- a/solution.py
+++ b/solution.py
@@ -127,7 +127,7 @@
 
 def boxcar_max(dedispersed, widths):
     total_rows = dedispersed.shape[0]
-    blocks_time = TS // TAPS
+    blocks_time = dedispersed.shape[1] // TAPS - 1
     window = dedispersed.reshape(total_rows, blocks_time + 1, TAPS)
     paired = jnp.concatenate([window[:, :-1], window[:, 1:]], axis=2).reshape(
         total_rows * blocks_time, 2 * TAPS
@@ -141,7 +141,7 @@
         preferred_element_type=jnp.float32,
     )
     best_value = jnp.max(result.reshape(total_rows * blocks_time, TEMPLATES, TAPS), axis=1)
-    return best_value.reshape(total_rows, TS)
+    return best_value.reshape(total_rows, blocks_time * TAPS)
 
 
 def per_device(filterbank, offsets, widths):
@@ -194,9 +194,11 @@
         pending = (tail, partner_tail, lower_head[:, head_width:], upper_head[:, head_width:], amounts, bit_index)
         head = new_head
     tail = finish_tail(pending)
-    current = jnp.concatenate([head, tail], axis=1)
-    dedispersed = current * (1.0 / math.sqrt(channels_all))
-    detection = boxcar_max(dedispersed, widths)
+    scale = 1.0 / math.sqrt(channels_all)
+    head_scaled = head * scale
+    head_detection = boxcar_max(head_scaled, widths)
+    tail_scaled = jnp.concatenate([head_scaled[:, -TAPS:], tail * scale], axis=1)
+    detection = jnp.concatenate([head_detection, boxcar_max(tail_scaled, widths)], axis=1)
     peak_series = butterfly(jnp.max(detection, axis=0), "band", jnp.maximum)
     return (detection, peak_series)
 

time: 74.3 us -> 74.1 us (level)
  waiting for transfers between devices: 33.8 us -> 33 us
    ppermute x8, waiting for transfers between devices: 22.6 us -> 21.8 us  [from_partner(): return lax.ppermute(value, axis, pairs)]
  transfers between devices with their start and end apart: 20 -> 20, of which waited for: 14 -> 14; matrix products, arithmetic and copies ran while one was open for 3% -> 4% of each run, Pallas kernels for 0% -> 0%
where the time goes in v25:
time: 74.1 us; the launch traced here: 73.9 us
  waiting for transfers between devices  33 us (45%)
  starting transfers between devices  21.4 us (29%)
  other arithmetic  10.3 us (14%)
  Pallas kernels  6.08 us (8%)
  between operations  1.41 us (2%)
  matrix products  1.33 us (2%)
    ppermute x8, waiting for transfers between devices, from_partner(): return lax.ppermute(value, axis, pairs)  21.8 us
    ppermute x12, starting transfers between devices, from_xor(): return lax.ppermute(value, axis, pairs)  14 us
    ppermute x12, waiting for transfers between devices, from_xor(): return lax.ppermute(value, axis, pairs)  11.2 us
    ppermute x8, starting transfers between devices, from_partner(): return lax.ppermute(value, axis, pairs)  7.36 us
    select_n x56, other arithmetic, shift_rows(): jnp.where(chosen, current[:, span:span + keep_len], current[:, :keep_len])  6.19 us
    pallas_call x1, Pallas kernels, local_tree(): pl.pallas_call(functools.partial(local_tree_kernel, tuple(widths_seq), fl...  6.08 us
  transfers between devices with their start and end apart: 20, of which 14 were waited for; matrix products, arithmetic and copies ran while one was open for 4% of the time, Pallas kernels for 0%

profile of v25, /device:TPU:0, one launch (start us, length us, event | category | flops | bytes accessed | tf_op | source)
XLA Modules:
  0.0 73.9 jit_solution(884811718102115255)
XLA Ops:
  0.6 1.1 %slice_reduce_fusion = f32[4480]{0:T(1024)S(1)} fusion(f32[32,6144]{1,0:T(8,128)} %x_ref.1), kind=kLoop, calls=%fused_computation.5 | loop fusion | flops 138880 | bytes 591360 | tf_op jit(solution)/shard_map/reduce_sum | solution.py:158
  1.8 3.0 %collective-permute-start.1 = (f32[1,4480]{1,0:T(1,128)S(1)}, f32[1,4480]{1,0:T(1,128)S(1)}, u32[]{:S(2)}, u32[]{:S(2)}) collective-permute-start(f32[1,4480]{1,0:T(1,128)S(1)} %broadcast_in_dim.535), channel_id=1, source_target_pairs={{0,2},{1,3},{2,0},{3,1},{4,6},{5,7},{6,4},{7,5},{8,10},{9,11},{10,... | collective-permute-start | bytes 53768 | tf_op jit(solution)/shard_map/ppermute | solution.py:27
  5.0 1.5 %collective-permute-done.1 = f32[1,4480]{1,0:T(1,128)S(1)} collective-permute-done((f32[1,4480]{1,0:T(1,128)S(1)}, f32[1,4480]{1,0:T(1,128)S(1)}, u32[]{:S(2)}, u32[]{:S(2)}) %collective-permute-start.1) | collective-permute-done | bytes 17952 | tf_op jit(solution)/shard_map/ppermute | solution.py:27
  6.5 1.4 %collective-permute-done.2 = f32[1,4480]{1,0:T(1,128)S(1)} collective-permute-done((f32[1,4480]{1,0:T(1,128)S(1)}, f32[1,4480]{1,0:T(1,128)S(1)}, u32[]{:S(2)}, u32[]{:S(2)}) %collective-permute-start.2) | collective-permute-done | bytes 17952 | tf_op jit(solution)/shard_map/ppermute | solution.py:27
  8.0 3.7 %collective-permute-start.5 = (f32[1,4480]{1,0:T(1,128)S(1)}, f32[1,4480]{1,0:T(1,128)S(1)}, u32[]{:S(2)}, u32[]{:S(2)}) collective-permute-start(f32[1,4480]{1,0:T(1,128)S(1)} %add_add_fusion.1), channel_id=1, source_target_pairs={{0,12},{1,13},{2,14},{3,15},{4,8},{5,9},{6,10},{7,11},{8,4},{9,5},... | collective-permute-start | bytes 53768 | tf_op jit(solution)/shard_map/ppermute | solution.py:27
  11.7 0.8 %collective-permute-start.3 = (f32[1,4480]{1,0:T(1,128)S(1)}, f32[1,4480]{1,0:T(1,128)S(1)}, u32[]{:S(2)}, u32[]{:S(2)}) collective-permute-start(f32[1,4480]{1,0:T(1,128)S(1)} %add_add_fusion.1), channel_id=1, source_target_pairs={{0,4},{1,5},{2,6},{3,7},{4,0},{5,1},{6,2},{7,3},{8,12},{9,13},{10,... | collective-permute-start | bytes 53768 | tf_op jit(solution)/shard_map/ppermute | solution.py:27
  12.5 1.4 %collective-permute-done.5 = f32[1,4480]{1,0:T(1,128)S(1)} collective-permute-done((f32[1,4480]{1,0:T(1,128)S(1)}, f32[1,4480]{1,0:T(1,128)S(1)}, u32[]{:S(2)}, u32[]{:S(2)}) %collective-permute-start.5) | collective-permute-done | bytes 17952 | tf_op jit(solution)/shard_map/ppermute | solution.py:27
  13.8 2.5 %collective-permute-done.4 = f32[1,4480]{1,0:T(1,128)S(1)} collective-permute-done((f32[1,4480]{1,0:T(1,128)S(1)}, f32[1,4480]{1,0:T(1,128)S(1)}, u32[]{:S(2)}, u32[]{:S(2)}) %collective-permute-start.4) | collective-permute-done | bytes 17952 | tf_op jit(solution)/shard_map/ppermute | solution.py:27
  16.3 0.6 add_add_fusion.total_ref
  17.0 6.1 %shard_map.50 = (f32[32,2048]{1,0:T(8,128)S(1)}, f32[32,1152]{1,0:T(8,128)S(1)}) custom-call(f32[32,6144]{1,0:T(8,128)} %x_ref.1, f32[1,4480]{1,0:T(1,128)} %add_add_fusion.total_ref, s32[9,32]{1,0:T(8,128)} %offsets_ref.1), custom_call_target="tpu_custom_call" | custom-call | flops 25395200 | bytes 983040 | tf_op jit(solution)/shard_map/pallas_call | solution.py:88
  23.2 1.4 %collective-permute-done.6 = f32[32,2048]{1,0:T(8,128)S(1)} collective-permute-done((f32[32,2048]{1,0:T(8,128)S(1)}, f32[32,2048]{1,0:T(8,128)S(1)}, u32[]{:S(2)}, u32[]{:S(2)}) %collective-permute-start.6) | collective-permute-done | bytes 262176 | tf_op jit(solution)/shard_map/ppermute | solution.py:22
  25.8 0.8 %collective-permute-start.8 = (f32[32,1792]{1,0:T(8,128)S(1)}, f32[32,1792]{1,0:T(8,128)S(1)}, u32[]{:S(2)}, u32[]{:S(2)}) collective-permute-start(f32[32,1792]{1,0:T(8,128)S(1)} %fusion.2), channel_id=1, source_target_pairs={{0,2},{1,3},{2,0},{3,1},{4,6},{5,7},{6,4},{7,5},{8,10},{9,11},{10,... | collective-permute-start | bytes 688136 | tf_op jit(solution)/shard_map/ppermute | solution.py:22
  26.7 1.3 %collective-permute-done.7 = f32[32,1152]{1,0:T(8,128)S(1)} collective-permute-done((f32[32,1152]{1,0:T(8,128)S(1)}, f32[32,1152]{1,0:T(8,128)S(1)}, u32[]{:S(2)}, u32[]{:S(2)}) %collective-permute-start.7) | collective-permute-done | bytes 147488 | tf_op jit(solution)/shard_map/ppermute | solution.py:22
  28.0 5.5 %collective-permute-done.8 = f32[32,1792]{1,0:T(8,128)S(1)} collective-permute-done((f32[32,1792]{1,0:T(8,128)S(1)}, f32[32,1792]{1,0:T(8,128)S(1)}, u32[]{:S(2)}, u32[]{:S(2)}) %collective-permute-start.8) | collective-permute-done | bytes 229408 | tf_op jit(solution)/shard_map/ppermute | solution.py:22
  35.5 0.8 %collective-permute-start.9 = (f32[32,1152]{1,0:T(8,128)S(1)}, f32[32,1152]{1,0:T(8,128)S(1)}, u32[]{:S(2)}, u32[]{:S(2)}) collective-permute-start(f32[32,1152]{1,0:T(8,128)S(1)} %fusion.17), channel_id=1, source_target_pairs={{0,2},{1,3},{2,0},{3,1},{4,6},{5,7},{6,4},{7,5},{8,10},{9,11},{10,... | collective-permute-start | bytes 442376 | tf_op jit(solution)/shard_map/ppermute | solution.py:22
  36.4 4.3 %collective-permute-done.9 = f32[32,1152]{1,0:T(8,128)S(1)} collective-permute-done((f32[32,1152]{1,0:T(8,128)S(1)}, f32[32,1152]{1,0:T(8,128)S(1)}, u32[]{:S(2)}, u32[]{:S(2)}) %collective-permute-start.9) | collective-permute-done | bytes 147488 | tf_op jit(solution)/shard_map/ppermute | solution.py:22
  41.7 2.1 %collective-permute-start.12 = (f32[32,1280]{1,0:T(8,128)S(1)}, f32[32,1280]{1,0:T(8,128)S(1)}, u32[]{:S(2)}, u32[]{:S(2)}) collective-permute-start(f32[32,1280]{1,0:T(8,128)S(1)} %fusion.12), channel_id=1, source_target_pairs={{0,8},{1,9},{2,10},{3,11},{4,12},{5,13},{6,14},{7,15},{8,0},{9,1},... | collective-permute-start | bytes 491528 | tf_op jit(solution)/shard_map/ppermute | solution.py:22
  44.7 2.1 %collective-permute-start.11 = (f32[32,1152]{1,0:T(8,128)S(1)}, f32[32,1152]{1,0:T(8,128)S(1)}, u32[]{:S(2)}, u32[]{:S(2)}) collective-permute-start(f32[32,1152]{1,0:T(8,128)S(1)} %fusion.16), channel_id=1, source_target_pairs={{0,4},{1,5},{2,6},{3,7},{4,0},{5,1},{6,2},{7,3},{8,12},{9,13},{10,... | collective-permute-start | bytes 442376 | tf_op jit(solution)/shard_map/ppermute | solution.py:22
  47.2 3.7 %collective-permute-done.11 = f32[32,1152]{1,0:T(8,128)S(1)} collective-permute-done((f32[32,1152]{1,0:T(8,128)S(1)}, f32[32,1152]{1,0:T(8,128)S(1)}, u32[]{:S(2)}, u32[]{:S(2)}) %collective-permute-start.11) | collective-permute-done | bytes 147488 | tf_op jit(solution)/shard_map/ppermute | solution.py:22
  53.0 1.5 %collective-permute-start.13 = (f32[32,1152]{1,0:T(8,128)S(1)}, f32[32,1152]{1,0:T(8,128)S(1)}, u32[]{:S(2)}, u32[]{:S(2)}) collective-permute-start(f32[32,1152]{1,0:T(8,128)S(1)} %fusion.15), channel_id=1, source_target_pairs={{0,8},{1,9},{2,10},{3,11},{4,12},{5,13},{6,14},{7,15},{8,0},{9,1},... | collective-permute-start | bytes 442376 | tf_op jit(solution)/shard_map/ppermute | solution.py:22
  54.4 0.7 convolution_reduce_fusion.1
  55.2 5.5 %collective-permute-done.13 = f32[32,1152]{1,0:T(8,128)S(1)} collective-permute-done((f32[32,1152]{1,0:T(8,128)S(1)}, f32[32,1152]{1,0:T(8,128)S(1)}, u32[]{:S(2)}, u32[]{:S(2)}) %collective-permute-start.13) | collective-permute-done | bytes 147488 | tf_op jit(solution)/shard_map/ppermute | solution.py:22
  61.8 0.7 convolution_reduce_fusion
  62.7 0.8 %collective-permute-start.15 = (f32[2048]{0:T(1024)S(1)}, f32[2048]{0:T(1024)S(1)}, u32[]{:S(2)}, u32[]{:S(2)}) collective-permute-start(f32[2048]{0:T(1024)S(1)} %reduce_max.29), channel_id=1, source_target_pairs={{0,2},{1,3},{2,0},{3,1},{4,6},{5,7},{6,4},{7,5},{8,10},{9,11},{10,... | collective-permute-start | bytes 24584 | tf_op jit(solution)/shard_map/ppermute | solution.py:27
  63.5 1.1 %collective-permute-start.14 = (f32[2048]{0:T(1024)S(1)}, f32[2048]{0:T(1024)S(1)}, u32[]{:S(2)}, u32[]{:S(2)}) collective-permute-start(f32[2048]{0:T(1024)S(1)} %reduce_max.29), channel_id=1, source_target_pairs={{0,1},{1,0},{2,3},{3,2},{4,5},{5,4},{6,7},{7,6},{8,9},{9,8},{10,11... | collective-permute-start | bytes 24584 | tf_op jit(solution)/shard_map/ppermute | solution.py:27
  64.5 1.2 %collective-permute-done.16 = f32[2048]{0:T(1024)S(1)} collective-permute-done((f32[2048]{0:T(1024)S(1)}, f32[2048]{0:T(1024)S(1)}, u32[]{:S(2)}, u32[]{:S(2)}) %collective-permute-start.16) | collective-permute-done | bytes 8224 | tf_op jit(solution)/shard_map/ppermute | solution.py:27
  65.7 0.7 collective-permute-done.15
  66.4 2.4 %collective-permute-start.19 = (f32[2048]{0:T(1024)S(1)}, f32[2048]{0:T(1024)S(1)}, u32[]{:S(2)}, u32[]{:S(2)}) collective-permute-start(f32[2048]{0:T(1024)S(1)} %maximum_maximum_fusion.1), channel_id=1, source_target_pairs={{0,12},{1,13},{2,14},{3,15},{4,8},{5,9},{6,10},{7,11},{8,4},{9,5},... | collective-permute-start | bytes 24584 | tf_op jit(solution)/shard_map/ppermute | solution.py:27
  68.8 2.1 %collective-permute-start.17 = (f32[2048]{0:T(1024)S(1)}, f32[2048]{0:T(1024)S(1)}, u32[]{:S(2)}, u32[]{:S(2)}) collective-permute-start(f32[2048]{0:T(1024)S(1)} %maximum_maximum_fusion.1), channel_id=1, source_target_pairs={{0,4},{1,5},{2,6},{3,7},{4,0},{5,1},{6,2},{7,3},{8,12},{9,13},{10,... | collective-permute-start | bytes 24584 | tf_op jit(solution)/shard_map/ppermute | solution.py:27
  70.9 1.1 %collective-permute-done.19 = f32[2048]{0:T(1024)S(1)} collective-permute-done((f32[2048]{0:T(1024)S(1)}, f32[2048]{0:T(1024)S(1)}, u32[]{:S(2)}, u32[]{:S(2)}) %collective-permute-start.19) | collective-permute-done | bytes 8224 | tf_op jit(solution)/shard_map/ppermute | solution.py:27
  71.9 1.4 %collective-permute-done.18 = f32[2048]{0:T(1024)S(1)} collective-permute-done((f32[2048]{0:T(1024)S(1)}, f32[2048]{0:T(1024)S(1)}, u32[]{:S(2)}, u32[]{:S(2)}) %collective-permute-start.18) | collective-permute-done | bytes 8224 | tf_op jit(solution)/shard_map/ppermute | solution.py:27
  73.3 0.6 maximum_maximum_fusion
  (127 shorter events, 8.8 us)
Async XLA Ops:
  0.6 22.5 %copy-start.1 = (s32[9,32]{1,0:T(8,128)S(1)}, s32[9,32]{1,0:T(8,128)}, u32[]{:S(2)}) copy-start(s32[9,32]{1,0:T(8,128)} %offsets_ref.1) | copy-start | bytes 3460
  1.8 4.7 %collective-permute-start.1 = (f32[1,4480]{1,0:T(1,128)S(1)}, f32[1,4480]{1,0:T(1,128)S(1)}, u32[]{:S(2)}, u32[]{:S(2)}) collective-permute-start(f32[1,4480]{1,0:T(1,128)S(1)} %broadcast_in_dim.535), channel_id=1, source_target_pairs={{0,2},{1,3},{2,0},{3,1},{4,6},{5,7},{6,4},{7,5},{8,10},{9,11},{10,... | collective-permute-start | bytes 53768 | tf_op jit(solution)/shard_map/ppermute | solution.py:27
  4.8 3.2 %collective-permute-start.2 = (f32[1,4480]{1,0:T(1,128)S(1)}, f32[1,4480]{1,0:T(1,128)S(1)}, u32[]{:S(2)}, u32[]{:S(2)}) collective-permute-start(f32[1,4480]{1,0:T(1,128)S(1)} %broadcast_in_dim.535), channel_id=1, source_target_pairs={{0,3},{1,2},{2,1},{3,0},{4,7},{5,6},{6,5},{7,4},{8,11},{9,10},{10,... | collective-permute-start | bytes 53768 | tf_op jit(solution)/shard_map/ppermute | solution.py:27
  4.8 3.2 %collective-permute-start = (f32[1,4480]{1,0:T(1,128)S(1)}, f32[1,4480]{1,0:T(1,128)S(1)}, u32[]{:S(2)}, u32[]{:S(2)}) collective-permute-start(f32[1,4480]{1,0:T(1,128)S(1)} %broadcast_in_dim.535), channel_id=1, source_target_pairs={{0,1},{1,0},{2,3},{3,2},{4,5},{5,4},{6,7},{7,6},{8,9},{9,8},{10,11... | collective-permute-start | bytes 53768 | tf_op jit(solution)/shard_map/ppermute | solution.py:27
  8.0 5.8 %collective-permute-start.5 = (f32[1,4480]{1,0:T(1,128)S(1)}, f32[1,4480]{1,0:T(1,128)S(1)}, u32[]{:S(2)}, u32[]{:S(2)}) collective-permute-start(f32[1,4480]{1,0:T(1,128)S(1)} %add_add_fusion.1), channel_id=1, source_target_pairs={{0,12},{1,13},{2,14},{3,15},{4,8},{5,9},{6,10},{7,11},{8,4},{9,5},... | collective-permute-start | bytes 53768 | tf_op jit(solution)/shard_map/ppermute | solution.py:27
  11.7 4.7 %collective-permute-start.4 = (f32[1,4480]{1,0:T(1,128)S(1)}, f32[1,4480]{1,0:T(1,128)S(1)}, u32[]{:S(2)}, u32[]{:S(2)}) collective-permute-start(f32[1,4480]{1,0:T(1,128)S(1)} %add_add_fusion.1), channel_id=1, source_target_pairs={{0,8},{1,9},{2,10},{3,11},{4,12},{5,13},{6,14},{7,15},{8,0},{9,1},... | collective-permute-start | bytes 53768 | tf_op jit(solution)/shard_map/ppermute | solution.py:27
  11.7 4.7 %collective-permute-start.3 = (f32[1,4480]{1,0:T(1,128)S(1)}, f32[1,4480]{1,0:T(1,128)S(1)}, u32[]{:S(2)}, u32[]{:S(2)}) collective-permute-start(f32[1,4480]{1,0:T(1,128)S(1)} %add_add_fusion.1), channel_id=1, source_target_pairs={{0,4},{1,5},{2,6},{3,7},{4,0},{5,1},{6,2},{7,3},{8,12},{9,13},{10,... | collective-permute-start | bytes 53768 | tf_op jit(solution)/shard_map/ppermute | solution.py:27
  23.1 1.6 %collective-permute-start.6 = (f32[32,2048]{1,0:T(8,128)S(1)}, f32[32,2048]{1,0:T(8,128)S(1)}, u32[]{:S(2)}, u32[]{:S(2)}) collective-permute-start(f32[32,2048]{1,0:T(8,128)S(1)} %get-tuple-element.16), channel_id=1, source_target_pairs={{0,1},{1,0},{2,3},{3,2},{4,5},{5,4},{6,7},{7,6},{8,9},{9,8},{10,11... | collective-permute-start | bytes 786440 | tf_op jit(solution)/shard_map/ppermute | solution.py:22
  25.4 1.2 %copy-start.2 = (s32[8]{0:T(128)S(1)}, s32[8]{0:T(128)}, u32[]{:S(2)}) copy-start(s32[8]{0:T(128)} %param.5) | copy-start | bytes 100
  25.8 7.7 %collective-permute-start.8 = (f32[32,1792]{1,0:T(8,128)S(1)}, f32[32,1792]{1,0:T(8,128)S(1)}, u32[]{:S(2)}, u32[]{:S(2)}) collective-permute-start(f32[32,1792]{1,0:T(8,128)S(1)} %fusion.2), channel_id=1, source_target_pairs={{0,2},{1,3},{2,0},{3,1},{4,6},{5,7},{6,4},{7,5},{8,10},{9,11},{10,... | collective-permute-start | bytes 688136 | tf_op jit(solution)/shard_map/ppermute | solution.py:22
  26.6 1.4 %collective-permute-start.7 = (f32[32,1152]{1,0:T(8,128)S(1)}, f32[32,1152]{1,0:T(8,128)S(1)}, u32[]{:S(2)}, u32[]{:S(2)}) collective-permute-start(f32[32,1152]{1,0:T(8,128)S(1)} %get-tuple-element.17), channel_id=1, source_target_pairs={{0,1},{1,0},{2,3},{3,2},{4,5},{5,4},{6,7},{7,6},{8,9},{9,8},{10,11... | collective-permute-start | bytes 442376 | tf_op jit(solution)/shard_map/ppermute | solution.py:22
  34.5 6.2 %collective-permute-start.10 = (f32[32,1536]{1,0:T(8,128)S(1)}, f32[32,1536]{1,0:T(8,128)S(1)}, u32[]{:S(2)}, u32[]{:S(2)}) collective-permute-start(f32[32,1536]{1,0:T(8,128)S(1)} %fusion.3), channel_id=1, source_target_pairs={{0,4},{1,5},{2,6},{3,7},{4,0},{5,1},{6,2},{7,3},{8,12},{9,13},{10,... | collective-permute-start | bytes 589832 | tf_op jit(solution)/shard_map/ppermute | solution.py:22
  35.5 5.2 %collective-permute-start.9 = (f32[32,1152]{1,0:T(8,128)S(1)}, f32[32,1152]{1,0:T(8,128)S(1)}, u32[]{:S(2)}, u32[]{:S(2)}) collective-permute-start(f32[32,1152]{1,0:T(8,128)S(1)} %fusion.17), channel_id=1, source_target_pairs={{0,2},{1,3},{2,0},{3,1},{4,6},{5,7},{6,4},{7,5},{8,10},{9,11},{10,... | collective-permute-start | bytes 442376 | tf_op jit(solution)/shard_map/ppermute | solution.py:22
  41.7 9.3 %collective-permute-start.12 = (f32[32,1280]{1,0:T(8,128)S(1)}, f32[32,1280]{1,0:T(8,128)S(1)}, u32[]{:S(2)}, u32[]{:S(2)}) collective-permute-start(f32[32,1280]{1,0:T(8,128)S(1)} %fusion.12), channel_id=1, source_target_pairs={{0,8},{1,9},{2,10},{3,11},{4,12},{5,13},{6,14},{7,15},{8,0},{9,1},... | collective-permute-start | bytes 491528 | tf_op jit(solution)/shard_map/ppermute | solution.py:22
  44.7 6.2 %collective-permute-start.11 = (f32[32,1152]{1,0:T(8,128)S(1)}, f32[32,1152]{1,0:T(8,128)S(1)}, u32[]{:S(2)}, u32[]{:S(2)}) collective-permute-start(f32[32,1152]{1,0:T(8,128)S(1)} %fusion.16), channel_id=1, source_target_pairs={{0,4},{1,5},{2,6},{3,7},{4,0},{5,1},{6,2},{7,3},{8,12},{9,13},{10,... | collective-permute-start | bytes 442376 | tf_op jit(solution)/shard_map/ppermute | solution.py:22
  53.0 7.7 %collective-permute-start.13 = (f32[32,1152]{1,0:T(8,128)S(1)}, f32[32,1152]{1,0:T(8,128)S(1)}, u32[]{:S(2)}, u32[]{:S(2)}) collective-permute-start(f32[32,1152]{1,0:T(8,128)S(1)} %fusion.15), channel_id=1, source_target_pairs={{0,8},{1,9},{2,10},{3,11},{4,12},{5,13},{6,14},{7,15},{8,0},{9,1},... | collective-permute-start | bytes 442376 | tf_op jit(solution)/shard_map/ppermute | solution.py:22
  62.5 11.4 %copy-start = (f32[32,2048]{1,0:T(8,128)}, f32[32,2048]{1,0:T(8,128)S(1)}, u32[]{:S(2)}) copy-start(f32[32,2048]{1,0:T(8,128)S(1)} %constant_dynamic-update-slice_fusion) | copy-start | bytes 786436
  62.6 3.1 %collective-permute-start.16 = (f32[2048]{0:T(1024)S(1)}, f32[2048]{0:T(1024)S(1)}, u32[]{:S(2)}, u32[]{:S(2)}) collective-permute-start(f32[2048]{0:T(1024)S(1)} %reduce_max.29), channel_id=1, source_target_pairs={{0,3},{1,2},{2,1},{3,0},{4,7},{5,6},{6,5},{7,4},{8,11},{9,10},{10,... | collective-permute-start | bytes 24584 | tf_op jit(solution)/shard_map/ppermute | solution.py:27
  62.7 3.7 %collective-permute-start.15 = (f32[2048]{0:T(1024)S(1)}, f32[2048]{0:T(1024)S(1)}, u32[]{:S(2)}, u32[]{:S(2)}) collective-permute-start(f32[2048]{0:T(1024)S(1)} %reduce_max.29), channel_id=1, source_target_pairs={{0,2},{1,3},{2,0},{3,1},{4,6},{5,7},{6,4},{7,5},{8,10},{9,11},{10,... | collective-permute-start | bytes 24584 | tf_op jit(solution)/shard_map/ppermute | solution.py:27
  63.5 2.9 %collective-permute-start.14 = (f32[2048]{0:T(1024)S(1)}, f32[2048]{0:T(1024)S(1)}, u32[]{:S(2)}, u32[]{:S(2)}) collective-permute-start(f32[2048]{0:T(1024)S(1)} %reduce_max.29), channel_id=1, source_target_pairs={{0,1},{1,0},{2,3},{3,2},{4,5},{5,4},{6,7},{7,6},{8,9},{9,8},{10,11... | collective-permute-start | bytes 24584 | tf_op jit(solution)/shard_map/ppermute | solution.py:27
  66.4 5.5 %collective-permute-start.19 = (f32[2048]{0:T(1024)S(1)}, f32[2048]{0:T(1024)S(1)}, u32[]{:S(2)}, u32[]{:S(2)}) collective-permute-start(f32[2048]{0:T(1024)S(1)} %maximum_maximum_fusion.1), channel_id=1, source_target_pairs={{0,12},{1,13},{2,14},{3,15},{4,8},{5,9},{6,10},{7,11},{8,4},{9,5},... | collective-permute-start | bytes 24584 | tf_op jit(solution)/shard_map/ppermute | solution.py:27
  68.8 4.5 %collective-permute-start.18 = (f32[2048]{0:T(1024)S(1)}, f32[2048]{0:T(1024)S(1)}, u32[]{:S(2)}, u32[]{:S(2)}) collective-permute-start(f32[2048]{0:T(1024)S(1)} %maximum_maximum_fusion.1), channel_id=1, source_target_pairs={{0,8},{1,9},{2,10},{3,11},{4,12},{5,13},{6,14},{7,15},{8,0},{9,1},... | collective-permute-start | bytes 24584 | tf_op jit(solution)/shard_map/ppermute | solution.py:27
  68.8 4.5 %collective-permute-start.17 = (f32[2048]{0:T(1024)S(1)}, f32[2048]{0:T(1024)S(1)}, u32[]{:S(2)}, u32[]{:S(2)}) collective-permute-start(f32[2048]{0:T(1024)S(1)} %maximum_maximum_fusion.1), channel_id=1, source_target_pairs={{0,4},{1,5},{2,6},{3,7},{4,0},{5,1},{6,2},{7,3},{8,12},{9,13},{10,... | collective-permute-start | bytes 24584 | tf_op jit(solution)/shard_map/ppermute | solution.py:27

commit v26 on v25

--- a/solution.py
+++ b/solution.py
@@ -27,11 +27,11 @@
     return lax.ppermute(value, axis, pairs)
 
 
-def butterfly(value, axis, combine):
+def butterfly(value, axis, combine, late_pairwise=False):
     bit_count = lax.axis_size(axis).bit_length() - 1
     low_bit = 0
     while low_bit < bit_count:
-        width = min(2, bit_count - low_bit)
+        width = 1 if late_pairwise and low_bit >= 2 else min(2, bit_count - low_bit)
         received = [value] + [from_xor(value, axis, k << low_bit) for k in range(1, 2**width)]
         while len(received) > 1:
             received = [combine(received[i], received[i + 1]) for i in range(0, len(received), 2)]
@@ -199,7 +199,7 @@
     head_detection = boxcar_max(head_scaled, widths)
     tail_scaled = jnp.concatenate([head_scaled[:, -TAPS:], tail * scale], axis=1)
     detection = jnp.concatenate([head_detection, boxcar_max(tail_scaled, widths)], axis=1)
-    peak_series = butterfly(jnp.max(detection, axis=0), "band", jnp.maximum)
+    peak_series = butterfly(jnp.max(detection, axis=0), "band", jnp.maximum, late_pairwise=True)
     return (detection, peak_series)
 
 

time: 74.1 us -> 75.4 us (1.018)
  waiting for transfers between devices: 33 us -> 37.9 us
  starting transfers between devices: 21.4 us -> 17.9 us
    ppermute x12 -> x11, waiting for transfers between devices: 11.2 us -> 16.1 us  [from_xor(): return lax.ppermute(value, axis, pairs)]
    ppermute x12 -> x11, starting transfers between devices: 14 us -> 10.5 us  [from_xor(): return lax.ppermute(value, axis, pairs)]
  transfers between devices with their start and end apart: 20 -> 19, of which waited for: 14 -> 14; matrix products, arithmetic and copies ran while one was open for 4% -> 4% of each run, Pallas kernels for 0% -> 0%
where the time goes in v26:
time: 75.4 us; the launch traced here: 75.3 us
  waiting for transfers between devices  37.9 us (50%)
  starting transfers between devices  17.9 us (24%)
  other arithmetic  10.3 us (14%)
  Pallas kernels  6.08 us (8%)
  between operations  1.41 us (2%)
  matrix products  1.33 us (2%)
    ppermute x8, waiting for transfers between devices, from_partner(): return lax.ppermute(value, axis, pairs)  21.8 us
    ppermute x11, waiting for transfers between devices, from_xor(): return lax.ppermute(value, axis, pairs)  16.1 us
    ppermute x11, starting transfers between devices, from_xor(): return lax.ppermute(value, axis, pairs)  10.5 us
    ppermute x8, starting transfers between devices, from_partner(): return lax.ppermute(value, axis, pairs)  7.36 us
    select_n x56, other arithmetic, shift_rows(): jnp.where(chosen, current[:, span:span + keep_len], current[:, :keep_len])  6.19 us
    pallas_call x1, Pallas kernels, local_tree(): pl.pallas_call(functools.partial(local_tree_kernel, tuple(widths_seq), fl...  6.08 us
  transfers between devices with their start and end apart: 19, of which 14 were waited for; matrix products, arithmetic and copies ran while one was open for 4% of the time, Pallas kernels for 0%

profile of v26, /device:TPU:0, one launch (start us, length us, event | category | flops | bytes accessed | tf_op | source)
XLA Modules:
  0.0 75.3 jit_solution(16525521160681274833)
XLA Ops:
  0.6 1.1 %slice_reduce_fusion = f32[4480]{0:T(1024)S(1)} fusion(f32[32,6144]{1,0:T(8,128)} %x_ref.1), kind=kLoop, calls=%fused_computation.5 | loop fusion | flops 138880 | bytes 591360 | tf_op jit(solution)/shard_map/reduce_sum | solution.py:158
  1.8 3.0 %collective-permute-start.1 = (f32[1,4480]{1,0:T(1,128)S(1)}, f32[1,4480]{1,0:T(1,128)S(1)}, u32[]{:S(2)}, u32[]{:S(2)}) collective-permute-start(f32[1,4480]{1,0:T(1,128)S(1)} %broadcast_in_dim.535), channel_id=1, source_target_pairs={{0,2},{1,3},{2,0},{3,1},{4,6},{5,7},{6,4},{7,5},{8,10},{9,11},{10,... | collective-permute-start | bytes 53768 | tf_op jit(solution)/shard_map/ppermute | solution.py:27
  5.0 1.5 %collective-permute-done.1 = f32[1,4480]{1,0:T(1,128)S(1)} collective-permute-done((f32[1,4480]{1,0:T(1,128)S(1)}, f32[1,4480]{1,0:T(1,128)S(1)}, u32[]{:S(2)}, u32[]{:S(2)}) %collective-permute-start.1) | collective-permute-done | bytes 17952 | tf_op jit(solution)/shard_map/ppermute | solution.py:27
  6.5 1.4 %collective-permute-done.2 = f32[1,4480]{1,0:T(1,128)S(1)} collective-permute-done((f32[1,4480]{1,0:T(1,128)S(1)}, f32[1,4480]{1,0:T(1,128)S(1)}, u32[]{:S(2)}, u32[]{:S(2)}) %collective-permute-start.2) | collective-permute-done | bytes 17952 | tf_op jit(solution)/shard_map/ppermute | solution.py:27
  8.0 3.7 %collective-permute-start.5 = (f32[1,4480]{1,0:T(1,128)S(1)}, f32[1,4480]{1,0:T(1,128)S(1)}, u32[]{:S(2)}, u32[]{:S(2)}) collective-permute-start(f32[1,4480]{1,0:T(1,128)S(1)} %add_add_fusion.1), channel_id=1, source_target_pairs={{0,12},{1,13},{2,14},{3,15},{4,8},{5,9},{6,10},{7,11},{8,4},{9,5},... | collective-permute-start | bytes 53768 | tf_op jit(solution)/shard_map/ppermute | solution.py:27
  11.7 0.8 %collective-permute-start.3 = (f32[1,4480]{1,0:T(1,128)S(1)}, f32[1,4480]{1,0:T(1,128)S(1)}, u32[]{:S(2)}, u32[]{:S(2)}) collective-permute-start(f32[1,4480]{1,0:T(1,128)S(1)} %add_add_fusion.1), channel_id=1, source_target_pairs={{0,4},{1,5},{2,6},{3,7},{4,0},{5,1},{6,2},{7,3},{8,12},{9,13},{10,... | collective-permute-start | bytes 53768 | tf_op jit(solution)/shard_map/ppermute | solution.py:27
  12.5 1.4 %collective-permute-done.5 = f32[1,4480]{1,0:T(1,128)S(1)} collective-permute-done((f32[1,4480]{1,0:T(1,128)S(1)}, f32[1,4480]{1,0:T(1,128)S(1)}, u32[]{:S(2)}, u32[]{:S(2)}) %collective-permute-start.5) | collective-permute-done | bytes 17952 | tf_op jit(solution)/shard_map/ppermute | solution.py:27
  13.8 2.5 %collective-permute-done.4 = f32[1,4480]{1,0:T(1,128)S(1)} collective-permute-done((f32[1,4480]{1,0:T(1,128)S(1)}, f32[1,4480]{1,0:T(1,128)S(1)}, u32[]{:S(2)}, u32[]{:S(2)}) %collective-permute-start.4) | collective-permute-done | bytes 17952 | tf_op jit(solution)/shard_map/ppermute | solution.py:27
  16.3 0.6 add_add_fusion.total_ref
  17.0 6.1 %shard_map.50 = (f32[32,2048]{1,0:T(8,128)S(1)}, f32[32,1152]{1,0:T(8,128)S(1)}) custom-call(f32[32,6144]{1,0:T(8,128)} %x_ref.1, f32[1,4480]{1,0:T(1,128)} %add_add_fusion.total_ref, s32[9,32]{1,0:T(8,128)} %offsets_ref.1), custom_call_target="tpu_custom_call" | custom-call | flops 25395200 | bytes 983040 | tf_op jit(solution)/shard_map/pallas_call | solution.py:88
  23.2 1.4 %collective-permute-done.6 = f32[32,2048]{1,0:T(8,128)S(1)} collective-permute-done((f32[32,2048]{1,0:T(8,128)S(1)}, f32[32,2048]{1,0:T(8,128)S(1)}, u32[]{:S(2)}, u32[]{:S(2)}) %collective-permute-start.6) | collective-permute-done | bytes 262176 | tf_op jit(solution)/shard_map/ppermute | solution.py:22
  25.8 0.8 %collective-permute-start.8 = (f32[32,1792]{1,0:T(8,128)S(1)}, f32[32,1792]{1,0:T(8,128)S(1)}, u32[]{:S(2)}, u32[]{:S(2)}) collective-permute-start(f32[32,1792]{1,0:T(8,128)S(1)} %fusion.2), channel_id=1, source_target_pairs={{0,2},{1,3},{2,0},{3,1},{4,6},{5,7},{6,4},{7,5},{8,10},{9,11},{10,... | collective-permute-start | bytes 688136 | tf_op jit(solution)/shard_map/ppermute | solution.py:22
  26.7 1.3 %collective-permute-done.7 = f32[32,1152]{1,0:T(8,128)S(1)} collective-permute-done((f32[32,1152]{1,0:T(8,128)S(1)}, f32[32,1152]{1,0:T(8,128)S(1)}, u32[]{:S(2)}, u32[]{:S(2)}) %collective-permute-start.7) | collective-permute-done | bytes 147488 | tf_op jit(solution)/shard_map/ppermute | solution.py:22
  28.0 5.5 %collective-permute-done.8 = f32[32,1792]{1,0:T(8,128)S(1)} collective-permute-done((f32[32,1792]{1,0:T(8,128)S(1)}, f32[32,1792]{1,0:T(8,128)S(1)}, u32[]{:S(2)}, u32[]{:S(2)}) %collective-permute-start.8) | collective-permute-done | bytes 229408 | tf_op jit(solution)/shard_map/ppermute | solution.py:22
  35.5 0.8 %collective-permute-start.9 = (f32[32,1152]{1,0:T(8,128)S(1)}, f32[32,1152]{1,0:T(8,128)S(1)}, u32[]{:S(2)}, u32[]{:S(2)}) collective-permute-start(f32[32,1152]{1,0:T(8,128)S(1)} %fusion.17), channel_id=1, source_target_pairs={{0,2},{1,3},{2,0},{3,1},{4,6},{5,7},{6,4},{7,5},{8,10},{9,11},{10,... | collective-permute-start | bytes 442376 | tf_op jit(solution)/shard_map/ppermute | solution.py:22
  36.4 4.3 %collective-permute-done.9 = f32[32,1152]{1,0:T(8,128)S(1)} collective-permute-done((f32[32,1152]{1,0:T(8,128)S(1)}, f32[32,1152]{1,0:T(8,128)S(1)}, u32[]{:S(2)}, u32[]{:S(2)}) %collective-permute-start.9) | collective-permute-done | bytes 147488 | tf_op jit(solution)/shard_map/ppermute | solution.py:22
  41.7 2.1 %collective-permute-start.12 = (f32[32,1280]{1,0:T(8,128)S(1)}, f32[32,1280]{1,0:T(8,128)S(1)}, u32[]{:S(2)}, u32[]{:S(2)}) collective-permute-start(f32[32,1280]{1,0:T(8,128)S(1)} %fusion.12), channel_id=1, source_target_pairs={{0,8},{1,9},{2,10},{3,11},{4,12},{5,13},{6,14},{7,15},{8,0},{9,1},... | collective-permute-start | bytes 491528 | tf_op jit(solution)/shard_map/ppermute | solution.py:22
  44.7 2.1 %collective-permute-start.11 = (f32[32,1152]{1,0:T(8,128)S(1)}, f32[32,1152]{1,0:T(8,128)S(1)}, u32[]{:S(2)}, u32[]{:S(2)}) collective-permute-start(f32[32,1152]{1,0:T(8,128)S(1)} %fusion.16), channel_id=1, source_target_pairs={{0,4},{1,5},{2,6},{3,7},{4,0},{5,1},{6,2},{7,3},{8,12},{9,13},{10,... | collective-permute-start | bytes 442376 | tf_op jit(solution)/shard_map/ppermute | solution.py:22
  46.9 0.3 fusion.1
  47.2 3.7 %collective-permute-done.11 = f32[32,1152]{1,0:T(8,128)S(1)} collective-permute-done((f32[32,1152]{1,0:T(8,128)S(1)}, f32[32,1152]{1,0:T(8,128)S(1)}, u32[]{:S(2)}, u32[]{:S(2)}) %collective-permute-start.11) | collective-permute-done | bytes 147488 | tf_op jit(solution)/shard_map/ppermute | solution.py:22
  53.0 1.5 %collective-permute-start.13 = (f32[32,1152]{1,0:T(8,128)S(1)}, f32[32,1152]{1,0:T(8,128)S(1)}, u32[]{:S(2)}, u32[]{:S(2)}) collective-permute-start(f32[32,1152]{1,0:T(8,128)S(1)} %fusion.15), channel_id=1, source_target_pairs={{0,8},{1,9},{2,10},{3,11},{4,12},{5,13},{6,14},{7,15},{8,0},{9,1},... | collective-permute-start | bytes 442376 | tf_op jit(solution)/shard_map/ppermute | solution.py:22
  54.4 0.7 convolution_reduce_fusion.1
  55.2 5.5 %collective-permute-done.13 = f32[32,1152]{1,0:T(8,128)S(1)} collective-permute-done((f32[32,1152]{1,0:T(8,128)S(1)}, f32[32,1152]{1,0:T(8,128)S(1)}, u32[]{:S(2)}, u32[]{:S(2)}) %collective-permute-start.13) | collective-permute-done | bytes 147488 | tf_op jit(solution)/shard_map/ppermute | solution.py:22
  61.8 0.7 convolution_reduce_fusion
  62.7 0.8 %collective-permute-start.15 = (f32[2048]{0:T(1024)S(1)}, f32[2048]{0:T(1024)S(1)}, u32[]{:S(2)}, u32[]{:S(2)}) collective-permute-start(f32[2048]{0:T(1024)S(1)} %reduce_max.29), channel_id=1, source_target_pairs={{0,2},{1,3},{2,0},{3,1},{4,6},{5,7},{6,4},{7,5},{8,10},{9,11},{10,... | collective-permute-start | bytes 24584 | tf_op jit(solution)/shard_map/ppermute | solution.py:27
  63.5 1.1 %collective-permute-start.14 = (f32[2048]{0:T(1024)S(1)}, f32[2048]{0:T(1024)S(1)}, u32[]{:S(2)}, u32[]{:S(2)}) collective-permute-start(f32[2048]{0:T(1024)S(1)} %reduce_max.29), channel_id=1, source_target_pairs={{0,1},{1,0},{2,3},{3,2},{4,5},{5,4},{6,7},{7,6},{8,9},{9,8},{10,11... | collective-permute-start | bytes 24584 | tf_op jit(solution)/shard_map/ppermute | solution.py:27
  64.5 1.2 %collective-permute-done.16 = f32[2048]{0:T(1024)S(1)} collective-permute-done((f32[2048]{0:T(1024)S(1)}, f32[2048]{0:T(1024)S(1)}, u32[]{:S(2)}, u32[]{:S(2)}) %collective-permute-start.16) | collective-permute-done | bytes 8224 | tf_op jit(solution)/shard_map/ppermute | solution.py:27
  65.7 0.7 collective-permute-done.15
  66.5 3.6 %collective-permute-done.17 = f32[2048]{0:T(1024)S(1)} collective-permute-done((f32[2048]{0:T(1024)S(1)}, f32[2048]{0:T(1024)S(1)}, u32[]{:S(2)}, u32[]{:S(2)}) %collective-permute-start.17) | collective-permute-done | bytes 8224 | tf_op jit(solution)/shard_map/ppermute | solution.py:27
  70.1 0.9 %collective-permute-start.18 = (f32[2048]{0:T(1024)S(1)}, f32[2048]{0:T(1024)S(1)}, u32[]{:S(2)}, u32[]{:S(2)}) collective-permute-start(f32[2048]{0:T(1024)S(1)} %max.18), channel_id=1, source_target_pairs={{0,8},{1,9},{2,10},{3,11},{4,12},{5,13},{6,14},{7,15},{8,0},{9,1},... | collective-permute-start | bytes 24584 | tf_op jit(solution)/shard_map/ppermute | solution.py:27
  71.0 3.7 %collective-permute-done.18 = f32[2048]{0:T(1024)S(1)} collective-permute-done((f32[2048]{0:T(1024)S(1)}, f32[2048]{0:T(1024)S(1)}, u32[]{:S(2)}, u32[]{:S(2)}) %collective-permute-start.18) | collective-permute-done | bytes 8224 | tf_op jit(solution)/shard_map/ppermute | solution.py:27
  74.7 0.6 max.19
  (126 shorter events, 8.5 us)
Async XLA Ops:
  0.6 22.5 %copy-start.1 = (s32[9,32]{1,0:T(8,128)S(1)}, s32[9,32]{1,0:T(8,128)}, u32[]{:S(2)}) copy-start(s32[9,32]{1,0:T(8,128)} %offsets_ref.1) | copy-start | bytes 3460
  1.8 4.7 %collective-permute-start.1 = (f32[1,4480]{1,0:T(1,128)S(1)}, f32[1,4480]{1,0:T(1,128)S(1)}, u32[]{:S(2)}, u32[]{:S(2)}) collective-permute-start(f32[1,4480]{1,0:T(1,128)S(1)} %broadcast_in_dim.535), channel_id=1, source_target_pairs={{0,2},{1,3},{2,0},{3,1},{4,6},{5,7},{6,4},{7,5},{8,10},{9,11},{10,... | collective-permute-start | bytes 53768 | tf_op jit(solution)/shard_map/ppermute | solution.py:27
  4.8 3.2 %collective-permute-start.2 = (f32[1,4480]{1,0:T(1,128)S(1)}, f32[1,4480]{1,0:T(1,128)S(1)}, u32[]{:S(2)}, u32[]{:S(2)}) collective-permute-start(f32[1,4480]{1,0:T(1,128)S(1)} %broadcast_in_dim.535), channel_id=1, source_target_pairs={{0,3},{1,2},{2,1},{3,0},{4,7},{5,6},{6,5},{7,4},{8,11},{9,10},{10,... | collective-permute-start | bytes 53768 | tf_op jit(solution)/shard_map/ppermute | solution.py:27
  4.8 3.2 %collective-permute-start = (f32[1,4480]{1,0:T(1,128)S(1)}, f32[1,4480]{1,0:T(1,128)S(1)}, u32[]{:S(2)}, u32[]{:S(2)}) collective-permute-start(f32[1,4480]{1,0:T(1,128)S(1)} %broadcast_in_dim.535), channel_id=1, source_target_pairs={{0,1},{1,0},{2,3},{3,2},{4,5},{5,4},{6,7},{7,6},{8,9},{9,8},{10,11... | collective-permute-start | bytes 53768 | tf_op jit(solution)/shard_map/ppermute | solution.py:27
  8.0 5.8 %collective-permute-start.5 = (f32[1,4480]{1,0:T(1,128)S(1)}, f32[1,4480]{1,0:T(1,128)S(1)}, u32[]{:S(2)}, u32[]{:S(2)}) collective-permute-start(f32[1,4480]{1,0:T(1,128)S(1)} %add_add_fusion.1), channel_id=1, source_target_pairs={{0,12},{1,13},{2,14},{3,15},{4,8},{5,9},{6,10},{7,11},{8,4},{9,5},... | collective-permute-start | bytes 53768 | tf_op jit(solution)/shard_map/ppermute | solution.py:27
  11.7 4.7 %collective-permute-start.4 = (f32[1,4480]{1,0:T(1,128)S(1)}, f32[1,4480]{1,0:T(1,128)S(1)}, u32[]{:S(2)}, u32[]{:S(2)}) collective-permute-start(f32[1,4480]{1,0:T(1,128)S(1)} %add_add_fusion.1), channel_id=1, source_target_pairs={{0,8},{1,9},{2,10},{3,11},{4,12},{5,13},{6,14},{7,15},{8,0},{9,1},... | collective-permute-start | bytes 53768 | tf_op jit(solution)/shard_map/ppermute | solution.py:27
  11.7 4.7 %collective-permute-start.3 = (f32[1,4480]{1,0:T(1,128)S(1)}, f32[1,4480]{1,0:T(1,128)S(1)}, u32[]{:S(2)}, u32[]{:S(2)}) collective-permute-start(f32[1,4480]{1,0:T(1,128)S(1)} %add_add_fusion.1), channel_id=1, source_target_pairs={{0,4},{1,5},{2,6},{3,7},{4,0},{5,1},{6,2},{7,3},{8,12},{9,13},{10,... | collective-permute-start | bytes 53768 | tf_op jit(solution)/shard_map/ppermute | solution.py:27
  23.1 1.6 %collective-permute-start.6 = (f32[32,2048]{1,0:T(8,128)S(1)}, f32[32,2048]{1,0:T(8,128)S(1)}, u32[]{:S(2)}, u32[]{:S(2)}) collective-permute-start(f32[32,2048]{1,0:T(8,128)S(1)} %get-tuple-element.16), channel_id=1, source_target_pairs={{0,1},{1,0},{2,3},{3,2},{4,5},{5,4},{6,7},{7,6},{8,9},{9,8},{10,11... | collective-permute-start | bytes 786440 | tf_op jit(solution)/shard_map/ppermute | solution.py:22
  25.4 1.2 %copy-start.2 = (s32[8]{0:T(128)S(1)}, s32[8]{0:T(128)}, u32[]{:S(2)}) copy-start(s32[8]{0:T(128)} %param.5) | copy-start | bytes 100
  25.8 7.7 %collective-permute-start.8 = (f32[32,1792]{1,0:T(8,128)S(1)}, f32[32,1792]{1,0:T(8,128)S(1)}, u32[]{:S(2)}, u32[]{:S(2)}) collective-permute-start(f32[32,1792]{1,0:T(8,128)S(1)} %fusion.2), channel_id=1, source_target_pairs={{0,2},{1,3},{2,0},{3,1},{4,6},{5,7},{6,4},{7,5},{8,10},{9,11},{10,... | collective-permute-start | bytes 688136 | tf_op jit(solution)/shard_map/ppermute | solution.py:22
  26.6 1.4 %collective-permute-start.7 = (f32[32,1152]{1,0:T(8,128)S(1)}, f32[32,1152]{1,0:T(8,128)S(1)}, u32[]{:S(2)}, u32[]{:S(2)}) collective-permute-start(f32[32,1152]{1,0:T(8,128)S(1)} %get-tuple-element.17), channel_id=1, source_target_pairs={{0,1},{1,0},{2,3},{3,2},{4,5},{5,4},{6,7},{7,6},{8,9},{9,8},{10,11... | collective-permute-start | bytes 442376 | tf_op jit(solution)/shard_map/ppermute | solution.py:22
  34.5 6.2 %collective-permute-start.10 = (f32[32,1536]{1,0:T(8,128)S(1)}, f32[32,1536]{1,0:T(8,128)S(1)}, u32[]{:S(2)}, u32[]{:S(2)}) collective-permute-start(f32[32,1536]{1,0:T(8,128)S(1)} %fusion.3), channel_id=1, source_target_pairs={{0,4},{1,5},{2,6},{3,7},{4,0},{5,1},{6,2},{7,3},{8,12},{9,13},{10,... | collective-permute-start | bytes 589832 | tf_op jit(solution)/shard_map/ppermute | solution.py:22
  35.5 5.2 %collective-permute-start.9 = (f32[32,1152]{1,0:T(8,128)S(1)}, f32[32,1152]{1,0:T(8,128)S(1)}, u32[]{:S(2)}, u32[]{:S(2)}) collective-permute-start(f32[32,1152]{1,0:T(8,128)S(1)} %fusion.17), channel_id=1, source_target_pairs={{0,2},{1,3},{2,0},{3,1},{4,6},{5,7},{6,4},{7,5},{8,10},{9,11},{10,... | collective-permute-start | bytes 442376 | tf_op jit(solution)/shard_map/ppermute | solution.py:22
  41.7 9.3 %collective-permute-start.12 = (f32[32,1280]{1,0:T(8,128)S(1)}, f32[32,1280]{1,0:T(8,128)S(1)}, u32[]{:S(2)}, u32[]{:S(2)}) collective-permute-start(f32[32,1280]{1,0:T(8,128)S(1)} %fusion.12), channel_id=1, source_target_pairs={{0,8},{1,9},{2,10},{3,11},{4,12},{5,13},{6,14},{7,15},{8,0},{9,1},... | collective-permute-start | bytes 491528 | tf_op jit(solution)/shard_map/ppermute | solution.py:22
  44.7 6.2 %collective-permute-start.11 = (f32[32,1152]{1,0:T(8,128)S(1)}, f32[32,1152]{1,0:T(8,128)S(1)}, u32[]{:S(2)}, u32[]{:S(2)}) collective-permute-start(f32[32,1152]{1,0:T(8,128)S(1)} %fusion.16), channel_id=1, source_target_pairs={{0,4},{1,5},{2,6},{3,7},{4,0},{5,1},{6,2},{7,3},{8,12},{9,13},{10,... | collective-permute-start | bytes 442376 | tf_op jit(solution)/shard_map/ppermute | solution.py:22
  53.0 7.7 %collective-permute-start.13 = (f32[32,1152]{1,0:T(8,128)S(1)}, f32[32,1152]{1,0:T(8,128)S(1)}, u32[]{:S(2)}, u32[]{:S(2)}) collective-permute-start(f32[32,1152]{1,0:T(8,128)S(1)} %fusion.15), channel_id=1, source_target_pairs={{0,8},{1,9},{2,10},{3,11},{4,12},{5,13},{6,14},{7,15},{8,0},{9,1},... | collective-permute-start | bytes 442376 | tf_op jit(solution)/shard_map/ppermute | solution.py:22
  62.5 12.7 %copy-start = (f32[32,2048]{1,0:T(8,128)}, f32[32,2048]{1,0:T(8,128)S(1)}, u32[]{:S(2)}) copy-start(f32[32,2048]{1,0:T(8,128)S(1)} %constant_dynamic-update-slice_fusion) | copy-start | bytes 786436
  62.6 3.1 %collective-permute-start.16 = (f32[2048]{0:T(1024)S(1)}, f32[2048]{0:T(1024)S(1)}, u32[]{:S(2)}, u32[]{:S(2)}) collective-permute-start(f32[2048]{0:T(1024)S(1)} %reduce_max.29), channel_id=1, source_target_pairs={{0,3},{1,2},{2,1},{3,0},{4,7},{5,6},{6,5},{7,4},{8,11},{9,10},{10,... | collective-permute-start | bytes 24584 | tf_op jit(solution)/shard_map/ppermute | solution.py:27
  62.7 3.7 %collective-permute-start.15 = (f32[2048]{0:T(1024)S(1)}, f32[2048]{0:T(1024)S(1)}, u32[]{:S(2)}, u32[]{:S(2)}) collective-permute-start(f32[2048]{0:T(1024)S(1)} %reduce_max.29), channel_id=1, source_target_pairs={{0,2},{1,3},{2,0},{3,1},{4,6},{5,7},{6,4},{7,5},{8,10},{9,11},{10,... | collective-permute-start | bytes 24584 | tf_op jit(solution)/shard_map/ppermute | solution.py:27
  63.5 2.9 %collective-permute-start.14 = (f32[2048]{0:T(1024)S(1)}, f32[2048]{0:T(1024)S(1)}, u32[]{:S(2)}, u32[]{:S(2)}) collective-permute-start(f32[2048]{0:T(1024)S(1)} %reduce_max.29), channel_id=1, source_target_pairs={{0,1},{1,0},{2,3},{3,2},{4,5},{5,4},{6,7},{7,6},{8,9},{9,8},{10,11... | collective-permute-start | bytes 24584 | tf_op jit(solution)/shard_map/ppermute | solution.py:27
  66.4 3.7 %collective-permute-start.17 = (f32[2048]{0:T(1024)S(1)}, f32[2048]{0:T(1024)S(1)}, u32[]{:S(2)}, u32[]{:S(2)}) collective-permute-start(f32[2048]{0:T(1024)S(1)} %maximum_maximum_fusion), channel_id=1, source_target_pairs={{0,4},{1,5},{2,6},{3,7},{4,0},{5,1},{6,2},{7,3},{8,12},{9,13},{10,... | collective-permute-start | bytes 24584 | tf_op jit(solution)/shard_map/ppermute | solution.py:27
  70.1 4.5 %collective-permute-start.18 = (f32[2048]{0:T(1024)S(1)}, f32[2048]{0:T(1024)S(1)}, u32[]{:S(2)}, u32[]{:S(2)}) collective-permute-start(f32[2048]{0:T(1024)S(1)} %max.18), channel_id=1, source_target_pairs={{0,8},{1,9},{2,10},{3,11},{4,12},{5,13},{6,14},{7,15},{8,0},{9,1},... | collective-permute-start | bytes 24584 | tf_op jit(solution)/shard_map/ppermute | solution.py:27
